TPU v7x, 32 devices: a whole 2x2x4 slice. The times are simulated.
32 devices in a mesh: groups: 2 (over y), seq: 8 (over z, x), wg: 2 (over core).
Axes of the slice: x: 2, y: 2, z: 4, core: 2. Of those that a mesh axis runs over, the one named last changes fastest.
Arguments:
- generator_rows: bfloat16 [2048, 2304], P(('groups', 'seq'), 'wg'), parts along dimension 0, may hold values from -120 to 120, as said below
- pre_gain: float32 [2304], replicated, may hold values from 0.1 to 1.9
- query_weight: bfloat16 [2304, 2048], P('seq', 'wg'), may hold values from -2 to 2, as said below
- key_weight: bfloat16 [2304, 1024], P('seq', 'wg'), may hold values from -2 to 2, as said below
- value_weight: bfloat16 [2304, 1024], P('seq', 'wg'), may hold values from -0.125 to 0.125
- out_weight: bfloat16 [2048, 2304], P('wg', 'seq'), may hold values from -0.125 to 0.125
- post_gain: float32 [2304], replicated, may hold values from 0.1 to 1.9
- final_gain: float32 [2304], replicated, may hold values from 0.1 to 1.9
- label_table: bfloat16 [64, 2304], replicated, may hold values from -0.375 to 0.375
- lengths: int32 [16], P('groups'), parts along dimension 0, may hold values from 65 to 127
- label_index: int32 [16], P('groups'), parts along dimension 0, may hold values from 0 to 63
Outputs:
- input_grad: bfloat16 [2048, 2304], P(('groups', 'seq'), 'wg'), parts along dimension 0
There are 2 independent parts, one for each index of `groups`. A program takes and returns all parts, laid end to end along the dimension named above; an argument that names none is the same for every part. Nothing has to cross between parts.
Inputs may be any that keep to these rules, and one draw needn't show every extreme that they name: `generator_rows`: finite real entries. `query_weight`: finite real entries. `key_weight`: finite real entries.
All inputs are finite; a program needn't handle non-finite values.
Results may differ from a plain program's by a relative error of at most 0.017.
The roundings to bfloat16 on the way count: a program that leaves them out, or rounds other values in their place, can miss the bound.
Values may be sent and summed in bfloat16 or wider, within the bound.
No kernel may reach another device: no remote copies, remote signals or barrier semaphores. Data moves between devices by JAX's collectives and lax.ppermute only.
A program may use at most 128 MiB of HBM per device.

v0:
```python
import jax
import jax.numpy as jnp
from jax import lax
from jax.sharding import PartitionSpec as P

HD = 128
LABELS = 64


EPSILON = 1e-06
ATTEND_CAP = 50.0
LABEL_CAP = 30.0
QUERY_SCALE = 1.0 / 12.0


def rope_tables(positions, head_width):
    frequency = 10000.0 ** (-2.0 * jnp.arange(head_width // 2, dtype=jnp.float32) / head_width)
    angles = positions.astype(jnp.float32)[:, None] * frequency[None, :]
    return (jnp.cos(angles), jnp.sin(angles))


def rotate(values, cos_table, sin_table):
    half_width = values.shape[-1] // 2
    lower_part = values[..., :half_width]
    upper_part = values[..., half_width:]
    return jnp.concatenate(
        [
            lower_part * cos_table - upper_part * sin_table,
            upper_part * cos_table + lower_part * sin_table,
        ],
        axis=-1,
    )


def rotate_back(values, cos_table, sin_table):
    half_width = values.shape[-1] // 2
    lower_part = values[..., :half_width]
    upper_part = values[..., half_width:]
    return jnp.concatenate(
        [
            lower_part * cos_table + upper_part * sin_table,
            upper_part * cos_table - lower_part * sin_table,
        ],
        axis=-1,
    )


def times_transposed(left_side, right_side):
    return lax.dot_general(
        left_side, right_side, (((1,), (1,)), ((), ())), preferred_element_type=jnp.float32
    )


def shards(
    generator_rows,
    pre_gain,
    query_weight,
    key_weight,
    value_weight,
    out_weight,
    post_gain,
    final_gain,
    label_table,
    lengths,
    label_index,
):
    seq_rank = lax.axis_index("seq")
    core_rank = lax.axis_index("wg")
    whole_rows = lax.all_gather(generator_rows, "wg", axis=1, tiled=True)
    guard_rows = lax.all_to_all(whole_rows, "seq", split_axis=0, concat_axis=0, tiled=True)
    w_query, w_key, w_value, w_out = (
        lax.all_gather(query_weight, "seq", axis=0, tiled=True),
        lax.all_gather(key_weight, "seq", axis=0, tiled=True),
        lax.all_gather(value_weight, "seq", axis=0, tiled=True),
        lax.all_gather(out_weight, "seq", axis=1, tiled=True),
    )
    tok_rows = guard_rows.shape[0]
    half_width = generator_rows.shape[1]
    local_heads = w_query.shape[1] // HD
    local_kv = w_key.shape[1] // HD
    group_size = local_heads // local_kv
    length = lax.dynamic_index_in_dim(lengths, seq_rank, 0, keepdims=False)
    target = lax.dynamic_index_in_dim(label_index, seq_rank, 0, keepdims=False)
    offsets = jnp.arange(tok_rows, dtype=jnp.int32)
    cos_table, sin_table = rope_tables(offsets, HD)
    inputs = guard_rows.astype(jnp.float32)
    scale_in = lax.rsqrt(jnp.mean(inputs * inputs, axis=-1, keepdims=True) + EPSILON)
    normed = (inputs * scale_in * pre_gain).astype(jnp.bfloat16)
    query_proj = (
        jnp.dot(normed, w_query, preferred_element_type=jnp.float32)
        .reshape(tok_rows, local_heads, HD)
        .transpose(1, 0, 2)
    )
    queries = (rotate(query_proj, cos_table, sin_table) * QUERY_SCALE).astype(jnp.bfloat16)
    key_proj = (
        jnp.dot(normed, w_key, preferred_element_type=jnp.float32)
        .reshape(tok_rows, local_kv, HD)
        .transpose(1, 0, 2)
    )
    keys_own = rotate(key_proj, cos_table, sin_table).astype(jnp.bfloat16)
    values_own = (
        jnp.dot(normed, w_value, preferred_element_type=jnp.float32)
        .astype(jnp.bfloat16)
        .reshape(tok_rows, local_kv, HD)
        .transpose(1, 0, 2)
    )
    allowed = (offsets[None, :] <= offsets[:, None]) & (offsets[None, :] < length)
    query_four = queries.reshape(local_kv, group_size, tok_rows, HD)
    raw_scores = jnp.einsum(
        "kgid,kjd->kgij", query_four, keys_own, preferred_element_type=jnp.float32
    )
    capped = jnp.tanh(raw_scores / ATTEND_CAP)
    weight_exp = jnp.where(allowed[None, None], jnp.exp(ATTEND_CAP * capped), 0.0)
    soft_weights = weight_exp / jnp.sum(weight_exp, axis=-1, keepdims=True)
    attend = soft_weights.astype(jnp.bfloat16)
    context = jnp.einsum(
        "kgij,kjd->kgid", attend, values_own, preferred_element_type=jnp.float32
    ).astype(jnp.bfloat16)
    context_rows = (
        context.reshape(local_heads, tok_rows, HD)
        .transpose(1, 0, 2)
        .reshape(tok_rows, local_heads * HD)
    )
    out_part = jnp.dot(context_rows, w_out, preferred_element_type=jnp.float32)
    attention = lax.psum(out_part.astype(jnp.bfloat16), "wg").astype(jnp.float32)
    scale_attn = lax.rsqrt(jnp.mean(attention * attention, axis=-1, keepdims=True) + EPSILON)
    mixed_rows = inputs + attention * scale_attn * post_gain
    scale_out = lax.rsqrt(jnp.mean(mixed_rows * mixed_rows, axis=-1, keepdims=True) + EPSILON)
    final_rows = (mixed_rows * scale_out * final_gain).astype(jnp.bfloat16)
    logits = times_transposed(final_rows, label_table)
    label_cap = jnp.tanh(logits / LABEL_CAP)
    label_exp = jnp.exp(LABEL_CAP * label_cap)
    chance = label_exp / jnp.sum(label_exp, axis=-1, keepdims=True)
    live_rows = (offsets < length)[:, None]
    onehot = (jnp.arange(LABELS, dtype=jnp.int32) == target).astype(jnp.float32)[None, :]
    grad_logit = (
        jnp.where(live_rows, chance - onehot, 0.0) * (1.0 - label_cap * label_cap)
    ).astype(jnp.bfloat16)
    grad_final = jnp.dot(grad_logit, label_table, preferred_element_type=jnp.float32)
    scaled_final = grad_final * final_gain
    cube_out = scale_out * scale_out * scale_out
    grad_mixed = scale_out * scaled_final - mixed_rows * cube_out * jnp.mean(
        scaled_final * mixed_rows, axis=-1, keepdims=True
    )
    scaled_post = grad_mixed * post_gain
    cube_attn = scale_attn * scale_attn * scale_attn
    grad_attention = scale_attn * scaled_post - attention * cube_attn * jnp.mean(
        scaled_post * attention, axis=-1, keepdims=True
    )
    grad_context = times_transposed(grad_attention.astype(jnp.bfloat16), w_out).astype(jnp.bfloat16)
    grad_four = grad_context.reshape(tok_rows, local_kv, group_size, HD).transpose(1, 2, 0, 3)
    grad_prob = jnp.einsum(
        "kgid,kjd->kgij", grad_four, values_own, preferred_element_type=jnp.float32
    )
    grad_score = (
        soft_weights
        * (grad_prob - jnp.sum(soft_weights * grad_prob, axis=-1, keepdims=True))
        * (1.0 - capped * capped)
    )
    score_round = grad_score.astype(jnp.bfloat16)
    grad_query = jnp.einsum(
        "kgij,kjd->kgid", score_round, keys_own, preferred_element_type=jnp.float32
    ).reshape(local_heads, tok_rows, HD)
    grad_queries = rotate_back(grad_query * QUERY_SCALE, cos_table, sin_table).astype(jnp.bfloat16)
    grad_key = jnp.einsum(
        "kgij,kgid->kjd", score_round, query_four, preferred_element_type=jnp.float32
    )
    grad_value = jnp.einsum("kgij,kgid->kjd", attend, grad_four, preferred_element_type=jnp.float32)
    grad_keys = rotate_back(grad_key, cos_table, sin_table).astype(jnp.bfloat16)
    grad_values = grad_value.astype(jnp.bfloat16)
    query_rows = grad_queries.transpose(1, 0, 2).reshape(tok_rows, local_heads * HD)
    key_rows = grad_keys.transpose(1, 0, 2).reshape(tok_rows, local_kv * HD)
    value_rows = grad_values.transpose(1, 0, 2).reshape(tok_rows, local_kv * HD)
    grad_part = (
        times_transposed(query_rows, w_query)
        + times_transposed(key_rows, w_key)
        + times_transposed(value_rows, w_value)
    )
    cube_in = scale_in * scale_in * scale_in
    grad_normed = lax.psum(grad_part.astype(jnp.bfloat16), "wg").astype(jnp.float32)
    scaled_in = grad_normed * pre_gain
    row_stat = jnp.mean(scaled_in * inputs, axis=-1, keepdims=True)
    grad_full = scale_in * scaled_in - inputs * cube_in * row_stat + grad_mixed
    grad_rows = lax.dynamic_slice_in_dim(grad_full, core_rank * half_width, half_width, 1)
    return lax.all_to_all(
        grad_rows.astype(jnp.bfloat16), "seq", split_axis=0, concat_axis=0, tiled=True
    )


def solution(mesh):
    return jax.shard_map(
        shards,
        mesh=mesh,
        in_specs=(
            P(("groups", "seq"), "wg"),
            P(),
            P("seq", "wg"),
            P("seq", "wg"),
            P("seq", "wg"),
            P("wg", "seq"),
            P(),
            P(),
            P(),
            P("groups"),
            P("groups"),
        ),
        out_specs=P(("groups", "seq"), "wg"),
        check_vma=False,
    )
```

profile of v0, /device:TPU:0, one launch (start us, length us, event | category | flops | bytes accessed | tf_op | source)
XLA Modules:
  0.0 376.7 jit_solution(12886535654456239035)
XLA Ops:
  6.5 0.7 all-gather.7.cloned.1.call-update
  7.3 0.7 all-gather.9.cloned.1.call-update
  8.1 0.7 all-gather.5.cloned.1.call-update
  8.8 0.5 all-gather.11.cloned.1.call-update
  9.4 2.4 all_gather.15
  11.8 7.2 %all-to-all-start = ((bf16[8,16,2304]{2,1,0:T(8,128)(2,1)}), bf16[8,16,2304]{2,1,0:T(8,128)(2,1)S(1)}, u32[]{:S(2)}, u32[]{:S(2)}) async-start(bf16[8,16,2304]{2,1,0:T(8,128)(2,1)} %bitcast), calls=%async_computation | async-start | bytes 1179648 | tf_op jit(solution)/shard_map/all_to_all | solution.py:70
  19.0 0.6 dynamic_slice.10
  19.6 0.7 iota_compare_fusion.1
  20.6 24.1 %all-to-all-done = bf16[8,16,2304]{2,1,0:T(8,128)(2,1)S(1)} async-done(((bf16[8,16,2304]{2,1,0:T(8,128)(2,1)}), bf16[8,16,2304]{2,1,0:T(8,128)(2,1)S(1)}, u32[]{:S(2)}, u32[]{:S(2)}) %all-to-all-start) | async-done | bytes 589856 | tf_op jit(solution)/shard_map/all_to_all | solution.py:70
  44.9 1.0 multiply_convert_fusion.2
  46.0 1.2 bitcast_convert_fusion
  47.1 25.5 %all-gather.7.cloned.1.call-done = bf16[2304,512]{1,0:T(8,128)(2,1)} async-done(((bf16[288,512]{1,0:T(8,128)(2,1)}), bf16[2304,512]{1,0:T(8,128)(2,1)}) %all-gather.7.cloned.1.call-update) | async-done | bytes 2359312 | tf_op jit(solution)/shard_map/all_gather | solution.py:73
  72.7 2.8 copy.15
  75.5 50.0 %all-gather.9.cloned.1.call-done = bf16[2304,512]{1,0:T(8,128)(2,1)} async-done(((bf16[288,512]{1,0:T(8,128)(2,1)}), bf16[2304,512]{1,0:T(8,128)(2,1)}) %all-gather.9.cloned.1.call-update) | async-done | bytes 2359312 | tf_op jit(solution)/shard_map/all_gather | solution.py:74
  125.5 2.5 convolution_convert_fusion.3
  128.1 0.7 copy.50
  128.8 1.8 convolution_bitcast_fusion.3
  130.7 75.5 %all-gather.5.cloned.1.call-done = bf16[2304,1024]{1,0:T(8,128)(2,1)} async-done(((bf16[288,1024]{1,0:T(8,128)(2,1)}), bf16[2304,1024]{1,0:T(8,128)(2,1)}) %all-gather.5.cloned.1.call-update) | async-done | bytes 4718608 | tf_op jit(solution)/shard_map/all_gather | solution.py:72
  206.1 6.8 %copy.12 = bf16[1024,2304]{1,0:T(8,128)(2,1)} copy(bf16[1024,2304]{0,1:T(8,128)(2,1)} %bitcast.103) | data formatting | bytes 9437184 | tf_op jit(solution)/shard_map/dot_general | solution.py:90
  213.0 4.0 %convolution_bitcast_fusion = f32[8,128,128]{1,2,0:T(8,128)S(1)} fusion(bf16[128,2304,1]{1,0,2:T(8,128)(2,1)S(1)} %bitcast.108, bf16[8,128,2304]{2,1,0:T(8,128)(2,1)} %bitcast.104), kind=kOutput, calls=%fused_computation.16 | convolution fusion | flops 603979776 | bytes 5832704 | tf_op jit(solution)/shard_map/dot_general | solution.py:90
  217.7 0.4 fusion.34
  218.1 0.3 copy-done.11
  218.4 0.3 convolution_convert_fusion.1
  218.7 0.2 copy-done.19
  218.9 67.3 %all-gather.11.cloned.1.call-done = bf16[1024,2304]{0,1:T(8,128)(2,1)} async-done(((bf16[1024,288]{0,1:T(8,128)(2,1)}), bf16[1024,2304]{0,1:T(8,128)(2,1)}) %all-gather.11.cloned.1.call-update) | async-done | bytes 4718608 | tf_op jit(solution)/shard_map/all_gather | solution.py:75
  286.3 4.9 %convolution_convert_fusion = bf16[128,2304]{1,0:T(8,128)(2,1)} fusion(bf16[128,1024]{0,1:T(8,128)(2,1)S(1)} %bitcast.118, bf16[1024,2304]{0,1:T(8,128)(2,1)} %all-gather.11.cloned.1.call-done), kind=kOutput, calls=%fused_computation.5 | convolution fusion | flops 604274688 | bytes 5570560 | tf_op jit(solution)/shard_map/dot_general | solution.py:124
  291.4 0.6 dynamic_slice.11
  292.0 0.6 compare_convert_fusion
  292.7 15.7 %all-reduce.3.cloned.1.call-done = bf16[128,2304]{1,0:T(8,128)(2,1)} async-done(((bf16[128,2304]{1,0:T(8,128)(2,1)}), bf16[128,2304]{1,0:T(8,128)(2,1)}) %all-reduce.3.cloned.1.call-update) | async-done | bytes 589840 | tf_op jit(solution)/shard_map/psum | solution.py:125
  308.3 1.3 fusion.7
  309.6 1.5 multiply_reduce_fusion.2
  311.1 0.4 fusion.43
  311.6 0.5 multiply_reduce_fusion.1
  312.2 0.5 fusion.13
  312.7 1.3 copy-done.1
  314.0 1.2 convolution_convert_fusion.2
  315.4 2.0 fusion.14
  317.7 1.7 convolution_bitcast_fusion.2
  319.4 2.6 convolution_multiply_fusion.1
  322.0 1.2 copy.24
  323.4 4.2 %fusion.66 = f32[128,2304]{1,0:T(8,128)S(1)} fusion(bf16[128,1024]{0,1:T(8,128)(2,1)S(1)} %bitcast.116, bf16[2304,1024]{1,0:T(8,128)(2,1)} %all-gather.5.cloned.1.call-done), kind=kOutput, calls=%fused_computation.121 | convolution fusion | flops 603979776 | bytes 6160384 | tf_op jit(solution)/shard_map/dot_general | solution.py:49
  327.6 0.9 convolution_add_fusion.1
  328.6 0.7 copy-done.4
  329.3 1.7 fusion.1
  331.1 20.2 %all-reduce.5.cloned.1.call-done = bf16[128,2304]{1,0:T(8,128)(2,1)} async-done(((bf16[128,2304]{1,0:T(8,128)(2,1)}), bf16[128,2304]{1,0:T(8,128)(2,1)}) %all-reduce.5.cloned.1.call-update) | async-done | bytes 589840 | tf_op jit(solution)/shard_map/psum | solution.py:180
  351.2 1.3 multiply_reduce_fusion
  352.8 16.4 %all_to_all.21 = bf16[8,16,1152]{2,1,0:T(8,128)(2,1)S(1)} all-to-all(bf16[8,16,1152]{2,1,0:T(8,128)(2,1)S(1)} %bitcast.110), channel_id=1, replica_groups=mesh['groups'=2,'seq'=8,'wg'=2] {'seq'}, dimensions={0} | all-to-all | bytes 589824 | tf_op jit(solution)/shard_map/all_to_all | solution.py:185
  369.2 0.7 copy.54
  (73 shorter events, 2.7 us)
Async XLA Ops:
  6.5 304.6 %copy-start = (bf16[64,2304]{1,0:T(8,128)(2,1)S(1)}, bf16[64,2304]{1,0:T(8,128)(2,1)}, u32[]{:S(2)}) copy-start(bf16[64,2304]{1,0:T(8,128)(2,1)} %param.19) | copy-start | bytes 884740
  6.5 2.8 copy-start.7
  6.5 66.1 %all-gather.7.cloned.1.call-start = ((), (), s32[]{:S(2)}) async-start(), calls=%async_computation.3 | async-start | bytes 2654208 | tf_op jit(solution)/shard_map/all_gather | solution.py:73
  7.3 118.2 %all-gather.9.cloned.1.call-start = ((), (), s32[]{:S(2)}) async-start(), calls=%async_computation.4 | async-start | bytes 2654208 | tf_op jit(solution)/shard_map/all_gather | solution.py:74
  8.0 198.1 %all-gather.5.cloned.1.call-start = ((), (), s32[]{:S(2)}) async-start(), calls=%async_computation.2 | async-start | bytes 5308416 | tf_op jit(solution)/shard_map/all_gather | solution.py:72
  8.7 277.5 %all-gather.11.cloned.1.call-start = ((), (), s32[]{:S(2)}) async-start(), calls=%async_computation.5 | async-start | bytes 5308416 | tf_op jit(solution)/shard_map/all_gather | solution.py:75
  9.3 9.7 %copy-start.17 = (s32[8]{0:T(128)S(1)}, s32[8]{0:T(128)}, u32[]{:S(2)}) copy-start(s32[8]{0:T(128)} %param.20) | copy-start | bytes 100
  9.3 35.6 %copy-start.12 = (f32[2304]{0:T(1024)S(1)}, f32[2304]{0:T(1024)}, u32[]{:S(2)}) copy-start(f32[2304]{0:T(1024)} %param.12) | copy-start | bytes 27652
  11.8 32.8 %all-to-all-start = ((bf16[8,16,2304]{2,1,0:T(8,128)(2,1)}), bf16[8,16,2304]{2,1,0:T(8,128)(2,1)S(1)}, u32[]{:S(2)}, u32[]{:S(2)}) async-start(bf16[8,16,2304]{2,1,0:T(8,128)(2,1)} %bitcast), calls=%async_computation | async-start | bytes 1179648 | tf_op jit(solution)/shard_map/all_to_all | solution.py:70
  19.0 289.3 %all-reduce.3.cloned.1.call-start = ((), (), s32[]{:S(2)}) async-start(), calls=%async_computation.6 | async-start | bytes 1179648 | tf_op jit(solution)/shard_map/psum | solution.py:125
  130.7 87.0 %copy-start.14 = (bf16[4,128,64]{1,2,0:T(8,128)(2,1)}, bf16[4,128,64]{1,2,0:T(8,128)(2,1)S(1)}, u32[]{:S(2)}) copy-start(bf16[4,128,64]{1,2,0:T(8,128)(2,1)S(1)} %get-tuple-element.18) | copy-start | bytes 196612
  206.1 6.8 %copy-start.6 = (bf16[8,16,2304]{2,1,0:T(8,128)(2,1)S(1)}, bf16[8,16,2304]{2,1,0:T(8,128)(2,1)}, u32[]{:S(2)}) copy-start(bf16[8,16,2304]{2,1,0:T(8,128)(2,1)} %multiply_convert_fusion.2) | copy-start | bytes 1769476
  217.5 0.9 copy-start.11
  217.7 1.0 copy-start.8
  218.1 0.8 copy-start.19
  218.1 0.8 copy-start.20
  286.3 5.2 %copy-start.18 = (s32[8]{0:T(128)S(1)}, s32[8]{0:T(128)}, u32[]{:S(2)}) copy-start(s32[8]{0:T(128)} %param.21) | copy-start | bytes 100
  291.1 18.4 %copy-start.13 = (f32[2304]{0:T(1024)S(1)}, f32[2304]{0:T(1024)}, u32[]{:S(2)}) copy-start(f32[2304]{0:T(1024)} %param.17) | copy-start | bytes 27652
  291.2 60.1 %all-reduce.5.cloned.1.call-start = ((), (), s32[]{:S(2)}) async-start(), calls=%async_computation.7 | async-start | bytes 1179648 | tf_op jit(solution)/shard_map/psum | solution.py:180
  309.6 1.5 copy-start.16
  311.1 1.1 copy-start.2
  311.6 2.4 copy-start.1
  314.0 1.4 copy-start.21
  315.4 2.2 copy-start.9
  317.7 1.8 copy-start.15
  323.4 4.2 %copy-start.3 = (bf16[2304,512]{1,0:T(8,128)(2,1)S(1)}, bf16[2304,512]{1,0:T(8,128)(2,1)}, u32[]{:S(2)}) copy-start(bf16[2304,512]{1,0:T(8,128)(2,1)} %all-gather.7.cloned.1.call-done) | copy-start | bytes 7077892
  327.6 1.7 copy-start.4
  327.6 1.7 copy-start.10
  331.1 21.5 %copy-start.5 = (f32[128,2304]{1,0:T(8,128)S(1)}, f32[128,2304]{1,0:T(8,128)}, u32[]{:S(2)}) copy-start(f32[128,2304]{1,0:T(8,128)} %bitcast_convert_fusion) | copy-start | bytes 3538948
Sparse Core Ops, SparseCore 0:
  9.5 63.0 all-gather.6
  74.9 50.6 all-gather.8
  127.7 78.4 all-gather.4
  208.2 78.0 all-gather.10
  291.3 16.9 all-reduce.2
  331.2 20.0 all-reduce.4
where the time goes:
time: 378 us; the launch traced here: 377 us
  waiting for transfers between devices  281 us (74%)
  matrix products  29.5 us (8%)
  blocking collectives  18.8 us (5%)
  local copies, waits for them, and re-layouts  16.9 us (4%)
  between operations  13.9 us (4%)
  other arithmetic  9.24 us (2%)
  starting transfers between devices  7.55 us (2%)
    all_gather x1, waiting for transfers between devices, shards(): lax.all_gather(query_weight, 'seq', axis=0, tiled=True)  75.5 us
    all_gather x1, waiting for transfers between devices, shards(): lax.all_gather(out_weight, 'seq', axis=1, tiled=True)  67.3 us
    all_gather x1, waiting for transfers between devices, shards(): lax.all_gather(value_weight, 'seq', axis=0, tiled=True)  50 us
    all_gather x1, waiting for transfers between devices, shards(): lax.all_gather(key_weight, 'seq', axis=0, tiled=True)  25.5 us
    all_to_all x1, waiting for transfers between devices, shards(): lax.all_to_all(whole_rows, 'seq', split_axis=0, concat_axis=0, tiled=True)  24.1 us
    psum x1, waiting for transfers between devices, shards(): lax.psum(grad_part.astype(jnp.bfloat16), 'wg').astype(jnp.float32)  20.2 us
    all_to_all x1, blocking collectives, shards(): lax.all_to_all(grad_rows.astype(jnp.bfloat16), 'seq', split_axis=0, conca...  16.4 us
    psum x1, waiting for transfers between devices, shards(): lax.psum(out_part.astype(jnp.bfloat16), 'wg').astype(jnp.float32)  15.7 us
  transfers between devices with their start and end apart: 7, of which 7 were waited for; matrix products, arithmetic and copies ran while one was open for 7% of the time, Pallas kernels for 0%

commit v1 on v0

--- a/solution.py
+++ b/solution.py
@@ -49,6 +49,11 @@
     return lax.dot_general(
         left_side, right_side, (((1,), (1,)), ((), ())), preferred_element_type=jnp.float32
     )
+
+
+def pair_sum(rounded_part):
+    other = lax.ppermute(rounded_part, "wg", perm=[(0, 1), (1, 0)])
+    return rounded_part.astype(jnp.float32) + other.astype(jnp.float32)
 
 
 def shards(
@@ -68,12 +73,14 @@
     core_rank = lax.axis_index("wg")
     whole_rows = lax.all_gather(generator_rows, "wg", axis=1, tiled=True)
     guard_rows = lax.all_to_all(whole_rows, "seq", split_axis=0, concat_axis=0, tiled=True)
-    w_query, w_key, w_value, w_out = (
-        lax.all_gather(query_weight, "seq", axis=0, tiled=True),
-        lax.all_gather(key_weight, "seq", axis=0, tiled=True),
-        lax.all_gather(value_weight, "seq", axis=0, tiled=True),
-        lax.all_gather(out_weight, "seq", axis=1, tiled=True),
-    )
+    q_cols = query_weight.shape[1]
+    k_cols = key_weight.shape[1]
+    packed = jnp.concatenate([query_weight, key_weight, value_weight, out_weight.T], axis=1)
+    gathered = lax.all_gather(packed, "seq", axis=0, tiled=True)
+    w_query = gathered[:, :q_cols]
+    w_key = gathered[:, q_cols:q_cols + k_cols]
+    w_value = gathered[:, q_cols + k_cols:q_cols + 2 * k_cols]
+    w_out_t = gathered[:, q_cols + 2 * k_cols:]
     tok_rows = guard_rows.shape[0]
     half_width = generator_rows.shape[1]
     local_heads = w_query.shape[1] // HD
@@ -121,8 +128,8 @@
         .transpose(1, 0, 2)
         .reshape(tok_rows, local_heads * HD)
     )
-    out_part = jnp.dot(context_rows, w_out, preferred_element_type=jnp.float32)
-    attention = lax.psum(out_part.astype(jnp.bfloat16), "wg").astype(jnp.float32)
+    out_part = times_transposed(context_rows, w_out_t)
+    attention = pair_sum(out_part.astype(jnp.bfloat16))
     scale_attn = lax.rsqrt(jnp.mean(attention * attention, axis=-1, keepdims=True) + EPSILON)
     mixed_rows = inputs + attention * scale_attn * post_gain
     scale_out = lax.rsqrt(jnp.mean(mixed_rows * mixed_rows, axis=-1, keepdims=True) + EPSILON)
@@ -147,7 +154,9 @@
     grad_attention = scale_attn * scaled_post - attention * cube_attn * jnp.mean(
         scaled_post * attention, axis=-1, keepdims=True
     )
-    grad_context = times_transposed(grad_attention.astype(jnp.bfloat16), w_out).astype(jnp.bfloat16)
+    grad_context = jnp.dot(
+        grad_attention.astype(jnp.bfloat16), w_out_t, preferred_element_type=jnp.float32
+    ).astype(jnp.bfloat16)
     grad_four = grad_context.reshape(tok_rows, local_kv, group_size, HD).transpose(1, 2, 0, 3)
     grad_prob = jnp.einsum(
         "kgid,kjd->kgij", grad_four, values_own, preferred_element_type=jnp.float32
@@ -177,7 +186,7 @@
         + times_transposed(value_rows, w_value)
     )
     cube_in = scale_in * scale_in * scale_in
-    grad_normed = lax.psum(grad_part.astype(jnp.bfloat16), "wg").astype(jnp.float32)
+    grad_normed = pair_sum(grad_part.astype(jnp.bfloat16))
     scaled_in = grad_normed * pre_gain
     row_stat = jnp.mean(scaled_in * inputs, axis=-1, keepdims=True)
     grad_full = scale_in * scaled_in - inputs * cube_in * row_stat + grad_mixed

time: 378 us -> 301 us (0.80)
  waiting for transfers between devices: 281 us -> 197 us
  local copies, waits for them, and re-layouts: 16.9 us -> 25.2 us
    all_gather x4 -> x1, waiting for transfers between devices: 218 us -> 165 us  [shards(): gathered = lax.all_gather(packed, 'seq', axis=0, tiled=True)]
    psum x2 -> x0, waiting for transfers between devices: 35.8 us -> none  [the longest x1 20.2 us: shards(): lax.psum(grad_part.astype(jnp.bfloat16), 'wg').astype(jnp.float32)]
    all_to_all x1, waiting for transfers between devices: 24.1 us -> 29.6 us  [shards(): lax.all_to_all(whole_rows, 'seq', split_axis=0, concat_axis=0, tiled=True)]
    dot_general x5, matrix products: 8.52 us -> 13.7 us  [times_transposed(): lax.dot_general(left_side, right_side, (((1,), (1,)), ((), ())), preferre...]
    dot_general x1 -> x2, local copies, waits for them, and re-layouts: 6.81 us -> 11.6 us  [shards(): jnp.dot(normed, w_query, preferred_element_type=jnp.float32)]
  transfers between devices with their start and end apart: 7 -> 4, of which waited for: 7 -> 4; matrix products, arithmetic and copies ran while one was open for 7% -> 2% of each run, Pallas kernels for 0% -> 0%
where the time goes in v1:
time: 301 us; the launch traced here: 300 us
  waiting for transfers between devices  197 us (65%)
  matrix products  32 us (11%)
  local copies, waits for them, and re-layouts  25.2 us (8%)
  blocking collectives  15.9 us (5%)
  between operations  13.8 us (5%)
  other arithmetic  8.41 us (3%)
  starting transfers between devices  7.44 us (2%)
    all_gather x1, waiting for transfers between devices, shards(): gathered = lax.all_gather(packed, 'seq', axis=0, tiled=True)  165 us
    all_to_all x1, waiting for transfers between devices, shards(): lax.all_to_all(whole_rows, 'seq', split_axis=0, concat_axis=0, tiled=True)  29.6 us
    dot_general x5, matrix products, times_transposed(): lax.dot_general(left_side, right_side, (((1,), (1,)), ((), ())), preferre...  13.7 us
    all_to_all x1, blocking collectives, shards(): lax.all_to_all(grad_rows.astype(jnp.bfloat16), 'seq', split_axis=0, conca...  13.3 us
    dot_general x2, local copies, waits for them, and re-layouts, shards(): jnp.dot(normed, w_query, preferred_element_type=jnp.float32)  11.6 us
    all_to_all x1, starting transfers between devices, shards(): lax.all_to_all(whole_rows, 'seq', split_axis=0, concat_axis=0, tiled=True)  7.17 us
    dot_general x2, local copies, waits for them, and re-layouts, shards(): jnp.dot(normed, w_key, preferred_element_type=jnp.float32)  6.22 us
  transfers between devices with their start and end apart: 4, of which 4 were waited for; matrix products, arithmetic and copies ran while one was open for 2% of the time, Pallas kernels for 0%

profile of v1, /device:TPU:0, one launch (start us, length us, event | category | flops | bytes accessed | tf_op | source)
XLA Modules:
  0.0 300.2 jit_solution(11342720285864173932)
XLA Ops:
  6.5 2.8 pad_maximum_fusion
  9.4 0.9 copy-done.6
  10.3 2.6 all_gather.6
  12.9 7.2 %all-to-all-start = ((bf16[8,16,2304]{2,1,0:T(8,128)(2,1)}), bf16[8,16,2304]{2,1,0:T(8,128)(2,1)S(1)}, u32[]{:S(2)}, u32[]{:S(2)}) async-start(bf16[8,16,2304]{2,1,0:T(8,128)(2,1)} %bitcast), calls=%async_computation | async-start | bytes 1179648 | tf_op jit(solution)/shard_map/all_to_all | solution.py:75
  20.1 0.6 dynamic_slice.10
  20.7 0.7 iota_compare_fusion.1
  21.4 0.2 multiply_cosine_fusion
  21.6 29.6 %all-to-all-done = bf16[8,16,2304]{2,1,0:T(8,128)(2,1)S(1)} async-done(((bf16[8,16,2304]{2,1,0:T(8,128)(2,1)}), bf16[8,16,2304]{2,1,0:T(8,128)(2,1)S(1)}, u32[]{:S(2)}, u32[]{:S(2)}) %all-to-all-start) | async-done | bytes 589856 | tf_op jit(solution)/shard_map/all_to_all | solution.py:75
  51.5 0.2 multiply_convert_fusion.2
  51.8 1.2 bitcast_convert_fusion
  53.0 165.3 %all-gather.2.cloned.1.call-done = bf16[2304,3072]{1,0:T(8,128)(2,1)} async-done(((bf16[288,3072]{1,0:T(8,128)(2,1)}), bf16[2304,3072]{1,0:T(8,128)(2,1)}) %all-gather.2.cloned.1.call-update) | async-done | bytes 14155792 | tf_op jit(solution)/shard_map/all_gather | solution.py:79
  218.3 5.0 %slice_bitcast_fusion = bf16[1024,2304]{0,1:T(8,128)(2,1)} fusion(bf16[2304,3072]{1,0:T(8,128)(2,1)} %all-gather.2.cloned.1.call-done), kind=kLoop, calls=%fused_computation.7 | loop fusion | bytes 9437184 | tf_op jit(solution)/shard_map/dot_general | solution.py:97
  223.3 6.7 %copy.12 = bf16[1024,2304]{1,0:T(8,128)(2,1)} copy(bf16[1024,2304]{0,1:T(8,128)(2,1)} %slice_bitcast_fusion) | data formatting | bytes 9437184 | tf_op jit(solution)/shard_map/dot_general | solution.py:97
  229.9 3.7 %convolution_bitcast_fusion = f32[8,128,128]{1,2,0:T(8,128)S(1)} fusion(bf16[128,2304,1]{1,0,2:T(8,128)(2,1)S(1)} %bitcast.102, bf16[8,128,2304]{2,1,0:T(8,128)(2,1)} %bitcast.100), kind=kOutput, calls=%fused_computation.25 | convolution fusion | flops 603979776 | bytes 5832704 | tf_op jit(solution)/shard_map/dot_general | solution.py:97
  233.7 1.0 copy.13
  234.8 1.0 copy.14
  235.8 3.2 %slice_bitcast_fusion.1 = bf16[512,2304]{0,1:T(8,128)(2,1)} fusion(bf16[2304,3072]{1,0:T(8,128)(2,1)} %all-gather.2.cloned.1.call-done), kind=kLoop, calls=%fused_computation.17 | loop fusion | bytes 4718592 | tf_op jit(solution)/shard_map/dot_general | solution.py:103
  239.0 3.0 %copy.15 = bf16[512,2304]{1,0:T(8,128)(2,1)S(1)} copy(bf16[512,2304]{0,1:T(8,128)(2,1)} %slice_bitcast_fusion.1) | data formatting | bytes 4718592 | tf_op jit(solution)/shard_map/dot_general | solution.py:103
  242.0 1.9 convolution_bitcast_fusion.3
  244.0 2.3 fusion.23
  246.5 0.2 fusion.43
  246.7 0.4 fusion.45
  247.1 0.3 convolution_convert_fusion
  247.4 0.5 copy-done.14
  247.9 4.0 %fusion.8 = bf16[128,2304]{1,0:T(8,128)(2,1)S(1)} fusion(bf16[128,1024]{0,1:T(8,128)(2,1)S(1)} %bitcast.116, bf16[2304,3072]{1,0:T(8,128)(2,1)} %all-gather.2.cloned.1.call-done), kind=kOutput, calls=%fused_computation.12 | convolution fusion | flops 604274688 | bytes 5570560 | tf_op jit(solution)/shard_map/dot_general | solution.py:49
  252.0 0.7 dynamic_slice.11
  252.7 0.7 compare_convert_fusion
  253.4 0.6 collective-permute-done
  254.0 0.3 multiply_reduce_fusion.4
  254.4 0.5 multiply_reduce_fusion.3
  254.8 0.2 copy-done.11
  255.1 0.4 fusion.54
  255.5 0.5 multiply_reduce_fusion.2
  256.0 0.5 multiply_reduce_fusion.1
  256.6 3.4 %fusion.20 = bf16[128,1024]{1,0:T(8,128)(2,1)S(1)} fusion(bf16[2304,3072]{1,0:T(8,128)(2,1)} %all-gather.2.cloned.1.call-done, f32[128,2304]{1,0:T(8,128)S(1)} %get-tuple-element.8, bf16[128,2304]{1,0:T(8,128)(2,1)S(1)} %collective-permute-done, bf16[128,2304]{1,0:T(8,128)(2,1)S(1)} %fusion.8, f32[128]{0:T(128)S(1)} %broadcast_multiply_fusion.1, ...), kind=kOutput, calls=%fused_computation.27 | convolution fusion | flops 606765056 | bytes 7350784 | tf_op jit(solution)/shard_map/dot_general | solution.py:157
  260.1 1.3 fusion.26
  261.5 0.2 fusion.48
  261.7 1.7 convolution_bitcast_fusion.2
  263.5 2.5 convolution_multiply_fusion.1
  266.0 1.2 copy.24
  267.4 4.0 %fusion.5 = f32[128,2304]{1,0:T(8,128)S(1)} fusion(bf16[128,1024]{0,1:T(8,128)(2,1)S(1)} %bitcast.113, bf16[2304,3072]{1,0:T(8,128)(2,1)} %all-gather.2.cloned.1.call-done), kind=kOutput, calls=%fused_computation.5 | convolution fusion | flops 603979776 | bytes 6160384 | tf_op jit(solution)/shard_map/dot_general | solution.py:49
  271.4 2.6 convolution_add_fusion.1
  274.1 2.6 fusion.7
  276.6 0.2 collective-permute-start.1
  276.8 1.9 collective-permute-done.1
  278.7 0.4 multiply_reduce_fusion
  279.3 13.3 %all_to_all.21 = bf16[8,16,1152]{2,1,0:T(8,128)(2,1)S(1)} all-to-all(bf16[8,16,1152]{2,1,0:T(8,128)(2,1)S(1)} %bitcast.105), channel_id=1, replica_groups=mesh['groups'=2,'seq'=8,'wg'=2] {'seq'}, dimensions={0} | all-to-all | bytes 589824 | tf_op jit(solution)/shard_map/all_to_all | solution.py:194
  292.6 0.7 copy.52
  (51 shorter events, 1.3 us)
Async XLA Ops:
  6.5 248.3 %copy-start = (bf16[64,2304]{1,0:T(8,128)(2,1)S(1)}, bf16[64,2304]{1,0:T(8,128)(2,1)}, u32[]{:S(2)}) copy-start(bf16[64,2304]{1,0:T(8,128)(2,1)} %param.19) | copy-start | bytes 884740
  6.5 211.8 %all-gather.2.cloned.1.call-start = ((), (), s32[]{:S(2)}) async-start(), calls=%async_computation.2 | async-start | bytes 15925248 | tf_op jit(solution)/shard_map/all_gather | solution.py:79
  9.4 1.0 copy-start.6
  10.3 9.7 %copy-start.12 = (s32[8]{0:T(128)S(1)}, s32[8]{0:T(128)}, u32[]{:S(2)}) copy-start(s32[8]{0:T(128)} %param.20) | copy-start | bytes 100
  10.3 41.2 %copy-start.10 = (f32[2304]{0:T(1024)S(1)}, f32[2304]{0:T(1024)}, u32[]{:S(2)}) copy-start(f32[2304]{0:T(1024)} %param.12) | copy-start | bytes 27652
  12.9 38.4 %all-to-all-start = ((bf16[8,16,2304]{2,1,0:T(8,128)(2,1)}), bf16[8,16,2304]{2,1,0:T(8,128)(2,1)S(1)}, u32[]{:S(2)}, u32[]{:S(2)}) async-start(bf16[8,16,2304]{2,1,0:T(8,128)(2,1)} %bitcast), calls=%async_computation | async-start | bytes 1179648 | tf_op jit(solution)/shard_map/all_to_all | solution.py:75
  51.8 178.2 %copy-start.1 = (bf16[8,16,2304]{2,1,0:T(8,128)(2,1)}, bf16[8,16,2304]{2,1,0:T(8,128)(2,1)S(1)}, u32[]{:S(2)}) copy-start(bf16[8,16,2304]{2,1,0:T(8,128)(2,1)S(1)} %multiply_convert_fusion.2) | copy-start | bytes 1769476
  242.0 2.0 copy-start.2
  244.0 2.7 copy-start.7
  244.0 2.5 copy-start.4
  244.0 2.5 copy-start.5
  247.1 0.8 copy-start.14
  247.9 4.1 %copy-start.13 = (s32[8]{0:T(128)S(1)}, s32[8]{0:T(128)}, u32[]{:S(2)}) copy-start(s32[8]{0:T(128)} %param.21) | copy-start | bytes 100
  251.9 2.4 copy-start.9
  251.9 2.1 collective-permute-start
  254.3 0.7 copy-start.11
  261.7 1.8 copy-start.8
  276.6 2.1 collective-permute-start.1
  276.8 2.2 copy-start.3
Sparse Core Ops, SparseCore 0:
  9.6 208.6 all-gather.1

commit v2 on v1

--- a/solution.py
+++ b/solution.py
@@ -1,3 +1,5 @@
+import functools
+
 import jax
 import jax.numpy as jnp
 from jax import lax
@@ -56,7 +58,38 @@
     return rounded_part.astype(jnp.float32) + other.astype(jnp.float32)
 
 
+def ring_order(n):
+    if n % 2:
+        return list(range(n))
+    return list(range(0, n, 2)) + list(range(n - 1, 0, -2))
+
+
+def ring_gather(front, back, seq_rank, n):
+    order = ring_order(n)
+    position = [0] * n
+    for place, member in enumerate(order):
+        position[member] = place
+    forward_pairs = [(order[p], order[(p + 1) % n]) for p in range(n)]
+    backward_pairs = [(order[p], order[(p - 1) % n]) for p in range(n)]
+    order_table = jnp.array(order, dtype=jnp.int32)
+    place = jnp.array(position, dtype=jnp.int32)[seq_rank]
+    rows = front.shape[0]
+    front_all = jnp.zeros((n * rows, front.shape[1]), front.dtype)
+    back_all = jnp.zeros((n * rows, back.shape[1]), back.dtype)
+    front_all = lax.dynamic_update_slice(front_all, front, (seq_rank * rows, 0))
+    back_all = lax.dynamic_update_slice(back_all, back, (seq_rank * rows, 0))
+    for step in range(1, n):
+        front = lax.ppermute(front, "seq", forward_pairs)
+        back = lax.ppermute(back, "seq", backward_pairs)
+        front_src = order_table[(place - step) % n]
+        back_src = order_table[(place + step) % n]
+        front_all = lax.dynamic_update_slice(front_all, front, (front_src * rows, 0))
+        back_all = lax.dynamic_update_slice(back_all, back, (back_src * rows, 0))
+    return front_all, back_all
+
+
 def shards(
+    n_seq,
     generator_rows,
     pre_gain,
     query_weight,
@@ -75,12 +108,13 @@
     guard_rows = lax.all_to_all(whole_rows, "seq", split_axis=0, concat_axis=0, tiled=True)
     q_cols = query_weight.shape[1]
     k_cols = key_weight.shape[1]
-    packed = jnp.concatenate([query_weight, key_weight, value_weight, out_weight.T], axis=1)
-    gathered = lax.all_gather(packed, "seq", axis=0, tiled=True)
-    w_query = gathered[:, :q_cols]
-    w_key = gathered[:, q_cols:q_cols + k_cols]
-    w_value = gathered[:, q_cols + k_cols:q_cols + 2 * k_cols]
-    w_out_t = gathered[:, q_cols + 2 * k_cols:]
+    front = jnp.concatenate([query_weight, key_weight], axis=1)
+    back = jnp.concatenate([value_weight, out_weight.T], axis=1)
+    front_all, back_all = ring_gather(front, back, seq_rank, n_seq)
+    w_query = front_all[:, :q_cols]
+    w_key = front_all[:, q_cols:]
+    w_value = back_all[:, :k_cols]
+    w_out_t = back_all[:, k_cols:]
     tok_rows = guard_rows.shape[0]
     half_width = generator_rows.shape[1]
     local_heads = w_query.shape[1] // HD
@@ -198,7 +232,7 @@
 
 def solution(mesh):
     return jax.shard_map(
-        shards,
+        functools.partial(shards, mesh.shape["seq"]),
         mesh=mesh,
         in_specs=(
             P(("groups", "seq"), "wg"),

time: 301 us -> 419 us (1.39); the launches traced: 300 us -> 413 us
  local copies, waits for them, and re-layouts: 25.2 us -> 243 us
  waiting for transfers between devices: 197 us -> 75.4 us
  starting transfers between devices: 7.44 us -> 23.8 us
  matrix products: 32 us -> 23.4 us
  between operations: 13.8 us -> 18.9 us
    dynamic_update_slice x0 -> x16, local copies, waits for them, and re-layouts: none -> 195 us  [the longest x7 86.4 us: ring_gather(): lax.dynamic_update_slice(front_all, front, (front_src * rows, 0))]
    all_gather x1 -> x0, waiting for transfers between devices: 165 us -> none  [shards(): gathered = lax.all_gather(packed, 'seq', axis=0, tiled=True)]
    ppermute x0 -> x14, waiting for transfers between devices: none -> 72.6 us  [the longest x7 71.9 us: ring_gather(): front = lax.ppermute(front, 'seq', forward_pairs)]
    all_to_all x1, waiting for transfers between devices: 29.6 us -> 0.01 us  [shards(): lax.all_to_all(whole_rows, 'seq', split_axis=0, concat_axis=0, tiled=True)]
    ppermute x0 -> x14, local copies, waits for them, and re-layouts: none -> 19.3 us  [the longest x7 9.69 us: ring_gather(): back = lax.ppermute(back, 'seq', backward_pairs)]
    ppermute x0 -> x14, starting transfers between devices: none -> 18.8 us  [the longest x7 10.5 us: ring_gather(): front = lax.ppermute(front, 'seq', forward_pairs)]
    dot_general x4 -> x0, local copies, waits for them, and re-layouts: 17.9 us -> none  [the longest x2 11.6 us: shards(): jnp.dot(normed, w_query, preferred_element_type=jnp.float32)]
    another operation x0 -> x2, local copies, waits for them, and re-layouts: none -> 6.69 us
  transfers between devices with their start and end apart: 4 -> 17, of which waited for: 4 -> 7; matrix products, arithmetic and copies ran while one was open for 2% -> 55% of each run, Pallas kernels for 0% -> 0%
where the time goes in v2:
time: 419 us; the launch traced here: 413 us
  local copies, waits for them, and re-layouts  243 us (58%)
  waiting for transfers between devices  75.4 us (18%)
  starting transfers between devices  23.8 us (6%)
  matrix products  23.4 us (6%)
  between operations  18.9 us (5%)
  blocking collectives  17.8 us (4%)
  other arithmetic  10.6 us (3%)
    dynamic_update_slice x7, local copies, waits for them, and re-layouts, ring_gather(): lax.dynamic_update_slice(front_all, front, (front_src * rows, 0))  86.4 us
    dynamic_update_slice x7, local copies, waits for them, and re-layouts, ring_gather(): back_all = lax.dynamic_update_slice(back_all, back, (back_src * rows, 0))  86.2 us
    ppermute x7, waiting for transfers between devices, ring_gather(): front = lax.ppermute(front, 'seq', forward_pairs)  71.9 us
    all_to_all x1, blocking collectives, shards(): lax.all_to_all(grad_rows.astype(jnp.bfloat16), 'seq', split_axis=0, conca...  15.4 us
    dynamic_update_slice x1, local copies, waits for them, and re-layouts, ring_gather(): front_all = lax.dynamic_update_slice(front_all, front, (seq_rank * rows, 0))  11.4 us
    dynamic_update_slice x1, local copies, waits for them, and re-layouts, ring_gather(): back_all = lax.dynamic_update_slice(back_all, back, (seq_rank * rows, 0))  11.3 us
    ppermute x7, starting transfers between devices, ring_gather(): front = lax.ppermute(front, 'seq', forward_pairs)  10.5 us
    dot_general x5, matrix products, times_transposed(): lax.dot_general(left_side, right_side, (((1,), (1,)), ((), ())), preferre...  9.88 us
  transfers between devices with their start and end apart: 17, of which 7 were waited for; matrix products, arithmetic and copies ran while one was open for 55% of the time, Pallas kernels for 0%

profile of v2, /device:TPU:0, one launch (start us, length us, event | category | flops | bytes accessed | tf_op | source)
XLA Modules:
  0.0 412.7 jit_solution(6030403729452878900)
XLA Ops:
  1.3 3.1 collective-permute-start
  5.4 18.5 %collective-permute-done = bf16[288,1536]{1,0:T(8,128)(2,1)S(1)} collective-permute-done((bf16[288,1536]{1,0:T(8,128)(2,1)S(1)}, bf16[288,1536]{1,0:T(8,128)(2,1)S(1)}, u32[]{:S(2)}, u32[]{:S(2)}) %collective-permute-start) | collective-permute-done | bytes 884768 | tf_op jit(solution)/shard_map/ppermute | solution.py:82
  23.9 1.8 collective-permute-start.1
  26.8 18.0 %collective-permute-done.1 = bf16[288,1536]{1,0:T(8,128)(2,1)S(1)} collective-permute-done((bf16[288,1536]{1,0:T(8,128)(2,1)S(1)}, bf16[288,1536]{1,0:T(8,128)(2,1)S(1)}, u32[]{:S(2)}, u32[]{:S(2)}) %collective-permute-start.1) | collective-permute-done | bytes 884768 | tf_op jit(solution)/shard_map/ppermute | solution.py:82
  47.8 17.9 %collective-permute-done.2 = bf16[288,1536]{1,0:T(8,128)(2,1)S(1)} collective-permute-done((bf16[288,1536]{1,0:T(8,128)(2,1)S(1)}, bf16[288,1536]{1,0:T(8,128)(2,1)S(1)}, u32[]{:S(2)}, u32[]{:S(2)}) %collective-permute-start.2) | collective-permute-done | bytes 884768 | tf_op jit(solution)/shard_map/ppermute | solution.py:82
  67.8 17.5 %collective-permute-done.3 = bf16[288,1536]{1,0:T(8,128)(2,1)} collective-permute-done((bf16[288,1536]{1,0:T(8,128)(2,1)S(1)}, bf16[288,1536]{1,0:T(8,128)(2,1)}, u32[]{:S(2)}, u32[]{:S(2)}) %collective-permute-start.3) | collective-permute-done | bytes 884768 | tf_op jit(solution)/shard_map/ppermute | solution.py:82
  86.5 2.3 all_gather.3
  88.9 4.8 %all-to-all-start = ((bf16[8,16,2304]{2,1,0:T(8,128)(2,1)}), bf16[8,16,2304]{2,1,0:T(8,128)(2,1)S(1)}, u32[]{:S(2)}, u32[]{:S(2)}) async-start(bf16[8,16,2304]{2,1,0:T(8,128)(2,1)} %bitcast), calls=%async_computation | async-start | bytes 1179648 | tf_op jit(solution)/shard_map/all_to_all | solution.py:108
  110.8 1.7 copy.25
  116.1 3.4 broadcast.215.clone.1
  119.5 11.4 %dynamic_update_slice.48 = bf16[2304,1536]{0,1:T(8,128)(2,1)} dynamic-update-slice(bf16[2304,1536]{0,1:T(8,128)(2,1)} %broadcast.215.clone.1, bf16[288,1536]{0,1:T(8,128)(2,1)S(1)} %copy.14, s32[]{:T(128)S(6)} %select_n.165, s32[]{:T(128)} %constant.151.clone.1) | dynamic-update-slice | bytes 1769476 | tf_op jit(solution)/shard_map/dynamic_update_slice | solution.py:79
  130.8 3.3 broadcast.215.clone
  134.1 11.3 %dynamic_update_slice.56 = bf16[2304,1536]{0,1:T(8,128)(2,1)} dynamic-update-slice(bf16[2304,1536]{0,1:T(8,128)(2,1)} %broadcast.215.clone, bf16[288,1536]{0,1:T(8,128)(2,1)S(1)} %copy.25, s32[]{:T(128)S(6)} %select_n.165, s32[]{:T(128)} %constant.151.clone.1) | dynamic-update-slice | bytes 1769476 | tf_op jit(solution)/shard_map/dynamic_update_slice | solution.py:80
  145.5 4.5 %collective-permute-start.11 = (bf16[288,1536]{1,0:T(8,128)(2,1)}, bf16[288,1536]{1,0:T(8,128)(2,1)}, u32[]{:S(2)}, u32[]{:S(2)}) collective-permute-start(bf16[288,1536]{1,0:T(8,128)(2,1)} %collective-permute-done.10), channel_id=1, source_target_pairs={{0,2},{4,0},{8,4},{12,8},{14,12},{10,14},{6,10},{2,6},{1,3},{5,1},... | collective-permute-start | bytes 2654216 | tf_op jit(solution)/shard_map/ppermute | solution.py:83
  152.2 1.6 copy.15
  153.9 12.7 %dynamic_update_slice.49 = bf16[2304,1536]{0,1:T(8,128)(2,1)} dynamic-update-slice(bf16[2304,1536]{0,1:T(8,128)(2,1)} %dynamic_update_slice.48, bf16[288,1536]{0,1:T(8,128)(2,1)S(1)} %copy.15, s32[]{:T(128)S(6)} %select_n.168, s32[]{:T(128)} %constant.151.clone.1) | dynamic-update-slice | bytes 1769476 | tf_op jit(solution)/shard_map/dynamic_update_slice | solution.py:86
  167.3 12.6 %dynamic_update_slice.57 = bf16[2304,1536]{0,1:T(8,128)(2,1)} dynamic-update-slice(bf16[2304,1536]{0,1:T(8,128)(2,1)} %dynamic_update_slice.56, bf16[288,1536]{0,1:T(8,128)(2,1)S(1)} %copy.26, s32[]{:T(128)S(6)} %select_n.190, s32[]{:T(128)} %constant.151.clone.1) | dynamic-update-slice | bytes 1769476 | tf_op jit(solution)/shard_map/dynamic_update_slice | solution.py:87
  185.0 12.7 %dynamic_update_slice.50 = bf16[2304,1536]{0,1:T(8,128)(2,1)} dynamic-update-slice(bf16[2304,1536]{0,1:T(8,128)(2,1)} %dynamic_update_slice.49, bf16[288,1536]{0,1:T(8,128)(2,1)S(1)} %copy.16, s32[]{:T(128)S(6)} %select_n.171, s32[]{:T(128)} %constant.151.clone.1) | dynamic-update-slice | bytes 1769476 | tf_op jit(solution)/shard_map/dynamic_update_slice | solution.py:86
  198.4 11.4 %dynamic_update_slice.58 = bf16[2304,1536]{0,1:T(8,128)(2,1)} dynamic-update-slice(bf16[2304,1536]{0,1:T(8,128)(2,1)} %dynamic_update_slice.57, bf16[288,1536]{0,1:T(8,128)(2,1)S(1)} %copy.27, s32[]{:T(128)S(6)} %select_n.193, s32[]{:T(128)} %constant.151.clone.1) | dynamic-update-slice | bytes 1769476 | tf_op jit(solution)/shard_map/dynamic_update_slice | solution.py:87
  210.5 12.6 %dynamic_update_slice.51 = bf16[2304,1536]{0,1:T(8,128)(2,1)} dynamic-update-slice(bf16[2304,1536]{0,1:T(8,128)(2,1)} %dynamic_update_slice.50, bf16[288,1536]{0,1:T(8,128)(2,1)S(1)} %copy.17, s32[]{:T(128)S(6)} %select_n.174, s32[]{:T(128)} %constant.151.clone.1) | dynamic-update-slice | bytes 1769476 | tf_op jit(solution)/shard_map/dynamic_update_slice | solution.py:86
  223.2 1.6 copy.28
  224.8 12.5 %dynamic_update_slice.59 = bf16[2304,1536]{0,1:T(8,128)(2,1)} dynamic-update-slice(bf16[2304,1536]{0,1:T(8,128)(2,1)} %dynamic_update_slice.58, bf16[288,1536]{0,1:T(8,128)(2,1)S(1)} %copy.28, s32[]{:T(128)S(6)} %select_n.196, s32[]{:T(128)} %constant.151.clone.1) | dynamic-update-slice | bytes 1769476 | tf_op jit(solution)/shard_map/dynamic_update_slice | solution.py:87
  238.9 11.9 %dynamic_update_slice.52 = bf16[2304,1536]{0,1:T(8,128)(2,1)} dynamic-update-slice(bf16[2304,1536]{0,1:T(8,128)(2,1)} %dynamic_update_slice.51, bf16[288,1536]{0,1:T(8,128)(2,1)S(1)} %copy.18, s32[]{:T(128)S(6)} %select_n.177, s32[]{:T(128)} %constant.151.clone.1) | dynamic-update-slice | bytes 1769476 | tf_op jit(solution)/shard_map/dynamic_update_slice | solution.py:86
  250.8 1.6 copy.29
  252.5 11.8 %dynamic_update_slice.60 = bf16[2304,1536]{0,1:T(8,128)(2,1)} dynamic-update-slice(bf16[2304,1536]{0,1:T(8,128)(2,1)} %dynamic_update_slice.59, bf16[288,1536]{0,1:T(8,128)(2,1)S(1)} %copy.29, s32[]{:T(128)S(6)} %select_n.199, s32[]{:T(128)} %constant.151.clone.1) | dynamic-update-slice | bytes 1769476 | tf_op jit(solution)/shard_map/dynamic_update_slice | solution.py:87
  264.3 1.6 copy.19
  266.0 12.5 %dynamic_update_slice.53 = bf16[2304,1536]{0,1:T(8,128)(2,1)} dynamic-update-slice(bf16[2304,1536]{0,1:T(8,128)(2,1)} %dynamic_update_slice.52, bf16[288,1536]{0,1:T(8,128)(2,1)S(1)} %copy.19, s32[]{:T(128)S(6)} %select_n.180, s32[]{:T(128)} %constant.151.clone.1) | dynamic-update-slice | bytes 1769476 | tf_op jit(solution)/shard_map/dynamic_update_slice | solution.py:86
  280.1 12.6 %dynamic_update_slice.61 = bf16[2304,1536]{0,1:T(8,128)(2,1)} dynamic-update-slice(bf16[2304,1536]{0,1:T(8,128)(2,1)} %dynamic_update_slice.60, bf16[288,1536]{0,1:T(8,128)(2,1)S(1)} %copy.30, s32[]{:T(128)S(6)} %select_n.202, s32[]{:T(128)} %constant.151.clone.1) | dynamic-update-slice | bytes 1769476 | tf_op jit(solution)/shard_map/dynamic_update_slice | solution.py:87
  294.4 11.3 %dynamic_update_slice.54 = bf16[2304,1536]{0,1:T(8,128)(2,1)} dynamic-update-slice(bf16[2304,1536]{0,1:T(8,128)(2,1)} %dynamic_update_slice.53, bf16[288,1536]{0,1:T(8,128)(2,1)S(1)} %copy.20, s32[]{:T(128)S(6)} %select_n.183, s32[]{:T(128)} %constant.151.clone.1) | dynamic-update-slice | bytes 1769476 | tf_op jit(solution)/shard_map/dynamic_update_slice | solution.py:86
  305.7 1.6 copy.31
  307.4 12.6 %dynamic_update_slice.62 = bf16[2304,1536]{0,1:T(8,128)(2,1)} dynamic-update-slice(bf16[2304,1536]{0,1:T(8,128)(2,1)} %dynamic_update_slice.61, bf16[288,1536]{0,1:T(8,128)(2,1)S(1)} %copy.31, s32[]{:T(128)S(6)} %select_n.205, s32[]{:T(128)} %constant.151.clone.1) | dynamic-update-slice | bytes 1769476 | tf_op jit(solution)/shard_map/dynamic_update_slice | solution.py:87
  321.4 1.6 copy.21
  323.0 12.6 %dynamic_update_slice.55 = bf16[2304,1536]{0,1:T(8,128)(2,1)} dynamic-update-slice(bf16[2304,1536]{0,1:T(8,128)(2,1)} %dynamic_update_slice.54, bf16[288,1536]{0,1:T(8,128)(2,1)S(1)} %copy.21, s32[]{:T(128)S(6)} %select_n.186, s32[]{:T(128)} %constant.151.clone.1) | dynamic-update-slice | bytes 1769476 | tf_op jit(solution)/shard_map/dynamic_update_slice | solution.py:86
  335.7 2.6 slice.48
  339.7 1.8 slice.51
  342.4 2.0 copy.22
  345.4 1.8 convolution_bitcast_fusion.3
  347.3 1.7 copy.32
  349.0 12.7 %dynamic_update_slice.63 = bf16[2304,1536]{0,1:T(8,128)(2,1)} dynamic-update-slice(bf16[2304,1536]{0,1:T(8,128)(2,1)} %dynamic_update_slice.62, bf16[288,1536]{0,1:T(8,128)(2,1)S(1)} %copy.32, s32[]{:T(128)S(6)} %select_n.208, s32[]{:T(128)} %constant.151.clone.1) | dynamic-update-slice | bytes 1769476 | tf_op jit(solution)/shard_map/dynamic_update_slice | solution.py:87
  361.7 2.7 fusion.22
  365.8 3.3 fusion.7
  374.9 1.7 fusion.19
  379.9 2.1 fusion.25
  382.1 2.0 copy.40
  386.3 2.3 fusion.69
  388.6 2.2 fusion.10
  392.6 2.1 collective-permute-done.15
  396.5 15.4 %all_to_all.21 = bf16[8,16,1152]{2,1,0:T(8,128)(2,1)S(1)} all-to-all(bf16[8,16,1152]{2,1,0:T(8,128)(2,1)S(1)} %bitcast.137), channel_id=1, replica_groups=mesh['groups'=2,'seq'=8,'wg'=2] {'seq'}, dimensions={0} | all-to-all | bytes 589824 | tf_op jit(solution)/shard_map/all_to_all | solution.py:228
  (180 shorter events, 48.1 us)
Async XLA Ops:
  0.0 372.0 %copy-start = (bf16[64,2304]{1,0:T(8,128)(2,1)S(1)}, bf16[64,2304]{1,0:T(8,128)(2,1)}, u32[]{:S(2)}) copy-start(bf16[64,2304]{1,0:T(8,128)(2,1)} %param.21) | copy-start | bytes 884740
  0.0 4.4 %copy-start.22 = (bf16[1024,288]{0,1:T(8,128)(2,1)S(1)}, bf16[1024,288]{0,1:T(8,128)(2,1)}, u32[]{:S(2)}) copy-start(bf16[1024,288]{0,1:T(8,128)(2,1)} %param.18) | copy-start | bytes 1769476
  0.0 4.4 %copy-start.23 = (bf16[288,512]{1,0:T(8,128)(2,1)S(1)}, bf16[288,512]{1,0:T(8,128)(2,1)}, u32[]{:S(2)}) copy-start(bf16[288,512]{1,0:T(8,128)(2,1)} %param.17) | copy-start | bytes 884740
  1.2 85.3 %copy-start.24 = (bf16[128,1152]{1,0:T(8,128)(2,1)S(1)}, bf16[128,1152]{1,0:T(8,128)(2,1)}, u32[]{:S(2)}) copy-start(bf16[128,1152]{1,0:T(8,128)(2,1)} %param.13) | copy-start | bytes 884740
  1.3 22.6 %collective-permute-start = (bf16[288,1536]{1,0:T(8,128)(2,1)S(1)}, bf16[288,1536]{1,0:T(8,128)(2,1)S(1)}, u32[]{:S(2)}, u32[]{:S(2)}) collective-permute-start(bf16[288,1536]{1,0:T(8,128)(2,1)S(1)} %constant_dynamic-update-slice_fusion), channel_id=1, source_target_pairs={{0,4},{4,8},{8,12},{12,14},{14,10},{10,6},{6,2},{2,0},{1,5},{5,9},... | collective-permute-start | bytes 2654216 | tf_op jit(solution)/shard_map/ppermute | solution.py:82
  5.4 88.3 %copy-start.41 = (s32[8]{0:T(128)S(1)}, s32[8]{0:T(128)}, u32[]{:S(2)}) copy-start(s32[8]{0:T(128)} %constant.182.clone) | copy-start | bytes 100
  5.4 98.2 %copy-start.27 = (s32[8]{0:T(128)S(1)}, s32[8]{0:T(128)}, u32[]{:S(2)}) copy-start(s32[8]{0:T(128)} %constant.181.clone) | copy-start | bytes 100
  5.4 21.1 %collective-permute-start.7 = (bf16[288,1536]{1,0:T(8,128)(2,1)S(1)}, bf16[288,1536]{1,0:T(8,128)(2,1)S(1)}, u32[]{:S(2)}, u32[]{:S(2)}) collective-permute-start(bf16[288,1536]{1,0:T(8,128)(2,1)S(1)} %pad_maximum_fusion), channel_id=1, source_target_pairs={{0,2},{4,0},{8,4},{12,8},{14,12},{10,14},{6,10},{2,6},{1,3},{5,1},... | collective-permute-start | bytes 2654216 | tf_op jit(solution)/shard_map/ppermute | solution.py:83
  23.9 62.6 %copy-start.18 = (bf16[288,1536]{1,0:T(8,128)(2,1)}, bf16[288,1536]{1,0:T(8,128)(2,1)S(1)}, u32[]{:S(2)}) copy-start(bf16[288,1536]{1,0:T(8,128)(2,1)S(1)} %collective-permute-done) | copy-start | bytes 2654212
  23.9 20.8 %collective-permute-start.1 = (bf16[288,1536]{1,0:T(8,128)(2,1)S(1)}, bf16[288,1536]{1,0:T(8,128)(2,1)S(1)}, u32[]{:S(2)}, u32[]{:S(2)}) collective-permute-start(bf16[288,1536]{1,0:T(8,128)(2,1)S(1)} %collective-permute-done), channel_id=1, source_target_pairs={{0,4},{4,8},{8,12},{12,14},{14,10},{10,6},{6,2},{2,0},{1,5},{5,9},... | collective-permute-start | bytes 2654216 | tf_op jit(solution)/shard_map/ppermute | solution.py:82
  26.5 58.8 %copy-start.16 = (bf16[288,1536]{1,0:T(8,128)(2,1)}, bf16[288,1536]{1,0:T(8,128)(2,1)S(1)}, u32[]{:S(2)}) copy-start(bf16[288,1536]{1,0:T(8,128)(2,1)S(1)} %collective-permute-done.7) | copy-start | bytes 2654212
  26.5 20.7 %collective-permute-start.8 = (bf16[288,1536]{1,0:T(8,128)(2,1)S(1)}, bf16[288,1536]{1,0:T(8,128)(2,1)S(1)}, u32[]{:S(2)}, u32[]{:S(2)}) collective-permute-start(bf16[288,1536]{1,0:T(8,128)(2,1)S(1)} %collective-permute-done.7), channel_id=1, source_target_pairs={{0,2},{4,0},{8,4},{12,8},{14,12},{10,14},{6,10},{2,6},{1,3},{5,1},... | collective-permute-start | bytes 2654216 | tf_op jit(solution)/shard_map/ppermute | solution.py:83
  45.7 19.9 %collective-permute-start.2 = (bf16[288,1536]{1,0:T(8,128)(2,1)S(1)}, bf16[288,1536]{1,0:T(8,128)(2,1)S(1)}, u32[]{:S(2)}, u32[]{:S(2)}) collective-permute-start(bf16[288,1536]{1,0:T(8,128)(2,1)S(1)} %collective-permute-done.1), channel_id=1, source_target_pairs={{0,4},{4,8},{8,12},{12,14},{14,10},{10,6},{6,2},{2,0},{1,5},{5,9},... | collective-permute-start | bytes 2654216 | tf_op jit(solution)/shard_map/ppermute | solution.py:82
  47.2 18.4 %copy-start.12 = (bf16[288,1536]{1,0:T(8,128)(2,1)}, bf16[288,1536]{1,0:T(8,128)(2,1)S(1)}, u32[]{:S(2)}) copy-start(bf16[288,1536]{1,0:T(8,128)(2,1)S(1)} %collective-permute-done.8) | copy-start | bytes 2654212
  47.2 19.7 %collective-permute-start.9 = (bf16[288,1536]{1,0:T(8,128)(2,1)S(1)}, bf16[288,1536]{1,0:T(8,128)(2,1)}, u32[]{:S(2)}, u32[]{:S(2)}) collective-permute-start(bf16[288,1536]{1,0:T(8,128)(2,1)S(1)} %collective-permute-done.8), channel_id=1, source_target_pairs={{0,2},{4,0},{8,4},{12,8},{14,12},{10,14},{6,10},{2,6},{1,3},{5,1},... | collective-permute-start | bytes 2654216 | tf_op jit(solution)/shard_map/ppermute | solution.py:83
  65.6 19.6 %collective-permute-start.3 = (bf16[288,1536]{1,0:T(8,128)(2,1)S(1)}, bf16[288,1536]{1,0:T(8,128)(2,1)}, u32[]{:S(2)}, u32[]{:S(2)}) collective-permute-start(bf16[288,1536]{1,0:T(8,128)(2,1)S(1)} %collective-permute-done.2), channel_id=1, source_target_pairs={{0,4},{4,8},{8,12},{12,14},{14,10},{10,6},{6,2},{2,0},{1,5},{5,9},... | collective-permute-start | bytes 2654216 | tf_op jit(solution)/shard_map/ppermute | solution.py:82
  66.9 78.5 %collective-permute-start.10 = (bf16[288,1536]{1,0:T(8,128)(2,1)}, bf16[288,1536]{1,0:T(8,128)(2,1)}, u32[]{:S(2)}, u32[]{:S(2)}) collective-permute-start(bf16[288,1536]{1,0:T(8,128)(2,1)} %collective-permute-done.9), channel_id=1, source_target_pairs={{0,2},{4,0},{8,4},{12,8},{14,12},{10,14},{6,10},{2,6},{1,3},{5,1},... | collective-permute-start | bytes 2654216 | tf_op jit(solution)/shard_map/ppermute | solution.py:83
  85.2 64.8 %collective-permute-start.4 = (bf16[288,1536]{1,0:T(8,128)(2,1)}, bf16[288,1536]{1,0:T(8,128)(2,1)}, u32[]{:S(2)}, u32[]{:S(2)}) collective-permute-start(bf16[288,1536]{1,0:T(8,128)(2,1)} %collective-permute-done.3), channel_id=1, source_target_pairs={{0,4},{4,8},{8,12},{12,14},{14,10},{10,6},{6,2},{2,0},{1,5},{5,9},... | collective-permute-start | bytes 2654216 | tf_op jit(solution)/shard_map/ppermute | solution.py:82
  88.9 91.0 %all-to-all-start = ((bf16[8,16,2304]{2,1,0:T(8,128)(2,1)}), bf16[8,16,2304]{2,1,0:T(8,128)(2,1)S(1)}, u32[]{:S(2)}, u32[]{:S(2)}) async-start(bf16[8,16,2304]{2,1,0:T(8,128)(2,1)} %bitcast), calls=%async_computation | async-start | bytes 1179648 | tf_op jit(solution)/shard_map/all_to_all | solution.py:108
  105.7 9.8 %copy-start.39 = (s32[8]{0:T(128)S(1)}, s32[8]{0:T(128)}, u32[]{:S(2)}) copy-start(s32[8]{0:T(128)} %param.22) | copy-start | bytes 100
  145.5 34.7 %collective-permute-start.11 = (bf16[288,1536]{1,0:T(8,128)(2,1)}, bf16[288,1536]{1,0:T(8,128)(2,1)}, u32[]{:S(2)}, u32[]{:S(2)}) collective-permute-start(bf16[288,1536]{1,0:T(8,128)(2,1)} %collective-permute-done.10), channel_id=1, source_target_pairs={{0,2},{4,0},{8,4},{12,8},{14,12},{10,14},{6,10},{2,6},{1,3},{5,1},... | collective-permute-start | bytes 2654216 | tf_op jit(solution)/shard_map/ppermute | solution.py:83
  150.0 30.8 %collective-permute-start.5 = (bf16[288,1536]{1,0:T(8,128)(2,1)}, bf16[288,1536]{1,0:T(8,128)(2,1)}, u32[]{:S(2)}, u32[]{:S(2)}) collective-permute-start(bf16[288,1536]{1,0:T(8,128)(2,1)} %collective-permute-done.4), channel_id=1, source_target_pairs={{0,4},{4,8},{8,12},{12,14},{14,10},{10,6},{6,2},{2,0},{1,5},{5,9},... | collective-permute-start | bytes 2654216 | tf_op jit(solution)/shard_map/ppermute | solution.py:82
  153.9 12.7 %copy-start.17 = (bf16[288,1536]{1,0:T(8,128)(2,1)S(1)}, bf16[288,1536]{1,0:T(8,128)(2,1)}, u32[]{:S(2)}) copy-start(bf16[288,1536]{1,0:T(8,128)(2,1)} %copy-done.16) | copy-start | bytes 2654212
  167.3 14.9 %copy-start.33 = (f32[2304]{0:T(1024)S(1)}, f32[2304]{0:T(1024)}, u32[]{:S(2)}) copy-start(f32[2304]{0:T(1024)} %param.14) | copy-start | bytes 27652
  179.9 191.6 %copy-start.1 = (bf16[8,16,2304]{2,1,0:T(8,128)(2,1)}, bf16[8,16,2304]{2,1,0:T(8,128)(2,1)S(1)}, u32[]{:S(2)}) copy-start(bf16[8,16,2304]{2,1,0:T(8,128)(2,1)S(1)} %all-to-all-done) | copy-start | bytes 1769476
  180.1 125.6 %collective-permute-start.12 = (bf16[288,1536]{1,0:T(8,128)(2,1)}, bf16[288,1536]{1,0:T(8,128)(2,1)}, u32[]{:S(2)}, u32[]{:S(2)}) collective-permute-start(bf16[288,1536]{1,0:T(8,128)(2,1)} %collective-permute-done.11), channel_id=1, source_target_pairs={{0,2},{4,0},{8,4},{12,8},{14,12},{10,14},{6,10},{2,6},{1,3},{5,1},... | collective-permute-start | bytes 2654216 | tf_op jit(solution)/shard_map/ppermute | solution.py:83
  180.8 140.6 %collective-permute-start.6 = (bf16[288,1536]{1,0:T(8,128)(2,1)}, bf16[288,1536]{1,0:T(8,128)(2,1)}, u32[]{:S(2)}, u32[]{:S(2)}) collective-permute-start(bf16[288,1536]{1,0:T(8,128)(2,1)} %collective-permute-done.5), channel_id=1, source_target_pairs={{0,4},{4,8},{8,12},{12,14},{14,10},{10,6},{6,2},{2,0},{1,5},{5,9},... | collective-permute-start | bytes 2654216 | tf_op jit(solution)/shard_map/ppermute | solution.py:82
  182.4 155.9 %copy-start.2 = (bf16[8,16,2304]{2,1,0:T(8,128)(2,1)}, bf16[8,16,2304]{2,1,0:T(8,128)(2,1)S(1)}, u32[]{:S(2)}) copy-start(bf16[8,16,2304]{2,1,0:T(8,128)(2,1)S(1)} %multiply_convert_fusion.2) | copy-start | bytes 1769476
  185.0 12.7 %copy-start.13 = (bf16[288,1536]{1,0:T(8,128)(2,1)S(1)}, bf16[288,1536]{1,0:T(8,128)(2,1)}, u32[]{:S(2)}) copy-start(bf16[288,1536]{1,0:T(8,128)(2,1)} %copy-done.12) | copy-start | bytes 2654212
  198.4 11.4 %copy-start.15 = (bf16[288,1536]{1,0:T(8,128)(2,1)S(1)}, bf16[288,1536]{1,0:T(8,128)(2,1)}, u32[]{:S(2)}) copy-start(bf16[288,1536]{1,0:T(8,128)(2,1)} %copy-done.14) | copy-start | bytes 2654212
  320.0 27.3 %collective-permute-start.13 = (bf16[288,1536]{1,0:T(8,128)(2,1)}, bf16[288,1536]{1,0:T(8,128)(2,1)}, u32[]{:S(2)}, u32[]{:S(2)}) collective-permute-start(bf16[288,1536]{1,0:T(8,128)(2,1)} %collective-permute-done.12), channel_id=1, source_target_pairs={{0,2},{4,0},{8,4},{12,8},{14,12},{10,14},{6,10},{2,6},{1,3},{5,1},... | collective-permute-start | bytes 2654216 | tf_op jit(solution)/shard_map/ppermute | solution.py:83
  347.3 17.4 %copy-start.28 = (bf16[4,128,64]{1,2,0:T(8,128)(2,1)}, bf16[4,128,64]{1,2,0:T(8,128)(2,1)S(1)}, u32[]{:S(2)}) copy-start(bf16[4,128,64]{1,2,0:T(8,128)(2,1)S(1)} %get-tuple-element.17) | copy-start | bytes 196612
  347.3 17.4 %copy-start.30 = (bf16[4,128,64]{1,2,0:T(8,128)(2,1)}, bf16[4,128,64]{1,2,0:T(8,128)(2,1)S(1)}, u32[]{:S(2)}) copy-start(bf16[4,128,64]{1,2,0:T(8,128)(2,1)S(1)} %get-tuple-element.18) | copy-start | bytes 196612
  349.0 12.7 %copy-start.6 = (f32[128,2304]{1,0:T(8,128)S(1)}, f32[128,2304]{1,0:T(8,128)}, u32[]{:S(2)}) copy-start(f32[128,2304]{1,0:T(8,128)} %bitcast_convert_fusion) | copy-start | bytes 3538948
  361.7 2.8 copy-start.8
  361.7 2.8 copy-start.9
  365.5 13.3 %copy-start.42 = (f32[4,2,128,128]{2,3,1,0:T(8,128)}, f32[4,2,128,128]{2,3,1,0:T(8,128)S(1)}, u32[]{:S(2)}) copy-start(f32[4,2,128,128]{2,3,1,0:T(8,128)S(1)} %get-tuple-element.40) | copy-start | bytes 1572868
  365.5 13.3 %copy-start.43 = (f32[4,2,128]{2,1,0:T(2,128)}, f32[4,2,128]{2,1,0:T(2,128)S(1)}, u32[]{:S(2)}) copy-start(f32[4,2,128]{2,1,0:T(2,128)S(1)} %get-tuple-element.39) | copy-start | bytes 12292
  365.8 3.4 copy-start.40
  365.8 9.1 %slice-start.2 = ((s8[7077888]{0:T(1024)(128)(4,1)}), s8[4194304]{0:T(1024)(128)(4,1)S(1)}, s32[]{:S(2)}) async-start(s8[7077888]{0:T(1024)(128)(4,1)} %bitcast.131), calls=%async_computation.4 | async-start | bytes 8388608
  369.1 2.4 copy-start.32
  369.1 2.1 collective-permute-start.14
  371.5 3.4 slice-start.3
  379.9 10.9 %slice-start = ((s8[7077888]{0:T(1024)(128)(4,1)}), s8[2883584]{0:T(1024)(128)(4,1)S(1)}, s32[]{:S(2)}) async-start(s8[7077888]{0:T(1024)(128)(4,1)} %bitcast.128), calls=%async_computation.2 | async-start | bytes 5767168
  386.3 4.6 %slice-start.1 = ((s8[7077888]{0:T(1024)(128)(4,1)}), s8[4194304]{0:T(1024)(128)(4,1)S(1)}, s32[]{:S(2)}) async-start(s8[7077888]{0:T(1024)(128)(4,1)} %bitcast.128), calls=%async_computation.3 | async-start | bytes 8388608
  392.5 2.2 collective-permute-start.15
  392.6 3.7 copy-start.5
  392.6 3.7 copy-start.7
  (17 other events, 21.1 us)

commit v3 on v2

--- a/solution.py
+++ b/solution.py
@@ -71,21 +71,26 @@
         position[member] = place
     forward_pairs = [(order[p], order[(p + 1) % n]) for p in range(n)]
     backward_pairs = [(order[p], order[(p - 1) % n]) for p in range(n)]
-    order_table = jnp.array(order, dtype=jnp.int32)
     place = jnp.array(position, dtype=jnp.int32)[seq_rank]
-    rows = front.shape[0]
-    front_all = jnp.zeros((n * rows, front.shape[1]), front.dtype)
-    back_all = jnp.zeros((n * rows, back.shape[1]), back.dtype)
-    front_all = lax.dynamic_update_slice(front_all, front, (seq_rank * rows, 0))
-    back_all = lax.dynamic_update_slice(back_all, back, (seq_rank * rows, 0))
+    steps = jnp.arange(n, dtype=jnp.int32)
+    block_of = jnp.array(order, dtype=jnp.int32)[(place - steps) % n]
+    slot_of = (place - jnp.array(position, dtype=jnp.int32)) % n
+    front_pieces = [front]
+    back_pieces = [back]
     for step in range(1, n):
-        front = lax.ppermute(front, "seq", forward_pairs)
-        back = lax.ppermute(back, "seq", backward_pairs)
-        front_src = order_table[(place - step) % n]
-        back_src = order_table[(place + step) % n]
-        front_all = lax.dynamic_update_slice(front_all, front, (front_src * rows, 0))
-        back_all = lax.dynamic_update_slice(back_all, back, (back_src * rows, 0))
-    return front_all, back_all
+        front_pieces.append(lax.ppermute(front_pieces[-1], "seq", forward_pairs))
+        back_pieces.append(lax.ppermute(back_pieces[-1], "seq", backward_pairs))
+    back_pieces = [back_pieces[(n - k) % n] for k in range(n)]
+    front_all = jnp.concatenate(front_pieces, axis=0)
+    back_all = jnp.concatenate(back_pieces, axis=0)
+    return front_all, back_all, block_of, slot_of
+
+
+def permute_blocks(values, block_order, n):
+    lead = values.shape[:-1]
+    width = values.shape[-1] // n
+    blocks = values.reshape(lead + (n, width))
+    return jnp.take(blocks, block_order, axis=-2).reshape(values.shape)
 
 
 def shards(
@@ -110,7 +115,12 @@
     k_cols = key_weight.shape[1]
     front = jnp.concatenate([query_weight, key_weight], axis=1)
     back = jnp.concatenate([value_weight, out_weight.T], axis=1)
-    front_all, back_all = ring_gather(front, back, seq_rank, n_seq)
+    front_all, back_all, block_of, slot_of = ring_gather(front, back, seq_rank, n_seq)
+    guard_rows = permute_blocks(guard_rows, block_of, n_seq)
+    pre_gain = permute_blocks(pre_gain, block_of, n_seq)
+    post_gain = permute_blocks(post_gain, block_of, n_seq)
+    final_gain = permute_blocks(final_gain, block_of, n_seq)
+    label_table = permute_blocks(label_table, block_of, n_seq)
     w_query = front_all[:, :q_cols]
     w_key = front_all[:, q_cols:]
     w_value = back_all[:, :k_cols]
@@ -224,6 +234,7 @@
     scaled_in = grad_normed * pre_gain
     row_stat = jnp.mean(scaled_in * inputs, axis=-1, keepdims=True)
     grad_full = scale_in * scaled_in - inputs * cube_in * row_stat + grad_mixed
+    grad_full = permute_blocks(grad_full, slot_of, n_seq)
     grad_rows = lax.dynamic_slice_in_dim(grad_full, core_rank * half_width, half_width, 1)
     return lax.all_to_all(
         grad_rows.astype(jnp.bfloat16), "seq", split_axis=0, concat_axis=0, tiled=True

time: 419 us -> 251 us (0.60); the launches traced: 413 us -> 250 us
  local copies, waits for them, and re-layouts: 243 us -> 64.8 us
  waiting for transfers between devices: 75.4 us -> 96.2 us
  between operations: 18.9 us -> 0.88 us
  other arithmetic: 10.6 us -> 16.9 us
  matrix products: 23.4 us -> 28.1 us
    dynamic_update_slice x16 -> x0, local copies, waits for them, and re-layouts: 195 us -> none  [the longest x7 86.4 us: ring_gather(): lax.dynamic_update_slice(front_all, front, (front_src * rows, 0))]
    ppermute x14, waiting for transfers between devices: 72.6 us -> 96.2 us  [the longest x7 93.4 us: ring_gather(): front_pieces.append(lax.ppermute(front_pieces[-1], 'seq', forward_pairs))]
    ppermute x14 -> x0, local copies, waits for them, and re-layouts: 19.3 us -> none  [the longest x7 9.69 us: ring_gather(): back = lax.ppermute(back, 'seq', backward_pairs)]
    unnamed x98 -> x123, local copies, waits for them, and re-layouts: 6.71 us -> 24.5 us
    dot_general x0 -> x4, local copies, waits for them, and re-layouts: none -> 16.6 us  [the longest x2 12.3 us: shards(): jnp.dot(normed, w_query, preferred_element_type=jnp.float32)]
    another operation x2 -> x0, local copies, waits for them, and re-layouts: 6.69 us -> none
    gather x0 -> x10, local copies, waits for them, and re-layouts: none -> 5.45 us  [the longest x9 4.81 us: permute_blocks(): return jnp.take(blocks, block_order, axis=-2).reshape(values.shape)]
    dot_general x5, matrix products: 9.88 us -> 15 us  [times_transposed(): lax.dot_general(left_side, right_side, (((1,), (1,)), ((), ())), preferre...]
  transfers between devices with their start and end apart: 17 -> 17, of which waited for: 7 -> 9; matrix products, arithmetic and copies ran while one was open for 55% -> 17% of each run, Pallas kernels for 0% -> 0%
where the time goes in v3:
time: 251 us; the launch traced here: 250 us
  waiting for transfers between devices  96.2 us (38%)
  local copies, waits for them, and re-layouts  64.8 us (26%)
  matrix products  28.1 us (11%)
  starting transfers between devices  26 us (10%)
  other arithmetic  16.9 us (7%)
  blocking collectives  16.7 us (7%)
    ppermute x7, waiting for transfers between devices, ring_gather(): front_pieces.append(lax.ppermute(front_pieces[-1], 'seq', forward_pairs))  93.4 us
    unnamed x123, local copies, waits for them, and re-layouts  24.5 us
    ppermute x7, starting transfers between devices, ring_gather(): front_pieces.append(lax.ppermute(front_pieces[-1], 'seq', forward_pairs))  17.4 us
    dot_general x5, matrix products, times_transposed(): lax.dot_general(left_side, right_side, (((1,), (1,)), ((), ())), preferre...  15 us
    all_to_all x1, blocking collectives, shards(): lax.all_to_all(grad_rows.astype(jnp.bfloat16), 'seq', split_axis=0, conca...  14.4 us
    dot_general x2, local copies, waits for them, and re-layouts, shards(): jnp.dot(normed, w_query, preferred_element_type=jnp.float32)  12.3 us
    all_to_all x1, starting transfers between devices, shards(): lax.all_to_all(whole_rows, 'seq', split_axis=0, concat_axis=0, tiled=True)  6.11 us
  transfers between devices with their start and end apart: 17, of which 9 were waited for; matrix products, arithmetic and copies ran while one was open for 17% of the time, Pallas kernels for 0%

profile of v3, /device:TPU:0, one launch (start us, length us, event | category | flops | bytes accessed | tf_op | source)
XLA Modules:
  0.0 249.7 jit_solution(13468445437599687560)
XLA Ops:
  0.0 1.3 pad_maximum_fusion
  1.3 3.1 %collective-permute-start = (bf16[288,1536]{1,0:T(8,128)(2,1)S(1)}, bf16[288,1536]{1,0:T(8,128)(2,1)}, u32[]{:S(2)}, u32[]{:S(2)}) collective-permute-start(bf16[288,1536]{1,0:T(8,128)(2,1)S(1)} %pad_maximum_fusion), channel_id=1, source_target_pairs={{0,4},{4,8},{8,12},{12,14},{14,10},{10,6},{6,2},{2,0},{1,5},{5,9},... | collective-permute-start | bytes 2654216 | tf_op jit(solution)/shard_map/ppermute | solution.py:81
  5.5 18.5 %collective-permute-done = bf16[288,1536]{1,0:T(8,128)(2,1)} collective-permute-done((bf16[288,1536]{1,0:T(8,128)(2,1)S(1)}, bf16[288,1536]{1,0:T(8,128)(2,1)}, u32[]{:S(2)}, u32[]{:S(2)}) %collective-permute-start) | collective-permute-done | bytes 884768 | tf_op jit(solution)/shard_map/ppermute | solution.py:81
  24.0 1.8 collective-permute-start.1
  26.9 2.3 all_gather.3
  29.3 6.1 %all-to-all-start = ((bf16[8,16,2304]{2,1,0:T(8,128)(2,1)}), bf16[8,16,2304]{2,1,0:T(8,128)(2,1)S(1)}, u32[]{:S(2)}, u32[]{:S(2)}) async-start(bf16[8,16,2304]{2,1,0:T(8,128)(2,1)} %bitcast.2), calls=%async_computation | async-start | bytes 1179648 | tf_op jit(solution)/shard_map/all_to_all | solution.py:113
  36.8 10.8 %collective-permute-done.1 = bf16[288,1536]{1,0:T(8,128)(2,1)} collective-permute-done((bf16[288,1536]{1,0:T(8,128)(2,1)}, bf16[288,1536]{1,0:T(8,128)(2,1)}, u32[]{:S(2)}, u32[]{:S(2)}) %collective-permute-start.1) | collective-permute-done | bytes 884768 | tf_op jit(solution)/shard_map/ppermute | solution.py:81
  47.6 2.5 %collective-permute-start.2 = (bf16[288,1536]{1,0:T(8,128)(2,1)}, bf16[288,1536]{1,0:T(8,128)(2,1)}, u32[]{:S(2)}, u32[]{:S(2)}) collective-permute-start(bf16[288,1536]{1,0:T(8,128)(2,1)} %collective-permute-done.1), channel_id=1, source_target_pairs={{0,4},{4,8},{8,12},{12,14},{14,10},{10,6},{6,2},{2,0},{1,5},{5,9},... | collective-permute-start | bytes 2654216 | tf_op jit(solution)/shard_map/ppermute | solution.py:81
  54.5 18.2 %collective-permute-done.2 = bf16[288,1536]{1,0:T(8,128)(2,1)} collective-permute-done((bf16[288,1536]{1,0:T(8,128)(2,1)}, bf16[288,1536]{1,0:T(8,128)(2,1)}, u32[]{:S(2)}, u32[]{:S(2)}) %collective-permute-start.2) | collective-permute-done | bytes 884768 | tf_op jit(solution)/shard_map/ppermute | solution.py:81
  72.7 4.7 %collective-permute-start.3 = (bf16[288,1536]{1,0:T(8,128)(2,1)}, bf16[288,1536]{1,0:T(8,128)(2,1)}, u32[]{:S(2)}, u32[]{:S(2)}) collective-permute-start(bf16[288,1536]{1,0:T(8,128)(2,1)} %collective-permute-done.2), channel_id=1, source_target_pairs={{0,4},{4,8},{8,12},{12,14},{14,10},{10,6},{6,2},{2,0},{1,5},{5,9},... | collective-permute-start | bytes 2654216 | tf_op jit(solution)/shard_map/ppermute | solution.py:81
  79.9 14.9 %collective-permute-done.3 = bf16[288,1536]{1,0:T(8,128)(2,1)} collective-permute-done((bf16[288,1536]{1,0:T(8,128)(2,1)}, bf16[288,1536]{1,0:T(8,128)(2,1)}, u32[]{:S(2)}, u32[]{:S(2)}) %collective-permute-start.3) | collective-permute-done | bytes 884768 | tf_op jit(solution)/shard_map/ppermute | solution.py:81
  94.8 2.5 collective-permute-start.4
  101.0 2.2 constant_dynamic-update-slice_fusion.6
  105.9 9.9 %collective-permute-done.4 = bf16[288,1536]{1,0:T(8,128)(2,1)} collective-permute-done((bf16[288,1536]{1,0:T(8,128)(2,1)}, bf16[288,1536]{1,0:T(8,128)(2,1)}, u32[]{:S(2)}, u32[]{:S(2)}) %collective-permute-start.4) | collective-permute-done | bytes 884768 | tf_op jit(solution)/shard_map/ppermute | solution.py:81
  115.8 1.3 collective-permute-start.5
  118.5 2.1 collective-permute-done.11
  120.8 2.1 constant_dynamic-update-slice_fusion.5
  122.9 12.9 %collective-permute-done.5 = bf16[288,1536]{1,0:T(8,128)(2,1)S(1)} collective-permute-done((bf16[288,1536]{1,0:T(8,128)(2,1)}, bf16[288,1536]{1,0:T(8,128)(2,1)S(1)}, u32[]{:S(2)}, u32[]{:S(2)}) %collective-permute-start.5) | collective-permute-done | bytes 884768 | tf_op jit(solution)/shard_map/ppermute | solution.py:81
  135.8 1.4 collective-permute-start.6
  137.3 2.1 constant_dynamic-update-slice_fusion.4
  139.4 2.1 constant_dynamic-update-slice_fusion.3
  141.5 2.2 constant_dynamic-update-slice_fusion.2
  145.3 8.0 %collective-permute-done.6 = bf16[288,1536]{1,0:T(8,128)(2,1)S(1)} collective-permute-done((bf16[288,1536]{1,0:T(8,128)(2,1)S(1)}, bf16[288,1536]{1,0:T(8,128)(2,1)S(1)}, u32[]{:S(2)}, u32[]{:S(2)}) %collective-permute-start.6) | collective-permute-done | bytes 884768 | tf_op jit(solution)/shard_map/ppermute | solution.py:81
  154.3 5.6 %slice_bitcast_fusion = bf16[1024,2304]{0,1:T(8,128)(2,1)} fusion(bf16[2304,1536]{1,0:T(8,128)(2,1)} %constant_dynamic-update-slice_fusion), kind=kLoop, calls=%fused_computation.14 | loop fusion | bytes 9437184 | tf_op jit(solution)/shard_map/dot_general | solution.py:141
  159.9 1.8 slice_bitcast_fusion.1
  163.2 1.3 constant_dynamic-update-slice_fusion.12
  167.0 2.8 %copy-done.7 = bf16[2304,1536]{1,0:T(8,128)(2,1)} copy-done((bf16[2304,1536]{1,0:T(8,128)(2,1)}, bf16[2304,1536]{1,0:T(8,128)(2,1)S(1)}, u32[]{:S(2)}) %copy-start.7) | copy-done | bytes 7077912
  171.0 1.7 copy.103
  172.7 6.7 %copy.54 = bf16[1024,2304]{1,0:T(8,128)(2,1)} copy(bf16[1024,2304]{0,1:T(8,128)(2,1)} %slice_bitcast_fusion) | data formatting | bytes 9437184 | tf_op jit(solution)/shard_map/dot_general | solution.py:141
  179.4 3.7 %convolution_bitcast_fusion = f32[8,128,128]{1,2,0:T(8,128)S(1)} fusion(bf16[128,2304,1]{0,1,2:T(8,128)(2,1)S(1)} %bitcast.116, bf16[8,128,2304]{2,1,0:T(8,128)(2,1)} %bitcast.113), kind=kOutput, calls=%fused_computation.39 | convolution fusion | flops 603979776 | bytes 5832704 | tf_op jit(solution)/shard_map/dot_general | solution.py:141
  184.0 1.9 copy.57
  186.0 2.0 copy.56
  187.9 2.5 copy.58
  190.4 2.5 %convolution_bitcast_fusion.3 = f32[4,128,128]{1,2,0:T(8,128)S(1)} fusion(bf16[128,2304,1]{0,1,2:T(8,128)(2,1)S(1)} %bitcast.117, bf16[4,128,2304]{2,1,0:T(8,128)(2,1)} %bitcast.115), kind=kOutput, calls=%fused_computation.63 | convolution fusion | flops 301989888 | bytes 3211264 | tf_op jit(solution)/shard_map/dot_general | solution.py:147
  194.7 4.1 %fusion.13 = bf16[128,2304]{1,0:T(8,128)(2,1)S(1)} fusion(bf16[128,1024]{0,1:T(8,128)(2,1)S(1)} %bitcast.137, bf16[2304,1536]{1,0:T(8,128)(2,1)} %copy-done.7), kind=kOutput, calls=%fused_computation.18 | convolution fusion | flops 604274688 | bytes 5570560 | tf_op jit(solution)/shard_map/dot_general | solution.py:51
  205.6 1.3 fusion.30
  208.8 1.3 convolution_multiply_fusion.1
  210.1 2.7 %fusion.19 = f32[128,2304]{1,0:T(8,128)S(1)} fusion(bf16[128,512]{0,1:T(8,128)(2,1)} %bitcast.135, bf16[2304,1536]{1,0:T(8,128)(2,1)} %copy-done.7), kind=kOutput, calls=%fused_computation.20 | convolution fusion | flops 301989888 | bytes 3670016 | tf_op jit(solution)/shard_map/dot_general | solution.py:51
  212.9 3.6 %fusion.23 = f32[128,2304]{1,0:T(8,128)} fusion(bf16[128,512]{0,1:T(8,128)(2,1)S(1)} %bitcast.134, bf16[2304,1536]{1,0:T(8,128)(2,1)} %constant_dynamic-update-slice_fusion), kind=kOutput, calls=%fused_computation.24 | convolution fusion | flops 301989888 | bytes 3670016 | tf_op jit(solution)/shard_map/dot_general | solution.py:51
  216.5 1.2 copy.71
  219.0 4.0 %fusion.16 = bf16[128,2304]{1,0:T(8,128)(2,1)S(1)} fusion(f32[128,2304]{1,0:T(8,128)S(1)} %fusion.19, f32[128,2304]{1,0:T(8,128)S(1)} %copy-done.1, bf16[128,1024]{0,1:T(8,128)(2,1)S(1)} %bitcast.130, bf16[2304,1536]{1,0:T(8,128)(2,1)} %constant_dynamic-update-slice_fusion), kind=kOutput, calls=%fused_computation.19 | convolution fusion | flops 604864512 | bytes 7929856 | tf_op jit(solution)/shard_map/dot_general | solution.py:51
  223.6 1.3 broadcast_in_dim.111
  224.9 1.4 broadcast_in_dim.112
  226.2 1.3 dynamic-slice
  227.6 1.5 fusion.41
  229.1 2.9 %fusion.40 = bf16[128,2304]{1,0:T(8,128)(2,1)} fusion(bf16[128,2304]{1,0:T(8,128)(2,1)} %collective-permute-done.15, bf16[128,2304]{1,0:T(8,128)(2,1)S(1)} %fusion.16, f32[128]{0:T(128)S(1)} %broadcast_multiply_fusion, f32[128]{0:T(128)} %get-tuple-element.20, f32[2304]{0:T(1024)S(1)} %copy-done.28, f32[128]{0:T(128)} %copy-done.38, ...), kind=kLoop, calls=%fused_computation.50 | loop fusion | flops 6488064 | bytes 4742912 | tf_op jit(solution)/shard_map/add | solution.py:236
  232.0 1.4 copy.75
  234.6 14.4 %all_to_all.21 = bf16[8,16,1152]{2,1,0:T(8,128)(2,1)S(1)} all-to-all(bf16[8,16,1152]{2,1,0:T(8,128)(2,1)S(1)} %bitcast.126), channel_id=1, replica_groups=mesh['groups'=2,'seq'=8,'wg'=2] {'seq'}, dimensions={0} | all-to-all | bytes 589824 | tf_op jit(solution)/shard_map/all_to_all | solution.py:239
  (208 shorter events, 40.5 us)
Async XLA Ops:
  0.0 4.4 %copy-start.21 = (bf16[1024,288]{0,1:T(8,128)(2,1)S(1)}, bf16[1024,288]{0,1:T(8,128)(2,1)}, u32[]{:S(2)}) copy-start(bf16[1024,288]{0,1:T(8,128)(2,1)} %param.21) | copy-start | bytes 1769476
  0.0 4.4 %copy-start.24 = (bf16[288,512]{1,0:T(8,128)(2,1)S(1)}, bf16[288,512]{1,0:T(8,128)(2,1)}, u32[]{:S(2)}) copy-start(bf16[288,512]{1,0:T(8,128)(2,1)} %param.20) | copy-start | bytes 884740
  1.3 22.7 %collective-permute-start = (bf16[288,1536]{1,0:T(8,128)(2,1)S(1)}, bf16[288,1536]{1,0:T(8,128)(2,1)}, u32[]{:S(2)}, u32[]{:S(2)}) collective-permute-start(bf16[288,1536]{1,0:T(8,128)(2,1)S(1)} %pad_maximum_fusion), channel_id=1, source_target_pairs={{0,4},{4,8},{8,12},{12,14},{14,10},{10,6},{6,2},{2,0},{1,5},{5,9},... | collective-permute-start | bytes 2654216 | tf_op jit(solution)/shard_map/ppermute | solution.py:81
  4.4 22.5 %copy-start.23 = (bf16[128,1152]{1,0:T(8,128)(2,1)S(1)}, bf16[128,1152]{1,0:T(8,128)(2,1)}, u32[]{:S(2)}) copy-start(bf16[128,1152]{1,0:T(8,128)(2,1)} %param.16) | copy-start | bytes 884740
  5.4 30.0 %copy-start.32 = (f32[2304]{0:T(1024)S(1)}, f32[2304]{0:T(1024)}, u32[]{:S(2)}) copy-start(f32[2304]{0:T(1024)} %param.23) | copy-start | bytes 27652
  5.4 30.0 %copy-start.33 = (f32[2304]{0:T(1024)S(1)}, f32[2304]{0:T(1024)}, u32[]{:S(2)}) copy-start(f32[2304]{0:T(1024)} %param.17) | copy-start | bytes 27652
  5.4 30.1 %copy-start.47 = (s32[8]{0:T(128)S(1)}, s32[8]{0:T(128)}, u32[]{:S(2)}) copy-start(s32[8]{0:T(128)} %constant.125.clone) | copy-start | bytes 100
  5.4 44.7 %copy-start = (s32[8]{0:T(128)S(1)}, s32[8]{0:T(128)}, u32[]{:S(2)}) copy-start(s32[8]{0:T(128)} %constant.126.clone) | copy-start | bytes 100
  5.4 45.4 %copy-start.44 = (s32[8]{0:T(128)S(1)}, s32[8]{0:T(128)}, u32[]{:S(2)}) copy-start(s32[8]{0:T(128)} %constant.127) | copy-start | bytes 100
  5.5 21.2 %collective-permute-start.7 = (bf16[288,1536]{1,0:T(8,128)(2,1)S(1)}, bf16[288,1536]{1,0:T(8,128)(2,1)S(1)}, u32[]{:S(2)}, u32[]{:S(2)}) collective-permute-start(bf16[288,1536]{1,0:T(8,128)(2,1)S(1)} %get-tuple-element.8), channel_id=1, source_target_pairs={{0,2},{4,0},{8,4},{12,8},{14,12},{10,14},{6,10},{2,6},{1,3},{5,1},... | collective-permute-start | bytes 2654216 | tf_op jit(solution)/shard_map/ppermute | solution.py:82
  24.0 23.6 %collective-permute-start.1 = (bf16[288,1536]{1,0:T(8,128)(2,1)}, bf16[288,1536]{1,0:T(8,128)(2,1)}, u32[]{:S(2)}, u32[]{:S(2)}) collective-permute-start(bf16[288,1536]{1,0:T(8,128)(2,1)} %collective-permute-done), channel_id=1, source_target_pairs={{0,4},{4,8},{8,12},{12,14},{14,10},{10,6},{6,2},{2,0},{1,5},{5,9},... | collective-permute-start | bytes 2654216 | tf_op jit(solution)/shard_map/ppermute | solution.py:81
  26.6 24.2 %copy-start.9 = (bf16[288,1536]{1,0:T(8,128)(2,1)}, bf16[288,1536]{1,0:T(8,128)(2,1)S(1)}, u32[]{:S(2)}) copy-start(bf16[288,1536]{1,0:T(8,128)(2,1)S(1)} %collective-permute-done.7) | copy-start | bytes 2654212
  26.6 27.8 %collective-permute-start.8 = (bf16[288,1536]{1,0:T(8,128)(2,1)S(1)}, bf16[288,1536]{1,0:T(8,128)(2,1)S(1)}, u32[]{:S(2)}, u32[]{:S(2)}) collective-permute-start(bf16[288,1536]{1,0:T(8,128)(2,1)S(1)} %collective-permute-done.7), channel_id=1, source_target_pairs={{0,2},{4,0},{8,4},{12,8},{14,12},{10,14},{6,10},{2,6},{1,3},{5,1},... | collective-permute-start | bytes 2654216 | tf_op jit(solution)/shard_map/ppermute | solution.py:82
  29.3 24.5 %copy-start.34 = (f32[2304]{0:T(1024)S(1)}, f32[2304]{0:T(1024)}, u32[]{:S(2)}) copy-start(f32[2304]{0:T(1024)} %param.22) | copy-start | bytes 27652
  29.3 49.0 %copy-start.45 = (s32[8]{0:T(128)S(1)}, s32[8]{0:T(128)}, u32[]{:S(2)}) copy-start(s32[8]{0:T(128)} %param.25) | copy-start | bytes 100
  29.3 49.7 %copy-start.4 = (bf16[288,1024]{1,0:T(8,128)(2,1)S(1)}, bf16[288,1024]{1,0:T(8,128)(2,1)}, u32[]{:S(2)}) copy-start(bf16[288,1024]{1,0:T(8,128)(2,1)} %param.18) | copy-start | bytes 1769476
  29.3 73.9 %all-to-all-start = ((bf16[8,16,2304]{2,1,0:T(8,128)(2,1)}), bf16[8,16,2304]{2,1,0:T(8,128)(2,1)S(1)}, u32[]{:S(2)}, u32[]{:S(2)}) async-start(bf16[8,16,2304]{2,1,0:T(8,128)(2,1)} %bitcast.2), calls=%async_computation | async-start | bytes 1179648 | tf_op jit(solution)/shard_map/all_to_all | solution.py:113
  35.4 62.6 %copy-start.8 = (bf16[288,512]{1,0:T(8,128)(2,1)S(1)}, bf16[288,512]{1,0:T(8,128)(2,1)}, u32[]{:S(2)}) copy-start(bf16[288,512]{1,0:T(8,128)(2,1)} %param.19) | copy-start | bytes 884740
  47.6 25.1 %collective-permute-start.2 = (bf16[288,1536]{1,0:T(8,128)(2,1)}, bf16[288,1536]{1,0:T(8,128)(2,1)}, u32[]{:S(2)}, u32[]{:S(2)}) collective-permute-start(bf16[288,1536]{1,0:T(8,128)(2,1)} %collective-permute-done.1), channel_id=1, source_target_pairs={{0,4},{4,8},{8,12},{12,14},{14,10},{10,6},{6,2},{2,0},{1,5},{5,9},... | collective-permute-start | bytes 2654216 | tf_op jit(solution)/shard_map/ppermute | solution.py:81
  54.4 48.8 %copy-start.11 = (bf16[288,1536]{1,0:T(8,128)(2,1)}, bf16[288,1536]{1,0:T(8,128)(2,1)S(1)}, u32[]{:S(2)}) copy-start(bf16[288,1536]{1,0:T(8,128)(2,1)S(1)} %collective-permute-done.8) | copy-start | bytes 2654212
  54.4 25.4 %collective-permute-start.9 = (bf16[288,1536]{1,0:T(8,128)(2,1)S(1)}, bf16[288,1536]{1,0:T(8,128)(2,1)S(1)}, u32[]{:S(2)}, u32[]{:S(2)}) collective-permute-start(bf16[288,1536]{1,0:T(8,128)(2,1)S(1)} %collective-permute-done.8), channel_id=1, source_target_pairs={{0,2},{4,0},{8,4},{12,8},{14,12},{10,14},{6,10},{2,6},{1,3},{5,1},... | collective-permute-start | bytes 2654216 | tf_op jit(solution)/shard_map/ppermute | solution.py:82
  72.7 22.1 %collective-permute-start.3 = (bf16[288,1536]{1,0:T(8,128)(2,1)}, bf16[288,1536]{1,0:T(8,128)(2,1)}, u32[]{:S(2)}, u32[]{:S(2)}) collective-permute-start(bf16[288,1536]{1,0:T(8,128)(2,1)} %collective-permute-done.2), channel_id=1, source_target_pairs={{0,4},{4,8},{8,12},{12,14},{14,10},{10,6},{6,2},{2,0},{1,5},{5,9},... | collective-permute-start | bytes 2654216 | tf_op jit(solution)/shard_map/ppermute | solution.py:81
  78.1 88.8 %copy-start.27 = (f32[2304]{0:T(1024)}, f32[2304]{0:T(1024)S(1)}, u32[]{:S(2)}) copy-start(f32[2304]{0:T(1024)S(1)} %mul.537) | copy-start | bytes 27652
  78.9 26.0 %copy-start.36 = (s32[1024]{0:T(1024)}, s32[1024]{0:T(1024)S(1)}, u32[]{:S(2)}) copy-start(s32[1024]{0:T(1024)S(1)} %pad_clamp_fusion.2) | copy-start | bytes 12292
  79.8 23.4 %copy-start.13 = (bf16[288,1536]{1,0:T(8,128)(2,1)}, bf16[288,1536]{1,0:T(8,128)(2,1)S(1)}, u32[]{:S(2)}) copy-start(bf16[288,1536]{1,0:T(8,128)(2,1)S(1)} %collective-permute-done.9) | copy-start | bytes 2654212
  79.8 20.4 %collective-permute-start.10 = (bf16[288,1536]{1,0:T(8,128)(2,1)S(1)}, bf16[288,1536]{1,0:T(8,128)(2,1)}, u32[]{:S(2)}, u32[]{:S(2)}) collective-permute-start(bf16[288,1536]{1,0:T(8,128)(2,1)S(1)} %collective-permute-done.9), channel_id=1, source_target_pairs={{0,2},{4,0},{8,4},{12,8},{14,12},{10,14},{6,10},{2,6},{1,3},{5,1},... | collective-permute-start | bytes 2654216 | tf_op jit(solution)/shard_map/ppermute | solution.py:82
  94.8 21.0 %collective-permute-start.4 = (bf16[288,1536]{1,0:T(8,128)(2,1)}, bf16[288,1536]{1,0:T(8,128)(2,1)}, u32[]{:S(2)}, u32[]{:S(2)}) collective-permute-start(bf16[288,1536]{1,0:T(8,128)(2,1)} %collective-permute-done.3), channel_id=1, source_target_pairs={{0,4},{4,8},{8,12},{12,14},{14,10},{10,6},{6,2},{2,0},{1,5},{5,9},... | collective-permute-start | bytes 2654216 | tf_op jit(solution)/shard_map/ppermute | solution.py:81
  98.0 5.2 %copy-start.42 = (pred[128]{0:T(512)(128)(4,1)}, pred[128]{0:T(512)(128)(4,1)S(1)}, u32[]{:S(2)}) copy-start(pred[128]{0:T(512)(128)(4,1)S(1)} %iota_compare_fusion.1) | copy-start | bytes 388
  100.3 20.3 %collective-permute-start.11 = (bf16[288,1536]{1,0:T(8,128)(2,1)}, bf16[288,1536]{1,0:T(8,128)(2,1)}, u32[]{:S(2)}, u32[]{:S(2)}) collective-permute-start(bf16[288,1536]{1,0:T(8,128)(2,1)} %collective-permute-done.10), channel_id=1, source_target_pairs={{0,2},{4,0},{8,4},{12,8},{14,12},{10,14},{6,10},{2,6},{1,3},{5,1},... | collective-permute-start | bytes 2654216 | tf_op jit(solution)/shard_map/ppermute | solution.py:82
  115.8 20.0 %collective-permute-start.5 = (bf16[288,1536]{1,0:T(8,128)(2,1)}, bf16[288,1536]{1,0:T(8,128)(2,1)S(1)}, u32[]{:S(2)}, u32[]{:S(2)}) collective-permute-start(bf16[288,1536]{1,0:T(8,128)(2,1)} %collective-permute-done.4), channel_id=1, source_target_pairs={{0,4},{4,8},{8,12},{12,14},{14,10},{10,6},{6,2},{2,0},{1,5},{5,9},... | collective-permute-start | bytes 2654216 | tf_op jit(solution)/shard_map/ppermute | solution.py:81
  118.1 48.9 %copy-start.38 = (f32[128]{0:T(128)}, f32[128]{0:T(128)S(1)}, u32[]{:S(2)}) copy-start(f32[128]{0:T(128)S(1)} %get-tuple-element.21) | copy-start | bytes 1540
  120.5 23.2 %collective-permute-start.12 = (bf16[288,1536]{1,0:T(8,128)(2,1)}, bf16[288,1536]{1,0:T(8,128)(2,1)S(1)}, u32[]{:S(2)}, u32[]{:S(2)}) collective-permute-start(bf16[288,1536]{1,0:T(8,128)(2,1)} %collective-permute-done.11), channel_id=1, source_target_pairs={{0,2},{4,0},{8,4},{12,8},{14,12},{10,14},{6,10},{2,6},{1,3},{5,1},... | collective-permute-start | bytes 2654216 | tf_op jit(solution)/shard_map/ppermute | solution.py:82
  135.8 17.5 %collective-permute-start.6 = (bf16[288,1536]{1,0:T(8,128)(2,1)S(1)}, bf16[288,1536]{1,0:T(8,128)(2,1)S(1)}, u32[]{:S(2)}, u32[]{:S(2)}) collective-permute-start(bf16[288,1536]{1,0:T(8,128)(2,1)S(1)} %collective-permute-done.5), channel_id=1, source_target_pairs={{0,4},{4,8},{8,12},{12,14},{14,10},{10,6},{6,2},{2,0},{1,5},{5,9},... | collective-permute-start | bytes 2654216 | tf_op jit(solution)/shard_map/ppermute | solution.py:81
  143.7 18.0 %collective-permute-start.13 = (bf16[288,1536]{1,0:T(8,128)(2,1)S(1)}, bf16[288,1536]{1,0:T(8,128)(2,1)S(1)}, u32[]{:S(2)}, u32[]{:S(2)}) collective-permute-start(bf16[288,1536]{1,0:T(8,128)(2,1)S(1)} %collective-permute-done.12), channel_id=1, source_target_pairs={{0,2},{4,0},{8,4},{12,8},{14,12},{10,14},{6,10},{2,6},{1,3},{5,1},... | collective-permute-start | bytes 2654216 | tf_op jit(solution)/shard_map/ppermute | solution.py:82
  153.3 8.4 %slice-start = ((s8[7077888]{0:T(1024)(128)(4,1)}), s8[4194304]{0:T(1024)(128)(4,1)S(1)}, s32[]{:S(2)}) async-start(s8[7077888]{0:T(1024)(128)(4,1)} %bitcast.122), calls=%async_computation.2 | async-start | bytes 8388608
  154.3 7.4 %slice-start.1 = ((s8[7077888]{0:T(1024)(128)(4,1)}), s8[2883584]{0:T(1024)(128)(4,1)S(1)}, s32[]{:S(2)}) async-start(s8[7077888]{0:T(1024)(128)(4,1)} %bitcast.122), calls=%async_computation.3 | async-start | bytes 5767168
  167.0 2.8 %copy-start.7 = (bf16[2304,1536]{1,0:T(8,128)(2,1)}, bf16[2304,1536]{1,0:T(8,128)(2,1)S(1)}, u32[]{:S(2)}) copy-start(bf16[2304,1536]{1,0:T(8,128)(2,1)S(1)} %constant_dynamic-update-slice_fusion.9) | copy-start | bytes 21233668
  179.4 3.7 %copy-start.15 = (f32[128,64]{0,1:T(8,128)S(1)}, f32[128,64]{0,1:T(8,128)}, u32[]{:S(2)}) copy-start(f32[128,64]{0,1:T(8,128)} %get-tuple-element.18) | copy-start | bytes 98308
  179.4 3.7 %copy-start.18 = (f32[128,64]{0,1:T(8,128)S(1)}, f32[128,64]{0,1:T(8,128)}, u32[]{:S(2)}) copy-start(f32[128,64]{0,1:T(8,128)} %get-tuple-element.19) | copy-start | bytes 98308
  194.7 4.2 %copy-start.30 = (f32[8,288]{1,0:T(8,128)S(1)}, f32[8,288]{1,0:T(8,128)}, u32[]{:S(2)}) copy-start(f32[8,288]{1,0:T(8,128)} %get-tuple-element.28) | copy-start | bytes 27652
  194.7 4.3 %copy-start.29 = (f32[8,288]{1,0:T(8,128)S(1)}, f32[8,288]{1,0:T(8,128)}, u32[]{:S(2)}) copy-start(f32[8,288]{1,0:T(8,128)} %get-tuple-element.26) | copy-start | bytes 27652
  194.7 4.3 %copy-start.25 = (bf16[64,2304]{1,0:T(8,128)(2,1)S(1)}, bf16[64,2304]{1,0:T(8,128)(2,1)}, u32[]{:S(2)}) copy-start(bf16[64,2304]{1,0:T(8,128)(2,1)} %param.24) | copy-start | bytes 884740
  198.8 3.5 %collective-permute-start.14 = (bf16[128,2304]{1,0:T(8,128)(2,1)S(1)}, bf16[128,2304]{1,0:T(8,128)(2,1)S(1)}, u32[]{:S(2)}, u32[]{:S(2)}) collective-permute-start(bf16[128,2304]{1,0:T(8,128)(2,1)S(1)} %fusion.13), channel_id=1, source_target_pairs={{0,1},{1,0},{2,3},{3,2},{4,5},{5,4},{6,7},{7,6},{8,9},{9,8},{10,11... | collective-permute-start | bytes 1769480 | tf_op jit(solution)/shard_map/ppermute | solution.py:57
  202.3 3.2 %slice-start.2 = ((s8[7077888]{0:T(1024)(128)(4,1)}), s8[4194304]{0:T(1024)(128)(4,1)S(1)}, s32[]{:S(2)}) async-start(s8[7077888]{0:T(1024)(128)(4,1)} %bitcast.124), calls=%async_computation.4 | async-start | bytes 8388608
  210.1 2.7 %copy-start.20 = (f32[128,64]{0,1:T(8,128)S(1)}, f32[128,64]{0,1:T(8,128)}, u32[]{:S(2)}) copy-start(f32[128,64]{0,1:T(8,128)} %get-tuple-element.19) | copy-start | bytes 98308
  223.0 6.0 %copy-start.3 = (f32[128,2304]{1,0:T(8,128)S(1)}, f32[128,2304]{1,0:T(8,128)}, u32[]{:S(2)}) copy-start(f32[128,2304]{1,0:T(8,128)} %copy-done.2) | copy-start | bytes 3538948
  223.1 4.5 %collective-permute-start.15 = (bf16[128,2304]{1,0:T(8,128)(2,1)S(1)}, bf16[128,2304]{1,0:T(8,128)(2,1)}, u32[]{:S(2)}, u32[]{:S(2)}) collective-permute-start(bf16[128,2304]{1,0:T(8,128)(2,1)S(1)} %fusion.16), channel_id=1, source_target_pairs={{0,1},{1,0},{2,3},{3,2},{4,5},{5,4},{6,7},{7,6},{8,9},{9,8},{10,11... | collective-permute-start | bytes 1769480 | tf_op jit(solution)/shard_map/ppermute | solution.py:57
  226.2 2.8 %copy-start.28 = (f32[2304]{0:T(1024)S(1)}, f32[2304]{0:T(1024)}, u32[]{:S(2)}) copy-start(f32[2304]{0:T(1024)} %copy-done.27) | copy-start | bytes 27652
  (23 other events, 39.0 us)

commit v4 on v3

--- a/solution.py
+++ b/solution.py
@@ -64,22 +64,47 @@
     return list(range(0, n, 2)) + list(range(n - 1, 0, -2))
 
 
-def ring_gather(front, back, seq_rank, n):
+def ring_gather(front, back, seq_rank, group_rank, n):
     order = ring_order(n)
     position = [0] * n
     for place, member in enumerate(order):
         position[member] = place
     forward_pairs = [(order[p], order[(p + 1) % n]) for p in range(n)]
     backward_pairs = [(order[p], order[(p - 1) % n]) for p in range(n)]
+    group_pairs = [(0, 1), (1, 0)]
     place = jnp.array(position, dtype=jnp.int32)[seq_rank]
     steps = jnp.arange(n, dtype=jnp.int32)
     block_of = jnp.array(order, dtype=jnp.int32)[(place - steps) % n]
     slot_of = (place - jnp.array(position, dtype=jnp.int32)) % n
+    first_group = group_rank == 0
+
+    def thirds(values):
+        width = values.shape[1] // 3
+        return [values[:, i * width:(i + 1) * width] for i in range(3)]
+
+    def carried(values):
+        left, middle, right = thirds(values)
+        return jnp.stack([jnp.where(first_group, left, right), middle])
+
+    front_ring = [carried(front)]
+    back_ring = [carried(back)]
+    for step in range(1, n):
+        front_ring.append(lax.ppermute(front_ring[-1], "seq", forward_pairs))
+        back_ring.append(lax.ppermute(back_ring[-1], "seq", backward_pairs))
     front_pieces = [front]
     back_pieces = [back]
     for step in range(1, n):
-        front_pieces.append(lax.ppermute(front_pieces[-1], "seq", forward_pairs))
-        back_pieces.append(lax.ppermute(back_pieces[-1], "seq", backward_pairs))
+        handed = lax.ppermute(
+            jnp.stack([front_ring[step][0], back_ring[step][0]]), "groups", group_pairs
+        )
+        for ring, pieces, other in ((front_ring, front_pieces, handed[0]), (back_ring, back_pieces, handed[1])):
+            own, middle = ring[step][0], ring[step][1]
+            pieces.append(
+                jnp.concatenate(
+                    [jnp.where(first_group, own, other), middle, jnp.where(first_group, other, own)],
+                    axis=1,
+                )
+            )
     back_pieces = [back_pieces[(n - k) % n] for k in range(n)]
     front_all = jnp.concatenate(front_pieces, axis=0)
     back_all = jnp.concatenate(back_pieces, axis=0)
@@ -115,7 +140,7 @@
     k_cols = key_weight.shape[1]
     front = jnp.concatenate([query_weight, key_weight], axis=1)
     back = jnp.concatenate([value_weight, out_weight.T], axis=1)
-    front_all, back_all, block_of, slot_of = ring_gather(front, back, seq_rank, n_seq)
+    front_all, back_all, block_of, slot_of = ring_gather(front, back, seq_rank, lax.axis_index("groups"), n_seq)
     guard_rows = permute_blocks(guard_rows, block_of, n_seq)
     pre_gain = permute_blocks(pre_gain, block_of, n_seq)
     post_gain = permute_blocks(post_gain, block_of, n_seq)

time: 251 us -> 225 us (0.90)
  waiting for transfers between devices: 96.2 us -> 57.6 us
  local copies, waits for them, and re-layouts: 64.8 us -> 52.6 us
  other arithmetic: 16.9 us -> 26.8 us
  starting transfers between devices: 26 us -> 32.9 us
  matrix products: 28.1 us -> 34.4 us
    ppermute x14 -> x21, waiting for transfers between devices: 96.2 us -> 56.1 us  [the longest x7 28.5 us: ring_gather(): lax.ppermute(jnp.stack([front_ring[step][0], back_ring[step][0]]), 'group...]
    unnamed x123 -> x121, local copies, waits for them, and re-layouts: 24.5 us -> 7.19 us
    ppermute x14 -> x21, starting transfers between devices: 19.3 us -> 26 us  [the longest x7 11 us: ring_gather(): lax.ppermute(jnp.stack([front_ring[step][0], back_ring[step][0]]), 'group...]
    slice x0 -> x14, local copies, waits for them, and re-layouts: none -> 4.14 us  [the longest x7 2.07 us: ring_gather(): back_ring[step][0]]
    select_n x0 -> x7, other arithmetic: none -> 3.48 us  [ring_gather(): jnp.where(first_group, own, other)]
    reshape x7, local copies, waits for them, and re-layouts: 2.6 us -> 5.41 us  [permute_blocks(): blocks = values.reshape(lead + (n, width))]
    unnamed x2 -> x17, other arithmetic: 0.01 us -> 2.75 us
    another operation x3 -> x13, other arithmetic: 0.16 us -> 2.9 us  [the longest x3 1.53 us: carried(): return jnp.stack([jnp.where(first_group, left, right), middle])]
  transfers between devices with their start and end apart: 17 -> 24, of which waited for: 9 -> 17; matrix products, arithmetic and copies ran while one was open for 17% -> 18% of each run, Pallas kernels for 0% -> 0%
where the time goes in v4:
time: 225 us; the launch traced here: 223 us
  waiting for transfers between devices  57.6 us (26%)
  local copies, waits for them, and re-layouts  52.6 us (23%)
  matrix products  34.4 us (15%)
  starting transfers between devices  32.9 us (15%)
  other arithmetic  26.8 us (12%)
  blocking collectives  17.8 us (8%)
    ppermute x7, waiting for transfers between devices, ring_gather(): lax.ppermute(jnp.stack([front_ring[step][0], back_ring[step][0]]), 'group...  28.5 us
    ppermute x7, waiting for transfers between devices, ring_gather(): back_ring.append(lax.ppermute(back_ring[-1], 'seq', backward_pairs))  25.2 us
    all_to_all x1, blocking collectives, shards(): lax.all_to_all(grad_rows.astype(jnp.bfloat16), 'seq', split_axis=0, conca...  15.3 us
    dot_general x5, matrix products, times_transposed(): lax.dot_general(left_side, right_side, (((1,), (1,)), ((), ())), preferre...  14 us
    ppermute x7, starting transfers between devices, ring_gather(): lax.ppermute(jnp.stack([front_ring[step][0], back_ring[step][0]]), 'group...  11 us
    dot_general x2, local copies, waits for them, and re-layouts, shards(): jnp.dot(normed, w_query, preferred_element_type=jnp.float32)  9.83 us
    ppermute x7, starting transfers between devices, ring_gather(): back_ring.append(lax.ppermute(back_ring[-1], 'seq', backward_pairs))  9.48 us
    unnamed x121, local copies, waits for them, and re-layouts  7.19 us
  transfers between devices with their start and end apart: 24, of which 17 were waited for; matrix products, arithmetic and copies ran while one was open for 18% of the time, Pallas kernels for 0%

profile of v4, /device:TPU:0, one launch (start us, length us, event | category | flops | bytes accessed | tf_op | source)
XLA Modules:
  0.0 223.4 jit_solution(6925674523428611066)
XLA Ops:
  1.5 3.0 %collective-permute-start.1 = (bf16[2,288,512]{2,1,0:T(8,128)(2,1)S(1)}, bf16[2,288,512]{2,1,0:T(8,128)(2,1)}, u32[]{:S(2)}, u32[]{:S(2)}) collective-permute-start(bf16[2,288,512]{2,1,0:T(8,128)(2,1)S(1)} %pad_maximum_fusion.1), channel_id=1, source_target_pairs={{0,2},{4,0},{8,4},{12,8},{14,12},{10,14},{6,10},{2,6},{1,3},{5,1},... | collective-permute-start | bytes 1769480 | tf_op jit(solution)/shard_map/ppermute | solution.py:93
  4.8 2.5 %all_gather.3 = bf16[128,2304]{1,0:T(8,128)(2,1)} all-gather(bf16[128,1152]{1,0:T(8,128)(2,1)S(1)} %copy-done.19), channel_id=1, replica_groups=mesh['groups'=2,'seq'=8,'wg'=2] {'wg'}, dimensions={1}, use_global_device_ids=true | all-gather | bytes 884736 | tf_op jit(solution)/shard_map/all_gather | solution.py:137
  7.3 6.2 %all-to-all-start = ((bf16[8,16,2304]{2,1,0:T(8,128)(2,1)}), bf16[8,16,2304]{2,1,0:T(8,128)(2,1)}, u32[]{:S(2)}, u32[]{:S(2)}) async-start(bf16[8,16,2304]{2,1,0:T(8,128)(2,1)} %bitcast.2), calls=%async_computation | async-start | bytes 1179648 | tf_op jit(solution)/shard_map/all_to_all | solution.py:138
  25.0 2.0 collective-permute-start.4
  31.5 1.5 all-to-all-done
  33.0 3.0 %reshape.497 = bf16[128,8,288]{2,1,0:T(8,128)(2,1)} reshape(bf16[8,16,2304]{2,1,0:T(8,128)(2,1)} %all-to-all-done) | data formatting | bytes 1179648 | tf_op jit(solution)/shard_map/reshape | solution.py:117
  36.0 1.6 copy.53
  40.3 1.6 fusion.23
  42.5 3.3 %collective-permute-start.7 = (bf16[2,288,512]{2,1,0:T(8,128)(2,1)}, bf16[2,288,512]{2,1,0:T(8,128)(2,1)S(1)}, u32[]{:S(2)}, u32[]{:S(2)}) collective-permute-start(bf16[2,288,512]{2,1,0:T(8,128)(2,1)} %collective-permute-done.4), channel_id=1, source_target_pairs={{0,2},{4,0},{8,4},{12,8},{14,12},{10,14},{6,10},{2,6},{1,3},{5,1},... | collective-permute-start | bytes 1769480 | tf_op jit(solution)/shard_map/ppermute | solution.py:93
  45.8 2.3 %fusion.25 = bf16[128,8,288]{0,2,1:T(8,128)(2,1)} fusion(f32[8,288]{1,0:T(8,128)S(1)} %get-tuple-element.85, f32[128]{0:T(128)S(1)} %get-tuple-element.79, bf16[8,128,288]{1,2,0:T(8,128)(2,1)} %gather_fusion.1, pred[8]{0:T(512)(128)(4,1)S(1)} %compare_and_fusion), kind=kLoop, calls=%fused_computation.43 | loop fusion | flops 1474560 | bytes 1189384 | tf_op jit(solution)/shard_map/convert_element_type | solution.py:164
  50.1 1.6 collective-permute-start.5
  53.2 4.5 %collective-permute-done.7 = bf16[2,288,512]{2,1,0:T(8,128)(2,1)S(1)} collective-permute-done((bf16[2,288,512]{2,1,0:T(8,128)(2,1)}, bf16[2,288,512]{2,1,0:T(8,128)(2,1)S(1)}, u32[]{:S(2)}, u32[]{:S(2)}) %collective-permute-start.7) | collective-permute-done | bytes 589856 | tf_op jit(solution)/shard_map/ppermute | solution.py:93
  59.9 1.6 collective-permute-start.8
  61.5 4.8 %collective-permute-done.5 = bf16[2,288,512]{2,1,0:T(8,128)(2,1)S(1)} collective-permute-done((bf16[2,288,512]{2,1,0:T(8,128)(2,1)S(1)}, bf16[2,288,512]{2,1,0:T(8,128)(2,1)S(1)}, u32[]{:S(2)}, u32[]{:S(2)}) %collective-permute-start.5) | collective-permute-done | bytes 589856 | tf_op jit(solution)/shard_map/ppermute | solution.py:97
  67.7 3.6 %collective-permute-done.10 = bf16[2,288,512]{2,1,0:T(8,128)(2,1)S(1)} collective-permute-done((bf16[2,288,512]{2,1,0:T(8,128)(2,1)S(1)}, bf16[2,288,512]{2,1,0:T(8,128)(2,1)S(1)}, u32[]{:S(2)}, u32[]{:S(2)}) %collective-permute-start.10) | collective-permute-done | bytes 589856 | tf_op jit(solution)/shard_map/ppermute | solution.py:93
  73.5 1.6 collective-permute-start.11
  75.1 3.9 %collective-permute-done.8 = bf16[2,288,512]{2,1,0:T(8,128)(2,1)S(1)} collective-permute-done((bf16[2,288,512]{2,1,0:T(8,128)(2,1)S(1)}, bf16[2,288,512]{2,1,0:T(8,128)(2,1)S(1)}, u32[]{:S(2)}, u32[]{:S(2)}) %collective-permute-start.8) | collective-permute-done | bytes 589856 | tf_op jit(solution)/shard_map/ppermute | solution.py:97
  79.1 5.7 %collective-permute-done.13 = bf16[2,288,512]{2,1,0:T(8,128)(2,1)S(1)} collective-permute-done((bf16[2,288,512]{2,1,0:T(8,128)(2,1)S(1)}, bf16[2,288,512]{2,1,0:T(8,128)(2,1)S(1)}, u32[]{:S(2)}, u32[]{:S(2)}) %collective-permute-start.13) | collective-permute-done | bytes 589856 | tf_op jit(solution)/shard_map/ppermute | solution.py:93
  87.0 1.6 collective-permute-start.14
  88.6 3.0 %collective-permute-done.11 = bf16[2,288,512]{2,1,0:T(8,128)(2,1)S(1)} collective-permute-done((bf16[2,288,512]{2,1,0:T(8,128)(2,1)S(1)}, bf16[2,288,512]{2,1,0:T(8,128)(2,1)S(1)}, u32[]{:S(2)}, u32[]{:S(2)}) %collective-permute-start.11) | collective-permute-done | bytes 589856 | tf_op jit(solution)/shard_map/ppermute | solution.py:97
  91.7 6.6 %collective-permute-done.16 = bf16[2,288,512]{2,1,0:T(8,128)(2,1)S(1)} collective-permute-done((bf16[2,288,512]{2,1,0:T(8,128)(2,1)S(1)}, bf16[2,288,512]{2,1,0:T(8,128)(2,1)S(1)}, u32[]{:S(2)}, u32[]{:S(2)}) %collective-permute-start.16) | collective-permute-done | bytes 589856 | tf_op jit(solution)/shard_map/ppermute | solution.py:93
  100.5 1.6 collective-permute-start.17
  102.1 2.2 collective-permute-done.14
  104.4 4.8 %collective-permute-done.19 = bf16[2,288,512]{2,1,0:T(8,128)(2,1)S(1)} collective-permute-done((bf16[2,288,512]{2,1,0:T(8,128)(2,1)S(1)}, bf16[2,288,512]{2,1,0:T(8,128)(2,1)S(1)}, u32[]{:S(2)}, u32[]{:S(2)}) %collective-permute-start.19) | collective-permute-done | bytes 589856 | tf_op jit(solution)/shard_map/ppermute | solution.py:93
  110.1 1.6 collective-permute-start.20
  111.7 5.2 %collective-permute-done.17 = bf16[2,288,512]{2,1,0:T(8,128)(2,1)S(1)} collective-permute-done((bf16[2,288,512]{2,1,0:T(8,128)(2,1)S(1)}, bf16[2,288,512]{2,1,0:T(8,128)(2,1)S(1)}, u32[]{:S(2)}, u32[]{:S(2)}) %collective-permute-start.17) | collective-permute-done | bytes 589856 | tf_op jit(solution)/shard_map/ppermute | solution.py:97
  117.1 9.5 %collective-permute-done.20 = bf16[2,288,512]{2,1,0:T(8,128)(2,1)S(1)} collective-permute-done((bf16[2,288,512]{2,1,0:T(8,128)(2,1)S(1)}, bf16[2,288,512]{2,1,0:T(8,128)(2,1)S(1)}, u32[]{:S(2)}, u32[]{:S(2)}) %collective-permute-start.20) | collective-permute-done | bytes 589856 | tf_op jit(solution)/shard_map/ppermute | solution.py:97
  126.8 3.0 %slice_bitcast_fusion = bf16[1024,2304]{0,1:T(8,128)(2,1)} fusion(bf16[2304,1536]{1,0:T(8,128)(2,1)S(1)} %maximum_dynamic-update-slice_fusion), kind=kLoop, calls=%fused_computation.14 | loop fusion | bytes 9437184 | tf_op jit(solution)/shard_map/dot_general | solution.py:166
  129.8 2.8 %copy-done.1 = bf16[2304,1536]{1,0:T(8,128)(2,1)} copy-done((bf16[2304,1536]{1,0:T(8,128)(2,1)}, bf16[2304,1536]{1,0:T(8,128)(2,1)S(1)}, u32[]{:S(2)}) %copy-start.1) | copy-done | bytes 7077912
  132.6 1.6 slice_bitcast_fusion.1
  134.7 2.9 %copy-done.8 = bf16[2304,1536]{1,0:T(8,128)(2,1)} copy-done((bf16[2304,1536]{1,0:T(8,128)(2,1)}, bf16[2304,1536]{1,0:T(8,128)(2,1)S(1)}, u32[]{:S(2)}) %copy-start.8) | copy-done | bytes 7077912
  139.0 6.8 %copy.54 = bf16[1024,2304]{1,0:T(8,128)(2,1)} copy(bf16[1024,2304]{0,1:T(8,128)(2,1)} %slice_bitcast_fusion) | data formatting | bytes 9437184 | tf_op jit(solution)/shard_map/dot_general | solution.py:166
  145.8 3.7 %convolution_bitcast_fusion = f32[8,128,128]{1,2,0:T(8,128)S(1)} fusion(bf16[128,2304,1]{0,1,2:T(8,128)(2,1)S(1)} %bitcast.210, bf16[8,128,2304]{2,1,0:T(8,128)(2,1)} %bitcast.205), kind=kOutput, calls=%fused_computation.37 | convolution fusion | flops 603979776 | bytes 5832704 | tf_op jit(solution)/shard_map/dot_general | solution.py:166
  150.5 2.0 copy.57
  152.4 1.9 copy.56
  154.4 2.5 %copy.58 = bf16[512,2304]{1,0:T(8,128)(2,1)} copy(bf16[512,2304]{0,1:T(8,128)(2,1)S(1)} %copy-done.2) | data formatting | bytes 4718592 | tf_op jit(solution)/shard_map/dot_general | solution.py:172
  156.9 2.5 %convolution_bitcast_fusion.3 = f32[4,128,128]{1,2,0:T(8,128)S(1)} fusion(bf16[128,2304,1]{0,1,2:T(8,128)(2,1)S(1)} %bitcast.211, bf16[4,128,2304]{2,1,0:T(8,128)(2,1)} %bitcast.209), kind=kOutput, calls=%fused_computation.61 | convolution fusion | flops 301989888 | bytes 3211264 | tf_op jit(solution)/shard_map/dot_general | solution.py:172
  161.0 4.1 %fusion.8 = bf16[128,2304]{1,0:T(8,128)(2,1)S(1)} fusion(bf16[128,1024]{0,1:T(8,128)(2,1)S(1)} %bitcast.232, bf16[2304,1536]{1,0:T(8,128)(2,1)} %copy-done.8), kind=kOutput, calls=%fused_computation.19 | convolution fusion | flops 604274688 | bytes 5570560 | tf_op jit(solution)/shard_map/dot_general | solution.py:51
  170.1 2.3 %multiply_reduce_fusion.1 = (f32[128]{0:T(128)S(1)}, f32[128,2304]{1,0:T(8,128)S(1)}) fusion(f32[2304]{0:T(1024)S(1)} %mul.543, f32[128]{0:T(128)S(1)} %get-tuple-element.81, bf16[128,2304]{1,0:T(8,128)(2,1)S(1)} %collective-permute-done.21, bf16[128,2304]{1,0:T(8,128)(2,1)S(1)} %fusion.8, bf16[128,2304]{1,0:T(8,128)(2,1)S(1)} %copy.61, ...), kind=kOutput, calls=%fused_computation.54 | convolution fusion | flops 41205632 | bytes 3299456 | tf_op jit(solution)/shard_map/dot_general | solution.py:215
  173.2 2.0 fusion.20
  177.4 2.9 %convolution_multiply_fusion.1 = f32[4,2,128,128]{3,2,1,0:T(8,128)} fusion(f32[4,2,128,128]{2,3,1,0:T(8,128)} %fusion.60, f32[4,2,128,128]{2,3,1,0:T(8,128)} %copy-done.52, bf16[4,128,64]{1,2,0:T(8,128)(2,1)} %copy-done.31, bf16[4,128,64]{1,2,0:T(8,128)(2,1)S(1)} %copy-done.30, f32[4,2,128]{2,1,0:T(2,128)} %copy-done.53, pred[128,128]{0,1:T(8,128)(4,1)} %fusion.65), kind=kOutput, calls=%fused_computation.34 | convolution fusion | flops 35652736 | bytes 1724416 | tf_op jit(solution)/shard_map/kgij,kjd->kgid/dot_general | solution.py:239
  180.3 2.8 %convolution_bitcast_fusion.2 = f32[4,128,128]{1,2,0:T(8,128)} fusion(bf16[4,2,128,128]{3,2,1,0:T(8,128)(2,1)S(1)} %copy-done.23, f32[4,2,128,128]{2,3,1,0:T(8,128)} %fusion.60, f32[4,2,128,128]{2,3,1,0:T(8,128)} %copy-done.52, f32[4,2,128]{2,1,0:T(2,128)} %copy-done.53, pred[128,128]{0,1:T(8,128)(4,1)} %fusion.65), kind=kOutput, calls=%fused_computation.60 | convolution fusion | flops 35259520 | bytes 1593344 | tf_op jit(solution)/shard_map/kgij,kgid->kjd/dot_general | solution.py:243
  183.1 2.0 fusion.35
  186.4 4.1 %fusion.5 = f32[128,2304]{1,0:T(8,128)S(1)} fusion(bf16[128,1024]{0,1:T(8,128)(2,1)S(1)} %bitcast.229, bf16[2304,1536]{1,0:T(8,128)(2,1)} %copy-done.1), kind=kOutput, calls=%fused_computation.12 | convolution fusion | flops 603979776 | bytes 6160384 | tf_op jit(solution)/shard_map/dot_general | solution.py:51
  190.6 2.6 %convolution_add_fusion.1 = f32[128,2304]{1,0:T(8,128)S(1)} fusion(f32[128,2304]{1,0:T(8,128)S(1)} %fusion.5, bf16[128,512]{0,1:T(8,128)(2,1)S(1)} %bitcast.228, bf16[2304,1536]{1,0:T(8,128)(2,1)} %copy-done.1), kind=kOutput, calls=%fused_computation.16 | convolution fusion | flops 302284800 | bytes 4849664 | tf_op jit(solution)/shard_map/dot_general | solution.py:51
  193.2 2.6 %fusion.7 = bf16[128,2304]{1,0:T(8,128)(2,1)S(1)} fusion(f32[128,2304]{1,0:T(8,128)S(1)} %convolution_add_fusion.1, bf16[128,512]{0,1:T(8,128)(2,1)S(1)} %bitcast.230, bf16[2304,1536]{1,0:T(8,128)(2,1)} %copy-done.8), kind=kOutput, calls=%fused_computation.18 | convolution fusion | flops 302579712 | bytes 4259840 | tf_op jit(solution)/shard_map/dot_general | solution.py:51
  201.9 2.9 %fusion.30 = bf16[128,2304]{1,0:T(8,128)(2,1)} fusion(bf16[128,2304]{1,0:T(8,128)(2,1)} %collective-permute-done.22, bf16[128,2304]{1,0:T(8,128)(2,1)S(1)} %fusion.7, f32[128]{0:T(128)S(1)} %broadcast_multiply_fusion, f32[128]{0:T(128)} %get-tuple-element.78, f32[2304]{0:T(1024)S(1)} %copy-done.28, f32[128]{0:T(128)} %copy-done.42, ...), kind=kLoop, calls=%fused_computation.48 | loop fusion | flops 6488064 | bytes 4742912 | tf_op jit(solution)/shard_map/add | solution.py:261
  207.4 15.3 %all_to_all.21 = bf16[8,16,1152]{2,1,0:T(8,128)(2,1)S(1)} all-to-all(bf16[8,16,1152]{2,1,0:T(8,128)(2,1)S(1)} %bitcast.222), channel_id=1, replica_groups=mesh['groups'=2,'seq'=8,'wg'=2] {'seq'}, dimensions={0} | all-to-all | bytes 589824 | tf_op jit(solution)/shard_map/all_to_all | solution.py:264
  (264 shorter events, 58.7 us)
Async XLA Ops:
  1.5 12.0 %copy-start.51 = (s32[8]{0:T(128)S(1)}, s32[8]{0:T(128)}, u32[]{:S(2)}) copy-start(s32[8]{0:T(128)} %constant.129.clone) | copy-start | bytes 100
  1.5 13.3 %copy-start = (s32[8]{0:T(128)S(1)}, s32[8]{0:T(128)}, u32[]{:S(2)}) copy-start(s32[8]{0:T(128)} %constant.130.clone) | copy-start | bytes 100
  1.5 23.5 %collective-permute-start.1 = (bf16[2,288,512]{2,1,0:T(8,128)(2,1)S(1)}, bf16[2,288,512]{2,1,0:T(8,128)(2,1)}, u32[]{:S(2)}, u32[]{:S(2)}) collective-permute-start(bf16[2,288,512]{2,1,0:T(8,128)(2,1)S(1)} %pad_maximum_fusion.1), channel_id=1, source_target_pairs={{0,2},{4,0},{8,4},{12,8},{14,12},{10,14},{6,10},{2,6},{1,3},{5,1},... | collective-permute-start | bytes 1769480 | tf_op jit(solution)/shard_map/ppermute | solution.py:93
  4.5 11.0 %copy-start.35 = (f32[2304]{0:T(1024)S(1)}, f32[2304]{0:T(1024)}, u32[]{:S(2)}) copy-start(f32[2304]{0:T(1024)} %param.23) | copy-start | bytes 27652
  4.5 11.0 %copy-start.48 = (s32[8]{0:T(128)S(1)}, s32[8]{0:T(128)}, u32[]{:S(2)}) copy-start(s32[8]{0:T(128)} %constant.131) | copy-start | bytes 100
  4.5 12.3 %copy-start.36 = (f32[2304]{0:T(1024)S(1)}, f32[2304]{0:T(1024)}, u32[]{:S(2)}) copy-start(f32[2304]{0:T(1024)} %param.17) | copy-start | bytes 27652
  4.5 14.1 %copy-start.37 = (f32[2304]{0:T(1024)S(1)}, f32[2304]{0:T(1024)}, u32[]{:S(2)}) copy-start(f32[2304]{0:T(1024)} %param.22) | copy-start | bytes 27652
  4.6 14.7 %copy-start.49 = (s32[8]{0:T(128)S(1)}, s32[8]{0:T(128)}, u32[]{:S(2)}) copy-start(s32[8]{0:T(128)} %param.25) | copy-start | bytes 100
  4.6 18.3 %copy-start.4 = (bf16[1024,288]{0,1:T(8,128)(2,1)S(1)}, bf16[1024,288]{0,1:T(8,128)(2,1)}, u32[]{:S(2)}) copy-start(bf16[1024,288]{0,1:T(8,128)(2,1)} %param.21) | copy-start | bytes 1769476
  4.6 18.3 %copy-start.9 = (bf16[288,512]{1,0:T(8,128)(2,1)S(1)}, bf16[288,512]{1,0:T(8,128)(2,1)}, u32[]{:S(2)}) copy-start(bf16[288,512]{1,0:T(8,128)(2,1)} %param.20) | copy-start | bytes 884740
  4.6 22.4 %collective-permute-start = (bf16[2,288,512]{2,1,0:T(8,128)(2,1)S(1)}, bf16[2,288,512]{2,1,0:T(8,128)(2,1)}, u32[]{:S(2)}, u32[]{:S(2)}) collective-permute-start(bf16[2,288,512]{2,1,0:T(8,128)(2,1)S(1)} %pad_maximum_fusion), channel_id=1, source_target_pairs={{0,4},{4,8},{8,12},{12,14},{14,10},{10,6},{6,2},{2,0},{1,5},{5,9},... | collective-permute-start | bytes 1769480 | tf_op jit(solution)/shard_map/ppermute | solution.py:92
  7.3 16.7 %copy-start.5 = (bf16[288,1024]{1,0:T(8,128)(2,1)S(1)}, bf16[288,1024]{1,0:T(8,128)(2,1)}, u32[]{:S(2)}) copy-start(bf16[288,1024]{1,0:T(8,128)(2,1)} %param.18) | copy-start | bytes 1769476
  7.3 16.7 %copy-start.10 = (bf16[288,512]{1,0:T(8,128)(2,1)S(1)}, bf16[288,512]{1,0:T(8,128)(2,1)}, u32[]{:S(2)}) copy-start(bf16[288,512]{1,0:T(8,128)(2,1)} %param.19) | copy-start | bytes 884740
  7.3 25.7 %all-to-all-start = ((bf16[8,16,2304]{2,1,0:T(8,128)(2,1)}), bf16[8,16,2304]{2,1,0:T(8,128)(2,1)}, u32[]{:S(2)}, u32[]{:S(2)}) async-start(bf16[8,16,2304]{2,1,0:T(8,128)(2,1)} %bitcast.2), calls=%async_computation | async-start | bytes 1179648 | tf_op jit(solution)/shard_map/all_to_all | solution.py:138
  22.8 111.9 %copy-start.27 = (f32[2304]{0:T(1024)}, f32[2304]{0:T(1024)S(1)}, u32[]{:S(2)}) copy-start(f32[2304]{0:T(1024)S(1)} %mul.537) | copy-start | bytes 27652
  25.0 17.5 %collective-permute-start.4 = (bf16[2,288,512]{2,1,0:T(8,128)(2,1)}, bf16[2,288,512]{2,1,0:T(8,128)(2,1)}, u32[]{:S(2)}, u32[]{:S(2)}) collective-permute-start(bf16[2,288,512]{2,1,0:T(8,128)(2,1)} %collective-permute-done.1), channel_id=1, source_target_pairs={{0,2},{4,0},{8,4},{12,8},{14,12},{10,14},{6,10},{2,6},{1,3},{5,1},... | collective-permute-start | bytes 1769480 | tf_op jit(solution)/shard_map/ppermute | solution.py:93
  27.0 18.7 %collective-permute-start.3 = (bf16[2,288,512]{2,1,0:T(8,128)(2,1)}, bf16[2,288,512]{2,1,0:T(8,128)(2,1)}, u32[]{:S(2)}, u32[]{:S(2)}) collective-permute-start(bf16[2,288,512]{2,1,0:T(8,128)(2,1)} %collective-permute-done), channel_id=1, source_target_pairs={{0,4},{4,8},{8,12},{12,14},{14,10},{10,6},{6,2},{2,0},{1,5},{5,9},... | collective-permute-start | bytes 1769480 | tf_op jit(solution)/shard_map/ppermute | solution.py:92
  27.1 10.4 %copy-start.40 = (s32[1024]{0:T(1024)}, s32[1024]{0:T(1024)S(1)}, u32[]{:S(2)}) copy-start(s32[1024]{0:T(1024)S(1)} %pad_clamp_fusion.2) | copy-start | bytes 12292
  29.1 30.7 %slice-start = ((s8[7077888]{0:T(1024)(128)(4,1)}), s8[2883584]{0:T(1024)(128)(4,1)S(1)}, s32[]{:S(2)}) async-start(s8[7077888]{0:T(1024)(128)(4,1)} %bitcast.206), calls=%async_computation.2 | async-start | bytes 5767168
  29.9 21.7 %collective-permute-start.2 = (bf16[2,288,512]{2,1,0:T(8,128)(2,1)}, bf16[2,288,512]{2,1,0:T(8,128)(2,1)}, u32[]{:S(2)}, u32[]{:S(2)}) collective-permute-start(bf16[2,288,512]{2,1,0:T(8,128)(2,1)} %pad_maximum_fusion.2), channel_id=1, source_target_pairs={{0,16},{16,0},{1,17},{17,1},{2,18},{18,2},{3,19},{19,3},{4,20},{20... | collective-permute-start | bytes 1769480 | tf_op jit(solution)/shard_map/ppermute | solution.py:97
  40.3 19.4 %slice-start.1 = ((s8[7077888]{0:T(1024)(128)(4,1)}), s8[4194304]{0:T(1024)(128)(4,1)S(1)}, s32[]{:S(2)}) async-start(s8[7077888]{0:T(1024)(128)(4,1)} %bitcast.206), calls=%async_computation.3 | async-start | bytes 8388608
  42.5 92.2 %copy-start.42 = (f32[128]{0:T(128)}, f32[128]{0:T(128)S(1)}, u32[]{:S(2)}) copy-start(f32[128]{0:T(128)S(1)} %get-tuple-element.79) | copy-start | bytes 1540
  42.5 15.2 %collective-permute-start.7 = (bf16[2,288,512]{2,1,0:T(8,128)(2,1)}, bf16[2,288,512]{2,1,0:T(8,128)(2,1)S(1)}, u32[]{:S(2)}, u32[]{:S(2)}) collective-permute-start(bf16[2,288,512]{2,1,0:T(8,128)(2,1)} %collective-permute-done.4), channel_id=1, source_target_pairs={{0,2},{4,0},{8,4},{12,8},{14,12},{10,14},{6,10},{2,6},{1,3},{5,1},... | collective-permute-start | bytes 1769480 | tf_op jit(solution)/shard_map/ppermute | solution.py:93
  45.8 12.5 %collective-permute-start.6 = (bf16[2,288,512]{2,1,0:T(8,128)(2,1)}, bf16[2,288,512]{2,1,0:T(8,128)(2,1)S(1)}, u32[]{:S(2)}, u32[]{:S(2)}) collective-permute-start(bf16[2,288,512]{2,1,0:T(8,128)(2,1)} %collective-permute-done.3), channel_id=1, source_target_pairs={{0,4},{4,8},{8,12},{12,14},{14,10},{10,6},{6,2},{2,0},{1,5},{5,9},... | collective-permute-start | bytes 1769480 | tf_op jit(solution)/shard_map/ppermute | solution.py:92
  50.1 16.2 %collective-permute-start.5 = (bf16[2,288,512]{2,1,0:T(8,128)(2,1)S(1)}, bf16[2,288,512]{2,1,0:T(8,128)(2,1)S(1)}, u32[]{:S(2)}, u32[]{:S(2)}) collective-permute-start(bf16[2,288,512]{2,1,0:T(8,128)(2,1)S(1)} %pad_maximum_fusion.3), channel_id=1, source_target_pairs={{0,16},{16,0},{1,17},{17,1},{2,18},{18,2},{3,19},{19,3},{4,20},{20... | collective-permute-start | bytes 1769480 | tf_op jit(solution)/shard_map/ppermute | solution.py:97
  57.7 13.6 %collective-permute-start.10 = (bf16[2,288,512]{2,1,0:T(8,128)(2,1)S(1)}, bf16[2,288,512]{2,1,0:T(8,128)(2,1)S(1)}, u32[]{:S(2)}, u32[]{:S(2)}) collective-permute-start(bf16[2,288,512]{2,1,0:T(8,128)(2,1)S(1)} %collective-permute-done.7), channel_id=1, source_target_pairs={{0,2},{4,0},{8,4},{12,8},{14,12},{10,14},{6,10},{2,6},{1,3},{5,1},... | collective-permute-start | bytes 1769480 | tf_op jit(solution)/shard_map/ppermute | solution.py:93
  58.3 13.8 %collective-permute-start.9 = (bf16[2,288,512]{2,1,0:T(8,128)(2,1)S(1)}, bf16[2,288,512]{2,1,0:T(8,128)(2,1)S(1)}, u32[]{:S(2)}, u32[]{:S(2)}) collective-permute-start(bf16[2,288,512]{2,1,0:T(8,128)(2,1)S(1)} %collective-permute-done.6), channel_id=1, source_target_pairs={{0,4},{4,8},{8,12},{12,14},{14,10},{10,6},{6,2},{2,0},{1,5},{5,9},... | collective-permute-start | bytes 1769480 | tf_op jit(solution)/shard_map/ppermute | solution.py:92
  59.9 19.0 %collective-permute-start.8 = (bf16[2,288,512]{2,1,0:T(8,128)(2,1)S(1)}, bf16[2,288,512]{2,1,0:T(8,128)(2,1)S(1)}, u32[]{:S(2)}, u32[]{:S(2)}) collective-permute-start(bf16[2,288,512]{2,1,0:T(8,128)(2,1)S(1)} %pad_maximum_fusion.4), channel_id=1, source_target_pairs={{0,16},{16,0},{1,17},{17,1},{2,18},{18,2},{3,19},{19,3},{4,20},{20... | collective-permute-start | bytes 1769480 | tf_op jit(solution)/shard_map/ppermute | solution.py:97
  71.3 13.5 %collective-permute-start.13 = (bf16[2,288,512]{2,1,0:T(8,128)(2,1)S(1)}, bf16[2,288,512]{2,1,0:T(8,128)(2,1)S(1)}, u32[]{:S(2)}, u32[]{:S(2)}) collective-permute-start(bf16[2,288,512]{2,1,0:T(8,128)(2,1)S(1)} %collective-permute-done.10), channel_id=1, source_target_pairs={{0,2},{4,0},{8,4},{12,8},{14,12},{10,14},{6,10},{2,6},{1,3},{5,1},... | collective-permute-start | bytes 1769480 | tf_op jit(solution)/shard_map/ppermute | solution.py:93
  72.0 13.5 %collective-permute-start.12 = (bf16[2,288,512]{2,1,0:T(8,128)(2,1)S(1)}, bf16[2,288,512]{2,1,0:T(8,128)(2,1)S(1)}, u32[]{:S(2)}, u32[]{:S(2)}) collective-permute-start(bf16[2,288,512]{2,1,0:T(8,128)(2,1)S(1)} %collective-permute-done.9), channel_id=1, source_target_pairs={{0,4},{4,8},{8,12},{12,14},{14,10},{10,6},{6,2},{2,0},{1,5},{5,9},... | collective-permute-start | bytes 1769480 | tf_op jit(solution)/shard_map/ppermute | solution.py:92
  73.5 18.1 %collective-permute-start.11 = (bf16[2,288,512]{2,1,0:T(8,128)(2,1)S(1)}, bf16[2,288,512]{2,1,0:T(8,128)(2,1)S(1)}, u32[]{:S(2)}, u32[]{:S(2)}) collective-permute-start(bf16[2,288,512]{2,1,0:T(8,128)(2,1)S(1)} %pad_maximum_fusion.5), channel_id=1, source_target_pairs={{0,16},{16,0},{1,17},{17,1},{2,18},{18,2},{3,19},{19,3},{4,20},{20... | collective-permute-start | bytes 1769480 | tf_op jit(solution)/shard_map/ppermute | solution.py:97
  84.8 13.5 %collective-permute-start.16 = (bf16[2,288,512]{2,1,0:T(8,128)(2,1)S(1)}, bf16[2,288,512]{2,1,0:T(8,128)(2,1)S(1)}, u32[]{:S(2)}, u32[]{:S(2)}) collective-permute-start(bf16[2,288,512]{2,1,0:T(8,128)(2,1)S(1)} %collective-permute-done.13), channel_id=1, source_target_pairs={{0,2},{4,0},{8,4},{12,8},{14,12},{10,14},{6,10},{2,6},{1,3},{5,1},... | collective-permute-start | bytes 1769480 | tf_op jit(solution)/shard_map/ppermute | solution.py:93
  85.5 13.5 %collective-permute-start.15 = (bf16[2,288,512]{2,1,0:T(8,128)(2,1)S(1)}, bf16[2,288,512]{2,1,0:T(8,128)(2,1)S(1)}, u32[]{:S(2)}, u32[]{:S(2)}) collective-permute-start(bf16[2,288,512]{2,1,0:T(8,128)(2,1)S(1)} %collective-permute-done.12), channel_id=1, source_target_pairs={{0,4},{4,8},{8,12},{12,14},{14,10},{10,6},{6,2},{2,0},{1,5},{5,9},... | collective-permute-start | bytes 1769480 | tf_op jit(solution)/shard_map/ppermute | solution.py:92
  87.0 17.2 %collective-permute-start.14 = (bf16[2,288,512]{2,1,0:T(8,128)(2,1)S(1)}, bf16[2,288,512]{2,1,0:T(8,128)(2,1)S(1)}, u32[]{:S(2)}, u32[]{:S(2)}) collective-permute-start(bf16[2,288,512]{2,1,0:T(8,128)(2,1)S(1)} %pad_maximum_fusion.6), channel_id=1, source_target_pairs={{0,16},{16,0},{1,17},{17,1},{2,18},{18,2},{3,19},{19,3},{4,20},{20... | collective-permute-start | bytes 1769480 | tf_op jit(solution)/shard_map/ppermute | solution.py:97
  98.3 10.9 %collective-permute-start.19 = (bf16[2,288,512]{2,1,0:T(8,128)(2,1)S(1)}, bf16[2,288,512]{2,1,0:T(8,128)(2,1)S(1)}, u32[]{:S(2)}, u32[]{:S(2)}) collective-permute-start(bf16[2,288,512]{2,1,0:T(8,128)(2,1)S(1)} %collective-permute-done.16), channel_id=1, source_target_pairs={{0,2},{4,0},{8,4},{12,8},{14,12},{10,14},{6,10},{2,6},{1,3},{5,1},... | collective-permute-start | bytes 1769480 | tf_op jit(solution)/shard_map/ppermute | solution.py:93
  99.0 10.9 %collective-permute-start.18 = (bf16[2,288,512]{2,1,0:T(8,128)(2,1)S(1)}, bf16[2,288,512]{2,1,0:T(8,128)(2,1)S(1)}, u32[]{:S(2)}, u32[]{:S(2)}) collective-permute-start(bf16[2,288,512]{2,1,0:T(8,128)(2,1)S(1)} %collective-permute-done.15), channel_id=1, source_target_pairs={{0,4},{4,8},{8,12},{12,14},{14,10},{10,6},{6,2},{2,0},{1,5},{5,9},... | collective-permute-start | bytes 1769480 | tf_op jit(solution)/shard_map/ppermute | solution.py:92
  100.5 16.4 %collective-permute-start.17 = (bf16[2,288,512]{2,1,0:T(8,128)(2,1)S(1)}, bf16[2,288,512]{2,1,0:T(8,128)(2,1)S(1)}, u32[]{:S(2)}, u32[]{:S(2)}) collective-permute-start(bf16[2,288,512]{2,1,0:T(8,128)(2,1)S(1)} %pad_maximum_fusion.7), channel_id=1, source_target_pairs={{0,16},{16,0},{1,17},{17,1},{2,18},{18,2},{3,19},{19,3},{4,20},{20... | collective-permute-start | bytes 1769480 | tf_op jit(solution)/shard_map/ppermute | solution.py:97
  110.1 16.5 %collective-permute-start.20 = (bf16[2,288,512]{2,1,0:T(8,128)(2,1)S(1)}, bf16[2,288,512]{2,1,0:T(8,128)(2,1)S(1)}, u32[]{:S(2)}, u32[]{:S(2)}) collective-permute-start(bf16[2,288,512]{2,1,0:T(8,128)(2,1)S(1)} %pad_maximum_fusion.8), channel_id=1, source_target_pairs={{0,16},{16,0},{1,17},{17,1},{2,18},{18,2},{3,19},{19,3},{4,20},{20... | collective-permute-start | bytes 1769480 | tf_op jit(solution)/shard_map/ppermute | solution.py:97
  126.7 7.5 %slice-start.2 = ((s8[7077888]{0:T(1024)(128)(4,1)}), s8[4194304]{0:T(1024)(128)(4,1)S(1)}, s32[]{:S(2)}) async-start(s8[7077888]{0:T(1024)(128)(4,1)} %bitcast.218), calls=%async_computation.4 | async-start | bytes 8388608
  126.8 5.8 %copy-start.1 = (bf16[2304,1536]{1,0:T(8,128)(2,1)}, bf16[2304,1536]{1,0:T(8,128)(2,1)S(1)}, u32[]{:S(2)}) copy-start(bf16[2304,1536]{1,0:T(8,128)(2,1)S(1)} %maximum_dynamic-update-slice_fusion) | copy-start | bytes 21233668
  126.8 7.4 %slice-start.3 = ((s8[7077888]{0:T(1024)(128)(4,1)}), s8[2883584]{0:T(1024)(128)(4,1)S(1)}, s32[]{:S(2)}) async-start(s8[7077888]{0:T(1024)(128)(4,1)} %bitcast.218), calls=%async_computation.5 | async-start | bytes 5767168
  138.2 7.6 %copy-start.17 = (bf16[128,512]{1,0:T(8,128)(2,1)}, bf16[128,512]{1,0:T(8,128)(2,1)S(1)}, u32[]{:S(2)}) copy-start(bf16[128,512]{1,0:T(8,128)(2,1)S(1)} %fusion.32) | copy-start | bytes 393220
  139.0 6.8 %copy-start.3 = (bf16[128,8,288]{0,2,1:T(8,128)(2,1)S(1)}, bf16[128,8,288]{0,2,1:T(8,128)(2,1)}, u32[]{:S(2)}) copy-start(bf16[128,8,288]{0,2,1:T(8,128)(2,1)} %fusion.25) | copy-start | bytes 1769476
  149.6 4.8 %copy-start.2 = (bf16[512,2304]{0,1:T(8,128)(2,1)S(1)}, bf16[512,2304]{0,1:T(8,128)(2,1)}, u32[]{:S(2)}) copy-start(bf16[512,2304]{0,1:T(8,128)(2,1)} %slice_bitcast_fusion.1) | copy-start | bytes 7077892
  161.0 4.3 %copy-start.20 = (bf16[64,2304]{1,0:T(8,128)(2,1)S(1)}, bf16[64,2304]{1,0:T(8,128)(2,1)}, u32[]{:S(2)}) copy-start(bf16[64,2304]{1,0:T(8,128)(2,1)} %param.24) | copy-start | bytes 884740
  165.1 3.5 %collective-permute-start.21 = (bf16[128,2304]{1,0:T(8,128)(2,1)S(1)}, bf16[128,2304]{1,0:T(8,128)(2,1)S(1)}, u32[]{:S(2)}, u32[]{:S(2)}) collective-permute-start(bf16[128,2304]{1,0:T(8,128)(2,1)S(1)} %fusion.8), channel_id=1, source_target_pairs={{0,1},{1,0},{2,3},{3,2},{4,5},{5,4},{6,7},{7,6},{8,9},{9,8},{10,11... | collective-permute-start | bytes 1769480 | tf_op jit(solution)/shard_map/ppermute | solution.py:57
  168.6 4.5 %slice-start.4 = ((s8[7077888]{0:T(1024)(128)(4,1)}), s8[4194304]{0:T(1024)(128)(4,1)S(1)}, s32[]{:S(2)}) async-start(s8[7077888]{0:T(1024)(128)(4,1)} %bitcast.220), calls=%async_computation.6 | async-start | bytes 8388608
  195.8 4.6 %collective-permute-start.22 = (bf16[128,2304]{1,0:T(8,128)(2,1)S(1)}, bf16[128,2304]{1,0:T(8,128)(2,1)}, u32[]{:S(2)}, u32[]{:S(2)}) collective-permute-start(bf16[128,2304]{1,0:T(8,128)(2,1)S(1)} %fusion.7), channel_id=1, source_target_pairs={{0,1},{1,0},{2,3},{3,2},{4,5},{5,4},{6,7},{7,6},{8,9},{9,8},{10,11... | collective-permute-start | bytes 1769480 | tf_op jit(solution)/shard_map/ppermute | solution.py:57
  (36 other events, 100.0 us)

commit v5 on v4

--- a/solution.py
+++ b/solution.py
@@ -9,6 +9,7 @@
 LABELS = 64
 
 
+PIECEWISE_RING = 16
 EPSILON = 1e-06
 ATTEND_CAP = 50.0
 LABEL_CAP = 30.0
@@ -106,9 +107,7 @@
                 )
             )
     back_pieces = [back_pieces[(n - k) % n] for k in range(n)]
-    front_all = jnp.concatenate(front_pieces, axis=0)
-    back_all = jnp.concatenate(back_pieces, axis=0)
-    return front_all, back_all, block_of, slot_of
+    return front_pieces, back_pieces, block_of, slot_of
 
 
 def permute_blocks(values, block_order, n):
@@ -140,20 +139,31 @@
     k_cols = key_weight.shape[1]
     front = jnp.concatenate([query_weight, key_weight], axis=1)
     back = jnp.concatenate([value_weight, out_weight.T], axis=1)
-    front_all, back_all, block_of, slot_of = ring_gather(front, back, seq_rank, lax.axis_index("groups"), n_seq)
+    front_pieces, back_pieces, block_of, slot_of = ring_gather(
+        front, back, seq_rank, lax.axis_index("groups"), n_seq
+    )
     guard_rows = permute_blocks(guard_rows, block_of, n_seq)
     pre_gain = permute_blocks(pre_gain, block_of, n_seq)
     post_gain = permute_blocks(post_gain, block_of, n_seq)
     final_gain = permute_blocks(final_gain, block_of, n_seq)
     label_table = permute_blocks(label_table, block_of, n_seq)
-    w_query = front_all[:, :q_cols]
-    w_key = front_all[:, q_cols:]
-    w_value = back_all[:, :k_cols]
-    w_out_t = back_all[:, k_cols:]
+    piecewise = n_seq <= PIECEWISE_RING
+    if piecewise:
+        w_query_t = jnp.concatenate([piece[:, :q_cols].T for piece in front_pieces], axis=1)
+        w_key_t = jnp.concatenate([piece[:, q_cols:].T for piece in front_pieces], axis=1)
+        w_value_t = jnp.concatenate([piece[:, :k_cols].T for piece in back_pieces], axis=1)
+        w_out = jnp.concatenate([piece[:, k_cols:].T for piece in back_pieces], axis=1)
+    else:
+        front_all = jnp.concatenate(front_pieces, axis=0)
+        back_all = jnp.concatenate(back_pieces, axis=0)
+        w_query_t = front_all[:, :q_cols].T
+        w_key_t = front_all[:, q_cols:].T
+        w_value_t = back_all[:, :k_cols].T
+        w_out = back_all[:, k_cols:].T
     tok_rows = guard_rows.shape[0]
     half_width = generator_rows.shape[1]
-    local_heads = w_query.shape[1] // HD
-    local_kv = w_key.shape[1] // HD
+    local_heads = q_cols // HD
+    local_kv = k_cols // HD
     group_size = local_heads // local_kv
     length = lax.dynamic_index_in_dim(lengths, seq_rank, 0, keepdims=False)
     target = lax.dynamic_index_in_dim(label_index, seq_rank, 0, keepdims=False)
@@ -162,20 +172,25 @@
     inputs = guard_rows.astype(jnp.float32)
     scale_in = lax.rsqrt(jnp.mean(inputs * inputs, axis=-1, keepdims=True) + EPSILON)
     normed = (inputs * scale_in * pre_gain).astype(jnp.bfloat16)
-    query_proj = (
-        jnp.dot(normed, w_query, preferred_element_type=jnp.float32)
-        .reshape(tok_rows, local_heads, HD)
-        .transpose(1, 0, 2)
-    )
+    if piecewise:
+        block_rows = front_pieces[0].shape[0]
+        front_proj = None
+        back_proj = None
+        for index, (front_piece, back_piece) in enumerate(zip(front_pieces, back_pieces)):
+            normed_block = normed[:, index * block_rows:(index + 1) * block_rows]
+            front_term = jnp.dot(normed_block, front_piece, preferred_element_type=jnp.float32)
+            back_term = jnp.dot(normed_block, back_piece[:, :k_cols], preferred_element_type=jnp.float32)
+            front_proj = front_term if front_proj is None else front_proj + front_term
+            back_proj = back_term if back_proj is None else back_proj + back_term
+    else:
+        front_proj = jnp.dot(normed, front_all, preferred_element_type=jnp.float32)
+        back_proj = jnp.dot(normed, back_all[:, :k_cols], preferred_element_type=jnp.float32)
+    query_proj = front_proj[:, :q_cols].reshape(tok_rows, local_heads, HD).transpose(1, 0, 2)
     queries = (rotate(query_proj, cos_table, sin_table) * QUERY_SCALE).astype(jnp.bfloat16)
-    key_proj = (
-        jnp.dot(normed, w_key, preferred_element_type=jnp.float32)
-        .reshape(tok_rows, local_kv, HD)
-        .transpose(1, 0, 2)
-    )
+    key_proj = front_proj[:, q_cols:].reshape(tok_rows, local_kv, HD).transpose(1, 0, 2)
     keys_own = rotate(key_proj, cos_table, sin_table).astype(jnp.bfloat16)
     values_own = (
-        jnp.dot(normed, w_value, preferred_element_type=jnp.float32)
+        back_proj
         .astype(jnp.bfloat16)
         .reshape(tok_rows, local_kv, HD)
         .transpose(1, 0, 2)
@@ -197,7 +212,7 @@
         .transpose(1, 0, 2)
         .reshape(tok_rows, local_heads * HD)
     )
-    out_part = times_transposed(context_rows, w_out_t)
+    out_part = jnp.dot(context_rows, w_out, preferred_element_type=jnp.float32)
     attention = pair_sum(out_part.astype(jnp.bfloat16))
     scale_attn = lax.rsqrt(jnp.mean(attention * attention, axis=-1, keepdims=True) + EPSILON)
     mixed_rows = inputs + attention * scale_attn * post_gain
@@ -223,9 +238,7 @@
     grad_attention = scale_attn * scaled_post - attention * cube_attn * jnp.mean(
         scaled_post * attention, axis=-1, keepdims=True
     )
-    grad_context = jnp.dot(
-        grad_attention.astype(jnp.bfloat16), w_out_t, preferred_element_type=jnp.float32
-    ).astype(jnp.bfloat16)
+    grad_context = times_transposed(grad_attention.astype(jnp.bfloat16), w_out).astype(jnp.bfloat16)
     grad_four = grad_context.reshape(tok_rows, local_kv, group_size, HD).transpose(1, 2, 0, 3)
     grad_prob = jnp.einsum(
         "kgid,kjd->kgij", grad_four, values_own, preferred_element_type=jnp.float32
@@ -250,9 +263,9 @@
     key_rows = grad_keys.transpose(1, 0, 2).reshape(tok_rows, local_kv * HD)
     value_rows = grad_values.transpose(1, 0, 2).reshape(tok_rows, local_kv * HD)
     grad_part = (
-        times_transposed(query_rows, w_query)
-        + times_transposed(key_rows, w_key)
-        + times_transposed(value_rows, w_value)
+        jnp.dot(query_rows, w_query_t, preferred_element_type=jnp.float32)
+        + jnp.dot(key_rows, w_key_t, preferred_element_type=jnp.float32)
+        + jnp.dot(value_rows, w_value_t, preferred_element_type=jnp.float32)
     )
     cube_in = scale_in * scale_in * scale_in
     grad_normed = pair_sum(grad_part.astype(jnp.bfloat16))

time: 225 us -> 226 us (level)
  other arithmetic: 26.8 us -> 41.5 us
  local copies, waits for them, and re-layouts: 52.6 us -> 45.8 us
  matrix products: 34.4 us -> 29.6 us
    ppermute x7, waiting for transfers between devices: 2.38 us -> 38.4 us  [ring_gather(): front_ring.append(lax.ppermute(front_ring[-1], 'seq', forward_pairs))]
    ppermute x7, waiting for transfers between devices: 28.5 us -> 6.88 us  [ring_gather(): lax.ppermute(jnp.stack([front_ring[step][0], back_ring[step][0]]), 'group...]
    ppermute x7, waiting for transfers between devices: 25.2 us -> 10.5 us  [ring_gather(): back_ring.append(lax.ppermute(back_ring[-1], 'seq', backward_pairs))]
    dot_general x4 -> x0, local copies, waits for them, and re-layouts: 14 us -> none  [the longest x2 9.83 us: shards(): jnp.dot(normed, w_query, preferred_element_type=jnp.float32)]
    unnamed x121 -> x205, local copies, waits for them, and re-layouts: 7.19 us -> 19 us
    dot_general x5 -> x2, matrix products: 14 us -> 2.75 us  [times_transposed(): lax.dot_general(left_side, right_side, (((1,), (1,)), ((), ())), preferre...]
    dot_general x4 -> x20, matrix products: 8.84 us -> 17.5 us  [the longest x1 4.18 us: shards(): out_part = jnp.dot(context_rows, w_out, preferred_element_type=jnp.float32)]
    ppermute x7, starting transfers between devices: 5.52 us -> 13.1 us  [ring_gather(): front_ring.append(lax.ppermute(front_ring[-1], 'seq', forward_pairs))]
  transfers between devices with their start and end apart: 24 -> 24, of which waited for: 17 -> 15; matrix products, arithmetic and copies ran while one was open for 18% -> 27% of each run, Pallas kernels for 0% -> 0%
where the time goes in v5:
time: 226 us; the launch traced here: 224 us
  waiting for transfers between devices  55.8 us (25%)
  local copies, waits for them, and re-layouts  45.8 us (20%)
  other arithmetic  41.5 us (18%)
  starting transfers between devices  31.7 us (14%)
  matrix products  29.6 us (13%)
  blocking collectives  18.6 us (8%)
    ppermute x7, waiting for transfers between devices, ring_gather(): front_ring.append(lax.ppermute(front_ring[-1], 'seq', forward_pairs))  38.4 us
    unnamed x205, local copies, waits for them, and re-layouts  19 us
    all_to_all x1, blocking collectives, shards(): lax.all_to_all(grad_rows.astype(jnp.bfloat16), 'seq', split_axis=0, conca...  14.2 us
    ppermute x7, starting transfers between devices, ring_gather(): front_ring.append(lax.ppermute(front_ring[-1], 'seq', forward_pairs))  13.1 us
    ppermute x7, waiting for transfers between devices, ring_gather(): back_ring.append(lax.ppermute(back_ring[-1], 'seq', backward_pairs))  10.5 us
    select_n x7, other arithmetic, ring_gather(): jnp.where(first_group, other, own)  9.87 us
    unnamed x25, other arithmetic  9.09 us
    ppermute x7, starting transfers between devices, ring_gather(): lax.ppermute(jnp.stack([front_ring[step][0], back_ring[step][0]]), 'group...  7.74 us
  transfers between devices with their start and end apart: 24, of which 15 were waited for; matrix products, arithmetic and copies ran while one was open for 27% of the time, Pallas kernels for 0%

profile of v5, /device:TPU:0, one launch (start us, length us, event | category | flops | bytes accessed | tf_op | source)
XLA Modules:
  0.0 224.3 jit_solution(8628421638102519205)
XLA Ops:
  0.0 4.3 %all_gather.3 = bf16[128,2304]{1,0:T(8,128)(2,1)} all-gather(bf16[128,1152]{1,0:T(8,128)(2,1)} %param.16), channel_id=1, replica_groups=mesh['groups'=2,'seq'=8,'wg'=2] {'wg'}, dimensions={1}, use_global_device_ids=true | all-gather | bytes 884736 | tf_op jit(solution)/shard_map/all_gather | solution.py:136
  4.4 6.9 %all-to-all-start = ((bf16[8,16,2304]{2,1,0:T(8,128)(2,1)}), bf16[8,16,2304]{2,1,0:T(8,128)(2,1)}, u32[]{:S(2)}, u32[]{:S(2)}) async-start(bf16[8,16,2304]{2,1,0:T(8,128)(2,1)} %bitcast.2), calls=%async_computation | async-start | bytes 1179648 | tf_op jit(solution)/shard_map/all_to_all | solution.py:137
  12.3 2.0 collective-permute-start
  32.7 1.6 collective-permute-done
  38.2 1.5 collective-permute-start.2
  39.8 4.6 %collective-permute-start.3 = (bf16[2,288,512]{2,1,0:T(8,128)(2,1)}, bf16[2,288,512]{2,1,0:T(8,128)(2,1)}, u32[]{:S(2)}, u32[]{:S(2)}) collective-permute-start(bf16[2,288,512]{2,1,0:T(8,128)(2,1)} %collective-permute-done), channel_id=1, source_target_pairs={{0,4},{4,8},{8,12},{12,14},{14,10},{10,6},{6,2},{2,0},{1,5},{5,9},... | collective-permute-start | bytes 1769480 | tf_op jit(solution)/shard_map/ppermute | solution.py:93
  44.4 2.3 %reshape.368 = bf16[128,8,288]{2,1,0:T(8,128)(2,1)S(1)} reshape(bf16[8,16,2304]{2,1,0:T(8,128)(2,1)} %all-to-all-done) | data formatting | bytes 1179648 | tf_op jit(solution)/shard_map/reshape | solution.py:116
  49.9 6.5 %collective-permute-done.3 = bf16[2,288,512]{2,1,0:T(8,128)(2,1)} collective-permute-done((bf16[2,288,512]{2,1,0:T(8,128)(2,1)}, bf16[2,288,512]{2,1,0:T(8,128)(2,1)}, u32[]{:S(2)}, u32[]{:S(2)}) %collective-permute-start.3) | collective-permute-done | bytes 589856 | tf_op jit(solution)/shard_map/ppermute | solution.py:93
  57.4 1.6 collective-permute-done.4
  60.6 1.7 collective-permute-start.6
  62.6 2.3 %fusion.130 = (bf16[288,512]{1,0:T(8,128)(2,1)S(1)}, bf16[288,512]{1,0:T(8,128)(2,1)S(1)}, bf16[288,512]{1,0:T(8,128)(2,1)S(1)}, bf16[288,512]{1,0:T(8,128)(2,1)}, bf16[288,512]{1,0:T(8,128)(2,1)}) fusion(bf16[2,288,512]{2,1,0:T(8,128)(2,1)} %collective-permute-done.2, pred[]{:T(512)S(6)} %eq.16, bf16[2,288,512]{2,1,0:T(8,128)(2,1)} %collective-permute-done, ...), kind=kLoop, calls=%fused_computation.280 | loop fusion | flops 442368 | bytes 3244033 | tf_op jit(solution)/shard_map/jit(_where)/select_n | solution.py:105
  65.9 1.3 fusion.89
  67.6 6.4 %collective-permute-done.6 = bf16[2,288,512]{2,1,0:T(8,128)(2,1)S(1)} collective-permute-done((bf16[2,288,512]{2,1,0:T(8,128)(2,1)}, bf16[2,288,512]{2,1,0:T(8,128)(2,1)S(1)}, u32[]{:S(2)}, u32[]{:S(2)}) %collective-permute-start.6) | collective-permute-done | bytes 589856 | tf_op jit(solution)/shard_map/ppermute | solution.py:93
  74.0 1.8 collective-permute-done.7
  75.9 1.6 collective-permute-start.8
  77.5 1.6 collective-permute-start.9
  79.5 2.4 %fusion.131 = (bf16[288,512]{1,0:T(8,128)(2,1)S(1)}, bf16[288,512]{1,0:T(8,128)(2,1)S(1)}, bf16[288,512]{1,0:T(8,128)(2,1)S(1)}, bf16[288,512]{1,0:T(8,128)(2,1)}, bf16[288,512]{1,0:T(8,128)(2,1)}) fusion(bf16[2,288,512]{2,1,0:T(8,128)(2,1)S(1)} %collective-permute-done.5, pred[]{:T(512)S(6)} %eq.16, bf16[2,288,512]{2,1,0:T(8,128)(2,1)} %collective-permute-done.3, ...), kind=kLoop, calls=%fused_computation.281 | loop fusion | flops 442368 | bytes 3244033 | tf_op jit(solution)/shard_map/jit(_where)/select_n | solution.py:105
  82.9 1.2 fusion.91
  84.5 5.0 %collective-permute-done.9 = bf16[2,288,512]{2,1,0:T(8,128)(2,1)S(1)} collective-permute-done((bf16[2,288,512]{2,1,0:T(8,128)(2,1)S(1)}, bf16[2,288,512]{2,1,0:T(8,128)(2,1)S(1)}, u32[]{:S(2)}, u32[]{:S(2)}) %collective-permute-start.9) | collective-permute-done | bytes 589856 | tf_op jit(solution)/shard_map/ppermute | solution.py:93
  89.5 1.7 collective-permute-done.10
  96.5 6.6 %collective-permute-done.12 = bf16[2,288,512]{2,1,0:T(8,128)(2,1)S(1)} collective-permute-done((bf16[2,288,512]{2,1,0:T(8,128)(2,1)S(1)}, bf16[2,288,512]{2,1,0:T(8,128)(2,1)S(1)}, u32[]{:S(2)}, u32[]{:S(2)}) %collective-permute-start.12) | collective-permute-done | bytes 589856 | tf_op jit(solution)/shard_map/ppermute | solution.py:93
  103.1 1.5 collective-permute-done.13
  104.7 1.5 collective-permute-start.14
  110.9 7.2 %collective-permute-done.15 = bf16[2,288,512]{2,1,0:T(8,128)(2,1)S(1)} collective-permute-done((bf16[2,288,512]{2,1,0:T(8,128)(2,1)S(1)}, bf16[2,288,512]{2,1,0:T(8,128)(2,1)S(1)}, u32[]{:S(2)}, u32[]{:S(2)}) %collective-permute-start.15) | collective-permute-done | bytes 589856 | tf_op jit(solution)/shard_map/ppermute | solution.py:93
  118.1 1.4 collective-permute-done.16
  120.7 1.3 collective-permute-start.18
  125.3 5.2 %collective-permute-done.18 = bf16[2,288,512]{2,1,0:T(8,128)(2,1)S(1)} collective-permute-done((bf16[2,288,512]{2,1,0:T(8,128)(2,1)S(1)}, bf16[2,288,512]{2,1,0:T(8,128)(2,1)S(1)}, u32[]{:S(2)}, u32[]{:S(2)}) %collective-permute-start.18) | collective-permute-done | bytes 589856 | tf_op jit(solution)/shard_map/ppermute | solution.py:93
  130.6 1.3 collective-permute-done.19
  135.3 6.9 %collective-permute-done.20 = bf16[2,288,512]{2,1,0:T(8,128)(2,1)S(1)} collective-permute-done((bf16[2,288,512]{2,1,0:T(8,128)(2,1)S(1)}, bf16[2,288,512]{2,1,0:T(8,128)(2,1)S(1)}, u32[]{:S(2)}, u32[]{:S(2)}) %collective-permute-start.20) | collective-permute-done | bytes 589856 | tf_op jit(solution)/shard_map/ppermute | solution.py:98
  154.9 2.2 copy-done.1
  157.1 4.2 %convolution_convert_fusion = bf16[128,2304]{1,0:T(8,128)(2,1)S(1)} fusion(bf16[128,1024]{0,1:T(8,128)(2,1)S(1)} %bitcast.335, bf16[1024,2304]{0,1:T(8,128)(2,1)} %copy-done.1), kind=kOutput, calls=%fused_computation.12 | convolution fusion | flops 604274688 | bytes 5570560 | tf_op jit(solution)/shard_map/dot_general | solution.py:215
  164.3 1.4 bitcast_dynamic-update-slice_fusion.1
  165.8 1.4 bitcast_dynamic-update-slice_fusion.13
  169.8 1.4 copy-done.6
  174.6 2.1 convolution_convert_fusion.2
  177.9 2.0 fusion.18
  180.9 2.7 %convolution_bitcast_fusion.1 = f32[4,128,128]{2,1,0:T(8,128)} fusion(bf16[4,2,128,128]{3,2,1,0:T(8,128)(2,1)} %copy-done.66, f32[4,2,128,128]{2,3,1,0:T(8,128)} %fusion.108, f32[4,2,128,128]{2,3,1,0:T(8,128)} %copy-done.92, f32[4,2,128]{2,1,0:T(2,128)S(1)} %copy-done.94, pred[128,128]{0,1:T(8,128)(4,1)S(1)} %copy-done.74), kind=kOutput, calls=%fused_computation.50 | convolution fusion | flops 35259520 | bytes 1593344 | tf_op jit(solution)/shard_map/kgij,kgid->kjd/dot_general | solution.py:256
  183.7 2.2 convolution_multiply_fusion.1
  185.9 1.4 add_convert_fusion.1
  188.1 1.7 copy.77
  191.4 4.1 %fusion.101 = f32[128,2304]{1,0:T(8,128)S(1)} fusion(bf16[1024,2304]{0,1:T(8,128)(2,1)} %fusion.78, bf16[16,8,8,128]{3,2,1,0:T(8,128)(2,1)S(1)} %bitcast.331), kind=kOutput, calls=%fused_computation.239 | convolution fusion | flops 603979776 | bytes 6160384 | tf_op jit(solution)/shard_map/dot_general | solution.py:266
  198.4 1.2 broadcast_in_dim.111
  199.6 1.4 broadcast_in_dim.112
  201.0 1.3 dynamic-slice
  202.4 1.5 fusion.12
  203.8 2.9 %fusion.11 = bf16[128,2304]{1,0:T(8,128)(2,1)} fusion(bf16[128,2304]{1,0:T(8,128)(2,1)} %collective-permute-done.22, bf16[128,2304]{1,0:T(8,128)(2,1)S(1)} %fusion.1, f32[128]{0:T(128)S(1)} %broadcast_multiply_fusion, f32[128]{0:T(128)} %get-tuple-element.61, f32[2304]{0:T(1024)S(1)} %copy-done.68, f32[128]{0:T(128)} %copy-done.81, ...), kind=kLoop, calls=%fused_computation.37 | loop fusion | flops 6488064 | bytes 4742912 | tf_op jit(solution)/shard_map/add | solution.py:274
  206.7 1.4 copy.79
  209.3 14.2 %all_to_all.21 = bf16[8,16,1152]{2,1,0:T(8,128)(2,1)S(1)} all-to-all(bf16[8,16,1152]{2,1,0:T(8,128)(2,1)S(1)} %bitcast.329), channel_id=1, replica_groups=mesh['groups'=2,'seq'=8,'wg'=2] {'seq'}, dimensions={0} | all-to-all | bytes 589824 | tf_op jit(solution)/shard_map/all_to_all | solution.py:277
  (369 shorter events, 80.9 us)
Async XLA Ops:
  0.0 11.3 %copy-start.11 = (bf16[288,512]{1,0:T(8,128)(2,1)S(1)}, bf16[288,512]{1,0:T(8,128)(2,1)}, u32[]{:S(2)}) copy-start(bf16[288,512]{1,0:T(8,128)(2,1)} %param.20) | copy-start | bytes 884740
  0.0 11.3 %copy-start.12 = (bf16[288,512]{1,0:T(8,128)(2,1)S(1)}, bf16[288,512]{1,0:T(8,128)(2,1)}, u32[]{:S(2)}) copy-start(bf16[288,512]{1,0:T(8,128)(2,1)} %param.19) | copy-start | bytes 884740
  0.0 11.3 %copy-start.2 = (bf16[288,1024]{1,0:T(8,128)(2,1)S(1)}, bf16[288,1024]{1,0:T(8,128)(2,1)}, u32[]{:S(2)}) copy-start(bf16[288,1024]{1,0:T(8,128)(2,1)} %param.18) | copy-start | bytes 1769476
  0.0 11.3 %copy-start.38 = (bf16[1024,288]{0,1:T(8,128)(2,1)S(1)}, bf16[1024,288]{0,1:T(8,128)(2,1)}, u32[]{:S(2)}) copy-start(bf16[1024,288]{0,1:T(8,128)(2,1)} %param.21) | copy-start | bytes 1769476
  4.4 40.0 %all-to-all-start = ((bf16[8,16,2304]{2,1,0:T(8,128)(2,1)}), bf16[8,16,2304]{2,1,0:T(8,128)(2,1)}, u32[]{:S(2)}, u32[]{:S(2)}) async-start(bf16[8,16,2304]{2,1,0:T(8,128)(2,1)} %bitcast.2), calls=%async_computation | async-start | bytes 1179648 | tf_op jit(solution)/shard_map/all_to_all | solution.py:137
  11.4 5.1 %copy-start = (s32[8]{0:T(128)S(1)}, s32[8]{0:T(128)}, u32[]{:S(2)}) copy-start(s32[8]{0:T(128)} %constant.130.clone) | copy-start | bytes 100
  12.3 21.9 %collective-permute-start = (bf16[2,288,512]{2,1,0:T(8,128)(2,1)}, bf16[2,288,512]{2,1,0:T(8,128)(2,1)}, u32[]{:S(2)}, u32[]{:S(2)}) collective-permute-start(bf16[2,288,512]{2,1,0:T(8,128)(2,1)} %pad_maximum_fusion), channel_id=1, source_target_pairs={{0,4},{4,8},{8,12},{12,14},{14,10},{10,6},{6,2},{2,0},{1,5},{5,9},... | collective-permute-start | bytes 1769480 | tf_op jit(solution)/shard_map/ppermute | solution.py:93
  14.3 5.7 %copy-start.87 = (s32[8]{0:T(128)S(1)}, s32[8]{0:T(128)}, u32[]{:S(2)}) copy-start(s32[8]{0:T(128)} %constant.131) | copy-start | bytes 100
  14.4 7.1 %copy-start.75 = (f32[2304]{0:T(1024)S(1)}, f32[2304]{0:T(1024)}, u32[]{:S(2)}) copy-start(f32[2304]{0:T(1024)} %param.17) | copy-start | bytes 27652
  15.3 6.2 %copy-start.76 = (f32[2304]{0:T(1024)S(1)}, f32[2304]{0:T(1024)}, u32[]{:S(2)}) copy-start(f32[2304]{0:T(1024)} %param.22) | copy-start | bytes 27652
  15.3 8.1 %copy-start.77 = (f32[2304]{0:T(1024)S(1)}, f32[2304]{0:T(1024)}, u32[]{:S(2)}) copy-start(f32[2304]{0:T(1024)} %param.23) | copy-start | bytes 27652
  15.3 10.3 %copy-start.64 = (bf16[64,2304]{1,0:T(8,128)(2,1)S(1)}, bf16[64,2304]{1,0:T(8,128)(2,1)}, u32[]{:S(2)}) copy-start(bf16[64,2304]{1,0:T(8,128)(2,1)} %param.24) | copy-start | bytes 884740
  15.3 21.1 %collective-permute-start.1 = (bf16[2,288,512]{2,1,0:T(8,128)(2,1)}, bf16[2,288,512]{2,1,0:T(8,128)(2,1)}, u32[]{:S(2)}, u32[]{:S(2)}) collective-permute-start(bf16[2,288,512]{2,1,0:T(8,128)(2,1)} %pad_maximum_fusion.1), channel_id=1, source_target_pairs={{0,2},{4,0},{8,4},{12,8},{14,12},{10,14},{6,10},{2,6},{1,3},{5,1},... | collective-permute-start | bytes 1769480 | tf_op jit(solution)/shard_map/ppermute | solution.py:94
  20.1 5.5 %copy-start.85 = (pred[128]{0:T(512)(128)(4,1)}, pred[128]{0:T(512)(128)(4,1)S(1)}, u32[]{:S(2)}) copy-start(pred[128]{0:T(512)(128)(4,1)S(1)} %iota_compare_fusion.1) | copy-start | bytes 388
  24.9 24.2 %copy-start.67 = (f32[2304]{0:T(1024)}, f32[2304]{0:T(1024)S(1)}, u32[]{:S(2)}) copy-start(f32[2304]{0:T(1024)S(1)} %mul.486) | copy-start | bytes 27652
  38.2 24.4 %collective-permute-start.2 = (bf16[2,288,512]{2,1,0:T(8,128)(2,1)}, bf16[2,288,512]{2,1,0:T(8,128)(2,1)}, u32[]{:S(2)}, u32[]{:S(2)}) collective-permute-start(bf16[2,288,512]{2,1,0:T(8,128)(2,1)} %pad_maximum_fusion.2), channel_id=1, source_target_pairs={{0,16},{16,0},{1,17},{17,1},{2,18},{18,2},{3,19},{19,3},{4,20},{20... | collective-permute-start | bytes 1769480 | tf_op jit(solution)/shard_map/ppermute | solution.py:98
  39.8 16.6 %collective-permute-start.3 = (bf16[2,288,512]{2,1,0:T(8,128)(2,1)}, bf16[2,288,512]{2,1,0:T(8,128)(2,1)}, u32[]{:S(2)}, u32[]{:S(2)}) collective-permute-start(bf16[2,288,512]{2,1,0:T(8,128)(2,1)} %collective-permute-done), channel_id=1, source_target_pairs={{0,4},{4,8},{8,12},{12,14},{14,10},{10,6},{6,2},{2,0},{1,5},{5,9},... | collective-permute-start | bytes 1769480 | tf_op jit(solution)/shard_map/ppermute | solution.py:93
  44.4 14.6 %collective-permute-start.4 = (bf16[2,288,512]{2,1,0:T(8,128)(2,1)}, bf16[2,288,512]{2,1,0:T(8,128)(2,1)}, u32[]{:S(2)}, u32[]{:S(2)}) collective-permute-start(bf16[2,288,512]{2,1,0:T(8,128)(2,1)} %collective-permute-done.1), channel_id=1, source_target_pairs={{0,2},{4,0},{8,4},{12,8},{14,12},{10,14},{6,10},{2,6},{1,3},{5,1},... | collective-permute-start | bytes 1769480 | tf_op jit(solution)/shard_map/ppermute | solution.py:94
  60.0 19.5 %collective-permute-start.5 = (bf16[2,288,512]{2,1,0:T(8,128)(2,1)S(1)}, bf16[2,288,512]{2,1,0:T(8,128)(2,1)S(1)}, u32[]{:S(2)}, u32[]{:S(2)}) collective-permute-start(bf16[2,288,512]{2,1,0:T(8,128)(2,1)S(1)} %pad_maximum_fusion.3), channel_id=1, source_target_pairs={{0,16},{16,0},{1,17},{17,1},{2,18},{18,2},{3,19},{19,3},{4,20},{20... | collective-permute-start | bytes 1769480 | tf_op jit(solution)/shard_map/ppermute | solution.py:98
  60.6 13.4 %collective-permute-start.6 = (bf16[2,288,512]{2,1,0:T(8,128)(2,1)}, bf16[2,288,512]{2,1,0:T(8,128)(2,1)S(1)}, u32[]{:S(2)}, u32[]{:S(2)}) collective-permute-start(bf16[2,288,512]{2,1,0:T(8,128)(2,1)} %collective-permute-done.3), channel_id=1, source_target_pairs={{0,4},{4,8},{8,12},{12,14},{14,10},{10,6},{6,2},{2,0},{1,5},{5,9},... | collective-permute-start | bytes 1769480 | tf_op jit(solution)/shard_map/ppermute | solution.py:93
  62.4 13.4 %collective-permute-start.7 = (bf16[2,288,512]{2,1,0:T(8,128)(2,1)}, bf16[2,288,512]{2,1,0:T(8,128)(2,1)S(1)}, u32[]{:S(2)}, u32[]{:S(2)}) collective-permute-start(bf16[2,288,512]{2,1,0:T(8,128)(2,1)} %collective-permute-done.4), channel_id=1, source_target_pairs={{0,2},{4,0},{8,4},{12,8},{14,12},{10,14},{6,10},{2,6},{1,3},{5,1},... | collective-permute-start | bytes 1769480 | tf_op jit(solution)/shard_map/ppermute | solution.py:94
  74.0 19.8 %copy-start.16 = (bf16[2,288,512]{2,1,0:T(8,128)(2,1)}, bf16[2,288,512]{2,1,0:T(8,128)(2,1)S(1)}, u32[]{:S(2)}) copy-start(bf16[2,288,512]{2,1,0:T(8,128)(2,1)S(1)} %collective-permute-done.6) | copy-start | bytes 1769476
  75.8 20.0 %copy-start.18 = (bf16[2,288,512]{2,1,0:T(8,128)(2,1)}, bf16[2,288,512]{2,1,0:T(8,128)(2,1)S(1)}, u32[]{:S(2)}) copy-start(bf16[2,288,512]{2,1,0:T(8,128)(2,1)S(1)} %collective-permute-done.7) | copy-start | bytes 1769476
  75.9 17.9 %collective-permute-start.8 = (bf16[2,288,512]{2,1,0:T(8,128)(2,1)S(1)}, bf16[2,288,512]{2,1,0:T(8,128)(2,1)S(1)}, u32[]{:S(2)}, u32[]{:S(2)}) collective-permute-start(bf16[2,288,512]{2,1,0:T(8,128)(2,1)S(1)} %pad_maximum_fusion.4), channel_id=1, source_target_pairs={{0,16},{16,0},{1,17},{17,1},{2,18},{18,2},{3,19},{19,3},{4,20},{20... | collective-permute-start | bytes 1769480 | tf_op jit(solution)/shard_map/ppermute | solution.py:98
  77.5 12.0 %collective-permute-start.9 = (bf16[2,288,512]{2,1,0:T(8,128)(2,1)S(1)}, bf16[2,288,512]{2,1,0:T(8,128)(2,1)S(1)}, u32[]{:S(2)}, u32[]{:S(2)}) collective-permute-start(bf16[2,288,512]{2,1,0:T(8,128)(2,1)S(1)} %collective-permute-done.6), channel_id=1, source_target_pairs={{0,4},{4,8},{8,12},{12,14},{14,10},{10,6},{6,2},{2,0},{1,5},{5,9},... | collective-permute-start | bytes 1769480 | tf_op jit(solution)/shard_map/ppermute | solution.py:93
  79.1 12.1 %collective-permute-start.10 = (bf16[2,288,512]{2,1,0:T(8,128)(2,1)S(1)}, bf16[2,288,512]{2,1,0:T(8,128)(2,1)S(1)}, u32[]{:S(2)}, u32[]{:S(2)}) collective-permute-start(bf16[2,288,512]{2,1,0:T(8,128)(2,1)S(1)} %collective-permute-done.7), channel_id=1, source_target_pairs={{0,2},{4,0},{8,4},{12,8},{14,12},{10,14},{6,10},{2,6},{1,3},{5,1},... | collective-permute-start | bytes 1769480 | tf_op jit(solution)/shard_map/ppermute | solution.py:94
  89.5 18.8 %copy-start.22 = (bf16[2,288,512]{2,1,0:T(8,128)(2,1)}, bf16[2,288,512]{2,1,0:T(8,128)(2,1)S(1)}, u32[]{:S(2)}) copy-start(bf16[2,288,512]{2,1,0:T(8,128)(2,1)S(1)} %collective-permute-done.9) | copy-start | bytes 1769476
  91.2 19.1 %copy-start.24 = (bf16[2,288,512]{2,1,0:T(8,128)(2,1)}, bf16[2,288,512]{2,1,0:T(8,128)(2,1)S(1)}, u32[]{:S(2)}) copy-start(bf16[2,288,512]{2,1,0:T(8,128)(2,1)S(1)} %collective-permute-done.10) | copy-start | bytes 1769476
  91.3 16.9 %collective-permute-start.11 = (bf16[2,288,512]{2,1,0:T(8,128)(2,1)S(1)}, bf16[2,288,512]{2,1,0:T(8,128)(2,1)S(1)}, u32[]{:S(2)}, u32[]{:S(2)}) collective-permute-start(bf16[2,288,512]{2,1,0:T(8,128)(2,1)S(1)} %pad_maximum_fusion.5), channel_id=1, source_target_pairs={{0,16},{16,0},{1,17},{17,1},{2,18},{18,2},{3,19},{19,3},{4,20},{20... | collective-permute-start | bytes 1769480 | tf_op jit(solution)/shard_map/ppermute | solution.py:98
  91.8 11.3 %collective-permute-start.12 = (bf16[2,288,512]{2,1,0:T(8,128)(2,1)S(1)}, bf16[2,288,512]{2,1,0:T(8,128)(2,1)S(1)}, u32[]{:S(2)}, u32[]{:S(2)}) collective-permute-start(bf16[2,288,512]{2,1,0:T(8,128)(2,1)S(1)} %collective-permute-done.9), channel_id=1, source_target_pairs={{0,4},{4,8},{8,12},{12,14},{14,10},{10,6},{6,2},{2,0},{1,5},{5,9},... | collective-permute-start | bytes 1769480 | tf_op jit(solution)/shard_map/ppermute | solution.py:93
  92.7 12.0 %collective-permute-start.13 = (bf16[2,288,512]{2,1,0:T(8,128)(2,1)S(1)}, bf16[2,288,512]{2,1,0:T(8,128)(2,1)S(1)}, u32[]{:S(2)}, u32[]{:S(2)}) collective-permute-start(bf16[2,288,512]{2,1,0:T(8,128)(2,1)S(1)} %collective-permute-done.10), channel_id=1, source_target_pairs={{0,2},{4,0},{8,4},{12,8},{14,12},{10,14},{6,10},{2,6},{1,3},{5,1},... | collective-permute-start | bytes 1769480 | tf_op jit(solution)/shard_map/ppermute | solution.py:94
  103.1 19.6 %copy-start.28 = (bf16[2,288,512]{2,1,0:T(8,128)(2,1)}, bf16[2,288,512]{2,1,0:T(8,128)(2,1)S(1)}, u32[]{:S(2)}) copy-start(bf16[2,288,512]{2,1,0:T(8,128)(2,1)S(1)} %collective-permute-done.12) | copy-start | bytes 1769476
  104.7 20.0 %copy-start.32 = (bf16[2,288,512]{2,1,0:T(8,128)(2,1)}, bf16[2,288,512]{2,1,0:T(8,128)(2,1)S(1)}, u32[]{:S(2)}) copy-start(bf16[2,288,512]{2,1,0:T(8,128)(2,1)S(1)} %collective-permute-done.13) | copy-start | bytes 1769476
  104.7 18.0 %collective-permute-start.14 = (bf16[2,288,512]{2,1,0:T(8,128)(2,1)S(1)}, bf16[2,288,512]{2,1,0:T(8,128)(2,1)S(1)}, u32[]{:S(2)}, u32[]{:S(2)}) collective-permute-start(bf16[2,288,512]{2,1,0:T(8,128)(2,1)S(1)} %pad_maximum_fusion.6), channel_id=1, source_target_pairs={{0,16},{16,0},{1,17},{17,1},{2,18},{18,2},{3,19},{19,3},{4,20},{20... | collective-permute-start | bytes 1769480 | tf_op jit(solution)/shard_map/ppermute | solution.py:98
  106.2 11.9 %collective-permute-start.15 = (bf16[2,288,512]{2,1,0:T(8,128)(2,1)S(1)}, bf16[2,288,512]{2,1,0:T(8,128)(2,1)S(1)}, u32[]{:S(2)}, u32[]{:S(2)}) collective-permute-start(bf16[2,288,512]{2,1,0:T(8,128)(2,1)S(1)} %collective-permute-done.12), channel_id=1, source_target_pairs={{0,4},{4,8},{8,12},{12,14},{14,10},{10,6},{6,2},{2,0},{1,5},{5,9},... | collective-permute-start | bytes 1769480 | tf_op jit(solution)/shard_map/ppermute | solution.py:93
  107.2 12.4 %collective-permute-start.16 = (bf16[2,288,512]{2,1,0:T(8,128)(2,1)S(1)}, bf16[2,288,512]{2,1,0:T(8,128)(2,1)S(1)}, u32[]{:S(2)}, u32[]{:S(2)}) collective-permute-start(bf16[2,288,512]{2,1,0:T(8,128)(2,1)S(1)} %collective-permute-done.13), channel_id=1, source_target_pairs={{0,2},{4,0},{8,4},{12,8},{14,12},{10,14},{6,10},{2,6},{1,3},{5,1},... | collective-permute-start | bytes 1769480 | tf_op jit(solution)/shard_map/ppermute | solution.py:94
  118.1 14.9 %copy-start.30 = (bf16[2,288,512]{2,1,0:T(8,128)(2,1)}, bf16[2,288,512]{2,1,0:T(8,128)(2,1)S(1)}, u32[]{:S(2)}) copy-start(bf16[2,288,512]{2,1,0:T(8,128)(2,1)S(1)} %collective-permute-done.15) | copy-start | bytes 1769476
  119.6 13.4 %collective-permute-start.17 = (bf16[2,288,512]{2,1,0:T(8,128)(2,1)S(1)}, bf16[2,288,512]{2,1,0:T(8,128)(2,1)S(1)}, u32[]{:S(2)}, u32[]{:S(2)}) collective-permute-start(bf16[2,288,512]{2,1,0:T(8,128)(2,1)S(1)} %pad_maximum_fusion.7), channel_id=1, source_target_pairs={{0,16},{16,0},{1,17},{17,1},{2,18},{18,2},{3,19},{19,3},{4,20},{20... | collective-permute-start | bytes 1769480 | tf_op jit(solution)/shard_map/ppermute | solution.py:98
  120.7 9.9 %collective-permute-start.18 = (bf16[2,288,512]{2,1,0:T(8,128)(2,1)S(1)}, bf16[2,288,512]{2,1,0:T(8,128)(2,1)S(1)}, u32[]{:S(2)}, u32[]{:S(2)}) collective-permute-start(bf16[2,288,512]{2,1,0:T(8,128)(2,1)S(1)} %collective-permute-done.15), channel_id=1, source_target_pairs={{0,4},{4,8},{8,12},{12,14},{14,10},{10,6},{6,2},{2,0},{1,5},{5,9},... | collective-permute-start | bytes 1769480 | tf_op jit(solution)/shard_map/ppermute | solution.py:93
  121.9 9.9 %collective-permute-start.19 = (bf16[2,288,512]{2,1,0:T(8,128)(2,1)S(1)}, bf16[2,288,512]{2,1,0:T(8,128)(2,1)S(1)}, u32[]{:S(2)}, u32[]{:S(2)}) collective-permute-start(bf16[2,288,512]{2,1,0:T(8,128)(2,1)S(1)} %collective-permute-done.16), channel_id=1, source_target_pairs={{0,2},{4,0},{8,4},{12,8},{14,12},{10,14},{6,10},{2,6},{1,3},{5,1},... | collective-permute-start | bytes 1769480 | tf_op jit(solution)/shard_map/ppermute | solution.py:94
  130.6 11.7 %copy-start.36 = (bf16[2,288,512]{2,1,0:T(8,128)(2,1)}, bf16[2,288,512]{2,1,0:T(8,128)(2,1)S(1)}, u32[]{:S(2)}) copy-start(bf16[2,288,512]{2,1,0:T(8,128)(2,1)S(1)} %collective-permute-done.18) | copy-start | bytes 1769476
  131.9 13.7 %copy-start.3 = (bf16[2,288,512]{2,1,0:T(8,128)(2,1)}, bf16[2,288,512]{2,1,0:T(8,128)(2,1)S(1)}, u32[]{:S(2)}) copy-start(bf16[2,288,512]{2,1,0:T(8,128)(2,1)S(1)} %collective-permute-done.19) | copy-start | bytes 1769476
  131.9 10.3 %collective-permute-start.20 = (bf16[2,288,512]{2,1,0:T(8,128)(2,1)S(1)}, bf16[2,288,512]{2,1,0:T(8,128)(2,1)S(1)}, u32[]{:S(2)}, u32[]{:S(2)}) collective-permute-start(bf16[2,288,512]{2,1,0:T(8,128)(2,1)S(1)} %pad_maximum_fusion.8), channel_id=1, source_target_pairs={{0,16},{16,0},{1,17},{17,1},{2,18},{18,2},{3,19},{19,3},{4,20},{20... | collective-permute-start | bytes 1769480 | tf_op jit(solution)/shard_map/ppermute | solution.py:98
  145.6 5.3 %slice-start = ((s8[4718592]{0:T(1024)(128)(4,1)}), s8[524288]{0:T(1024)(128)(4,1)S(1)}, s32[]{:S(2)}) async-start(s8[4718592]{0:T(1024)(128)(4,1)} %bitcast.317), calls=%async_computation.2 | async-start | bytes 1048576
  157.1 4.5 %copy-start.33 = (bf16[2,288,512]{2,1,0:T(8,128)(2,1)S(1)}, bf16[2,288,512]{2,1,0:T(8,128)(2,1)}, u32[]{:S(2)}) copy-start(bf16[2,288,512]{2,1,0:T(8,128)(2,1)} %copy-done.32) | copy-start | bytes 1769476
  157.1 4.5 %copy-start.35 = (bf16[2,288,512]{2,1,0:T(8,128)(2,1)S(1)}, bf16[2,288,512]{2,1,0:T(8,128)(2,1)}, u32[]{:S(2)}) copy-start(bf16[2,288,512]{2,1,0:T(8,128)(2,1)} %copy-done.34) | copy-start | bytes 1769476
  161.3 8.4 %collective-permute-start.21 = (bf16[128,2304]{1,0:T(8,128)(2,1)S(1)}, bf16[128,2304]{1,0:T(8,128)(2,1)S(1)}, u32[]{:S(2)}, u32[]{:S(2)}) collective-permute-start(bf16[128,2304]{1,0:T(8,128)(2,1)S(1)} %convolution_convert_fusion), channel_id=1, source_target_pairs={{0,1},{1,0},{2,3},{3,2},{4,5},{5,4},{6,7},{7,6},{8,9},{9,8},{10,11... | collective-permute-start | bytes 1769480 | tf_op jit(solution)/shard_map/ppermute | solution.py:58
  198.2 4.2 %collective-permute-start.22 = (bf16[128,2304]{1,0:T(8,128)(2,1)S(1)}, bf16[128,2304]{1,0:T(8,128)(2,1)}, u32[]{:S(2)}, u32[]{:S(2)}) collective-permute-start(bf16[128,2304]{1,0:T(8,128)(2,1)S(1)} %fusion.1), channel_id=1, source_target_pairs={{0,1},{1,0},{2,3},{3,2},{4,5},{5,4},{6,7},{7,6},{8,9},{9,8},{10,11... | collective-permute-start | bytes 1769480 | tf_op jit(solution)/shard_map/ppermute | solution.py:58
  (75 other events, 139.5 us)

commit v6 on v5

--- a/solution.py
+++ b/solution.py
@@ -105,6 +105,11 @@
                     [jnp.where(first_group, own, other), middle, jnp.where(first_group, other, own)],
                     axis=1,
                 )
+            )
+    if n <= PIECEWISE_RING:
+        for step in range(n - 1):
+            front_pieces[step], back_pieces[step], _, _ = lax.optimization_barrier(
+                (front_pieces[step], back_pieces[step], front_ring[step + 1], back_ring[step + 1])
             )
     back_pieces = [back_pieces[(n - k) % n] for k in range(n)]
     return front_pieces, back_pieces, block_of, slot_of

time: 226 us -> 221 us (0.978)
  other arithmetic: 41.5 us -> 30.7 us
  local copies, waits for them, and re-layouts: 45.8 us -> 53.2 us
  waiting for transfers between devices: 55.8 us -> 61.5 us
  matrix products: 29.6 us -> 26.6 us
  starting transfers between devices: 31.7 us -> 28.9 us
    ppermute x7, waiting for transfers between devices: 6.88 us -> 37.8 us  [ring_gather(): lax.ppermute(jnp.stack([front_ring[step][0], back_ring[step][0]]), 'group...]
    ppermute x7, waiting for transfers between devices: 38.4 us -> 10.9 us  [ring_gather(): front_ring.append(lax.ppermute(front_ring[-1], 'seq', forward_pairs))]
    select_n x7 -> x1, other arithmetic: 9.87 us -> 0.94 us  [ring_gather(): jnp.where(first_group, other, own)]
    unnamed x25 -> x2, other arithmetic: 9.09 us -> 2.95 us
    unnamed x205 -> x145, local copies, waits for them, and re-layouts: 19 us -> 23.2 us
    select_n x0 -> x6, other arithmetic: none -> 3.38 us  [ring_gather(): jnp.where(first_group, own, other)]
    dot_general x1, matrix products: 4.18 us -> 1.67 us  [shards(): out_part = jnp.dot(context_rows, w_out, preferred_element_type=jnp.float32)]
    ppermute x7, waiting for transfers between devices: 10.5 us -> 12.8 us  [ring_gather(): back_ring.append(lax.ppermute(back_ring[-1], 'seq', backward_pairs))]
  transfers between devices with their start and end apart: 24 -> 24, of which waited for: 15 -> 16; matrix products, arithmetic and copies ran while one was open for 27% -> 21% of each run, Pallas kernels for 0% -> 0%
where the time goes in v6:
time: 221 us; the launch traced here: 220 us
  waiting for transfers between devices  61.5 us (28%)
  local copies, waits for them, and re-layouts  53.2 us (24%)
  other arithmetic  30.7 us (14%)
  starting transfers between devices  28.9 us (13%)
  matrix products  26.6 us (12%)
  blocking collectives  18.1 us (8%)
    ppermute x7, waiting for transfers between devices, ring_gather(): lax.ppermute(jnp.stack([front_ring[step][0], back_ring[step][0]]), 'group...  37.8 us
    unnamed x145, local copies, waits for them, and re-layouts  23.2 us
    all_to_all x1, blocking collectives, shards(): lax.all_to_all(grad_rows.astype(jnp.bfloat16), 'seq', split_axis=0, conca...  15.6 us
    ppermute x7, waiting for transfers between devices, ring_gather(): back_ring.append(lax.ppermute(back_ring[-1], 'seq', backward_pairs))  12.8 us
    ppermute x7, starting transfers between devices, ring_gather(): front_ring.append(lax.ppermute(front_ring[-1], 'seq', forward_pairs))  12.3 us
    ppermute x7, waiting for transfers between devices, ring_gather(): front_ring.append(lax.ppermute(front_ring[-1], 'seq', forward_pairs))  10.9 us
    ppermute x7, starting transfers between devices, ring_gather(): lax.ppermute(jnp.stack([front_ring[step][0], back_ring[step][0]]), 'group...  6.84 us
    all_to_all x1, starting transfers between devices, shards(): lax.all_to_all(whole_rows, 'seq', split_axis=0, concat_axis=0, tiled=True)  6.11 us
  transfers between devices with their start and end apart: 24, of which 16 were waited for; matrix products, arithmetic and copies ran while one was open for 21% of the time, Pallas kernels for 0%

profile of v6, /device:TPU:0, one launch (start us, length us, event | category | flops | bytes accessed | tf_op | source)
XLA Modules:
  0.0 220.2 jit_solution(6145959976341451925)
XLA Ops:
  0.0 1.4 fusion.39
  2.3 3.0 %collective-permute-start = (bf16[2,288,512]{2,1,0:T(8,128)(2,1)}, bf16[2,288,512]{2,1,0:T(8,128)(2,1)}, u32[]{:S(2)}, u32[]{:S(2)}) collective-permute-start(bf16[2,288,512]{2,1,0:T(8,128)(2,1)} %pad_maximum_fusion.14), channel_id=1, source_target_pairs={{0,4},{4,8},{8,12},{12,14},{14,10},{10,6},{6,2},{2,0},{1,5},{5,9},... | collective-permute-start | bytes 1769480 | tf_op jit(solution)/shard_map/ppermute | solution.py:93
  6.3 2.5 %all_gather.3 = bf16[128,2304]{1,0:T(8,128)(2,1)} all-gather(bf16[128,1152]{1,0:T(8,128)(2,1)S(1)} %copy-done.26), channel_id=1, replica_groups=mesh['groups'=2,'seq'=8,'wg'=2] {'wg'}, dimensions={1}, use_global_device_ids=true | all-gather | bytes 884736 | tf_op jit(solution)/shard_map/all_gather | solution.py:141
  8.8 6.1 %all-to-all-start = ((bf16[8,16,2304]{2,1,0:T(8,128)(2,1)}), bf16[8,16,2304]{2,1,0:T(8,128)(2,1)}, u32[]{:S(2)}, u32[]{:S(2)}) async-start(bf16[8,16,2304]{2,1,0:T(8,128)(2,1)} %bitcast.2), calls=%async_computation | async-start | bytes 1179648 | tf_op jit(solution)/shard_map/all_to_all | solution.py:142
  26.8 1.2 compare_convert_fusion
  32.4 1.5 collective-permute-start.2
  33.9 2.0 collective-permute-start.3
  39.3 2.3 %reshape.368 = bf16[128,8,288]{2,1,0:T(8,128)(2,1)S(1)} reshape(bf16[8,16,2304]{2,1,0:T(8,128)(2,1)} %all-to-all-done) | data formatting | bytes 1179648 | tf_op jit(solution)/shard_map/reshape | solution.py:121
  44.8 4.2 %collective-permute-done.3 = bf16[2,288,512]{2,1,0:T(8,128)(2,1)} collective-permute-done((bf16[2,288,512]{2,1,0:T(8,128)(2,1)}, bf16[2,288,512]{2,1,0:T(8,128)(2,1)}, u32[]{:S(2)}, u32[]{:S(2)}) %collective-permute-start.3) | collective-permute-done | bytes 589856 | tf_op jit(solution)/shard_map/ppermute | solution.py:93
  52.1 1.5 select_bitcast_fusion.23
  53.8 1.5 copy-done.7
  55.3 1.5 collective-permute-start.6
  58.7 6.3 %collective-permute-done.5 = bf16[2,288,512]{2,1,0:T(8,128)(2,1)S(1)} collective-permute-done((bf16[2,288,512]{2,1,0:T(8,128)(2,1)S(1)}, bf16[2,288,512]{2,1,0:T(8,128)(2,1)S(1)}, u32[]{:S(2)}, u32[]{:S(2)}) %collective-permute-start.5) | collective-permute-done | bytes 589856 | tf_op jit(solution)/shard_map/ppermute | solution.py:98
  65.0 1.4 select_bitcast_fusion.19
  66.6 2.2 collective-permute-done.6
  70.0 1.7 collective-permute-start.8
  72.3 1.6 collective-permute-start.9
  75.2 6.9 %collective-permute-done.8 = bf16[2,288,512]{2,1,0:T(8,128)(2,1)S(1)} collective-permute-done((bf16[2,288,512]{2,1,0:T(8,128)(2,1)S(1)}, bf16[2,288,512]{2,1,0:T(8,128)(2,1)S(1)}, u32[]{:S(2)}, u32[]{:S(2)}) %collective-permute-start.8) | collective-permute-done | bytes 589856 | tf_op jit(solution)/shard_map/ppermute | solution.py:98
  83.4 1.9 collective-permute-done.9
  85.4 1.2 collective-permute-start.12
  88.8 7.6 %collective-permute-done.11 = bf16[2,288,512]{2,1,0:T(8,128)(2,1)S(1)} collective-permute-done((bf16[2,288,512]{2,1,0:T(8,128)(2,1)S(1)}, bf16[2,288,512]{2,1,0:T(8,128)(2,1)S(1)}, u32[]{:S(2)}, u32[]{:S(2)}) %collective-permute-start.11) | collective-permute-done | bytes 589856 | tf_op jit(solution)/shard_map/ppermute | solution.py:98
  96.7 2.0 collective-permute-done.12
  98.8 1.2 collective-permute-start.14
  100.1 1.5 collective-permute-start.15
  103.5 8.1 %collective-permute-done.14 = bf16[2,288,512]{2,1,0:T(8,128)(2,1)S(1)} collective-permute-done((bf16[2,288,512]{2,1,0:T(8,128)(2,1)S(1)}, bf16[2,288,512]{2,1,0:T(8,128)(2,1)S(1)}, u32[]{:S(2)}, u32[]{:S(2)}) %collective-permute-start.14) | collective-permute-done | bytes 589856 | tf_op jit(solution)/shard_map/ppermute | solution.py:98
  111.8 3.6 %collective-permute-done.16 = bf16[2,288,512]{2,1,0:T(8,128)(2,1)S(1)} collective-permute-done((bf16[2,288,512]{2,1,0:T(8,128)(2,1)S(1)}, bf16[2,288,512]{2,1,0:T(8,128)(2,1)S(1)}, u32[]{:S(2)}, u32[]{:S(2)}) %collective-permute-start.16) | collective-permute-done | bytes 589856 | tf_op jit(solution)/shard_map/ppermute | solution.py:94
  117.0 1.4 collective-permute-start.18
  119.8 6.5 %collective-permute-done.19 = bf16[2,288,512]{2,1,0:T(8,128)(2,1)S(1)} collective-permute-done((bf16[2,288,512]{2,1,0:T(8,128)(2,1)S(1)}, bf16[2,288,512]{2,1,0:T(8,128)(2,1)S(1)}, u32[]{:S(2)}, u32[]{:S(2)}) %collective-permute-start.19) | collective-permute-done | bytes 589856 | tf_op jit(solution)/shard_map/ppermute | solution.py:94
  127.9 2.7 %collective-permute-done.17 = bf16[2,288,512]{2,1,0:T(8,128)(2,1)S(1)} collective-permute-done((bf16[2,288,512]{2,1,0:T(8,128)(2,1)S(1)}, bf16[2,288,512]{2,1,0:T(8,128)(2,1)S(1)}, u32[]{:S(2)}, u32[]{:S(2)}) %collective-permute-start.17) | collective-permute-done | bytes 589856 | tf_op jit(solution)/shard_map/ppermute | solution.py:98
  131.9 6.2 %collective-permute-done.20 = bf16[2,288,512]{2,1,0:T(8,128)(2,1)S(1)} collective-permute-done((bf16[2,288,512]{2,1,0:T(8,128)(2,1)S(1)}, bf16[2,288,512]{2,1,0:T(8,128)(2,1)S(1)}, u32[]{:S(2)}, u32[]{:S(2)}) %collective-permute-start.20) | collective-permute-done | bytes 589856 | tf_op jit(solution)/shard_map/ppermute | solution.py:98
  149.6 2.1 fusion.28
  151.6 1.9 bitcast_dynamic-update-slice_fusion.12
  160.8 1.7 convolution_convert_fusion
  168.0 2.0 convolution_convert_fusion.2
  171.2 2.0 fusion.15
  174.2 2.8 %convolution_bitcast_fusion.1 = f32[4,128,128]{2,1,0:T(8,128)} fusion(bf16[4,2,128,128]{3,2,1,0:T(8,128)(2,1)} %copy-done.29, f32[4,2,128,128]{2,3,1,0:T(8,128)} %fusion.56, f32[4,2,128,128]{2,3,1,0:T(8,128)} %copy-done.55, f32[4,2,128]{2,1,0:T(2,128)S(1)} %copy-done.57, pred[128,128]{0,1:T(8,128)(4,1)S(1)} %copy-done.37), kind=kOutput, calls=%fused_computation.50 | convolution fusion | flops 35259520 | bytes 1593344 | tf_op jit(solution)/shard_map/kgij,kgid->kjd/dot_general | solution.py:261
  177.0 2.2 %convolution_multiply_fusion.1 = f32[4,2,128,128]{3,2,1,0:T(8,128)S(1)} fusion(f32[4,2,128,128]{2,3,1,0:T(8,128)} %fusion.56, f32[4,2,128,128]{2,3,1,0:T(8,128)} %copy-done.55, bf16[4,128,64]{2,1,0:T(8,128)(2,1)} %get-tuple-element.104, bf16[4,128,64]{2,1,0:T(8,128)(2,1)} %copy-done.32, f32[4,2,128]{2,1,0:T(2,128)} %copy-done.56, ...), kind=kOutput, calls=%fused_computation.27 | convolution fusion | flops 35652736 | bytes 1724416 | tf_op jit(solution)/shard_map/kgij,kjd->kgid/dot_general | solution.py:257
  179.2 1.2 add_convert_fusion.1
  181.2 1.7 copy.77
  184.8 4.1 %fusion.41 = f32[128,2304]{1,0:T(8,128)S(1)} fusion(bf16[1024,2304]{0,1:T(8,128)(2,1)} %fusion.29, bf16[16,8,8,128]{3,2,1,0:T(8,128)(2,1)S(1)} %bitcast.294), kind=kOutput, calls=%fused_computation.198 | convolution fusion | flops 603979776 | bytes 6160384 | tf_op jit(solution)/shard_map/dot_general | solution.py:271
  189.9 2.6 %fusion.1 = bf16[128,2304]{1,0:T(8,128)(2,1)S(1)} fusion(f32[128,2304]{1,0:T(8,128)S(1)} %convolution_add_fusion.1, bf16[128,512]{0,1:T(8,128)(2,1)S(1)} %bitcast.299, bf16[512,2304]{0,1:T(8,128)(2,1)} %bitcast_dynamic-update-slice_fusion.16), kind=kOutput, calls=%fused_computation.11 | convolution fusion | flops 302579712 | bytes 4259840 | tf_op jit(solution)/shard_map/dot_general | solution.py:273
  193.0 1.2 broadcast_in_dim.111
  194.2 1.4 broadcast_in_dim.112
  195.6 1.3 dynamic-slice
  196.9 1.5 fusion.13
  198.4 2.9 %fusion.12 = bf16[128,2304]{1,0:T(8,128)(2,1)} fusion(bf16[128,2304]{1,0:T(8,128)(2,1)} %collective-permute-done.22, bf16[128,2304]{1,0:T(8,128)(2,1)S(1)} %fusion.1, f32[128]{0:T(128)S(1)} %broadcast_multiply_fusion, f32[128]{0:T(128)} %get-tuple-element.107, f32[2304]{0:T(1024)S(1)} %mul.486, f32[128]{0:T(128)} %copy-done.44, ...), kind=kLoop, calls=%fused_computation.37 | loop fusion | flops 6488064 | bytes 4742912 | tf_op jit(solution)/shard_map/add | solution.py:279
  201.3 1.4 copy.79
  203.9 15.6 %all_to_all.21 = bf16[8,16,1152]{2,1,0:T(8,128)(2,1)S(1)} all-to-all(bf16[8,16,1152]{2,1,0:T(8,128)(2,1)S(1)} %bitcast.292), channel_id=1, replica_groups=mesh['groups'=2,'seq'=8,'wg'=2] {'seq'}, dimensions={0} | all-to-all | bytes 589824 | tf_op jit(solution)/shard_map/all_to_all | solution.py:282
  (298 shorter events, 76.6 us)
Async XLA Ops:
  1.4 4.9 %copy-start.26 = (bf16[128,1152]{1,0:T(8,128)(2,1)S(1)}, bf16[128,1152]{1,0:T(8,128)(2,1)}, u32[]{:S(2)}) copy-start(bf16[128,1152]{1,0:T(8,128)(2,1)} %param.16) | copy-start | bytes 884740
  2.3 12.5 %copy-start.53 = (s32[8]{0:T(128)S(1)}, s32[8]{0:T(128)}, u32[]{:S(2)}) copy-start(s32[8]{0:T(128)} %constant.129.clone) | copy-start | bytes 100
  2.3 13.8 %copy-start = (s32[8]{0:T(128)S(1)}, s32[8]{0:T(128)}, u32[]{:S(2)}) copy-start(s32[8]{0:T(128)} %constant.130.clone) | copy-start | bytes 100
  2.3 27.2 %collective-permute-start = (bf16[2,288,512]{2,1,0:T(8,128)(2,1)}, bf16[2,288,512]{2,1,0:T(8,128)(2,1)}, u32[]{:S(2)}, u32[]{:S(2)}) collective-permute-start(bf16[2,288,512]{2,1,0:T(8,128)(2,1)} %pad_maximum_fusion.14), channel_id=1, source_target_pairs={{0,4},{4,8},{8,12},{12,14},{14,10},{10,6},{6,2},{2,0},{1,5},{5,9},... | collective-permute-start | bytes 1769480 | tf_op jit(solution)/shard_map/ppermute | solution.py:93
  5.4 11.5 %copy-start.50 = (s32[8]{0:T(128)S(1)}, s32[8]{0:T(128)}, u32[]{:S(2)}) copy-start(s32[8]{0:T(128)} %constant.131) | copy-start | bytes 100
  5.4 12.6 %copy-start.38 = (f32[2304]{0:T(1024)S(1)}, f32[2304]{0:T(1024)}, u32[]{:S(2)}) copy-start(f32[2304]{0:T(1024)} %param.17) | copy-start | bytes 27652
  5.4 12.7 %copy-start.39 = (f32[2304]{0:T(1024)S(1)}, f32[2304]{0:T(1024)}, u32[]{:S(2)}) copy-start(f32[2304]{0:T(1024)} %param.22) | copy-start | bytes 27652
  5.4 14.5 %copy-start.40 = (f32[2304]{0:T(1024)S(1)}, f32[2304]{0:T(1024)}, u32[]{:S(2)}) copy-start(f32[2304]{0:T(1024)} %param.23) | copy-start | bytes 27652
  6.3 14.6 %copy-start.51 = (s32[8]{0:T(128)S(1)}, s32[8]{0:T(128)}, u32[]{:S(2)}) copy-start(s32[8]{0:T(128)} %param.25) | copy-start | bytes 100
  6.3 17.3 %copy-start.27 = (bf16[64,2304]{1,0:T(8,128)(2,1)S(1)}, bf16[64,2304]{1,0:T(8,128)(2,1)}, u32[]{:S(2)}) copy-start(bf16[64,2304]{1,0:T(8,128)(2,1)} %param.24) | copy-start | bytes 884740
  6.3 24.3 %collective-permute-start.1 = (bf16[2,288,512]{2,1,0:T(8,128)(2,1)}, bf16[2,288,512]{2,1,0:T(8,128)(2,1)}, u32[]{:S(2)}, u32[]{:S(2)}) collective-permute-start(bf16[2,288,512]{2,1,0:T(8,128)(2,1)} %pad_maximum_fusion.15), channel_id=1, source_target_pairs={{0,2},{4,0},{8,4},{12,8},{14,12},{10,14},{6,10},{2,6},{1,3},{5,1},... | collective-permute-start | bytes 1769480 | tf_op jit(solution)/shard_map/ppermute | solution.py:94
  8.8 30.6 %all-to-all-start = ((bf16[8,16,2304]{2,1,0:T(8,128)(2,1)}), bf16[8,16,2304]{2,1,0:T(8,128)(2,1)}, u32[]{:S(2)}, u32[]{:S(2)}) async-start(bf16[8,16,2304]{2,1,0:T(8,128)(2,1)} %bitcast.2), calls=%async_computation | async-start | bytes 1179648 | tf_op jit(solution)/shard_map/all_to_all | solution.py:142
  22.2 136.6 %copy-start.36 = (pred[128,128]{0,1:T(8,128)(4,1)}, pred[128,128]{0,1:T(8,128)(4,1)S(1)}, u32[]{:S(2)}) copy-start(pred[128,128]{0,1:T(8,128)(4,1)S(1)} %fusion.79) | copy-start | bytes 49156
  23.6 4.7 %copy-start.10 = (bf16[288,1024]{1,0:T(8,128)(2,1)S(1)}, bf16[288,1024]{1,0:T(8,128)(2,1)}, u32[]{:S(2)}) copy-start(bf16[288,1024]{1,0:T(8,128)(2,1)} %param.18) | copy-start | bytes 1769476
  23.6 4.7 %copy-start.11 = (bf16[1024,288]{0,1:T(8,128)(2,1)S(1)}, bf16[1024,288]{0,1:T(8,128)(2,1)}, u32[]{:S(2)}) copy-start(bf16[1024,288]{0,1:T(8,128)(2,1)} %param.21) | copy-start | bytes 1769476
  23.6 4.7 %copy-start.18 = (bf16[288,512]{1,0:T(8,128)(2,1)S(1)}, bf16[288,512]{1,0:T(8,128)(2,1)}, u32[]{:S(2)}) copy-start(bf16[288,512]{1,0:T(8,128)(2,1)} %param.19) | copy-start | bytes 884740
  28.4 113.9 %copy-start.14 = (f32[128,64]{1,0:T(8,128)}, f32[128,64]{1,0:T(8,128)S(1)}, u32[]{:S(2)}) copy-start(f32[128,64]{1,0:T(8,128)S(1)} %get-tuple-element.105) | copy-start | bytes 98308
  28.4 113.9 %copy-start.16 = (f32[128,64]{1,0:T(8,128)}, f32[128,64]{1,0:T(8,128)S(1)}, u32[]{:S(2)}) copy-start(f32[128,64]{1,0:T(8,128)S(1)} %get-tuple-element.106) | copy-start | bytes 98308
  32.4 19.7 %collective-permute-start.2 = (bf16[2,288,512]{2,1,0:T(8,128)(2,1)}, bf16[2,288,512]{2,1,0:T(8,128)(2,1)}, u32[]{:S(2)}, u32[]{:S(2)}) collective-permute-start(bf16[2,288,512]{2,1,0:T(8,128)(2,1)} %pad_maximum_fusion.16), channel_id=1, source_target_pairs={{0,16},{16,0},{1,17},{17,1},{2,18},{18,2},{3,19},{19,3},{4,20},{20... | collective-permute-start | bytes 1769480 | tf_op jit(solution)/shard_map/ppermute | solution.py:98
  33.9 15.1 %collective-permute-start.3 = (bf16[2,288,512]{2,1,0:T(8,128)(2,1)}, bf16[2,288,512]{2,1,0:T(8,128)(2,1)}, u32[]{:S(2)}, u32[]{:S(2)}) collective-permute-start(bf16[2,288,512]{2,1,0:T(8,128)(2,1)} %collective-permute-done), channel_id=1, source_target_pairs={{0,4},{4,8},{8,12},{12,14},{14,10},{10,6},{6,2},{2,0},{1,5},{5,9},... | collective-permute-start | bytes 1769480 | tf_op jit(solution)/shard_map/ppermute | solution.py:93
  35.9 14.6 %collective-permute-start.4 = (bf16[2,288,512]{2,1,0:T(8,128)(2,1)}, bf16[2,288,512]{2,1,0:T(8,128)(2,1)}, u32[]{:S(2)}, u32[]{:S(2)}) collective-permute-start(bf16[2,288,512]{2,1,0:T(8,128)(2,1)} %collective-permute-done.1), channel_id=1, source_target_pairs={{0,2},{4,0},{8,4},{12,8},{14,12},{10,14},{6,10},{2,6},{1,3},{5,1},... | collective-permute-start | bytes 1769480 | tf_op jit(solution)/shard_map/ppermute | solution.py:94
  51.5 13.5 %collective-permute-start.5 = (bf16[2,288,512]{2,1,0:T(8,128)(2,1)S(1)}, bf16[2,288,512]{2,1,0:T(8,128)(2,1)S(1)}, u32[]{:S(2)}, u32[]{:S(2)}) collective-permute-start(bf16[2,288,512]{2,1,0:T(8,128)(2,1)S(1)} %pad_maximum_fusion.17), channel_id=1, source_target_pairs={{0,16},{16,0},{1,17},{17,1},{2,18},{18,2},{3,19},{19,3},{4,20},{20... | collective-permute-start | bytes 1769480 | tf_op jit(solution)/shard_map/ppermute | solution.py:98
  55.3 13.4 %collective-permute-start.6 = (bf16[2,288,512]{2,1,0:T(8,128)(2,1)}, bf16[2,288,512]{2,1,0:T(8,128)(2,1)S(1)}, u32[]{:S(2)}, u32[]{:S(2)}) collective-permute-start(bf16[2,288,512]{2,1,0:T(8,128)(2,1)} %collective-permute-done.3), channel_id=1, source_target_pairs={{0,4},{4,8},{8,12},{12,14},{14,10},{10,6},{6,2},{2,0},{1,5},{5,9},... | collective-permute-start | bytes 1769480 | tf_op jit(solution)/shard_map/ppermute | solution.py:93
  56.9 13.1 %collective-permute-start.7 = (bf16[2,288,512]{2,1,0:T(8,128)(2,1)}, bf16[2,288,512]{2,1,0:T(8,128)(2,1)S(1)}, u32[]{:S(2)}, u32[]{:S(2)}) collective-permute-start(bf16[2,288,512]{2,1,0:T(8,128)(2,1)} %collective-permute-done.4), channel_id=1, source_target_pairs={{0,2},{4,0},{8,4},{12,8},{14,12},{10,14},{6,10},{2,6},{1,3},{5,1},... | collective-permute-start | bytes 1769480 | tf_op jit(solution)/shard_map/ppermute | solution.py:94
  70.0 12.0 %collective-permute-start.8 = (bf16[2,288,512]{2,1,0:T(8,128)(2,1)S(1)}, bf16[2,288,512]{2,1,0:T(8,128)(2,1)S(1)}, u32[]{:S(2)}, u32[]{:S(2)}) collective-permute-start(bf16[2,288,512]{2,1,0:T(8,128)(2,1)S(1)} %pad_maximum_fusion.18), channel_id=1, source_target_pairs={{0,16},{16,0},{1,17},{17,1},{2,18},{18,2},{3,19},{19,3},{4,20},{20... | collective-permute-start | bytes 1769480 | tf_op jit(solution)/shard_map/ppermute | solution.py:98
  71.8 11.5 %collective-permute-start.10 = (bf16[2,288,512]{2,1,0:T(8,128)(2,1)S(1)}, bf16[2,288,512]{2,1,0:T(8,128)(2,1)S(1)}, u32[]{:S(2)}, u32[]{:S(2)}) collective-permute-start(bf16[2,288,512]{2,1,0:T(8,128)(2,1)S(1)} %collective-permute-done.7), channel_id=1, source_target_pairs={{0,2},{4,0},{8,4},{12,8},{14,12},{10,14},{6,10},{2,6},{1,3},{5,1},... | collective-permute-start | bytes 1769480 | tf_op jit(solution)/shard_map/ppermute | solution.py:94
  72.3 12.9 %collective-permute-start.9 = (bf16[2,288,512]{2,1,0:T(8,128)(2,1)S(1)}, bf16[2,288,512]{2,1,0:T(8,128)(2,1)S(1)}, u32[]{:S(2)}, u32[]{:S(2)}) collective-permute-start(bf16[2,288,512]{2,1,0:T(8,128)(2,1)S(1)} %collective-permute-done.6), channel_id=1, source_target_pairs={{0,4},{4,8},{8,12},{12,14},{14,10},{10,6},{6,2},{2,0},{1,5},{5,9},... | collective-permute-start | bytes 1769480 | tf_op jit(solution)/shard_map/ppermute | solution.py:93
  85.3 11.1 %collective-permute-start.11 = (bf16[2,288,512]{2,1,0:T(8,128)(2,1)S(1)}, bf16[2,288,512]{2,1,0:T(8,128)(2,1)S(1)}, u32[]{:S(2)}, u32[]{:S(2)}) collective-permute-start(bf16[2,288,512]{2,1,0:T(8,128)(2,1)S(1)} %pad_maximum_fusion.19), channel_id=1, source_target_pairs={{0,16},{16,0},{1,17},{17,1},{2,18},{18,2},{3,19},{19,3},{4,20},{20... | collective-permute-start | bytes 1769480 | tf_op jit(solution)/shard_map/ppermute | solution.py:98
  85.4 13.3 %collective-permute-start.12 = (bf16[2,288,512]{2,1,0:T(8,128)(2,1)S(1)}, bf16[2,288,512]{2,1,0:T(8,128)(2,1)S(1)}, u32[]{:S(2)}, u32[]{:S(2)}) collective-permute-start(bf16[2,288,512]{2,1,0:T(8,128)(2,1)S(1)} %collective-permute-done.9), channel_id=1, source_target_pairs={{0,4},{4,8},{8,12},{12,14},{14,10},{10,6},{6,2},{2,0},{1,5},{5,9},... | collective-permute-start | bytes 1769480 | tf_op jit(solution)/shard_map/ppermute | solution.py:93
  86.6 12.1 %collective-permute-start.13 = (bf16[2,288,512]{2,1,0:T(8,128)(2,1)S(1)}, bf16[2,288,512]{2,1,0:T(8,128)(2,1)S(1)}, u32[]{:S(2)}, u32[]{:S(2)}) collective-permute-start(bf16[2,288,512]{2,1,0:T(8,128)(2,1)S(1)} %collective-permute-done.10), channel_id=1, source_target_pairs={{0,2},{4,0},{8,4},{12,8},{14,12},{10,14},{6,10},{2,6},{1,3},{5,1},... | collective-permute-start | bytes 1769480 | tf_op jit(solution)/shard_map/ppermute | solution.py:94
  96.6 50.4 %copy-start.2 = (bf16[288,1536]{1,0:T(8,128)(2,1)}, bf16[288,1536]{1,0:T(8,128)(2,1)S(1)}, u32[]{:S(2)}) copy-start(bf16[288,1536]{1,0:T(8,128)(2,1)S(1)} %pad_maximum_fusion.9) | copy-start | bytes 2654212
  98.8 12.7 %collective-permute-start.14 = (bf16[2,288,512]{2,1,0:T(8,128)(2,1)S(1)}, bf16[2,288,512]{2,1,0:T(8,128)(2,1)S(1)}, u32[]{:S(2)}, u32[]{:S(2)}) collective-permute-start(bf16[2,288,512]{2,1,0:T(8,128)(2,1)S(1)} %pad_maximum_fusion.20), channel_id=1, source_target_pairs={{0,16},{16,0},{1,17},{17,1},{2,18},{18,2},{3,19},{19,3},{4,20},{20... | collective-permute-start | bytes 1769480 | tf_op jit(solution)/shard_map/ppermute | solution.py:98
  100.1 11.8 %collective-permute-start.15 = (bf16[2,288,512]{2,1,0:T(8,128)(2,1)S(1)}, bf16[2,288,512]{2,1,0:T(8,128)(2,1)S(1)}, u32[]{:S(2)}, u32[]{:S(2)}) collective-permute-start(bf16[2,288,512]{2,1,0:T(8,128)(2,1)S(1)} %collective-permute-done.12), channel_id=1, source_target_pairs={{0,4},{4,8},{8,12},{12,14},{14,10},{10,6},{6,2},{2,0},{1,5},{5,9},... | collective-permute-start | bytes 1769480 | tf_op jit(solution)/shard_map/ppermute | solution.py:93
  101.6 13.9 %collective-permute-start.16 = (bf16[2,288,512]{2,1,0:T(8,128)(2,1)S(1)}, bf16[2,288,512]{2,1,0:T(8,128)(2,1)S(1)}, u32[]{:S(2)}, u32[]{:S(2)}) collective-permute-start(bf16[2,288,512]{2,1,0:T(8,128)(2,1)S(1)} %collective-permute-done.13), channel_id=1, source_target_pairs={{0,2},{4,0},{8,4},{12,8},{14,12},{10,14},{6,10},{2,6},{1,3},{5,1},... | collective-permute-start | bytes 1769480 | tf_op jit(solution)/shard_map/ppermute | solution.py:94
  111.7 34.3 %copy-start.4 = (bf16[288,1536]{1,0:T(8,128)(2,1)}, bf16[288,1536]{1,0:T(8,128)(2,1)S(1)}, u32[]{:S(2)}) copy-start(bf16[288,1536]{1,0:T(8,128)(2,1)S(1)} %pad_maximum_fusion.11) | copy-start | bytes 2654212
  115.6 15.1 %collective-permute-start.17 = (bf16[2,288,512]{2,1,0:T(8,128)(2,1)S(1)}, bf16[2,288,512]{2,1,0:T(8,128)(2,1)S(1)}, u32[]{:S(2)}, u32[]{:S(2)}) collective-permute-start(bf16[2,288,512]{2,1,0:T(8,128)(2,1)S(1)} %pad_maximum_fusion.21), channel_id=1, source_target_pairs={{0,16},{16,0},{1,17},{17,1},{2,18},{18,2},{3,19},{19,3},{4,20},{20... | collective-permute-start | bytes 1769480 | tf_op jit(solution)/shard_map/ppermute | solution.py:98
  116.4 9.9 %collective-permute-start.19 = (bf16[2,288,512]{2,1,0:T(8,128)(2,1)S(1)}, bf16[2,288,512]{2,1,0:T(8,128)(2,1)S(1)}, u32[]{:S(2)}, u32[]{:S(2)}) collective-permute-start(bf16[2,288,512]{2,1,0:T(8,128)(2,1)S(1)} %collective-permute-done.16), channel_id=1, source_target_pairs={{0,2},{4,0},{8,4},{12,8},{14,12},{10,14},{6,10},{2,6},{1,3},{5,1},... | collective-permute-start | bytes 1769480 | tf_op jit(solution)/shard_map/ppermute | solution.py:94
  117.0 9.9 %collective-permute-start.18 = (bf16[2,288,512]{2,1,0:T(8,128)(2,1)S(1)}, bf16[2,288,512]{2,1,0:T(8,128)(2,1)S(1)}, u32[]{:S(2)}, u32[]{:S(2)}) collective-permute-start(bf16[2,288,512]{2,1,0:T(8,128)(2,1)S(1)} %collective-permute-done.15), channel_id=1, source_target_pairs={{0,4},{4,8},{8,12},{12,14},{14,10},{10,6},{6,2},{2,0},{1,5},{5,9},... | collective-permute-start | bytes 1769480 | tf_op jit(solution)/shard_map/ppermute | solution.py:93
  127.0 11.2 %collective-permute-start.20 = (bf16[2,288,512]{2,1,0:T(8,128)(2,1)S(1)}, bf16[2,288,512]{2,1,0:T(8,128)(2,1)S(1)}, u32[]{:S(2)}, u32[]{:S(2)}) collective-permute-start(bf16[2,288,512]{2,1,0:T(8,128)(2,1)S(1)} %pad_maximum_fusion.22), channel_id=1, source_target_pairs={{0,16},{16,0},{1,17},{17,1},{2,18},{18,2},{3,19},{19,3},{4,20},{20... | collective-permute-start | bytes 1769480 | tf_op jit(solution)/shard_map/ppermute | solution.py:98
  130.8 14.2 %copy-start.6 = (bf16[288,1536]{1,0:T(8,128)(2,1)}, bf16[288,1536]{1,0:T(8,128)(2,1)S(1)}, u32[]{:S(2)}) copy-start(bf16[288,1536]{1,0:T(8,128)(2,1)S(1)} %pad_maximum_fusion.13) | copy-start | bytes 2654212
  143.0 15.3 %copy-start.32 = (bf16[4,128,64]{2,1,0:T(8,128)(2,1)}, bf16[4,128,64]{2,1,0:T(8,128)(2,1)S(1)}, u32[]{:S(2)}) copy-start(bf16[4,128,64]{2,1,0:T(8,128)(2,1)S(1)} %get-tuple-element.103) | copy-start | bytes 196612
  148.8 5.7 %copy-start.19 = (bf16[128,512]{1,0:T(8,128)(2,1)}, bf16[128,512]{1,0:T(8,128)(2,1)S(1)}, u32[]{:S(2)}) copy-start(bf16[128,512]{1,0:T(8,128)(2,1)S(1)} %fusion.14) | copy-start | bytes 393220
  149.6 4.0 %copy-start.5 = (bf16[288,1536]{1,0:T(8,128)(2,1)S(1)}, bf16[288,1536]{1,0:T(8,128)(2,1)}, u32[]{:S(2)}) copy-start(bf16[288,1536]{1,0:T(8,128)(2,1)} %copy-done.4) | copy-start | bytes 2654212
  149.6 4.9 %copy-start.3 = (bf16[288,1536]{1,0:T(8,128)(2,1)S(1)}, bf16[288,1536]{1,0:T(8,128)(2,1)}, u32[]{:S(2)}) copy-start(bf16[288,1536]{1,0:T(8,128)(2,1)} %copy-done.2) | copy-start | bytes 2654212
  162.5 2.5 %collective-permute-start.21 = (bf16[128,2304]{1,0:T(8,128)(2,1)S(1)}, bf16[128,2304]{1,0:T(8,128)(2,1)S(1)}, u32[]{:S(2)}, u32[]{:S(2)}) collective-permute-start(bf16[128,2304]{1,0:T(8,128)(2,1)S(1)} %convolution_convert_fusion), channel_id=1, source_target_pairs={{0,1},{1,0},{2,3},{3,2},{4,5},{5,4},{6,7},{7,6},{8,9},{9,8},{10,11... | collective-permute-start | bytes 1769480 | tf_op jit(solution)/shard_map/ppermute | solution.py:58
  184.8 4.2 %copy-start.9 = (bf16[512,2304]{0,1:T(8,128)(2,1)S(1)}, bf16[512,2304]{0,1:T(8,128)(2,1)}, u32[]{:S(2)}) copy-start(bf16[512,2304]{0,1:T(8,128)(2,1)} %copy-done.8) | copy-start | bytes 7077892
  184.8 4.2 %copy-start.25 = (bf16[128,4,128]{0,2,1:T(8,128)(2,1)S(1)}, bf16[128,4,128]{0,2,1:T(8,128)(2,1)}, u32[]{:S(2)}) copy-start(bf16[128,4,128]{0,2,1:T(8,128)(2,1)} %copy.77) | copy-start | bytes 393220
  192.5 4.5 %collective-permute-start.22 = (bf16[128,2304]{1,0:T(8,128)(2,1)S(1)}, bf16[128,2304]{1,0:T(8,128)(2,1)}, u32[]{:S(2)}, u32[]{:S(2)}) collective-permute-start(bf16[128,2304]{1,0:T(8,128)(2,1)S(1)} %fusion.1), channel_id=1, source_target_pairs={{0,1},{1,0},{2,3},{3,2},{4,5},{5,4},{6,7},{7,6},{8,9},{9,8},{10,11... | collective-permute-start | bytes 1769480 | tf_op jit(solution)/shard_map/ppermute | solution.py:58
  (34 other events, 61.6 us)

commit v7 on v6

--- a/solution.py
+++ b/solution.py
@@ -138,8 +138,8 @@
 ):
     seq_rank = lax.axis_index("seq")
     core_rank = lax.axis_index("wg")
-    whole_rows = lax.all_gather(generator_rows, "wg", axis=1, tiled=True)
-    guard_rows = lax.all_to_all(whole_rows, "seq", split_axis=0, concat_axis=0, tiled=True)
+    guard_half = lax.all_to_all(generator_rows, "seq", split_axis=0, concat_axis=0, tiled=True)
+    guard_rows = lax.all_gather(guard_half, "wg", axis=1, tiled=True)
     q_cols = query_weight.shape[1]
     k_cols = key_weight.shape[1]
     front = jnp.concatenate([query_weight, key_weight], axis=1)

time: 221 us -> 221 us (level)
  waiting for transfers between devices: 61.5 us -> 76.2 us
  local copies, waits for them, and re-layouts: 53.2 us -> 40.5 us
    unnamed x145 -> x143, local copies, waits for them, and re-layouts: 23.2 us -> 14.9 us
    ppermute x7, waiting for transfers between devices: 10.9 us -> 17.9 us  [ring_gather(): front_ring.append(lax.ppermute(front_ring[-1], 'seq', forward_pairs))]
    ppermute x7, waiting for transfers between devices: 37.8 us -> 44.3 us  [ring_gather(): lax.ppermute(jnp.stack([front_ring[step][0], back_ring[step][0]]), 'group...]
    reshape x7 -> x5, local copies, waits for them, and re-layouts: 3.71 us -> 0.88 us  [permute_blocks(): blocks = values.reshape(lead + (n, width))]
  transfers between devices with their start and end apart: 24 -> 24, of which waited for: 16 -> 17; matrix products, arithmetic and copies ran while one was open for 21% -> 15% of each run, Pallas kernels for 0% -> 0%
where the time goes in v7:
time: 221 us; the launch traced here: 220 us
  waiting for transfers between devices  76.2 us (34%)
  local copies, waits for them, and re-layouts  40.5 us (18%)
  starting transfers between devices  29.4 us (13%)
  other arithmetic  28.5 us (13%)
  matrix products  26.6 us (12%)
  blocking collectives  17.2 us (8%)
    ppermute x7, waiting for transfers between devices, ring_gather(): lax.ppermute(jnp.stack([front_ring[step][0], back_ring[step][0]]), 'group...  44.3 us
    ppermute x7, waiting for transfers between devices, ring_gather(): front_ring.append(lax.ppermute(front_ring[-1], 'seq', forward_pairs))  17.9 us
    unnamed x143, local copies, waits for them, and re-layouts  14.9 us
    all_to_all x1, blocking collectives, shards(): lax.all_to_all(grad_rows.astype(jnp.bfloat16), 'seq', split_axis=0, conca...  14.7 us
    ppermute x7, waiting for transfers between devices, ring_gather(): back_ring.append(lax.ppermute(back_ring[-1], 'seq', backward_pairs))  12.5 us
    ppermute x7, starting transfers between devices, ring_gather(): front_ring.append(lax.ppermute(front_ring[-1], 'seq', forward_pairs))  10.8 us
    ppermute x7, starting transfers between devices, ring_gather(): lax.ppermute(jnp.stack([front_ring[step][0], back_ring[step][0]]), 'group...  7.12 us
    all_to_all x1, starting transfers between devices, shards(): lax.all_to_all(generator_rows, 'seq', split_axis=0, concat_axis=0, tiled=...  6.25 us
  transfers between devices with their start and end apart: 24, of which 17 were waited for; matrix products, arithmetic and copies ran while one was open for 15% of the time, Pallas kernels for 0%

profile of v7, /device:TPU:0, one launch (start us, length us, event | category | flops | bytes accessed | tf_op | source)
XLA Modules:
  0.0 219.8 jit_solution(6010899366799996931)
XLA Ops:
  0.0 1.4 fusion.39
  2.4 3.0 %collective-permute-start = (bf16[2,288,512]{2,1,0:T(8,128)(2,1)}, bf16[2,288,512]{2,1,0:T(8,128)(2,1)}, u32[]{:S(2)}, u32[]{:S(2)}) collective-permute-start(bf16[2,288,512]{2,1,0:T(8,128)(2,1)} %pad_maximum_fusion.14), channel_id=1, source_target_pairs={{0,4},{4,8},{8,12},{12,14},{14,10},{10,6},{6,2},{2,0},{1,5},{5,9},... | collective-permute-start | bytes 1769480 | tf_op jit(solution)/shard_map/ppermute | solution.py:93
  6.3 6.3 %all-to-all-start = ((bf16[8,16,1152]{2,1,0:T(8,128)(2,1)}), bf16[8,16,1152]{2,1,0:T(8,128)(2,1)}, u32[]{:S(2)}, u32[]{:S(2)}) async-start(bf16[8,16,1152]{2,1,0:T(8,128)(2,1)} %bitcast.2), calls=%async_computation | async-start | bytes 589824 | tf_op jit(solution)/shard_map/all_to_all | solution.py:141
  14.6 1.2 compare_and_fusion.1
  20.4 1.2 compare_convert_fusion
  27.3 1.5 all-to-all-done
  28.8 2.4 %all_gather.3 = bf16[128,2304]{1,0:T(8,128)(2,1)S(1)} all-gather(bf16[128,1152]{1,0:T(8,128)(2,1)} %bitcast.3), channel_id=1, replica_groups=mesh['groups'=2,'seq'=8,'wg'=2] {'wg'}, dimensions={1}, use_global_device_ids=true | all-gather | bytes 884736 | tf_op jit(solution)/shard_map/all_gather | solution.py:142
  35.6 1.6 collective-permute-start.2
  39.0 1.5 collective-permute-start.4
  41.6 12.1 %collective-permute-done.3 = bf16[2,288,512]{2,1,0:T(8,128)(2,1)S(1)} collective-permute-done((bf16[2,288,512]{2,1,0:T(8,128)(2,1)}, bf16[2,288,512]{2,1,0:T(8,128)(2,1)S(1)}, u32[]{:S(2)}, u32[]{:S(2)}) %collective-permute-start.3) | collective-permute-done | bytes 589856 | tf_op jit(solution)/shard_map/ppermute | solution.py:93
  54.7 1.4 select_bitcast_fusion.23
  56.2 1.5 collective-permute-start.6
  58.8 9.4 %collective-permute-done.5 = bf16[2,288,512]{2,1,0:T(8,128)(2,1)S(1)} collective-permute-done((bf16[2,288,512]{2,1,0:T(8,128)(2,1)S(1)}, bf16[2,288,512]{2,1,0:T(8,128)(2,1)S(1)}, u32[]{:S(2)}, u32[]{:S(2)}) %collective-permute-start.5) | collective-permute-done | bytes 589856 | tf_op jit(solution)/shard_map/ppermute | solution.py:98
  68.5 1.5 collective-permute-done.6
  71.2 1.6 collective-permute-start.8
  73.5 1.4 collective-permute-start.9
  75.4 8.3 %collective-permute-done.8 = bf16[2,288,512]{2,1,0:T(8,128)(2,1)S(1)} collective-permute-done((bf16[2,288,512]{2,1,0:T(8,128)(2,1)S(1)}, bf16[2,288,512]{2,1,0:T(8,128)(2,1)S(1)}, u32[]{:S(2)}, u32[]{:S(2)}) %collective-permute-start.8) | collective-permute-done | bytes 589856 | tf_op jit(solution)/shard_map/ppermute | solution.py:98
  85.0 1.5 collective-permute-done.9
  86.8 1.2 collective-permute-start.12
  89.3 8.0 %collective-permute-done.11 = bf16[2,288,512]{2,1,0:T(8,128)(2,1)S(1)} collective-permute-done((bf16[2,288,512]{2,1,0:T(8,128)(2,1)S(1)}, bf16[2,288,512]{2,1,0:T(8,128)(2,1)S(1)}, u32[]{:S(2)}, u32[]{:S(2)}) %collective-permute-start.11) | collective-permute-done | bytes 589856 | tf_op jit(solution)/shard_map/ppermute | solution.py:98
  97.6 2.5 %collective-permute-done.12 = bf16[2,288,512]{2,1,0:T(8,128)(2,1)S(1)} collective-permute-done((bf16[2,288,512]{2,1,0:T(8,128)(2,1)S(1)}, bf16[2,288,512]{2,1,0:T(8,128)(2,1)S(1)}, u32[]{:S(2)}, u32[]{:S(2)}) %collective-permute-start.12) | collective-permute-done | bytes 589856 | tf_op jit(solution)/shard_map/ppermute | solution.py:93
  100.9 1.3 collective-permute-start.15
  103.5 9.3 %collective-permute-done.14 = bf16[2,288,512]{2,1,0:T(8,128)(2,1)S(1)} collective-permute-done((bf16[2,288,512]{2,1,0:T(8,128)(2,1)S(1)}, bf16[2,288,512]{2,1,0:T(8,128)(2,1)S(1)}, u32[]{:S(2)}, u32[]{:S(2)}) %collective-permute-start.14) | collective-permute-done | bytes 589856 | tf_op jit(solution)/shard_map/ppermute | solution.py:98
  113.0 2.8 %collective-permute-done.16 = bf16[2,288,512]{2,1,0:T(8,128)(2,1)S(1)} collective-permute-done((bf16[2,288,512]{2,1,0:T(8,128)(2,1)S(1)}, bf16[2,288,512]{2,1,0:T(8,128)(2,1)S(1)}, u32[]{:S(2)}, u32[]{:S(2)}) %collective-permute-start.16) | collective-permute-done | bytes 589856 | tf_op jit(solution)/shard_map/ppermute | solution.py:94
  115.9 1.8 collective-permute-start.17
  118.0 1.7 collective-permute-start.18
  120.3 7.3 %collective-permute-done.19 = bf16[2,288,512]{2,1,0:T(8,128)(2,1)S(1)} collective-permute-done((bf16[2,288,512]{2,1,0:T(8,128)(2,1)S(1)}, bf16[2,288,512]{2,1,0:T(8,128)(2,1)S(1)}, u32[]{:S(2)}, u32[]{:S(2)}) %collective-permute-start.19) | collective-permute-done | bytes 589856 | tf_op jit(solution)/shard_map/ppermute | solution.py:94
  128.7 1.7 collective-permute-done.17
  130.8 7.7 %collective-permute-done.20 = bf16[2,288,512]{2,1,0:T(8,128)(2,1)S(1)} collective-permute-done((bf16[2,288,512]{2,1,0:T(8,128)(2,1)S(1)}, bf16[2,288,512]{2,1,0:T(8,128)(2,1)S(1)}, u32[]{:S(2)}, u32[]{:S(2)}) %collective-permute-start.20) | collective-permute-done | bytes 589856 | tf_op jit(solution)/shard_map/ppermute | solution.py:98
  149.8 2.1 fusion.28
  151.9 1.9 bitcast_dynamic-update-slice_fusion.12
  159.9 1.2 copy-done.1
  161.1 1.7 convolution_convert_fusion
  168.3 2.0 convolution_convert_fusion.2
  171.5 2.0 fusion.15
  174.5 2.8 %convolution_bitcast_fusion.1 = f32[4,128,128]{2,1,0:T(8,128)} fusion(bf16[4,2,128,128]{3,2,1,0:T(8,128)(2,1)} %copy-done.28, f32[4,2,128,128]{2,3,1,0:T(8,128)} %fusion.56, f32[4,2,128,128]{2,3,1,0:T(8,128)} %copy-done.54, f32[4,2,128]{2,1,0:T(2,128)S(1)} %copy-done.56, pred[128,128]{0,1:T(8,128)(4,1)S(1)} %copy-done.36), kind=kOutput, calls=%fused_computation.50 | convolution fusion | flops 35259520 | bytes 1593344 | tf_op jit(solution)/shard_map/kgij,kgid->kjd/dot_general | solution.py:261
  177.3 2.2 %convolution_multiply_fusion.1 = f32[4,2,128,128]{3,2,1,0:T(8,128)S(1)} fusion(f32[4,2,128,128]{2,3,1,0:T(8,128)} %fusion.56, f32[4,2,128,128]{2,3,1,0:T(8,128)} %copy-done.54, bf16[4,128,64]{2,1,0:T(8,128)(2,1)} %get-tuple-element.104, bf16[4,128,64]{2,1,0:T(8,128)(2,1)} %copy-done.31, f32[4,2,128]{2,1,0:T(2,128)} %copy-done.55, ...), kind=kOutput, calls=%fused_computation.27 | convolution fusion | flops 35652736 | bytes 1724416 | tf_op jit(solution)/shard_map/kgij,kjd->kgid/dot_general | solution.py:257
  179.5 1.2 add_convert_fusion.1
  181.5 1.7 copy.77
  185.1 4.1 %fusion.41 = f32[128,2304]{1,0:T(8,128)S(1)} fusion(bf16[1024,2304]{0,1:T(8,128)(2,1)} %fusion.29, bf16[16,8,8,128]{3,2,1,0:T(8,128)(2,1)S(1)} %bitcast.297), kind=kOutput, calls=%fused_computation.198 | convolution fusion | flops 603979776 | bytes 6160384 | tf_op jit(solution)/shard_map/dot_general | solution.py:271
  190.2 2.6 %fusion.1 = bf16[128,2304]{1,0:T(8,128)(2,1)S(1)} fusion(f32[128,2304]{1,0:T(8,128)S(1)} %convolution_add_fusion.1, bf16[128,512]{0,1:T(8,128)(2,1)S(1)} %bitcast.302, bf16[512,2304]{0,1:T(8,128)(2,1)} %bitcast_dynamic-update-slice_fusion.16), kind=kOutput, calls=%fused_computation.11 | convolution fusion | flops 302579712 | bytes 4259840 | tf_op jit(solution)/shard_map/dot_general | solution.py:273
  193.3 1.3 broadcast_in_dim.111
  194.6 1.4 broadcast_in_dim.112
  196.0 1.3 dynamic-slice
  197.3 1.5 fusion.13
  198.8 2.9 %fusion.12 = bf16[128,2304]{1,0:T(8,128)(2,1)} fusion(bf16[128,2304]{1,0:T(8,128)(2,1)} %collective-permute-done.22, bf16[128,2304]{1,0:T(8,128)(2,1)S(1)} %fusion.1, f32[128]{0:T(128)S(1)} %broadcast_multiply_fusion, f32[128]{0:T(128)} %get-tuple-element.107, f32[2304]{0:T(1024)S(1)} %mul.486, f32[128]{0:T(128)} %copy-done.43, ...), kind=kLoop, calls=%fused_computation.37 | loop fusion | flops 6488064 | bytes 4742912 | tf_op jit(solution)/shard_map/add | solution.py:279
  201.7 1.4 copy.79
  204.3 14.7 %all_to_all.24 = bf16[8,16,1152]{2,1,0:T(8,128)(2,1)S(1)} all-to-all(bf16[8,16,1152]{2,1,0:T(8,128)(2,1)S(1)} %bitcast.295), channel_id=1, replica_groups=mesh['groups'=2,'seq'=8,'wg'=2] {'seq'}, dimensions={0} | all-to-all | bytes 589824 | tf_op jit(solution)/shard_map/all_to_all | solution.py:282
  (295 shorter events, 64.5 us)
Async XLA Ops:
  1.4 11.2 %copy-start.52 = (s32[8]{0:T(128)S(1)}, s32[8]{0:T(128)}, u32[]{:S(2)}) copy-start(s32[8]{0:T(128)} %constant.129.clone) | copy-start | bytes 100
  1.4 12.4 %copy-start = (s32[8]{0:T(128)S(1)}, s32[8]{0:T(128)}, u32[]{:S(2)}) copy-start(s32[8]{0:T(128)} %constant.130.clone) | copy-start | bytes 100
  1.4 13.1 %copy-start.49 = (s32[8]{0:T(128)S(1)}, s32[8]{0:T(128)}, u32[]{:S(2)}) copy-start(s32[8]{0:T(128)} %constant.131) | copy-start | bytes 100
  1.5 14.4 %copy-start.37 = (f32[2304]{0:T(1024)S(1)}, f32[2304]{0:T(1024)}, u32[]{:S(2)}) copy-start(f32[2304]{0:T(1024)} %param.17) | copy-start | bytes 27652
  1.5 14.4 %copy-start.38 = (f32[2304]{0:T(1024)S(1)}, f32[2304]{0:T(1024)}, u32[]{:S(2)}) copy-start(f32[2304]{0:T(1024)} %param.22) | copy-start | bytes 27652
  1.5 16.2 %copy-start.39 = (f32[2304]{0:T(1024)S(1)}, f32[2304]{0:T(1024)}, u32[]{:S(2)}) copy-start(f32[2304]{0:T(1024)} %param.23) | copy-start | bytes 27652
  1.5 16.9 %copy-start.50 = (s32[8]{0:T(128)S(1)}, s32[8]{0:T(128)}, u32[]{:S(2)}) copy-start(s32[8]{0:T(128)} %param.25) | copy-start | bytes 100
  1.5 18.2 %copy-start.51 = (s32[8]{0:T(128)S(1)}, s32[8]{0:T(128)}, u32[]{:S(2)}) copy-start(s32[8]{0:T(128)} %param.26) | copy-start | bytes 100
  2.4 20.8 %copy-start.26 = (bf16[64,2304]{1,0:T(8,128)(2,1)S(1)}, bf16[64,2304]{1,0:T(8,128)(2,1)}, u32[]{:S(2)}) copy-start(bf16[64,2304]{1,0:T(8,128)(2,1)} %param.24) | copy-start | bytes 884740
  2.4 31.1 %collective-permute-start = (bf16[2,288,512]{2,1,0:T(8,128)(2,1)}, bf16[2,288,512]{2,1,0:T(8,128)(2,1)}, u32[]{:S(2)}, u32[]{:S(2)}) collective-permute-start(bf16[2,288,512]{2,1,0:T(8,128)(2,1)} %pad_maximum_fusion.14), channel_id=1, source_target_pairs={{0,4},{4,8},{8,12},{12,14},{14,10},{10,6},{6,2},{2,0},{1,5},{5,9},... | collective-permute-start | bytes 1769480 | tf_op jit(solution)/shard_map/ppermute | solution.py:93
  6.3 28.2 %collective-permute-start.1 = (bf16[2,288,512]{2,1,0:T(8,128)(2,1)}, bf16[2,288,512]{2,1,0:T(8,128)(2,1)}, u32[]{:S(2)}, u32[]{:S(2)}) collective-permute-start(bf16[2,288,512]{2,1,0:T(8,128)(2,1)} %pad_maximum_fusion.15), channel_id=1, source_target_pairs={{0,2},{4,0},{8,4},{12,8},{14,12},{10,14},{6,10},{2,6},{1,3},{5,1},... | collective-permute-start | bytes 1769480 | tf_op jit(solution)/shard_map/ppermute | solution.py:94
  6.3 22.4 %all-to-all-start = ((bf16[8,16,1152]{2,1,0:T(8,128)(2,1)}), bf16[8,16,1152]{2,1,0:T(8,128)(2,1)}, u32[]{:S(2)}, u32[]{:S(2)}) async-start(bf16[8,16,1152]{2,1,0:T(8,128)(2,1)} %bitcast.2), calls=%async_computation | async-start | bytes 589824 | tf_op jit(solution)/shard_map/all_to_all | solution.py:141
  19.7 139.4 %copy-start.35 = (pred[128,128]{0,1:T(8,128)(4,1)}, pred[128,128]{0,1:T(8,128)(4,1)S(1)}, u32[]{:S(2)}) copy-start(pred[128,128]{0,1:T(8,128)(4,1)S(1)} %fusion.79) | copy-start | bytes 49156
  26.1 116.4 %copy-start.14 = (f32[128,64]{1,0:T(8,128)}, f32[128,64]{1,0:T(8,128)S(1)}, u32[]{:S(2)}) copy-start(f32[128,64]{1,0:T(8,128)S(1)} %get-tuple-element.105) | copy-start | bytes 98308
  26.1 116.4 %copy-start.16 = (f32[128,64]{1,0:T(8,128)}, f32[128,64]{1,0:T(8,128)S(1)}, u32[]{:S(2)}) copy-start(f32[128,64]{1,0:T(8,128)S(1)} %get-tuple-element.106) | copy-start | bytes 98308
  35.6 19.1 %collective-permute-start.2 = (bf16[2,288,512]{2,1,0:T(8,128)(2,1)S(1)}, bf16[2,288,512]{2,1,0:T(8,128)(2,1)S(1)}, u32[]{:S(2)}, u32[]{:S(2)}) collective-permute-start(bf16[2,288,512]{2,1,0:T(8,128)(2,1)S(1)} %pad_maximum_fusion.16), channel_id=1, source_target_pairs={{0,16},{16,0},{1,17},{17,1},{2,18},{18,2},{3,19},{19,3},{4,20},{20... | collective-permute-start | bytes 1769480 | tf_op jit(solution)/shard_map/ppermute | solution.py:98
  38.4 15.4 %collective-permute-start.3 = (bf16[2,288,512]{2,1,0:T(8,128)(2,1)}, bf16[2,288,512]{2,1,0:T(8,128)(2,1)S(1)}, u32[]{:S(2)}, u32[]{:S(2)}) collective-permute-start(bf16[2,288,512]{2,1,0:T(8,128)(2,1)} %collective-permute-done), channel_id=1, source_target_pairs={{0,4},{4,8},{8,12},{12,14},{14,10},{10,6},{6,2},{2,0},{1,5},{5,9},... | collective-permute-start | bytes 1769480 | tf_op jit(solution)/shard_map/ppermute | solution.py:93
  39.0 15.0 %collective-permute-start.4 = (bf16[2,288,512]{2,1,0:T(8,128)(2,1)}, bf16[2,288,512]{2,1,0:T(8,128)(2,1)S(1)}, u32[]{:S(2)}, u32[]{:S(2)}) collective-permute-start(bf16[2,288,512]{2,1,0:T(8,128)(2,1)} %collective-permute-done.1), channel_id=1, source_target_pairs={{0,2},{4,0},{8,4},{12,8},{14,12},{10,14},{6,10},{2,6},{1,3},{5,1},... | collective-permute-start | bytes 1769480 | tf_op jit(solution)/shard_map/ppermute | solution.py:94
  54.1 14.1 %collective-permute-start.5 = (bf16[2,288,512]{2,1,0:T(8,128)(2,1)S(1)}, bf16[2,288,512]{2,1,0:T(8,128)(2,1)S(1)}, u32[]{:S(2)}, u32[]{:S(2)}) collective-permute-start(bf16[2,288,512]{2,1,0:T(8,128)(2,1)S(1)} %pad_maximum_fusion.17), channel_id=1, source_target_pairs={{0,16},{16,0},{1,17},{17,1},{2,18},{18,2},{3,19},{19,3},{4,20},{20... | collective-permute-start | bytes 1769480 | tf_op jit(solution)/shard_map/ppermute | solution.py:98
  56.2 13.8 %collective-permute-start.6 = (bf16[2,288,512]{2,1,0:T(8,128)(2,1)S(1)}, bf16[2,288,512]{2,1,0:T(8,128)(2,1)S(1)}, u32[]{:S(2)}, u32[]{:S(2)}) collective-permute-start(bf16[2,288,512]{2,1,0:T(8,128)(2,1)S(1)} %collective-permute-done.3), channel_id=1, source_target_pairs={{0,4},{4,8},{8,12},{12,14},{14,10},{10,6},{6,2},{2,0},{1,5},{5,9},... | collective-permute-start | bytes 1769480 | tf_op jit(solution)/shard_map/ppermute | solution.py:93
  57.7 13.4 %collective-permute-start.7 = (bf16[2,288,512]{2,1,0:T(8,128)(2,1)S(1)}, bf16[2,288,512]{2,1,0:T(8,128)(2,1)S(1)}, u32[]{:S(2)}, u32[]{:S(2)}) collective-permute-start(bf16[2,288,512]{2,1,0:T(8,128)(2,1)S(1)} %collective-permute-done.4), channel_id=1, source_target_pairs={{0,2},{4,0},{8,4},{12,8},{14,12},{10,14},{6,10},{2,6},{1,3},{5,1},... | collective-permute-start | bytes 1769480 | tf_op jit(solution)/shard_map/ppermute | solution.py:94
  71.2 12.5 %collective-permute-start.8 = (bf16[2,288,512]{2,1,0:T(8,128)(2,1)S(1)}, bf16[2,288,512]{2,1,0:T(8,128)(2,1)S(1)}, u32[]{:S(2)}, u32[]{:S(2)}) collective-permute-start(bf16[2,288,512]{2,1,0:T(8,128)(2,1)S(1)} %pad_maximum_fusion.18), channel_id=1, source_target_pairs={{0,16},{16,0},{1,17},{17,1},{2,18},{18,2},{3,19},{19,3},{4,20},{20... | collective-permute-start | bytes 1769480 | tf_op jit(solution)/shard_map/ppermute | solution.py:98
  72.8 12.2 %collective-permute-start.10 = (bf16[2,288,512]{2,1,0:T(8,128)(2,1)S(1)}, bf16[2,288,512]{2,1,0:T(8,128)(2,1)S(1)}, u32[]{:S(2)}, u32[]{:S(2)}) collective-permute-start(bf16[2,288,512]{2,1,0:T(8,128)(2,1)S(1)} %collective-permute-done.7), channel_id=1, source_target_pairs={{0,2},{4,0},{8,4},{12,8},{14,12},{10,14},{6,10},{2,6},{1,3},{5,1},... | collective-permute-start | bytes 1769480 | tf_op jit(solution)/shard_map/ppermute | solution.py:94
  73.5 13.0 %collective-permute-start.9 = (bf16[2,288,512]{2,1,0:T(8,128)(2,1)S(1)}, bf16[2,288,512]{2,1,0:T(8,128)(2,1)S(1)}, u32[]{:S(2)}, u32[]{:S(2)}) collective-permute-start(bf16[2,288,512]{2,1,0:T(8,128)(2,1)S(1)} %collective-permute-done.6), channel_id=1, source_target_pairs={{0,4},{4,8},{8,12},{12,14},{14,10},{10,6},{6,2},{2,0},{1,5},{5,9},... | collective-permute-start | bytes 1769480 | tf_op jit(solution)/shard_map/ppermute | solution.py:93
  86.6 10.7 %collective-permute-start.11 = (bf16[2,288,512]{2,1,0:T(8,128)(2,1)S(1)}, bf16[2,288,512]{2,1,0:T(8,128)(2,1)S(1)}, u32[]{:S(2)}, u32[]{:S(2)}) collective-permute-start(bf16[2,288,512]{2,1,0:T(8,128)(2,1)S(1)} %pad_maximum_fusion.19), channel_id=1, source_target_pairs={{0,16},{16,0},{1,17},{17,1},{2,18},{18,2},{3,19},{19,3},{4,20},{20... | collective-permute-start | bytes 1769480 | tf_op jit(solution)/shard_map/ppermute | solution.py:98
  86.8 13.3 %collective-permute-start.12 = (bf16[2,288,512]{2,1,0:T(8,128)(2,1)S(1)}, bf16[2,288,512]{2,1,0:T(8,128)(2,1)S(1)}, u32[]{:S(2)}, u32[]{:S(2)}) collective-permute-start(bf16[2,288,512]{2,1,0:T(8,128)(2,1)S(1)} %collective-permute-done.9), channel_id=1, source_target_pairs={{0,4},{4,8},{8,12},{12,14},{14,10},{10,6},{6,2},{2,0},{1,5},{5,9},... | collective-permute-start | bytes 1769480 | tf_op jit(solution)/shard_map/ppermute | solution.py:93
  88.0 12.0 %collective-permute-start.13 = (bf16[2,288,512]{2,1,0:T(8,128)(2,1)S(1)}, bf16[2,288,512]{2,1,0:T(8,128)(2,1)S(1)}, u32[]{:S(2)}, u32[]{:S(2)}) collective-permute-start(bf16[2,288,512]{2,1,0:T(8,128)(2,1)S(1)} %collective-permute-done.10), channel_id=1, source_target_pairs={{0,2},{4,0},{8,4},{12,8},{14,12},{10,14},{6,10},{2,6},{1,3},{5,1},... | collective-permute-start | bytes 1769480 | tf_op jit(solution)/shard_map/ppermute | solution.py:94
  97.5 49.8 %copy-start.3 = (bf16[288,1536]{1,0:T(8,128)(2,1)}, bf16[288,1536]{1,0:T(8,128)(2,1)S(1)}, u32[]{:S(2)}) copy-start(bf16[288,1536]{1,0:T(8,128)(2,1)S(1)} %pad_maximum_fusion.9) | copy-start | bytes 2654212
  100.1 12.6 %collective-permute-start.14 = (bf16[2,288,512]{2,1,0:T(8,128)(2,1)S(1)}, bf16[2,288,512]{2,1,0:T(8,128)(2,1)S(1)}, u32[]{:S(2)}, u32[]{:S(2)}) collective-permute-start(bf16[2,288,512]{2,1,0:T(8,128)(2,1)S(1)} %pad_maximum_fusion.20), channel_id=1, source_target_pairs={{0,16},{16,0},{1,17},{17,1},{2,18},{18,2},{3,19},{19,3},{4,20},{20... | collective-permute-start | bytes 1769480 | tf_op jit(solution)/shard_map/ppermute | solution.py:98
  100.9 12.1 %collective-permute-start.15 = (bf16[2,288,512]{2,1,0:T(8,128)(2,1)S(1)}, bf16[2,288,512]{2,1,0:T(8,128)(2,1)S(1)}, u32[]{:S(2)}, u32[]{:S(2)}) collective-permute-start(bf16[2,288,512]{2,1,0:T(8,128)(2,1)S(1)} %collective-permute-done.12), channel_id=1, source_target_pairs={{0,4},{4,8},{8,12},{12,14},{14,10},{10,6},{6,2},{2,0},{1,5},{5,9},... | collective-permute-start | bytes 1769480 | tf_op jit(solution)/shard_map/ppermute | solution.py:93
  102.2 13.5 %collective-permute-start.16 = (bf16[2,288,512]{2,1,0:T(8,128)(2,1)S(1)}, bf16[2,288,512]{2,1,0:T(8,128)(2,1)S(1)}, u32[]{:S(2)}, u32[]{:S(2)}) collective-permute-start(bf16[2,288,512]{2,1,0:T(8,128)(2,1)S(1)} %collective-permute-done.13), channel_id=1, source_target_pairs={{0,2},{4,0},{8,4},{12,8},{14,12},{10,14},{6,10},{2,6},{1,3},{5,1},... | collective-permute-start | bytes 1769480 | tf_op jit(solution)/shard_map/ppermute | solution.py:94
  112.9 33.4 %copy-start.5 = (bf16[288,1536]{1,0:T(8,128)(2,1)}, bf16[288,1536]{1,0:T(8,128)(2,1)S(1)}, u32[]{:S(2)}) copy-start(bf16[288,1536]{1,0:T(8,128)(2,1)S(1)} %pad_maximum_fusion.11) | copy-start | bytes 2654212
  115.9 14.5 %collective-permute-start.17 = (bf16[2,288,512]{2,1,0:T(8,128)(2,1)S(1)}, bf16[2,288,512]{2,1,0:T(8,128)(2,1)S(1)}, u32[]{:S(2)}, u32[]{:S(2)}) collective-permute-start(bf16[2,288,512]{2,1,0:T(8,128)(2,1)S(1)} %pad_maximum_fusion.21), channel_id=1, source_target_pairs={{0,16},{16,0},{1,17},{17,1},{2,18},{18,2},{3,19},{19,3},{4,20},{20... | collective-permute-start | bytes 1769480 | tf_op jit(solution)/shard_map/ppermute | solution.py:98
  117.7 9.9 %collective-permute-start.19 = (bf16[2,288,512]{2,1,0:T(8,128)(2,1)S(1)}, bf16[2,288,512]{2,1,0:T(8,128)(2,1)S(1)}, u32[]{:S(2)}, u32[]{:S(2)}) collective-permute-start(bf16[2,288,512]{2,1,0:T(8,128)(2,1)S(1)} %collective-permute-done.16), channel_id=1, source_target_pairs={{0,2},{4,0},{8,4},{12,8},{14,12},{10,14},{6,10},{2,6},{1,3},{5,1},... | collective-permute-start | bytes 1769480 | tf_op jit(solution)/shard_map/ppermute | solution.py:94
  118.0 9.9 %collective-permute-start.18 = (bf16[2,288,512]{2,1,0:T(8,128)(2,1)S(1)}, bf16[2,288,512]{2,1,0:T(8,128)(2,1)S(1)}, u32[]{:S(2)}, u32[]{:S(2)}) collective-permute-start(bf16[2,288,512]{2,1,0:T(8,128)(2,1)S(1)} %collective-permute-done.15), channel_id=1, source_target_pairs={{0,4},{4,8},{8,12},{12,14},{14,10},{10,6},{6,2},{2,0},{1,5},{5,9},... | collective-permute-start | bytes 1769480 | tf_op jit(solution)/shard_map/ppermute | solution.py:93
  128.0 10.5 %collective-permute-start.20 = (bf16[2,288,512]{2,1,0:T(8,128)(2,1)S(1)}, bf16[2,288,512]{2,1,0:T(8,128)(2,1)S(1)}, u32[]{:S(2)}, u32[]{:S(2)}) collective-permute-start(bf16[2,288,512]{2,1,0:T(8,128)(2,1)S(1)} %pad_maximum_fusion.22), channel_id=1, source_target_pairs={{0,16},{16,0},{1,17},{17,1},{2,18},{18,2},{3,19},{19,3},{4,20},{20... | collective-permute-start | bytes 1769480 | tf_op jit(solution)/shard_map/ppermute | solution.py:98
  130.6 14.7 %copy-start.7 = (bf16[288,1536]{1,0:T(8,128)(2,1)}, bf16[288,1536]{1,0:T(8,128)(2,1)S(1)}, u32[]{:S(2)}) copy-start(bf16[288,1536]{1,0:T(8,128)(2,1)S(1)} %pad_maximum_fusion.13) | copy-start | bytes 2654212
  130.8 9.1 %copy-start.2 = (bf16[1024,2304]{0,1:T(8,128)(2,1)}, bf16[1024,2304]{0,1:T(8,128)(2,1)S(1)}, u32[]{:S(2)}) copy-start(bf16[1024,2304]{0,1:T(8,128)(2,1)S(1)} %bitcast_dynamic-update-slice_fusion) | copy-start | bytes 14155780
  143.3 15.3 %copy-start.31 = (bf16[4,128,64]{2,1,0:T(8,128)(2,1)}, bf16[4,128,64]{2,1,0:T(8,128)(2,1)S(1)}, u32[]{:S(2)}) copy-start(bf16[4,128,64]{2,1,0:T(8,128)(2,1)S(1)} %get-tuple-element.103) | copy-start | bytes 196612
  149.1 5.6 %copy-start.19 = (bf16[128,512]{1,0:T(8,128)(2,1)}, bf16[128,512]{1,0:T(8,128)(2,1)S(1)}, u32[]{:S(2)}) copy-start(bf16[128,512]{1,0:T(8,128)(2,1)S(1)} %fusion.14) | copy-start | bytes 393220
  149.8 4.0 %copy-start.6 = (bf16[288,1536]{1,0:T(8,128)(2,1)S(1)}, bf16[288,1536]{1,0:T(8,128)(2,1)}, u32[]{:S(2)}) copy-start(bf16[288,1536]{1,0:T(8,128)(2,1)} %copy-done.5) | copy-start | bytes 2654212
  149.8 4.9 %copy-start.4 = (bf16[288,1536]{1,0:T(8,128)(2,1)S(1)}, bf16[288,1536]{1,0:T(8,128)(2,1)}, u32[]{:S(2)}) copy-start(bf16[288,1536]{1,0:T(8,128)(2,1)} %copy-done.3) | copy-start | bytes 2654212
  162.8 2.5 %collective-permute-start.21 = (bf16[128,2304]{1,0:T(8,128)(2,1)S(1)}, bf16[128,2304]{1,0:T(8,128)(2,1)S(1)}, u32[]{:S(2)}, u32[]{:S(2)}) collective-permute-start(bf16[128,2304]{1,0:T(8,128)(2,1)S(1)} %convolution_convert_fusion), channel_id=1, source_target_pairs={{0,1},{1,0},{2,3},{3,2},{4,5},{5,4},{6,7},{7,6},{8,9},{9,8},{10,11... | collective-permute-start | bytes 1769480 | tf_op jit(solution)/shard_map/ppermute | solution.py:58
  168.3 3.2 %copy-start.36 = (pred[128,128]{0,1:T(8,128)(4,1)S(1)}, pred[128,128]{0,1:T(8,128)(4,1)}, u32[]{:S(2)}) copy-start(pred[128,128]{0,1:T(8,128)(4,1)} %copy-done.35) | copy-start | bytes 49156
  168.3 3.2 %copy-start.56 = (f32[4,2,128]{2,1,0:T(2,128)S(1)}, f32[4,2,128]{2,1,0:T(2,128)}, u32[]{:S(2)}) copy-start(f32[4,2,128]{2,1,0:T(2,128)} %copy-done.55) | copy-start | bytes 12292
  185.0 4.2 %copy-start.9 = (bf16[512,2304]{0,1:T(8,128)(2,1)S(1)}, bf16[512,2304]{0,1:T(8,128)(2,1)}, u32[]{:S(2)}) copy-start(bf16[512,2304]{0,1:T(8,128)(2,1)} %copy-done.8) | copy-start | bytes 7077892
  185.0 4.2 %copy-start.25 = (bf16[128,4,128]{0,2,1:T(8,128)(2,1)S(1)}, bf16[128,4,128]{0,2,1:T(8,128)(2,1)}, u32[]{:S(2)}) copy-start(bf16[128,4,128]{0,2,1:T(8,128)(2,1)} %copy.77) | copy-start | bytes 393220
  192.8 4.6 %collective-permute-start.22 = (bf16[128,2304]{1,0:T(8,128)(2,1)S(1)}, bf16[128,2304]{1,0:T(8,128)(2,1)}, u32[]{:S(2)}, u32[]{:S(2)}) collective-permute-start(bf16[128,2304]{1,0:T(8,128)(2,1)S(1)} %fusion.1), channel_id=1, source_target_pairs={{0,1},{1,0},{2,3},{3,2},{4,5},{5,4},{6,7},{7,6},{8,9},{9,8},{10,11... | collective-permute-start | bytes 1769480 | tf_op jit(solution)/shard_map/ppermute | solution.py:58
  (33 other events, 62.1 us)

commit v8 on v7

--- a/solution.py
+++ b/solution.py
@@ -112,7 +112,7 @@
                 (front_pieces[step], back_pieces[step], front_ring[step + 1], back_ring[step + 1])
             )
     back_pieces = [back_pieces[(n - k) % n] for k in range(n)]
-    return front_pieces, back_pieces, block_of, slot_of
+    return front_pieces, back_pieces, block_of, slot_of, front_ring[1]
 
 
 def permute_blocks(values, block_order, n):
@@ -138,15 +138,18 @@
 ):
     seq_rank = lax.axis_index("seq")
     core_rank = lax.axis_index("wg")
-    guard_half = lax.all_to_all(generator_rows, "seq", split_axis=0, concat_axis=0, tiled=True)
-    guard_rows = lax.all_gather(guard_half, "wg", axis=1, tiled=True)
     q_cols = query_weight.shape[1]
     k_cols = key_weight.shape[1]
     front = jnp.concatenate([query_weight, key_weight], axis=1)
     back = jnp.concatenate([value_weight, out_weight.T], axis=1)
-    front_pieces, back_pieces, block_of, slot_of = ring_gather(
+    front_pieces, back_pieces, block_of, slot_of, first_arrival = ring_gather(
         front, back, seq_rank, lax.axis_index("groups"), n_seq
     )
+    generator_rows, pre_gain, post_gain, final_gain, label_table, lengths, label_index, _ = lax.optimization_barrier(
+        (generator_rows, pre_gain, post_gain, final_gain, label_table, lengths, label_index, first_arrival)
+    )
+    guard_half = lax.all_to_all(generator_rows, "seq", split_axis=0, concat_axis=0, tiled=True)
+    guard_rows = lax.all_gather(guard_half, "wg", axis=1, tiled=True)
     guard_rows = permute_blocks(guard_rows, block_of, n_seq)
     pre_gain = permute_blocks(pre_gain, block_of, n_seq)
     post_gain = permute_blocks(post_gain, block_of, n_seq)

time: 221 us -> 229 us (1.036)
  local copies, waits for them, and re-layouts: 40.5 us -> 53.8 us
  waiting for transfers between devices: 76.2 us -> 70 us
  other arithmetic: 28.5 us -> 31.9 us
    unnamed x143 -> x149, local copies, waits for them, and re-layouts: 14.9 us -> 26.1 us
    ppermute x7, waiting for transfers between devices: 44.3 us -> 34.8 us  [ring_gather(): lax.ppermute(jnp.stack([front_ring[step][0], back_ring[step][0]]), 'group...]
    ppermute x7, waiting for transfers between devices: 17.9 us -> 24.2 us  [ring_gather(): front_ring.append(lax.ppermute(front_ring[-1], 'seq', forward_pairs))]
    ppermute x7, starting transfers between devices: 10.8 us -> 14.1 us  [ring_gather(): front_ring.append(lax.ppermute(front_ring[-1], 'seq', forward_pairs))]
    ppermute x7, starting transfers between devices: 4.68 us -> 1.9 us  [ring_gather(): back_ring.append(lax.ppermute(back_ring[-1], 'seq', backward_pairs))]
  transfers between devices with their start and end apart: 24 -> 24, of which waited for: 17 -> 20; matrix products, arithmetic and copies ran while one was open for 15% -> 19% of each run, Pallas kernels for 0% -> 0%
where the time goes in v8:
time: 229 us; the launch traced here: 228 us
  waiting for transfers between devices  70 us (31%)
  local copies, waits for them, and re-layouts  53.8 us (23%)
  other arithmetic  31.9 us (14%)
  starting transfers between devices  29.7 us (13%)
  matrix products  25.6 us (11%)
  blocking collectives  15.6 us (7%)
    ppermute x7, waiting for transfers between devices, ring_gather(): lax.ppermute(jnp.stack([front_ring[step][0], back_ring[step][0]]), 'group...  34.8 us
    unnamed x149, local copies, waits for them, and re-layouts  26.1 us
    ppermute x7, waiting for transfers between devices, ring_gather(): front_ring.append(lax.ppermute(front_ring[-1], 'seq', forward_pairs))  24.2 us
    ppermute x7, starting transfers between devices, ring_gather(): front_ring.append(lax.ppermute(front_ring[-1], 'seq', forward_pairs))  14.1 us
    all_to_all x1, blocking collectives, shards(): lax.all_to_all(grad_rows.astype(jnp.bfloat16), 'seq', split_axis=0, conca...  13.2 us
    ppermute x7, waiting for transfers between devices, ring_gather(): back_ring.append(lax.ppermute(back_ring[-1], 'seq', backward_pairs))  11 us
    ppermute x7, starting transfers between devices, ring_gather(): lax.ppermute(jnp.stack([front_ring[step][0], back_ring[step][0]]), 'group...  8.27 us
    gather x9, local copies, waits for them, and re-layouts, permute_blocks(): return jnp.take(blocks, block_order, axis=-2).reshape(values.shape)  5.42 us
  transfers between devices with their start and end apart: 24, of which 20 were waited for; matrix products, arithmetic and copies ran while one was open for 19% of the time, Pallas kernels for 0%

profile of v8, /device:TPU:0, one launch (start us, length us, event | category | flops | bytes accessed | tf_op | source)
XLA Modules:
  0.0 227.8 jit_solution(9781082220253342061)
XLA Ops:
  0.0 1.4 fusion.39
  2.4 3.0 %collective-permute-start = (bf16[2,288,512]{2,1,0:T(8,128)(2,1)}, bf16[2,288,512]{2,1,0:T(8,128)(2,1)}, u32[]{:S(2)}, u32[]{:S(2)}) collective-permute-start(bf16[2,288,512]{2,1,0:T(8,128)(2,1)} %pad_maximum_fusion.14), channel_id=1, source_target_pairs={{0,4},{4,8},{8,12},{12,14},{14,10},{10,6},{6,2},{2,0},{1,5},{5,9},... | collective-permute-start | bytes 1769480 | tf_op jit(solution)/shard_map/ppermute | solution.py:93
  12.4 6.6 %collective-permute-done = bf16[2,288,512]{2,1,0:T(8,128)(2,1)} collective-permute-done((bf16[2,288,512]{2,1,0:T(8,128)(2,1)}, bf16[2,288,512]{2,1,0:T(8,128)(2,1)}, u32[]{:S(2)}, u32[]{:S(2)}) %collective-permute-start) | collective-permute-done | bytes 589856 | tf_op jit(solution)/shard_map/ppermute | solution.py:93
  20.0 1.4 collective-permute-done.1
  23.3 1.5 collective-permute-start.2
  28.3 4.8 %all-to-all-start = ((bf16[8,16,1152]{2,1,0:T(8,128)(2,1)}), bf16[8,16,1152]{2,1,0:T(8,128)(2,1)S(1)}, u32[]{:S(2)}, u32[]{:S(2)}) async-start(bf16[8,16,1152]{2,1,0:T(8,128)(2,1)} %bitcast.4), calls=%async_computation | async-start | bytes 589824 | tf_op jit(solution)/shard_map/all_to_all | solution.py:151
  40.7 2.0 collective-permute-start.3
  44.6 2.3 %all_gather.3 = bf16[128,2304]{1,0:T(8,128)(2,1)S(1)} all-gather(bf16[128,1152]{1,0:T(8,128)(2,1)S(1)} %bitcast.295), channel_id=1, replica_groups=mesh['groups'=2,'seq'=8,'wg'=2] {'wg'}, dimensions={1}, use_global_device_ids=true | all-gather | bytes 884736 | tf_op jit(solution)/shard_map/all_gather | solution.py:152
  50.0 4.5 %collective-permute-done.3 = bf16[2,288,512]{2,1,0:T(8,128)(2,1)} collective-permute-done((bf16[2,288,512]{2,1,0:T(8,128)(2,1)}, bf16[2,288,512]{2,1,0:T(8,128)(2,1)}, u32[]{:S(2)}, u32[]{:S(2)}) %collective-permute-start.3) | collective-permute-done | bytes 589856 | tf_op jit(solution)/shard_map/ppermute | solution.py:93
  57.6 1.5 select_bitcast_fusion.23
  59.3 1.5 copy-done.9
  60.8 1.5 collective-permute-start.6
  64.2 5.0 %collective-permute-done.5 = bf16[2,288,512]{2,1,0:T(8,128)(2,1)S(1)} collective-permute-done((bf16[2,288,512]{2,1,0:T(8,128)(2,1)S(1)}, bf16[2,288,512]{2,1,0:T(8,128)(2,1)S(1)}, u32[]{:S(2)}, u32[]{:S(2)}) %collective-permute-start.5) | collective-permute-done | bytes 589856 | tf_op jit(solution)/shard_map/ppermute | solution.py:98
  69.2 1.4 select_bitcast_fusion.19
  70.7 2.2 collective-permute-done.6
  74.2 1.9 collective-permute-start.8
  76.1 1.5 collective-permute-start.9
  79.5 6.2 %collective-permute-done.8 = bf16[2,288,512]{2,1,0:T(8,128)(2,1)S(1)} collective-permute-done((bf16[2,288,512]{2,1,0:T(8,128)(2,1)S(1)}, bf16[2,288,512]{2,1,0:T(8,128)(2,1)S(1)}, u32[]{:S(2)}, u32[]{:S(2)}) %collective-permute-start.8) | collective-permute-done | bytes 589856 | tf_op jit(solution)/shard_map/ppermute | solution.py:98
  87.2 1.5 collective-permute-done.10
  93.1 7.6 %collective-permute-done.11 = bf16[2,288,512]{2,1,0:T(8,128)(2,1)S(1)} collective-permute-done((bf16[2,288,512]{2,1,0:T(8,128)(2,1)S(1)}, bf16[2,288,512]{2,1,0:T(8,128)(2,1)S(1)}, u32[]{:S(2)}, u32[]{:S(2)}) %collective-permute-start.11) | collective-permute-done | bytes 589856 | tf_op jit(solution)/shard_map/ppermute | solution.py:98
  101.9 1.4 collective-permute-done.13
  103.4 2.2 collective-permute-start.14
  105.6 2.4 %collective-permute-start.15 = (bf16[2,288,512]{2,1,0:T(8,128)(2,1)S(1)}, bf16[2,288,512]{2,1,0:T(8,128)(2,1)S(1)}, u32[]{:S(2)}, u32[]{:S(2)}) collective-permute-start(bf16[2,288,512]{2,1,0:T(8,128)(2,1)S(1)} %collective-permute-done.12), channel_id=1, source_target_pairs={{0,4},{4,8},{8,12},{12,14},{14,10},{10,6},{6,2},{2,0},{1,5},{5,9},... | collective-permute-start | bytes 1769480 | tf_op jit(solution)/shard_map/ppermute | solution.py:93
  109.3 7.4 %collective-permute-done.14 = bf16[2,288,512]{2,1,0:T(8,128)(2,1)S(1)} collective-permute-done((bf16[2,288,512]{2,1,0:T(8,128)(2,1)S(1)}, bf16[2,288,512]{2,1,0:T(8,128)(2,1)S(1)}, u32[]{:S(2)}, u32[]{:S(2)}) %collective-permute-start.14) | collective-permute-done | bytes 589856 | tf_op jit(solution)/shard_map/ppermute | solution.py:98
  117.0 2.7 %collective-permute-done.15 = bf16[2,288,512]{2,1,0:T(8,128)(2,1)S(1)} collective-permute-done((bf16[2,288,512]{2,1,0:T(8,128)(2,1)S(1)}, bf16[2,288,512]{2,1,0:T(8,128)(2,1)S(1)}, u32[]{:S(2)}, u32[]{:S(2)}) %collective-permute-start.15) | collective-permute-done | bytes 589856 | tf_op jit(solution)/shard_map/ppermute | solution.py:93
  119.6 2.8 %collective-permute-done.16 = bf16[2,288,512]{2,1,0:T(8,128)(2,1)S(1)} collective-permute-done((bf16[2,288,512]{2,1,0:T(8,128)(2,1)S(1)}, bf16[2,288,512]{2,1,0:T(8,128)(2,1)S(1)}, u32[]{:S(2)}, u32[]{:S(2)}) %collective-permute-start.16) | collective-permute-done | bytes 589856 | tf_op jit(solution)/shard_map/ppermute | solution.py:94
  123.7 2.3 %collective-permute-start.18 = (bf16[2,288,512]{2,1,0:T(8,128)(2,1)S(1)}, bf16[2,288,512]{2,1,0:T(8,128)(2,1)S(1)}, u32[]{:S(2)}, u32[]{:S(2)}) collective-permute-start(bf16[2,288,512]{2,1,0:T(8,128)(2,1)S(1)} %collective-permute-done.15), channel_id=1, source_target_pairs={{0,4},{4,8},{8,12},{12,14},{14,10},{10,6},{6,2},{2,0},{1,5},{5,9},... | collective-permute-start | bytes 1769480 | tf_op jit(solution)/shard_map/ppermute | solution.py:93
  127.4 6.2 %collective-permute-done.18 = bf16[2,288,512]{2,1,0:T(8,128)(2,1)S(1)} collective-permute-done((bf16[2,288,512]{2,1,0:T(8,128)(2,1)S(1)}, bf16[2,288,512]{2,1,0:T(8,128)(2,1)S(1)}, u32[]{:S(2)}, u32[]{:S(2)}) %collective-permute-start.18) | collective-permute-done | bytes 589856 | tf_op jit(solution)/shard_map/ppermute | solution.py:93
  133.6 2.3 %collective-permute-done.19 = bf16[2,288,512]{2,1,0:T(8,128)(2,1)S(1)} collective-permute-done((bf16[2,288,512]{2,1,0:T(8,128)(2,1)S(1)}, bf16[2,288,512]{2,1,0:T(8,128)(2,1)S(1)}, u32[]{:S(2)}, u32[]{:S(2)}) %collective-permute-start.19) | collective-permute-done | bytes 589856 | tf_op jit(solution)/shard_map/ppermute | solution.py:94
  136.1 2.2 collective-permute-done.17
  139.6 6.3 %collective-permute-done.20 = bf16[2,288,512]{2,1,0:T(8,128)(2,1)S(1)} collective-permute-done((bf16[2,288,512]{2,1,0:T(8,128)(2,1)S(1)}, bf16[2,288,512]{2,1,0:T(8,128)(2,1)S(1)}, u32[]{:S(2)}, u32[]{:S(2)}) %collective-permute-start.20) | collective-permute-done | bytes 589856 | tf_op jit(solution)/shard_map/ppermute | solution.py:98
  157.5 1.7 copy.119
  159.2 2.0 fusion.28
  161.2 2.0 bitcast_dynamic-update-slice_fusion.12
  163.2 1.9 bitcast_dynamic-update-slice_fusion.11
  171.4 1.7 convolution_convert_fusion
  178.7 2.0 convolution_convert_fusion.2
  181.8 2.0 fusion.15
  184.8 2.8 %convolution_bitcast_fusion.1 = f32[4,128,128]{2,1,0:T(8,128)} fusion(bf16[4,2,128,128]{3,2,1,0:T(8,128)(2,1)} %copy-done.28, f32[4,2,128,128]{2,3,1,0:T(8,128)} %fusion.56, f32[4,2,128,128]{2,3,1,0:T(8,128)} %copy-done.57, f32[4,2,128]{2,1,0:T(2,128)S(1)} %copy-done.59, pred[128,128]{0,1:T(8,128)(4,1)S(1)} %copy-done.36), kind=kOutput, calls=%fused_computation.50 | convolution fusion | flops 35259520 | bytes 1593344 | tf_op jit(solution)/shard_map/kgij,kgid->kjd/dot_general | solution.py:264
  187.7 2.3 convolution_multiply_fusion.1
  192.0 1.7 copy.77
  195.5 4.2 %fusion.41 = f32[128,2304]{1,0:T(8,128)S(1)} fusion(bf16[1024,2304]{0,1:T(8,128)(2,1)} %fusion.29, bf16[16,8,8,128]{3,2,1,0:T(8,128)(2,1)S(1)} %bitcast.298), kind=kOutput, calls=%fused_computation.198 | convolution fusion | flops 603979776 | bytes 6160384 | tf_op jit(solution)/shard_map/dot_general | solution.py:274
  204.1 1.4 broadcast_in_dim.112
  205.5 1.3 dynamic-slice
  206.9 1.5 fusion.13
  208.3 2.9 %fusion.12 = bf16[128,2304]{1,0:T(8,128)(2,1)} fusion(bf16[128,2304]{1,0:T(8,128)(2,1)} %collective-permute-done.22, bf16[128,2304]{1,0:T(8,128)(2,1)S(1)} %fusion.1, f32[128]{0:T(128)S(1)} %broadcast_multiply_fusion, f32[128]{0:T(128)} %get-tuple-element.121, f32[2304]{0:T(1024)S(1)} %mul.486, f32[128]{0:T(128)} %copy-done.46, ...), kind=kLoop, calls=%fused_computation.37 | loop fusion | flops 6488064 | bytes 4742912 | tf_op jit(solution)/shard_map/add | solution.py:282
  211.2 1.4 copy.79
  213.8 13.2 %all_to_all.24 = bf16[8,16,1152]{2,1,0:T(8,128)(2,1)S(1)} all-to-all(bf16[8,16,1152]{2,1,0:T(8,128)(2,1)S(1)} %bitcast.296), channel_id=1, replica_groups=mesh['groups'=2,'seq'=8,'wg'=2] {'seq'}, dimensions={0} | all-to-all | bytes 589824 | tf_op jit(solution)/shard_map/all_to_all | solution.py:285
  (301 shorter events, 83.1 us)
Async XLA Ops:
  1.4 4.9 %copy-start.55 = (s32[8]{0:T(128)S(1)}, s32[8]{0:T(128)}, u32[]{:S(2)}) copy-start(s32[8]{0:T(128)} %constant.129.clone) | copy-start | bytes 100
  1.4 6.1 %copy-start = (s32[8]{0:T(128)S(1)}, s32[8]{0:T(128)}, u32[]{:S(2)}) copy-start(s32[8]{0:T(128)} %constant.130.clone) | copy-start | bytes 100
  1.4 6.8 %copy-start.52 = (s32[8]{0:T(128)S(1)}, s32[8]{0:T(128)}, u32[]{:S(2)}) copy-start(s32[8]{0:T(128)} %constant.131) | copy-start | bytes 100
  1.5 9.8 %copy-start.12 = (bf16[288,1024]{1,0:T(8,128)(2,1)S(1)}, bf16[288,1024]{1,0:T(8,128)(2,1)}, u32[]{:S(2)}) copy-start(bf16[288,1024]{1,0:T(8,128)(2,1)} %param.18) | copy-start | bytes 1769476
  1.5 9.8 %copy-start.13 = (bf16[1024,288]{0,1:T(8,128)(2,1)S(1)}, bf16[1024,288]{0,1:T(8,128)(2,1)}, u32[]{:S(2)}) copy-start(bf16[1024,288]{0,1:T(8,128)(2,1)} %param.21) | copy-start | bytes 1769476
  1.5 9.8 %copy-start.19 = (bf16[288,512]{1,0:T(8,128)(2,1)S(1)}, bf16[288,512]{1,0:T(8,128)(2,1)}, u32[]{:S(2)}) copy-start(bf16[288,512]{1,0:T(8,128)(2,1)} %param.19) | copy-start | bytes 884740
  2.4 16.6 %collective-permute-start = (bf16[2,288,512]{2,1,0:T(8,128)(2,1)}, bf16[2,288,512]{2,1,0:T(8,128)(2,1)}, u32[]{:S(2)}, u32[]{:S(2)}) collective-permute-start(bf16[2,288,512]{2,1,0:T(8,128)(2,1)} %pad_maximum_fusion.14), channel_id=1, source_target_pairs={{0,4},{4,8},{8,12},{12,14},{14,10},{10,6},{6,2},{2,0},{1,5},{5,9},... | collective-permute-start | bytes 1769480 | tf_op jit(solution)/shard_map/ppermute | solution.py:93
  6.3 15.1 %collective-permute-start.1 = (bf16[2,288,512]{2,1,0:T(8,128)(2,1)}, bf16[2,288,512]{2,1,0:T(8,128)(2,1)}, u32[]{:S(2)}, u32[]{:S(2)}) collective-permute-start(bf16[2,288,512]{2,1,0:T(8,128)(2,1)} %pad_maximum_fusion.15), channel_id=1, source_target_pairs={{0,2},{4,0},{8,4},{12,8},{14,12},{10,14},{6,10},{2,6},{1,3},{5,1},... | collective-permute-start | bytes 1769480 | tf_op jit(solution)/shard_map/ppermute | solution.py:94
  8.2 27.3 %copy-start.43 = (pred[8]{0:T(512)(128)(4,1)}, pred[8]{0:T(512)(128)(4,1)S(1)}, u32[]{:S(2)}) copy-start(pred[8]{0:T(512)(128)(4,1)S(1)} %compare_and_fusion) | copy-start | bytes 28
  9.5 29.3 %copy-start.42 = (s32[1024]{0:T(1024)}, s32[1024]{0:T(1024)S(1)}, u32[]{:S(2)}) copy-start(s32[1024]{0:T(1024)S(1)} %pad_clamp_fusion.2) | copy-start | bytes 12292
  12.4 14.0 %copy-start.37 = (f32[2304]{0:T(1024)S(1)}, f32[2304]{0:T(1024)}, u32[]{:S(2)}) copy-start(f32[2304]{0:T(1024)} %param.17) | copy-start | bytes 27652
  12.4 14.0 %copy-start.38 = (f32[2304]{0:T(1024)S(1)}, f32[2304]{0:T(1024)}, u32[]{:S(2)}) copy-start(f32[2304]{0:T(1024)} %param.22) | copy-start | bytes 27652
  12.4 15.2 %copy-start.39 = (f32[2304]{0:T(1024)S(1)}, f32[2304]{0:T(1024)}, u32[]{:S(2)}) copy-start(f32[2304]{0:T(1024)} %param.23) | copy-start | bytes 27652
  22.4 10.7 %copy-start.53 = (s32[8]{0:T(128)S(1)}, s32[8]{0:T(128)}, u32[]{:S(2)}) copy-start(s32[8]{0:T(128)} %param.25) | copy-start | bytes 100
  22.4 12.5 %copy-start.54 = (s32[8]{0:T(128)S(1)}, s32[8]{0:T(128)}, u32[]{:S(2)}) copy-start(s32[8]{0:T(128)} %param.26) | copy-start | bytes 100
  22.4 15.7 %copy-start.26 = (bf16[64,2304]{1,0:T(8,128)(2,1)S(1)}, bf16[64,2304]{1,0:T(8,128)(2,1)}, u32[]{:S(2)}) copy-start(bf16[64,2304]{1,0:T(8,128)(2,1)} %param.24) | copy-start | bytes 884740
  23.3 34.3 %collective-permute-start.2 = (bf16[2,288,512]{2,1,0:T(8,128)(2,1)}, bf16[2,288,512]{2,1,0:T(8,128)(2,1)}, u32[]{:S(2)}, u32[]{:S(2)}) collective-permute-start(bf16[2,288,512]{2,1,0:T(8,128)(2,1)} %pad_maximum_fusion.16), channel_id=1, source_target_pairs={{0,16},{16,0},{1,17},{17,1},{2,18},{18,2},{3,19},{19,3},{4,20},{20... | collective-permute-start | bytes 1769480 | tf_op jit(solution)/shard_map/ppermute | solution.py:98
  28.3 16.3 %all-to-all-start = ((bf16[8,16,1152]{2,1,0:T(8,128)(2,1)}), bf16[8,16,1152]{2,1,0:T(8,128)(2,1)S(1)}, u32[]{:S(2)}, u32[]{:S(2)}) async-start(bf16[8,16,1152]{2,1,0:T(8,128)(2,1)} %bitcast.4), calls=%async_computation | async-start | bytes 589824 | tf_op jit(solution)/shard_map/all_to_all | solution.py:151
  40.7 13.8 %collective-permute-start.3 = (bf16[2,288,512]{2,1,0:T(8,128)(2,1)}, bf16[2,288,512]{2,1,0:T(8,128)(2,1)}, u32[]{:S(2)}, u32[]{:S(2)}) collective-permute-start(bf16[2,288,512]{2,1,0:T(8,128)(2,1)} %collective-permute-done), channel_id=1, source_target_pairs={{0,4},{4,8},{8,12},{12,14},{14,10},{10,6},{6,2},{2,0},{1,5},{5,9},... | collective-permute-start | bytes 1769480 | tf_op jit(solution)/shard_map/ppermute | solution.py:93
  42.7 13.2 %collective-permute-start.4 = (bf16[2,288,512]{2,1,0:T(8,128)(2,1)}, bf16[2,288,512]{2,1,0:T(8,128)(2,1)}, u32[]{:S(2)}, u32[]{:S(2)}) collective-permute-start(bf16[2,288,512]{2,1,0:T(8,128)(2,1)} %collective-permute-done.1), channel_id=1, source_target_pairs={{0,2},{4,0},{8,4},{12,8},{14,12},{10,14},{6,10},{2,6},{1,3},{5,1},... | collective-permute-start | bytes 1769480 | tf_op jit(solution)/shard_map/ppermute | solution.py:94
  44.6 3.5 %copy-start.44 = (pred[8]{0:T(512)(128)(4,1)S(1)}, pred[8]{0:T(512)(128)(4,1)}, u32[]{:S(2)}) copy-start(pred[8]{0:T(512)(128)(4,1)} %copy-done.43) | copy-start | bytes 28
  57.0 12.2 %collective-permute-start.5 = (bf16[2,288,512]{2,1,0:T(8,128)(2,1)S(1)}, bf16[2,288,512]{2,1,0:T(8,128)(2,1)S(1)}, u32[]{:S(2)}, u32[]{:S(2)}) collective-permute-start(bf16[2,288,512]{2,1,0:T(8,128)(2,1)S(1)} %pad_maximum_fusion.17), channel_id=1, source_target_pairs={{0,16},{16,0},{1,17},{17,1},{2,18},{18,2},{3,19},{19,3},{4,20},{20... | collective-permute-start | bytes 1769480 | tf_op jit(solution)/shard_map/ppermute | solution.py:98
  60.8 12.1 %collective-permute-start.6 = (bf16[2,288,512]{2,1,0:T(8,128)(2,1)}, bf16[2,288,512]{2,1,0:T(8,128)(2,1)S(1)}, u32[]{:S(2)}, u32[]{:S(2)}) collective-permute-start(bf16[2,288,512]{2,1,0:T(8,128)(2,1)} %collective-permute-done.3), channel_id=1, source_target_pairs={{0,4},{4,8},{8,12},{12,14},{14,10},{10,6},{6,2},{2,0},{1,5},{5,9},... | collective-permute-start | bytes 1769480 | tf_op jit(solution)/shard_map/ppermute | solution.py:93
  62.3 11.7 %collective-permute-start.7 = (bf16[2,288,512]{2,1,0:T(8,128)(2,1)}, bf16[2,288,512]{2,1,0:T(8,128)(2,1)S(1)}, u32[]{:S(2)}, u32[]{:S(2)}) collective-permute-start(bf16[2,288,512]{2,1,0:T(8,128)(2,1)} %collective-permute-done.4), channel_id=1, source_target_pairs={{0,2},{4,0},{8,4},{12,8},{14,12},{10,14},{6,10},{2,6},{1,3},{5,1},... | collective-permute-start | bytes 1769480 | tf_op jit(solution)/shard_map/ppermute | solution.py:94
  74.2 11.5 %collective-permute-start.8 = (bf16[2,288,512]{2,1,0:T(8,128)(2,1)S(1)}, bf16[2,288,512]{2,1,0:T(8,128)(2,1)S(1)}, u32[]{:S(2)}, u32[]{:S(2)}) collective-permute-start(bf16[2,288,512]{2,1,0:T(8,128)(2,1)S(1)} %pad_maximum_fusion.18), channel_id=1, source_target_pairs={{0,16},{16,0},{1,17},{17,1},{2,18},{18,2},{3,19},{19,3},{4,20},{20... | collective-permute-start | bytes 1769480 | tf_op jit(solution)/shard_map/ppermute | solution.py:98
  76.1 11.1 %collective-permute-start.9 = (bf16[2,288,512]{2,1,0:T(8,128)(2,1)S(1)}, bf16[2,288,512]{2,1,0:T(8,128)(2,1)S(1)}, u32[]{:S(2)}, u32[]{:S(2)}) collective-permute-start(bf16[2,288,512]{2,1,0:T(8,128)(2,1)S(1)} %collective-permute-done.6), channel_id=1, source_target_pairs={{0,4},{4,8},{8,12},{12,14},{14,10},{10,6},{6,2},{2,0},{1,5},{5,9},... | collective-permute-start | bytes 1769480 | tf_op jit(solution)/shard_map/ppermute | solution.py:93
  77.6 11.1 %collective-permute-start.10 = (bf16[2,288,512]{2,1,0:T(8,128)(2,1)S(1)}, bf16[2,288,512]{2,1,0:T(8,128)(2,1)S(1)}, u32[]{:S(2)}, u32[]{:S(2)}) collective-permute-start(bf16[2,288,512]{2,1,0:T(8,128)(2,1)S(1)} %collective-permute-done.7), channel_id=1, source_target_pairs={{0,2},{4,0},{8,4},{12,8},{14,12},{10,14},{6,10},{2,6},{1,3},{5,1},... | collective-permute-start | bytes 1769480 | tf_op jit(solution)/shard_map/ppermute | solution.py:94
  85.9 70.1 %copy-start.2 = (bf16[288,1536]{1,0:T(8,128)(2,1)}, bf16[288,1536]{1,0:T(8,128)(2,1)S(1)}, u32[]{:S(2)}) copy-start(bf16[288,1536]{1,0:T(8,128)(2,1)S(1)} %pad_maximum_fusion.7) | copy-start | bytes 2654212
  88.8 11.9 %collective-permute-start.11 = (bf16[2,288,512]{2,1,0:T(8,128)(2,1)S(1)}, bf16[2,288,512]{2,1,0:T(8,128)(2,1)S(1)}, u32[]{:S(2)}, u32[]{:S(2)}) collective-permute-start(bf16[2,288,512]{2,1,0:T(8,128)(2,1)S(1)} %pad_maximum_fusion.19), channel_id=1, source_target_pairs={{0,16},{16,0},{1,17},{17,1},{2,18},{18,2},{3,19},{19,3},{4,20},{20... | collective-permute-start | bytes 1769480 | tf_op jit(solution)/shard_map/ppermute | solution.py:98
  89.7 12.2 %collective-permute-start.12 = (bf16[2,288,512]{2,1,0:T(8,128)(2,1)S(1)}, bf16[2,288,512]{2,1,0:T(8,128)(2,1)S(1)}, u32[]{:S(2)}, u32[]{:S(2)}) collective-permute-start(bf16[2,288,512]{2,1,0:T(8,128)(2,1)S(1)} %collective-permute-done.9), channel_id=1, source_target_pairs={{0,4},{4,8},{8,12},{12,14},{14,10},{10,6},{6,2},{2,0},{1,5},{5,9},... | collective-permute-start | bytes 1769480 | tf_op jit(solution)/shard_map/ppermute | solution.py:93
  91.0 12.3 %collective-permute-start.13 = (bf16[2,288,512]{2,1,0:T(8,128)(2,1)S(1)}, bf16[2,288,512]{2,1,0:T(8,128)(2,1)S(1)}, u32[]{:S(2)}, u32[]{:S(2)}) collective-permute-start(bf16[2,288,512]{2,1,0:T(8,128)(2,1)S(1)} %collective-permute-done.10), channel_id=1, source_target_pairs={{0,2},{4,0},{8,4},{12,8},{14,12},{10,14},{6,10},{2,6},{1,3},{5,1},... | collective-permute-start | bytes 1769480 | tf_op jit(solution)/shard_map/ppermute | solution.py:94
  100.9 54.2 %copy-start.4 = (bf16[288,1536]{1,0:T(8,128)(2,1)}, bf16[288,1536]{1,0:T(8,128)(2,1)S(1)}, u32[]{:S(2)}) copy-start(bf16[288,1536]{1,0:T(8,128)(2,1)S(1)} %pad_maximum_fusion.9) | copy-start | bytes 2654212
  103.4 13.3 %collective-permute-start.14 = (bf16[2,288,512]{2,1,0:T(8,128)(2,1)S(1)}, bf16[2,288,512]{2,1,0:T(8,128)(2,1)S(1)}, u32[]{:S(2)}, u32[]{:S(2)}) collective-permute-start(bf16[2,288,512]{2,1,0:T(8,128)(2,1)S(1)} %pad_maximum_fusion.20), channel_id=1, source_target_pairs={{0,16},{16,0},{1,17},{17,1},{2,18},{18,2},{3,19},{19,3},{4,20},{20... | collective-permute-start | bytes 1769480 | tf_op jit(solution)/shard_map/ppermute | solution.py:98
  105.6 14.1 %collective-permute-start.15 = (bf16[2,288,512]{2,1,0:T(8,128)(2,1)S(1)}, bf16[2,288,512]{2,1,0:T(8,128)(2,1)S(1)}, u32[]{:S(2)}, u32[]{:S(2)}) collective-permute-start(bf16[2,288,512]{2,1,0:T(8,128)(2,1)S(1)} %collective-permute-done.12), channel_id=1, source_target_pairs={{0,4},{4,8},{8,12},{12,14},{14,10},{10,6},{6,2},{2,0},{1,5},{5,9},... | collective-permute-start | bytes 1769480 | tf_op jit(solution)/shard_map/ppermute | solution.py:93
  107.9 14.5 %collective-permute-start.16 = (bf16[2,288,512]{2,1,0:T(8,128)(2,1)S(1)}, bf16[2,288,512]{2,1,0:T(8,128)(2,1)S(1)}, u32[]{:S(2)}, u32[]{:S(2)}) collective-permute-start(bf16[2,288,512]{2,1,0:T(8,128)(2,1)S(1)} %collective-permute-done.13), channel_id=1, source_target_pairs={{0,2},{4,0},{8,4},{12,8},{14,12},{10,14},{6,10},{2,6},{1,3},{5,1},... | collective-permute-start | bytes 1769480 | tf_op jit(solution)/shard_map/ppermute | solution.py:94
  116.9 37.2 %copy-start.6 = (bf16[288,1536]{1,0:T(8,128)(2,1)}, bf16[288,1536]{1,0:T(8,128)(2,1)S(1)}, u32[]{:S(2)}) copy-start(bf16[288,1536]{1,0:T(8,128)(2,1)S(1)} %pad_maximum_fusion.11) | copy-start | bytes 2654212
  122.5 15.8 %collective-permute-start.17 = (bf16[2,288,512]{2,1,0:T(8,128)(2,1)S(1)}, bf16[2,288,512]{2,1,0:T(8,128)(2,1)S(1)}, u32[]{:S(2)}, u32[]{:S(2)}) collective-permute-start(bf16[2,288,512]{2,1,0:T(8,128)(2,1)S(1)} %pad_maximum_fusion.21), channel_id=1, source_target_pairs={{0,16},{16,0},{1,17},{17,1},{2,18},{18,2},{3,19},{19,3},{4,20},{20... | collective-permute-start | bytes 1769480 | tf_op jit(solution)/shard_map/ppermute | solution.py:98
  123.7 9.9 %collective-permute-start.18 = (bf16[2,288,512]{2,1,0:T(8,128)(2,1)S(1)}, bf16[2,288,512]{2,1,0:T(8,128)(2,1)S(1)}, u32[]{:S(2)}, u32[]{:S(2)}) collective-permute-start(bf16[2,288,512]{2,1,0:T(8,128)(2,1)S(1)} %collective-permute-done.15), channel_id=1, source_target_pairs={{0,4},{4,8},{8,12},{12,14},{14,10},{10,6},{6,2},{2,0},{1,5},{5,9},... | collective-permute-start | bytes 1769480 | tf_op jit(solution)/shard_map/ppermute | solution.py:93
  126.0 9.9 %collective-permute-start.19 = (bf16[2,288,512]{2,1,0:T(8,128)(2,1)S(1)}, bf16[2,288,512]{2,1,0:T(8,128)(2,1)S(1)}, u32[]{:S(2)}, u32[]{:S(2)}) collective-permute-start(bf16[2,288,512]{2,1,0:T(8,128)(2,1)S(1)} %collective-permute-done.16), channel_id=1, source_target_pairs={{0,2},{4,0},{8,4},{12,8},{14,12},{10,14},{6,10},{2,6},{1,3},{5,1},... | collective-permute-start | bytes 1769480 | tf_op jit(solution)/shard_map/ppermute | solution.py:94
  136.0 9.9 %collective-permute-start.20 = (bf16[2,288,512]{2,1,0:T(8,128)(2,1)S(1)}, bf16[2,288,512]{2,1,0:T(8,128)(2,1)S(1)}, u32[]{:S(2)}, u32[]{:S(2)}) collective-permute-start(bf16[2,288,512]{2,1,0:T(8,128)(2,1)S(1)} %pad_maximum_fusion.22), channel_id=1, source_target_pairs={{0,16},{16,0},{1,17},{17,1},{2,18},{18,2},{3,19},{19,3},{4,20},{20... | collective-permute-start | bytes 1769480 | tf_op jit(solution)/shard_map/ppermute | solution.py:98
  138.5 14.5 %copy-start.7 = (bf16[288,1536]{1,0:T(8,128)(2,1)}, bf16[288,1536]{1,0:T(8,128)(2,1)S(1)}, u32[]{:S(2)}) copy-start(bf16[288,1536]{1,0:T(8,128)(2,1)S(1)} %pad_maximum_fusion.13) | copy-start | bytes 2654212
  159.2 6.0 %copy-start.5 = (bf16[288,1536]{1,0:T(8,128)(2,1)S(1)}, bf16[288,1536]{1,0:T(8,128)(2,1)}, u32[]{:S(2)}) copy-start(bf16[288,1536]{1,0:T(8,128)(2,1)} %copy-done.4) | copy-start | bytes 2654212
  161.2 4.8 %copy-start.3 = (bf16[288,1536]{1,0:T(8,128)(2,1)S(1)}, bf16[288,1536]{1,0:T(8,128)(2,1)}, u32[]{:S(2)}) copy-start(bf16[288,1536]{1,0:T(8,128)(2,1)} %copy-done.2) | copy-start | bytes 2654212
  173.1 2.5 %collective-permute-start.21 = (bf16[128,2304]{1,0:T(8,128)(2,1)S(1)}, bf16[128,2304]{1,0:T(8,128)(2,1)S(1)}, u32[]{:S(2)}, u32[]{:S(2)}) collective-permute-start(bf16[128,2304]{1,0:T(8,128)(2,1)S(1)} %convolution_convert_fusion), channel_id=1, source_target_pairs={{0,1},{1,0},{2,3},{3,2},{4,5},{5,4},{6,7},{7,6},{8,9},{9,8},{10,11... | collective-permute-start | bytes 1769480 | tf_op jit(solution)/shard_map/ppermute | solution.py:58
  178.6 3.2 %copy-start.36 = (pred[128,128]{0,1:T(8,128)(4,1)S(1)}, pred[128,128]{0,1:T(8,128)(4,1)}, u32[]{:S(2)}) copy-start(pred[128,128]{0,1:T(8,128)(4,1)} %fusion.79) | copy-start | bytes 49156
  195.5 4.2 %copy-start.11 = (bf16[512,2304]{0,1:T(8,128)(2,1)S(1)}, bf16[512,2304]{0,1:T(8,128)(2,1)}, u32[]{:S(2)}) copy-start(bf16[512,2304]{0,1:T(8,128)(2,1)} %copy-done.10) | copy-start | bytes 7077892
  195.5 4.2 %copy-start.25 = (bf16[128,4,128]{0,2,1:T(8,128)(2,1)S(1)}, bf16[128,4,128]{0,2,1:T(8,128)(2,1)}, u32[]{:S(2)}) copy-start(bf16[128,4,128]{0,2,1:T(8,128)(2,1)} %copy.77) | copy-start | bytes 393220
  202.3 4.5 %collective-permute-start.22 = (bf16[128,2304]{1,0:T(8,128)(2,1)S(1)}, bf16[128,2304]{1,0:T(8,128)(2,1)}, u32[]{:S(2)}, u32[]{:S(2)}) collective-permute-start(bf16[128,2304]{1,0:T(8,128)(2,1)S(1)} %fusion.1), channel_id=1, source_target_pairs={{0,1},{1,0},{2,3},{3,2},{4,5},{5,4},{6,7},{7,6},{8,9},{9,8},{10,11... | collective-permute-start | bytes 1769480 | tf_op jit(solution)/shard_map/ppermute | solution.py:58
  (36 other events, 65.3 us)

commit v9 on v7

--- a/solution.py
+++ b/solution.py
@@ -65,6 +65,18 @@
     return list(range(0, n, 2)) + list(range(n - 1, 0, -2))
 
 
+def ring_member(place, n):
+    if n % 2:
+        return place
+    return jnp.where(place < n // 2, 2 * place, 2 * (n - 1 - place) + 1)
+
+
+def ring_position(member, n):
+    if n % 2:
+        return member
+    return jnp.where(member % 2 == 0, member // 2, n - 1 - member // 2)
+
+
 def ring_gather(front, back, seq_rank, group_rank, n):
     order = ring_order(n)
     position = [0] * n
@@ -73,10 +85,10 @@
     forward_pairs = [(order[p], order[(p + 1) % n]) for p in range(n)]
     backward_pairs = [(order[p], order[(p - 1) % n]) for p in range(n)]
     group_pairs = [(0, 1), (1, 0)]
-    place = jnp.array(position, dtype=jnp.int32)[seq_rank]
+    place = ring_position(seq_rank, n)
     steps = jnp.arange(n, dtype=jnp.int32)
-    block_of = jnp.array(order, dtype=jnp.int32)[(place - steps) % n]
-    slot_of = (place - jnp.array(position, dtype=jnp.int32)) % n
+    block_of = ring_member((place - steps) % n, n)
+    slot_of = (place - ring_position(steps, n)) % n
     first_group = group_rank == 0
 
     def thirds(values):
@@ -148,9 +160,9 @@
         front, back, seq_rank, lax.axis_index("groups"), n_seq
     )
     guard_rows = permute_blocks(guard_rows, block_of, n_seq)
-    pre_gain = permute_blocks(pre_gain, block_of, n_seq)
-    post_gain = permute_blocks(post_gain, block_of, n_seq)
-    final_gain = permute_blocks(final_gain, block_of, n_seq)
+    pre_gain, post_gain, final_gain = permute_blocks(
+        jnp.stack([pre_gain, post_gain, final_gain]), block_of, n_seq
+    )
     label_table = permute_blocks(label_table, block_of, n_seq)
     piecewise = n_seq <= PIECEWISE_RING
     if piecewise:

time: 221 us -> 221 us (level)
  waiting for transfers between devices: 76.2 us -> 78.6 us
    all_to_all x1, waiting for transfers between devices: 1.49 us -> 5.53 us  [shards(): lax.all_to_all(generator_rows, 'seq', split_axis=0, concat_axis=0, tiled=...]
    ppermute x7, starting transfers between devices: 10.8 us -> 7.49 us  [ring_gather(): front_ring.append(lax.ppermute(front_ring[-1], 'seq', forward_pairs))]
    ppermute x7, starting transfers between devices: 4.68 us -> 7.94 us  [ring_gather(): back_ring.append(lax.ppermute(back_ring[-1], 'seq', backward_pairs))]
    ppermute x7, waiting for transfers between devices: 12.5 us -> 9.97 us  [ring_gather(): back_ring.append(lax.ppermute(back_ring[-1], 'seq', backward_pairs))]
    gather x9 -> x7, local copies, waits for them, and re-layouts: 5.29 us -> 4.2 us  [permute_blocks(): return jnp.take(blocks, block_order, axis=-2).reshape(values.shape)]
    unnamed x143 -> x137, local copies, waits for them, and re-layouts: 14.9 us -> 15 us
  transfers between devices with their start and end apart: 24 -> 24, of which waited for: 17 -> 16; matrix products, arithmetic and copies ran while one was open for 15% -> 13% of each run, Pallas kernels for 0% -> 0%
where the time goes in v9:
time: 221 us; the launch traced here: 220 us
  waiting for transfers between devices  78.6 us (36%)
  local copies, waits for them, and re-layouts  38.4 us (17%)
  starting transfers between devices  30.2 us (14%)
  other arithmetic  27.4 us (12%)
  matrix products  26.8 us (12%)
  blocking collectives  17.7 us (8%)
    ppermute x7, waiting for transfers between devices, ring_gather(): lax.ppermute(jnp.stack([front_ring[step][0], back_ring[step][0]]), 'group...  44.5 us
    ppermute x7, waiting for transfers between devices, ring_gather(): front_ring.append(lax.ppermute(front_ring[-1], 'seq', forward_pairs))  18.6 us
    all_to_all x1, blocking collectives, shards(): lax.all_to_all(grad_rows.astype(jnp.bfloat16), 'seq', split_axis=0, conca...  15.3 us
    unnamed x137, local copies, waits for them, and re-layouts  15 us
    ppermute x7, waiting for transfers between devices, ring_gather(): back_ring.append(lax.ppermute(back_ring[-1], 'seq', backward_pairs))  9.97 us
    ppermute x7, starting transfers between devices, ring_gather(): back_ring.append(lax.ppermute(back_ring[-1], 'seq', backward_pairs))  7.94 us
    ppermute x7, starting transfers between devices, ring_gather(): lax.ppermute(jnp.stack([front_ring[step][0], back_ring[step][0]]), 'group...  7.9 us
    ppermute x7, starting transfers between devices, ring_gather(): front_ring.append(lax.ppermute(front_ring[-1], 'seq', forward_pairs))  7.49 us
  transfers between devices with their start and end apart: 24, of which 16 were waited for; matrix products, arithmetic and copies ran while one was open for 13% of the time, Pallas kernels for 0%

profile of v9, /device:TPU:0, one launch (start us, length us, event | category | flops | bytes accessed | tf_op | source)
XLA Modules:
  0.0 220.5 jit_solution(2171707354987693737)
XLA Ops:
  0.0 1.4 fusion.39
  2.4 3.0 %collective-permute-start = (bf16[2,288,512]{2,1,0:T(8,128)(2,1)}, bf16[2,288,512]{2,1,0:T(8,128)(2,1)}, u32[]{:S(2)}, u32[]{:S(2)}) collective-permute-start(bf16[2,288,512]{2,1,0:T(8,128)(2,1)} %pad_maximum_fusion.14), channel_id=1, source_target_pairs={{0,4},{4,8},{8,12},{12,14},{14,10},{10,6},{6,2},{2,0},{1,5},{5,9},... | collective-permute-start | bytes 1769480 | tf_op jit(solution)/shard_map/ppermute | solution.py:105
  6.3 6.3 %all-to-all-start = ((bf16[8,16,1152]{2,1,0:T(8,128)(2,1)}), bf16[8,16,1152]{2,1,0:T(8,128)(2,1)}, u32[]{:S(2)}, u32[]{:S(2)}) async-start(bf16[8,16,1152]{2,1,0:T(8,128)(2,1)} %bitcast), calls=%async_computation | async-start | bytes 589824 | tf_op jit(solution)/shard_map/all_to_all | solution.py:153
  16.2 1.2 compare_convert_fusion
  22.0 1.1 pad_maximum_fusion
  23.2 5.5 %all-to-all-done = bf16[8,16,1152]{2,1,0:T(8,128)(2,1)} async-done(((bf16[8,16,1152]{2,1,0:T(8,128)(2,1)}), bf16[8,16,1152]{2,1,0:T(8,128)(2,1)}, u32[]{:S(2)}, u32[]{:S(2)}) %all-to-all-start) | async-done | bytes 294944 | tf_op jit(solution)/shard_map/all_to_all | solution.py:153
  28.7 2.4 %all_gather.3 = bf16[128,2304]{1,0:T(8,128)(2,1)S(1)} all-gather(bf16[128,1152]{1,0:T(8,128)(2,1)} %bitcast.1), channel_id=1, replica_groups=mesh['groups'=2,'seq'=8,'wg'=2] {'wg'}, dimensions={1}, use_global_device_ids=true | all-gather | bytes 884736 | tf_op jit(solution)/shard_map/all_gather | solution.py:154
  35.6 1.6 collective-permute-start.2
  38.4 2.0 collective-permute-start.4
  41.6 12.1 %collective-permute-done.3 = bf16[2,288,512]{2,1,0:T(8,128)(2,1)S(1)} collective-permute-done((bf16[2,288,512]{2,1,0:T(8,128)(2,1)}, bf16[2,288,512]{2,1,0:T(8,128)(2,1)S(1)}, u32[]{:S(2)}, u32[]{:S(2)}) %collective-permute-start.3) | collective-permute-done | bytes 589856 | tf_op jit(solution)/shard_map/ppermute | solution.py:105
  54.5 1.4 select_bitcast_fusion.23
  56.0 1.3 collective-permute-start.6
  58.6 9.6 %collective-permute-done.5 = bf16[2,288,512]{2,1,0:T(8,128)(2,1)S(1)} collective-permute-done((bf16[2,288,512]{2,1,0:T(8,128)(2,1)S(1)}, bf16[2,288,512]{2,1,0:T(8,128)(2,1)S(1)}, u32[]{:S(2)}, u32[]{:S(2)}) %collective-permute-start.5) | collective-permute-done | bytes 589856 | tf_op jit(solution)/shard_map/ppermute | solution.py:110
  68.5 1.5 collective-permute-done.6
  70.7 1.6 collective-permute-start.8
  72.3 1.2 collective-permute-start.10
  74.9 8.3 %collective-permute-done.8 = bf16[2,288,512]{2,1,0:T(8,128)(2,1)S(1)} collective-permute-done((bf16[2,288,512]{2,1,0:T(8,128)(2,1)S(1)}, bf16[2,288,512]{2,1,0:T(8,128)(2,1)S(1)}, u32[]{:S(2)}, u32[]{:S(2)}) %collective-permute-start.8) | collective-permute-done | bytes 589856 | tf_op jit(solution)/shard_map/ppermute | solution.py:110
  83.5 1.1 collective-permute-done.10
  84.6 2.0 collective-permute-done.9
  87.7 1.2 collective-permute-start.13
  89.4 8.4 %collective-permute-done.11 = bf16[2,288,512]{2,1,0:T(8,128)(2,1)S(1)} collective-permute-done((bf16[2,288,512]{2,1,0:T(8,128)(2,1)S(1)}, bf16[2,288,512]{2,1,0:T(8,128)(2,1)S(1)}, u32[]{:S(2)}, u32[]{:S(2)}) %collective-permute-start.11) | collective-permute-done | bytes 589856 | tf_op jit(solution)/shard_map/ppermute | solution.py:110
  98.0 2.0 collective-permute-done.12
  101.2 1.8 collective-permute-start.16
  103.4 9.0 %collective-permute-done.14 = bf16[2,288,512]{2,1,0:T(8,128)(2,1)S(1)} collective-permute-done((bf16[2,288,512]{2,1,0:T(8,128)(2,1)S(1)}, bf16[2,288,512]{2,1,0:T(8,128)(2,1)S(1)}, u32[]{:S(2)}, u32[]{:S(2)}) %collective-permute-start.14) | collective-permute-done | bytes 589856 | tf_op jit(solution)/shard_map/ppermute | solution.py:110
  113.7 3.0 %collective-permute-start.17 = (bf16[2,288,512]{2,1,0:T(8,128)(2,1)S(1)}, bf16[2,288,512]{2,1,0:T(8,128)(2,1)S(1)}, u32[]{:S(2)}, u32[]{:S(2)}) collective-permute-start(bf16[2,288,512]{2,1,0:T(8,128)(2,1)S(1)} %pad_maximum_fusion.21), channel_id=1, source_target_pairs={{0,16},{16,0},{1,17},{17,1},{2,18},{18,2},{3,19},{19,3},{4,20},{20... | collective-permute-start | bytes 1769480 | tf_op jit(solution)/shard_map/ppermute | solution.py:110
  117.7 1.1 collective-permute-start.18
  119.3 7.3 %collective-permute-done.19 = bf16[2,288,512]{2,1,0:T(8,128)(2,1)S(1)} collective-permute-done((bf16[2,288,512]{2,1,0:T(8,128)(2,1)S(1)}, bf16[2,288,512]{2,1,0:T(8,128)(2,1)S(1)}, u32[]{:S(2)}, u32[]{:S(2)}) %collective-permute-start.19) | collective-permute-done | bytes 589856 | tf_op jit(solution)/shard_map/ppermute | solution.py:106
  129.3 8.4 %collective-permute-done.20 = bf16[2,288,512]{2,1,0:T(8,128)(2,1)S(1)} collective-permute-done((bf16[2,288,512]{2,1,0:T(8,128)(2,1)S(1)}, bf16[2,288,512]{2,1,0:T(8,128)(2,1)S(1)}, u32[]{:S(2)}, u32[]{:S(2)}) %collective-permute-start.20) | collective-permute-done | bytes 589856 | tf_op jit(solution)/shard_map/ppermute | solution.py:110
  149.1 2.1 fusion.28
  151.2 1.9 bitcast_dynamic-update-slice_fusion.12
  159.2 1.2 copy-done
  160.3 1.7 convolution_convert_fusion
  167.6 2.0 convolution_convert_fusion.2
  169.6 1.2 copy.92
  170.7 2.0 fusion.15
  173.7 2.9 %convolution_bitcast_fusion.1 = f32[4,128,128]{2,1,0:T(8,128)} fusion(bf16[4,2,128,128]{3,2,1,0:T(8,128)(2,1)} %copy-done.27, f32[4,2,128,128]{2,3,1,0:T(8,128)} %fusion.56, f32[4,2,128,128]{2,3,1,0:T(8,128)} %copy-done.51, f32[4,2,128]{2,1,0:T(2,128)S(1)} %copy-done.53, pred[128,128]{0,1:T(8,128)(4,1)S(1)} %copy-done.35), kind=kOutput, calls=%fused_computation.47 | convolution fusion | flops 35259520 | bytes 1593344 | tf_op jit(solution)/shard_map/kgij,kgid->kjd/dot_general | solution.py:273
  176.7 2.4 %convolution_multiply_fusion.1 = f32[4,2,128,128]{3,2,1,0:T(8,128)S(1)} fusion(f32[4,2,128,128]{2,3,1,0:T(8,128)} %fusion.56, f32[4,2,128,128]{2,3,1,0:T(8,128)} %copy-done.51, bf16[4,128,64]{2,1,0:T(8,128)(2,1)} %get-tuple-element.104, bf16[4,128,64]{2,1,0:T(8,128)(2,1)} %copy-done.30, f32[4,2,128]{2,1,0:T(2,128)} %copy-done.52, ...), kind=kOutput, calls=%fused_computation.24 | convolution fusion | flops 35652736 | bytes 1724416 | tf_op jit(solution)/shard_map/kgij,kjd->kgid/dot_general | solution.py:269
  179.0 1.2 add_convert_fusion.1
  181.0 1.7 copy.74
  184.6 4.1 %fusion.41 = f32[128,2304]{1,0:T(8,128)S(1)} fusion(bf16[1024,2304]{0,1:T(8,128)(2,1)} %fusion.29, bf16[16,8,8,128]{3,2,1,0:T(8,128)(2,1)S(1)} %bitcast.296), kind=kOutput, calls=%fused_computation.195 | convolution fusion | flops 603979776 | bytes 6160384 | tf_op jit(solution)/shard_map/dot_general | solution.py:283
  189.7 2.6 %fusion.1 = bf16[128,2304]{1,0:T(8,128)(2,1)S(1)} fusion(f32[128,2304]{1,0:T(8,128)S(1)} %convolution_add_fusion.1, bf16[128,512]{0,1:T(8,128)(2,1)S(1)} %bitcast.301, bf16[512,2304]{0,1:T(8,128)(2,1)} %bitcast_dynamic-update-slice_fusion.16), kind=kOutput, calls=%fused_computation.8 | convolution fusion | flops 302579712 | bytes 4259840 | tf_op jit(solution)/shard_map/dot_general | solution.py:285
  192.8 1.3 broadcast_in_dim.109
  194.2 1.4 broadcast_in_dim.110
  195.5 1.3 dynamic-slice
  197.5 1.5 fusion.13
  199.0 2.9 %fusion.12 = bf16[128,2304]{1,0:T(8,128)(2,1)} fusion(bf16[128,2304]{1,0:T(8,128)(2,1)} %collective-permute-done.22, bf16[128,2304]{1,0:T(8,128)(2,1)S(1)} %fusion.1, f32[128]{0:T(128)S(1)} %broadcast_multiply_fusion, f32[128]{0:T(128)} %get-tuple-element.107, f32[2304]{0:T(1024)S(1)} %mul.518, f32[128]{0:T(128)} %copy-done.42, ...), kind=kLoop, calls=%fused_computation.34 | loop fusion | flops 6488064 | bytes 4742912 | tf_op jit(solution)/shard_map/add | solution.py:291
  201.8 1.4 copy.76
  204.5 15.3 %all_to_all.24 = bf16[8,16,1152]{2,1,0:T(8,128)(2,1)S(1)} all-to-all(bf16[8,16,1152]{2,1,0:T(8,128)(2,1)S(1)} %bitcast.294), channel_id=1, replica_groups=mesh['groups'=2,'seq'=8,'wg'=2] {'seq'}, dimensions={0} | all-to-all | bytes 589824 | tf_op jit(solution)/shard_map/all_to_all | solution.py:294
  (284 shorter events, 60.5 us)
Async XLA Ops:
  1.4 11.7 %copy-start.36 = (f32[2304]{0:T(1024)S(1)}, f32[2304]{0:T(1024)}, u32[]{:S(2)}) copy-start(f32[2304]{0:T(1024)} %param.12) | copy-start | bytes 27652
  1.4 11.8 %copy-start.37 = (f32[2304]{0:T(1024)S(1)}, f32[2304]{0:T(1024)}, u32[]{:S(2)}) copy-start(f32[2304]{0:T(1024)} %param.17) | copy-start | bytes 27652
  1.4 11.9 %copy-start.38 = (f32[2304]{0:T(1024)S(1)}, f32[2304]{0:T(1024)}, u32[]{:S(2)}) copy-start(f32[2304]{0:T(1024)} %param.18) | copy-start | bytes 27652
  1.5 12.8 %copy-start.48 = (s32[8]{0:T(128)S(1)}, s32[8]{0:T(128)}, u32[]{:S(2)}) copy-start(s32[8]{0:T(128)} %param.20) | copy-start | bytes 100
  1.5 14.1 %copy-start.49 = (s32[8]{0:T(128)S(1)}, s32[8]{0:T(128)}, u32[]{:S(2)}) copy-start(s32[8]{0:T(128)} %param.21) | copy-start | bytes 100
  1.5 16.9 %copy-start.25 = (bf16[64,2304]{1,0:T(8,128)(2,1)S(1)}, bf16[64,2304]{1,0:T(8,128)(2,1)}, u32[]{:S(2)}) copy-start(bf16[64,2304]{1,0:T(8,128)(2,1)} %param.19) | copy-start | bytes 884740
  2.4 31.2 %collective-permute-start = (bf16[2,288,512]{2,1,0:T(8,128)(2,1)}, bf16[2,288,512]{2,1,0:T(8,128)(2,1)}, u32[]{:S(2)}, u32[]{:S(2)}) collective-permute-start(bf16[2,288,512]{2,1,0:T(8,128)(2,1)} %pad_maximum_fusion.14), channel_id=1, source_target_pairs={{0,4},{4,8},{8,12},{12,14},{14,10},{10,6},{6,2},{2,0},{1,5},{5,9},... | collective-permute-start | bytes 1769480 | tf_op jit(solution)/shard_map/ppermute | solution.py:105
  6.3 28.3 %collective-permute-start.1 = (bf16[2,288,512]{2,1,0:T(8,128)(2,1)}, bf16[2,288,512]{2,1,0:T(8,128)(2,1)}, u32[]{:S(2)}, u32[]{:S(2)}) collective-permute-start(bf16[2,288,512]{2,1,0:T(8,128)(2,1)} %pad_maximum_fusion.15), channel_id=1, source_target_pairs={{0,2},{4,0},{8,4},{12,8},{14,12},{10,14},{6,10},{2,6},{1,3},{5,1},... | collective-permute-start | bytes 1769480 | tf_op jit(solution)/shard_map/ppermute | solution.py:106
  6.3 22.4 %all-to-all-start = ((bf16[8,16,1152]{2,1,0:T(8,128)(2,1)}), bf16[8,16,1152]{2,1,0:T(8,128)(2,1)}, u32[]{:S(2)}, u32[]{:S(2)}) async-start(bf16[8,16,1152]{2,1,0:T(8,128)(2,1)} %bitcast), calls=%async_computation | async-start | bytes 589824 | tf_op jit(solution)/shard_map/all_to_all | solution.py:153
  15.6 142.7 %copy-start.34 = (pred[128,128]{0,1:T(8,128)(4,1)}, pred[128,128]{0,1:T(8,128)(4,1)S(1)}, u32[]{:S(2)}) copy-start(pred[128,128]{0,1:T(8,128)(4,1)S(1)} %fusion.79) | copy-start | bytes 49156
  19.0 3.0 %copy-start.9 = (bf16[288,1024]{1,0:T(8,128)(2,1)S(1)}, bf16[288,1024]{1,0:T(8,128)(2,1)}, u32[]{:S(2)}) copy-start(bf16[288,1024]{1,0:T(8,128)(2,1)} %param.13) | copy-start | bytes 1769476
  22.0 119.6 %copy-start.13 = (f32[128,64]{1,0:T(8,128)}, f32[128,64]{1,0:T(8,128)S(1)}, u32[]{:S(2)}) copy-start(f32[128,64]{1,0:T(8,128)S(1)} %get-tuple-element.105) | copy-start | bytes 98308
  22.0 119.6 %copy-start.15 = (f32[128,64]{1,0:T(8,128)}, f32[128,64]{1,0:T(8,128)S(1)}, u32[]{:S(2)}) copy-start(f32[128,64]{1,0:T(8,128)S(1)} %get-tuple-element.106) | copy-start | bytes 98308
  35.6 18.9 %collective-permute-start.2 = (bf16[2,288,512]{2,1,0:T(8,128)(2,1)S(1)}, bf16[2,288,512]{2,1,0:T(8,128)(2,1)S(1)}, u32[]{:S(2)}, u32[]{:S(2)}) collective-permute-start(bf16[2,288,512]{2,1,0:T(8,128)(2,1)S(1)} %pad_maximum_fusion.16), channel_id=1, source_target_pairs={{0,16},{16,0},{1,17},{17,1},{2,18},{18,2},{3,19},{19,3},{4,20},{20... | collective-permute-start | bytes 1769480 | tf_op jit(solution)/shard_map/ppermute | solution.py:110
  38.4 15.4 %collective-permute-start.3 = (bf16[2,288,512]{2,1,0:T(8,128)(2,1)}, bf16[2,288,512]{2,1,0:T(8,128)(2,1)S(1)}, u32[]{:S(2)}, u32[]{:S(2)}) collective-permute-start(bf16[2,288,512]{2,1,0:T(8,128)(2,1)} %collective-permute-done), channel_id=1, source_target_pairs={{0,4},{4,8},{8,12},{12,14},{14,10},{10,6},{6,2},{2,0},{1,5},{5,9},... | collective-permute-start | bytes 1769480 | tf_op jit(solution)/shard_map/ppermute | solution.py:105
  38.4 15.4 %collective-permute-start.4 = (bf16[2,288,512]{2,1,0:T(8,128)(2,1)}, bf16[2,288,512]{2,1,0:T(8,128)(2,1)S(1)}, u32[]{:S(2)}, u32[]{:S(2)}) collective-permute-start(bf16[2,288,512]{2,1,0:T(8,128)(2,1)} %collective-permute-done.1), channel_id=1, source_target_pairs={{0,2},{4,0},{8,4},{12,8},{14,12},{10,14},{6,10},{2,6},{1,3},{5,1},... | collective-permute-start | bytes 1769480 | tf_op jit(solution)/shard_map/ppermute | solution.py:106
  53.9 14.3 %collective-permute-start.5 = (bf16[2,288,512]{2,1,0:T(8,128)(2,1)S(1)}, bf16[2,288,512]{2,1,0:T(8,128)(2,1)S(1)}, u32[]{:S(2)}, u32[]{:S(2)}) collective-permute-start(bf16[2,288,512]{2,1,0:T(8,128)(2,1)S(1)} %pad_maximum_fusion.17), channel_id=1, source_target_pairs={{0,16},{16,0},{1,17},{17,1},{2,18},{18,2},{3,19},{19,3},{4,20},{20... | collective-permute-start | bytes 1769480 | tf_op jit(solution)/shard_map/ppermute | solution.py:110
  56.0 14.0 %collective-permute-start.6 = (bf16[2,288,512]{2,1,0:T(8,128)(2,1)S(1)}, bf16[2,288,512]{2,1,0:T(8,128)(2,1)S(1)}, u32[]{:S(2)}, u32[]{:S(2)}) collective-permute-start(bf16[2,288,512]{2,1,0:T(8,128)(2,1)S(1)} %collective-permute-done.3), channel_id=1, source_target_pairs={{0,4},{4,8},{8,12},{12,14},{14,10},{10,6},{6,2},{2,0},{1,5},{5,9},... | collective-permute-start | bytes 1769480 | tf_op jit(solution)/shard_map/ppermute | solution.py:105
  57.3 13.4 %collective-permute-start.7 = (bf16[2,288,512]{2,1,0:T(8,128)(2,1)S(1)}, bf16[2,288,512]{2,1,0:T(8,128)(2,1)S(1)}, u32[]{:S(2)}, u32[]{:S(2)}) collective-permute-start(bf16[2,288,512]{2,1,0:T(8,128)(2,1)S(1)} %collective-permute-done.4), channel_id=1, source_target_pairs={{0,2},{4,0},{8,4},{12,8},{14,12},{10,14},{6,10},{2,6},{1,3},{5,1},... | collective-permute-start | bytes 1769480 | tf_op jit(solution)/shard_map/ppermute | solution.py:106
  70.7 12.5 %collective-permute-start.8 = (bf16[2,288,512]{2,1,0:T(8,128)(2,1)S(1)}, bf16[2,288,512]{2,1,0:T(8,128)(2,1)S(1)}, u32[]{:S(2)}, u32[]{:S(2)}) collective-permute-start(bf16[2,288,512]{2,1,0:T(8,128)(2,1)S(1)} %pad_maximum_fusion.18), channel_id=1, source_target_pairs={{0,16},{16,0},{1,17},{17,1},{2,18},{18,2},{3,19},{19,3},{4,20},{20... | collective-permute-start | bytes 1769480 | tf_op jit(solution)/shard_map/ppermute | solution.py:110
  72.3 12.2 %collective-permute-start.10 = (bf16[2,288,512]{2,1,0:T(8,128)(2,1)S(1)}, bf16[2,288,512]{2,1,0:T(8,128)(2,1)S(1)}, u32[]{:S(2)}, u32[]{:S(2)}) collective-permute-start(bf16[2,288,512]{2,1,0:T(8,128)(2,1)S(1)} %collective-permute-done.7), channel_id=1, source_target_pairs={{0,2},{4,0},{8,4},{12,8},{14,12},{10,14},{6,10},{2,6},{1,3},{5,1},... | collective-permute-start | bytes 1769480 | tf_op jit(solution)/shard_map/ppermute | solution.py:106
  73.5 13.0 %collective-permute-start.9 = (bf16[2,288,512]{2,1,0:T(8,128)(2,1)S(1)}, bf16[2,288,512]{2,1,0:T(8,128)(2,1)S(1)}, u32[]{:S(2)}, u32[]{:S(2)}) collective-permute-start(bf16[2,288,512]{2,1,0:T(8,128)(2,1)S(1)} %collective-permute-done.6), channel_id=1, source_target_pairs={{0,4},{4,8},{8,12},{12,14},{14,10},{10,6},{6,2},{2,0},{1,5},{5,9},... | collective-permute-start | bytes 1769480 | tf_op jit(solution)/shard_map/ppermute | solution.py:105
  86.7 11.1 %collective-permute-start.11 = (bf16[2,288,512]{2,1,0:T(8,128)(2,1)S(1)}, bf16[2,288,512]{2,1,0:T(8,128)(2,1)S(1)}, u32[]{:S(2)}, u32[]{:S(2)}) collective-permute-start(bf16[2,288,512]{2,1,0:T(8,128)(2,1)S(1)} %pad_maximum_fusion.19), channel_id=1, source_target_pairs={{0,16},{16,0},{1,17},{17,1},{2,18},{18,2},{3,19},{19,3},{4,20},{20... | collective-permute-start | bytes 1769480 | tf_op jit(solution)/shard_map/ppermute | solution.py:110
  86.8 13.3 %collective-permute-start.12 = (bf16[2,288,512]{2,1,0:T(8,128)(2,1)S(1)}, bf16[2,288,512]{2,1,0:T(8,128)(2,1)S(1)}, u32[]{:S(2)}, u32[]{:S(2)}) collective-permute-start(bf16[2,288,512]{2,1,0:T(8,128)(2,1)S(1)} %collective-permute-done.9), channel_id=1, source_target_pairs={{0,4},{4,8},{8,12},{12,14},{14,10},{10,6},{6,2},{2,0},{1,5},{5,9},... | collective-permute-start | bytes 1769480 | tf_op jit(solution)/shard_map/ppermute | solution.py:105
  87.7 12.4 %collective-permute-start.13 = (bf16[2,288,512]{2,1,0:T(8,128)(2,1)S(1)}, bf16[2,288,512]{2,1,0:T(8,128)(2,1)S(1)}, u32[]{:S(2)}, u32[]{:S(2)}) collective-permute-start(bf16[2,288,512]{2,1,0:T(8,128)(2,1)S(1)} %collective-permute-done.10), channel_id=1, source_target_pairs={{0,2},{4,0},{8,4},{12,8},{14,12},{10,14},{6,10},{2,6},{1,3},{5,1},... | collective-permute-start | bytes 1769480 | tf_op jit(solution)/shard_map/ppermute | solution.py:106
  97.9 48.5 %copy-start.2 = (bf16[288,1536]{1,0:T(8,128)(2,1)}, bf16[288,1536]{1,0:T(8,128)(2,1)S(1)}, u32[]{:S(2)}) copy-start(bf16[288,1536]{1,0:T(8,128)(2,1)S(1)} %pad_maximum_fusion.9) | copy-start | bytes 2654212
  100.2 12.2 %collective-permute-start.14 = (bf16[2,288,512]{2,1,0:T(8,128)(2,1)S(1)}, bf16[2,288,512]{2,1,0:T(8,128)(2,1)S(1)}, u32[]{:S(2)}, u32[]{:S(2)}) collective-permute-start(bf16[2,288,512]{2,1,0:T(8,128)(2,1)S(1)} %pad_maximum_fusion.20), channel_id=1, source_target_pairs={{0,16},{16,0},{1,17},{17,1},{2,18},{18,2},{3,19},{19,3},{4,20},{20... | collective-permute-start | bytes 1769480 | tf_op jit(solution)/shard_map/ppermute | solution.py:110
  100.8 11.8 %collective-permute-start.15 = (bf16[2,288,512]{2,1,0:T(8,128)(2,1)S(1)}, bf16[2,288,512]{2,1,0:T(8,128)(2,1)S(1)}, u32[]{:S(2)}, u32[]{:S(2)}) collective-permute-start(bf16[2,288,512]{2,1,0:T(8,128)(2,1)S(1)} %collective-permute-done.12), channel_id=1, source_target_pairs={{0,4},{4,8},{8,12},{12,14},{14,10},{10,6},{6,2},{2,0},{1,5},{5,9},... | collective-permute-start | bytes 1769480 | tf_op jit(solution)/shard_map/ppermute | solution.py:105
  101.2 12.4 %collective-permute-start.16 = (bf16[2,288,512]{2,1,0:T(8,128)(2,1)S(1)}, bf16[2,288,512]{2,1,0:T(8,128)(2,1)S(1)}, u32[]{:S(2)}, u32[]{:S(2)}) collective-permute-start(bf16[2,288,512]{2,1,0:T(8,128)(2,1)S(1)} %collective-permute-done.13), channel_id=1, source_target_pairs={{0,2},{4,0},{8,4},{12,8},{14,12},{10,14},{6,10},{2,6},{1,3},{5,1},... | collective-permute-start | bytes 1769480 | tf_op jit(solution)/shard_map/ppermute | solution.py:106
  112.6 32.9 %copy-start.4 = (bf16[288,1536]{1,0:T(8,128)(2,1)}, bf16[288,1536]{1,0:T(8,128)(2,1)S(1)}, u32[]{:S(2)}) copy-start(bf16[288,1536]{1,0:T(8,128)(2,1)S(1)} %pad_maximum_fusion.11) | copy-start | bytes 2654212
  113.7 15.2 %collective-permute-start.17 = (bf16[2,288,512]{2,1,0:T(8,128)(2,1)S(1)}, bf16[2,288,512]{2,1,0:T(8,128)(2,1)S(1)}, u32[]{:S(2)}, u32[]{:S(2)}) collective-permute-start(bf16[2,288,512]{2,1,0:T(8,128)(2,1)S(1)} %pad_maximum_fusion.21), channel_id=1, source_target_pairs={{0,16},{16,0},{1,17},{17,1},{2,18},{18,2},{3,19},{19,3},{4,20},{20... | collective-permute-start | bytes 1769480 | tf_op jit(solution)/shard_map/ppermute | solution.py:110
  116.7 9.9 %collective-permute-start.19 = (bf16[2,288,512]{2,1,0:T(8,128)(2,1)S(1)}, bf16[2,288,512]{2,1,0:T(8,128)(2,1)S(1)}, u32[]{:S(2)}, u32[]{:S(2)}) collective-permute-start(bf16[2,288,512]{2,1,0:T(8,128)(2,1)S(1)} %collective-permute-done.16), channel_id=1, source_target_pairs={{0,2},{4,0},{8,4},{12,8},{14,12},{10,14},{6,10},{2,6},{1,3},{5,1},... | collective-permute-start | bytes 1769480 | tf_op jit(solution)/shard_map/ppermute | solution.py:106
  117.7 9.9 %collective-permute-start.18 = (bf16[2,288,512]{2,1,0:T(8,128)(2,1)S(1)}, bf16[2,288,512]{2,1,0:T(8,128)(2,1)S(1)}, u32[]{:S(2)}, u32[]{:S(2)}) collective-permute-start(bf16[2,288,512]{2,1,0:T(8,128)(2,1)S(1)} %collective-permute-done.15), channel_id=1, source_target_pairs={{0,4},{4,8},{8,12},{12,14},{14,10},{10,6},{6,2},{2,0},{1,5},{5,9},... | collective-permute-start | bytes 1769480 | tf_op jit(solution)/shard_map/ppermute | solution.py:105
  127.7 9.9 %collective-permute-start.20 = (bf16[2,288,512]{2,1,0:T(8,128)(2,1)S(1)}, bf16[2,288,512]{2,1,0:T(8,128)(2,1)S(1)}, u32[]{:S(2)}, u32[]{:S(2)}) collective-permute-start(bf16[2,288,512]{2,1,0:T(8,128)(2,1)S(1)} %pad_maximum_fusion.22), channel_id=1, source_target_pairs={{0,16},{16,0},{1,17},{17,1},{2,18},{18,2},{3,19},{19,3},{4,20},{20... | collective-permute-start | bytes 1769480 | tf_op jit(solution)/shard_map/ppermute | solution.py:110
  129.1 15.4 %copy-start.6 = (bf16[288,1536]{1,0:T(8,128)(2,1)}, bf16[288,1536]{1,0:T(8,128)(2,1)S(1)}, u32[]{:S(2)}) copy-start(bf16[288,1536]{1,0:T(8,128)(2,1)S(1)} %pad_maximum_fusion.13) | copy-start | bytes 2654212
  129.2 9.7 %copy-start.1 = (bf16[1024,2304]{0,1:T(8,128)(2,1)}, bf16[1024,2304]{0,1:T(8,128)(2,1)S(1)}, u32[]{:S(2)}) copy-start(bf16[1024,2304]{0,1:T(8,128)(2,1)S(1)} %bitcast_dynamic-update-slice_fusion) | copy-start | bytes 14155780
  142.5 15.5 %copy-start.30 = (bf16[4,128,64]{2,1,0:T(8,128)(2,1)}, bf16[4,128,64]{2,1,0:T(8,128)(2,1)S(1)}, u32[]{:S(2)}) copy-start(bf16[4,128,64]{2,1,0:T(8,128)(2,1)S(1)} %get-tuple-element.103) | copy-start | bytes 196612
  148.3 5.7 %copy-start.18 = (bf16[128,512]{1,0:T(8,128)(2,1)}, bf16[128,512]{1,0:T(8,128)(2,1)S(1)}, u32[]{:S(2)}) copy-start(bf16[128,512]{1,0:T(8,128)(2,1)S(1)} %fusion.14) | copy-start | bytes 393220
  149.1 4.0 %copy-start.5 = (bf16[288,1536]{1,0:T(8,128)(2,1)S(1)}, bf16[288,1536]{1,0:T(8,128)(2,1)}, u32[]{:S(2)}) copy-start(bf16[288,1536]{1,0:T(8,128)(2,1)} %copy-done.4) | copy-start | bytes 2654212
  149.1 4.9 %copy-start.3 = (bf16[288,1536]{1,0:T(8,128)(2,1)S(1)}, bf16[288,1536]{1,0:T(8,128)(2,1)}, u32[]{:S(2)}) copy-start(bf16[288,1536]{1,0:T(8,128)(2,1)} %copy-done.2) | copy-start | bytes 2654212
  162.0 2.5 %collective-permute-start.21 = (bf16[128,2304]{1,0:T(8,128)(2,1)S(1)}, bf16[128,2304]{1,0:T(8,128)(2,1)S(1)}, u32[]{:S(2)}, u32[]{:S(2)}) collective-permute-start(bf16[128,2304]{1,0:T(8,128)(2,1)S(1)} %convolution_convert_fusion), channel_id=1, source_target_pairs={{0,1},{1,0},{2,3},{3,2},{4,5},{5,4},{6,7},{7,6},{8,9},{9,8},{10,11... | collective-permute-start | bytes 1769480 | tf_op jit(solution)/shard_map/ppermute | solution.py:58
  167.5 3.2 %copy-start.35 = (pred[128,128]{0,1:T(8,128)(4,1)S(1)}, pred[128,128]{0,1:T(8,128)(4,1)}, u32[]{:S(2)}) copy-start(pred[128,128]{0,1:T(8,128)(4,1)} %copy-done.34) | copy-start | bytes 49156
  167.6 3.2 %copy-start.53 = (f32[4,2,128]{2,1,0:T(2,128)S(1)}, f32[4,2,128]{2,1,0:T(2,128)}, u32[]{:S(2)}) copy-start(f32[4,2,128]{2,1,0:T(2,128)} %copy-done.52) | copy-start | bytes 12292
  169.6 3.2 %copy-start.19 = (bf16[128,512]{1,0:T(8,128)(2,1)S(1)}, bf16[128,512]{1,0:T(8,128)(2,1)}, u32[]{:S(2)}) copy-start(bf16[128,512]{1,0:T(8,128)(2,1)} %copy-done.18) | copy-start | bytes 393220
  184.6 4.2 %copy-start.8 = (bf16[512,2304]{0,1:T(8,128)(2,1)S(1)}, bf16[512,2304]{0,1:T(8,128)(2,1)}, u32[]{:S(2)}) copy-start(bf16[512,2304]{0,1:T(8,128)(2,1)} %copy-done.7) | copy-start | bytes 7077892
  184.6 4.2 %copy-start.24 = (bf16[128,4,128]{0,2,1:T(8,128)(2,1)S(1)}, bf16[128,4,128]{0,2,1:T(8,128)(2,1)}, u32[]{:S(2)}) copy-start(bf16[128,4,128]{0,2,1:T(8,128)(2,1)} %copy.74) | copy-start | bytes 393220
  192.3 5.2 %collective-permute-start.22 = (bf16[128,2304]{1,0:T(8,128)(2,1)S(1)}, bf16[128,2304]{1,0:T(8,128)(2,1)}, u32[]{:S(2)}, u32[]{:S(2)}) collective-permute-start(bf16[128,2304]{1,0:T(8,128)(2,1)S(1)} %fusion.1), channel_id=1, source_target_pairs={{0,1},{1,0},{2,3},{3,2},{4,5},{5,4},{6,7},{7,6},{8,9},{9,8},{10,11... | collective-permute-start | bytes 1769480 | tf_op jit(solution)/shard_map/ppermute | solution.py:58
  195.5 3.4 %copy-start.29 = (f32[2304]{0:T(1024)S(1)}, f32[2304]{0:T(1024)}, u32[]{:S(2)}) copy-start(f32[2304]{0:T(1024)} %mul.541) | copy-start | bytes 27652
  (30 other events, 53.4 us)

commit v10 on v9

--- a/solution.py
+++ b/solution.py
@@ -289,11 +289,12 @@
     scaled_in = grad_normed * pre_gain
     row_stat = jnp.mean(scaled_in * inputs, axis=-1, keepdims=True)
     grad_full = scale_in * scaled_in - inputs * cube_in * row_stat + grad_mixed
-    grad_full = permute_blocks(grad_full, slot_of, n_seq)
-    grad_rows = lax.dynamic_slice_in_dim(grad_full, core_rank * half_width, half_width, 1)
-    return lax.all_to_all(
-        grad_rows.astype(jnp.bfloat16), "seq", split_axis=0, concat_axis=0, tiled=True
-    )
+    block_width = grad_full.shape[1] // n_seq
+    half_blocks = half_width // block_width
+    own_blocks = core_rank * half_blocks + jnp.arange(half_blocks, dtype=jnp.int32)
+    grad_blocks = grad_full.astype(jnp.bfloat16).reshape(tok_rows, n_seq, block_width)
+    grad_rows = jnp.take(grad_blocks, slot_of[own_blocks], axis=1).reshape(tok_rows, half_width)
+    return lax.all_to_all(grad_rows, "seq", split_axis=0, concat_axis=0, tiled=True)
 
 
 def solution(mesh):

time: 221 us -> 208 us (0.941)
  local copies, waits for them, and re-layouts: 38.4 us -> 32.7 us
  matrix products: 26.8 us -> 22.7 us
  other arithmetic: 27.4 us -> 23.8 us
    add x1 -> x0, other arithmetic: 2.88 us -> none  [shards(): grad_full = scale_in * scaled_in - inputs * cube_in * row_stat + grad_mixed]
    broadcast_in_dim x4 -> x2, local copies, waits for them, and re-layouts: 2.83 us -> 0.16 us  [permute_blocks(): return jnp.take(blocks, block_order, axis=-2).reshape(values.shape)]
    unnamed x137 -> x141, local copies, waits for them, and re-layouts: 15 us -> 14.6 us
where the time goes in v10:
time: 208 us; the launch traced here: 207 us
  waiting for transfers between devices  78.4 us (38%)
  local copies, waits for them, and re-layouts  32.7 us (16%)
  starting transfers between devices  30.4 us (15%)
  other arithmetic  23.8 us (11%)
  matrix products  22.7 us (11%)
  blocking collectives  17.8 us (9%)
    ppermute x7, waiting for transfers between devices, ring_gather(): lax.ppermute(jnp.stack([front_ring[step][0], back_ring[step][0]]), 'group...  44.4 us
    ppermute x7, waiting for transfers between devices, ring_gather(): front_ring.append(lax.ppermute(front_ring[-1], 'seq', forward_pairs))  18.6 us
    all_to_all x1, blocking collectives, shards(): lax.all_to_all(grad_rows, 'seq', split_axis=0, concat_axis=0, tiled=True)  15.4 us
    unnamed x141, local copies, waits for them, and re-layouts  14.6 us
    ppermute x7, waiting for transfers between devices, ring_gather(): back_ring.append(lax.ppermute(back_ring[-1], 'seq', backward_pairs))  9.78 us
    ppermute x7, starting transfers between devices, ring_gather(): lax.ppermute(jnp.stack([front_ring[step][0], back_ring[step][0]]), 'group...  8.12 us
    ppermute x7, starting transfers between devices, ring_gather(): back_ring.append(lax.ppermute(back_ring[-1], 'seq', backward_pairs))  7.97 us
    ppermute x7, starting transfers between devices, ring_gather(): front_ring.append(lax.ppermute(front_ring[-1], 'seq', forward_pairs))  7.47 us
  transfers between devices with their start and end apart: 24, of which 16 were waited for; matrix products, arithmetic and copies ran while one was open for 13% of the time, Pallas kernels for 0%

profile of v10, /device:TPU:0, one launch (start us, length us, event | category | flops | bytes accessed | tf_op | source)
XLA Modules:
  0.0 207.2 jit_solution(15284192343733501557)
XLA Ops:
  0.0 1.4 fusion.39
  2.4 3.0 %collective-permute-start = (bf16[2,288,512]{2,1,0:T(8,128)(2,1)}, bf16[2,288,512]{2,1,0:T(8,128)(2,1)}, u32[]{:S(2)}, u32[]{:S(2)}) collective-permute-start(bf16[2,288,512]{2,1,0:T(8,128)(2,1)} %pad_maximum_fusion.14), channel_id=1, source_target_pairs={{0,4},{4,8},{8,12},{12,14},{14,10},{10,6},{6,2},{2,0},{1,5},{5,9},... | collective-permute-start | bytes 1769480 | tf_op jit(solution)/shard_map/ppermute | solution.py:105
  6.3 6.3 %all-to-all-start = ((bf16[8,16,1152]{2,1,0:T(8,128)(2,1)}), bf16[8,16,1152]{2,1,0:T(8,128)(2,1)}, u32[]{:S(2)}, u32[]{:S(2)}) async-start(bf16[8,16,1152]{2,1,0:T(8,128)(2,1)} %bitcast.1), calls=%async_computation | async-start | bytes 589824 | tf_op jit(solution)/shard_map/all_to_all | solution.py:153
  16.3 1.1 compare_convert_fusion
  19.9 1.0 gather.32
  22.0 1.1 pad_maximum_fusion
  23.1 5.6 %all-to-all-done = bf16[8,16,1152]{2,1,0:T(8,128)(2,1)} async-done(((bf16[8,16,1152]{2,1,0:T(8,128)(2,1)}), bf16[8,16,1152]{2,1,0:T(8,128)(2,1)}, u32[]{:S(2)}, u32[]{:S(2)}) %all-to-all-start) | async-done | bytes 294944 | tf_op jit(solution)/shard_map/all_to_all | solution.py:153
  28.7 2.4 %all_gather.3 = bf16[128,2304]{1,0:T(8,128)(2,1)S(1)} all-gather(bf16[128,1152]{1,0:T(8,128)(2,1)} %bitcast.2), channel_id=1, replica_groups=mesh['groups'=2,'seq'=8,'wg'=2] {'wg'}, dimensions={1}, use_global_device_ids=true | all-gather | bytes 884736 | tf_op jit(solution)/shard_map/all_gather | solution.py:154
  33.5 1.0 slice.408
  34.5 1.0 slice.409
  35.5 1.6 collective-permute-start.2
  38.4 2.0 collective-permute-start.4
  41.5 12.1 %collective-permute-done.3 = bf16[2,288,512]{2,1,0:T(8,128)(2,1)S(1)} collective-permute-done((bf16[2,288,512]{2,1,0:T(8,128)(2,1)}, bf16[2,288,512]{2,1,0:T(8,128)(2,1)S(1)}, u32[]{:S(2)}, u32[]{:S(2)}) %collective-permute-start.3) | collective-permute-done | bytes 589856 | tf_op jit(solution)/shard_map/ppermute | solution.py:105
  54.4 1.4 select_bitcast_fusion.23
  55.9 1.3 collective-permute-start.6
  58.5 9.6 %collective-permute-done.5 = bf16[2,288,512]{2,1,0:T(8,128)(2,1)S(1)} collective-permute-done((bf16[2,288,512]{2,1,0:T(8,128)(2,1)S(1)}, bf16[2,288,512]{2,1,0:T(8,128)(2,1)S(1)}, u32[]{:S(2)}, u32[]{:S(2)}) %collective-permute-start.5) | collective-permute-done | bytes 589856 | tf_op jit(solution)/shard_map/ppermute | solution.py:110
  68.4 1.5 collective-permute-done.6
  70.6 1.6 collective-permute-start.8
  72.3 1.2 collective-permute-start.10
  74.8 8.3 %collective-permute-done.8 = bf16[2,288,512]{2,1,0:T(8,128)(2,1)S(1)} collective-permute-done((bf16[2,288,512]{2,1,0:T(8,128)(2,1)S(1)}, bf16[2,288,512]{2,1,0:T(8,128)(2,1)S(1)}, u32[]{:S(2)}, u32[]{:S(2)}) %collective-permute-start.8) | collective-permute-done | bytes 589856 | tf_op jit(solution)/shard_map/ppermute | solution.py:110
  83.4 1.0 collective-permute-done.10
  84.4 2.0 collective-permute-done.9
  87.6 1.2 collective-permute-start.13
  89.3 8.4 %collective-permute-done.11 = bf16[2,288,512]{2,1,0:T(8,128)(2,1)S(1)} collective-permute-done((bf16[2,288,512]{2,1,0:T(8,128)(2,1)S(1)}, bf16[2,288,512]{2,1,0:T(8,128)(2,1)S(1)}, u32[]{:S(2)}, u32[]{:S(2)}) %collective-permute-start.11) | collective-permute-done | bytes 589856 | tf_op jit(solution)/shard_map/ppermute | solution.py:110
  97.9 2.1 collective-permute-done.12
  101.1 1.8 collective-permute-start.16
  103.3 9.1 %collective-permute-done.14 = bf16[2,288,512]{2,1,0:T(8,128)(2,1)S(1)} collective-permute-done((bf16[2,288,512]{2,1,0:T(8,128)(2,1)S(1)}, bf16[2,288,512]{2,1,0:T(8,128)(2,1)S(1)}, u32[]{:S(2)}, u32[]{:S(2)}) %collective-permute-start.14) | collective-permute-done | bytes 589856 | tf_op jit(solution)/shard_map/ppermute | solution.py:110
  113.6 3.2 %collective-permute-start.17 = (bf16[2,288,512]{2,1,0:T(8,128)(2,1)S(1)}, bf16[2,288,512]{2,1,0:T(8,128)(2,1)S(1)}, u32[]{:S(2)}, u32[]{:S(2)}) collective-permute-start(bf16[2,288,512]{2,1,0:T(8,128)(2,1)S(1)} %pad_maximum_fusion.21), channel_id=1, source_target_pairs={{0,16},{16,0},{1,17},{17,1},{2,18},{18,2},{3,19},{19,3},{4,20},{20... | collective-permute-start | bytes 1769480 | tf_op jit(solution)/shard_map/ppermute | solution.py:110
  116.7 1.0 collective-permute-start.19
  117.7 1.1 collective-permute-start.18
  119.3 7.3 %collective-permute-done.19 = bf16[2,288,512]{2,1,0:T(8,128)(2,1)S(1)} collective-permute-done((bf16[2,288,512]{2,1,0:T(8,128)(2,1)S(1)}, bf16[2,288,512]{2,1,0:T(8,128)(2,1)S(1)}, u32[]{:S(2)}, u32[]{:S(2)}) %collective-permute-start.19) | collective-permute-done | bytes 589856 | tf_op jit(solution)/shard_map/ppermute | solution.py:106
  126.6 0.9 collective-permute-done.18
  129.3 8.3 %collective-permute-done.20 = bf16[2,288,512]{2,1,0:T(8,128)(2,1)S(1)} collective-permute-done((bf16[2,288,512]{2,1,0:T(8,128)(2,1)S(1)}, bf16[2,288,512]{2,1,0:T(8,128)(2,1)S(1)}, u32[]{:S(2)}, u32[]{:S(2)}) %collective-permute-start.20) | collective-permute-done | bytes 589856 | tf_op jit(solution)/shard_map/ppermute | solution.py:110
  137.6 0.9 fusion.78
  149.0 2.1 %fusion.28 = bf16[1024,2304]{0,1:T(8,128)(2,1)} fusion(bf16[1024,2304]{0,1:T(8,128)(2,1)} %bitcast_dynamic-update-slice_fusion.13, bf16[288,512]{1,0:T(8,128)(2,1)} %get-tuple-element.69, bf16[288,512]{1,0:T(8,128)(2,1)} %get-tuple-element.70), kind=kLoop, calls=%fused_computation.94 | loop fusion | flops 1179648 | bytes 1179648
  151.1 1.9 bitcast_dynamic-update-slice_fusion.12
  153.9 1.0 bitcast_dynamic-update-slice_fusion.10
  154.9 1.0 bitcast_dynamic-update-slice_fusion.9
  159.1 1.2 copy-done
  160.3 1.7 convolution_convert_fusion
  167.8 1.3 convolution_convert_fusion.2
  169.3 0.9 fusion.16
  170.5 1.7 convolution_bitcast_fusion.1
  172.2 1.9 convolution_multiply_fusion.1
  176.5 4.1 %fusion.41 = f32[128,2304]{1,0:T(8,128)S(1)} fusion(bf16[1024,2304]{0,1:T(8,128)(2,1)} %fusion.29, bf16[16,8,8,128]{3,2,1,0:T(8,128)(2,1)S(1)} %bitcast.296), kind=kOutput, calls=%fused_computation.196 | convolution fusion | flops 603979776 | bytes 6160384 | tf_op jit(solution)/shard_map/dot_general | solution.py:283
  181.6 2.6 %fusion.1 = bf16[128,2304]{1,0:T(8,128)(2,1)S(1)} fusion(f32[128,2304]{1,0:T(8,128)S(1)} %convolution_add_fusion.1, bf16[128,512]{0,1:T(8,128)(2,1)S(1)} %bitcast.301, bf16[512,2304]{0,1:T(8,128)(2,1)} %bitcast_dynamic-update-slice_fusion.16), kind=kOutput, calls=%fused_computation.9 | convolution fusion | flops 302579712 | bytes 4259840 | tf_op jit(solution)/shard_map/dot_general | solution.py:285
  187.3 2.2 %fusion.13 = bf16[128,2304]{1,0:T(8,128)(2,1)S(1)} fusion(bf16[128,2304]{1,0:T(8,128)(2,1)S(1)} %collective-permute-done.22, bf16[128,2304]{1,0:T(8,128)(2,1)S(1)} %fusion.1, f32[128]{0:T(128)S(1)} %broadcast_multiply_fusion, f32[128]{0:T(128)} %get-tuple-element.107, f32[2304]{0:T(1024)S(1)} %mul.519, f32[128]{0:T(128)} %copy-done.43, ...), kind=kLoop, calls=%fused_computation.36 | loop fusion | flops 6488064 | bytes 4742912 | tf_op jit(solution)/shard_map/convert_element_type | solution.py:295
  191.2 15.4 %all_to_all.21 = bf16[8,16,1152]{2,1,0:T(8,128)(2,1)S(1)} all-to-all(bf16[8,16,1152]{2,1,0:T(8,128)(2,1)S(1)} %broadcast_select_fusion.4), channel_id=1, replica_groups=mesh['groups'=2,'seq'=8,'wg'=2] {'seq'}, dimensions={0} | all-to-all | bytes 589824 | tf_op jit(solution)/shard_map/all_to_all | solution.py:297
  (293 shorter events, 54.2 us)
Async XLA Ops:
  1.4 11.2 %copy-start.37 = (f32[2304]{0:T(1024)S(1)}, f32[2304]{0:T(1024)}, u32[]{:S(2)}) copy-start(f32[2304]{0:T(1024)} %param.12) | copy-start | bytes 27652
  1.4 11.3 %copy-start.38 = (f32[2304]{0:T(1024)S(1)}, f32[2304]{0:T(1024)}, u32[]{:S(2)}) copy-start(f32[2304]{0:T(1024)} %param.17) | copy-start | bytes 27652
  1.4 11.3 %copy-start.39 = (f32[2304]{0:T(1024)S(1)}, f32[2304]{0:T(1024)}, u32[]{:S(2)}) copy-start(f32[2304]{0:T(1024)} %param.18) | copy-start | bytes 27652
  1.5 12.2 %copy-start.49 = (s32[8]{0:T(128)S(1)}, s32[8]{0:T(128)}, u32[]{:S(2)}) copy-start(s32[8]{0:T(128)} %param.20) | copy-start | bytes 100
  1.5 13.6 %copy-start.50 = (s32[8]{0:T(128)S(1)}, s32[8]{0:T(128)}, u32[]{:S(2)}) copy-start(s32[8]{0:T(128)} %param.21) | copy-start | bytes 100
  1.5 16.8 %copy-start.26 = (bf16[64,2304]{1,0:T(8,128)(2,1)S(1)}, bf16[64,2304]{1,0:T(8,128)(2,1)}, u32[]{:S(2)}) copy-start(bf16[64,2304]{1,0:T(8,128)(2,1)} %param.19) | copy-start | bytes 884740
  2.4 31.1 %collective-permute-start = (bf16[2,288,512]{2,1,0:T(8,128)(2,1)}, bf16[2,288,512]{2,1,0:T(8,128)(2,1)}, u32[]{:S(2)}, u32[]{:S(2)}) collective-permute-start(bf16[2,288,512]{2,1,0:T(8,128)(2,1)} %pad_maximum_fusion.14), channel_id=1, source_target_pairs={{0,4},{4,8},{8,12},{12,14},{14,10},{10,6},{6,2},{2,0},{1,5},{5,9},... | collective-permute-start | bytes 1769480 | tf_op jit(solution)/shard_map/ppermute | solution.py:105
  6.3 28.2 %collective-permute-start.1 = (bf16[2,288,512]{2,1,0:T(8,128)(2,1)}, bf16[2,288,512]{2,1,0:T(8,128)(2,1)}, u32[]{:S(2)}, u32[]{:S(2)}) collective-permute-start(bf16[2,288,512]{2,1,0:T(8,128)(2,1)} %pad_maximum_fusion.15), channel_id=1, source_target_pairs={{0,2},{4,0},{8,4},{12,8},{14,12},{10,14},{6,10},{2,6},{1,3},{5,1},... | collective-permute-start | bytes 1769480 | tf_op jit(solution)/shard_map/ppermute | solution.py:106
  6.3 22.4 %all-to-all-start = ((bf16[8,16,1152]{2,1,0:T(8,128)(2,1)}), bf16[8,16,1152]{2,1,0:T(8,128)(2,1)}, u32[]{:S(2)}, u32[]{:S(2)}) async-start(bf16[8,16,1152]{2,1,0:T(8,128)(2,1)} %bitcast.1), calls=%async_computation | async-start | bytes 589824 | tf_op jit(solution)/shard_map/all_to_all | solution.py:153
  15.1 143.2 %copy-start.35 = (pred[128,128]{0,1:T(8,128)(4,1)}, pred[128,128]{0,1:T(8,128)(4,1)S(1)}, u32[]{:S(2)}) copy-start(pred[128,128]{0,1:T(8,128)(4,1)S(1)} %fusion.79) | copy-start | bytes 49156
  18.9 3.0 %copy-start.10 = (bf16[288,1024]{1,0:T(8,128)(2,1)S(1)}, bf16[288,1024]{1,0:T(8,128)(2,1)}, u32[]{:S(2)}) copy-start(bf16[288,1024]{1,0:T(8,128)(2,1)} %param.13) | copy-start | bytes 1769476
  18.9 3.0 %copy-start.11 = (bf16[1024,288]{0,1:T(8,128)(2,1)S(1)}, bf16[1024,288]{0,1:T(8,128)(2,1)}, u32[]{:S(2)}) copy-start(bf16[1024,288]{0,1:T(8,128)(2,1)} %param.16) | copy-start | bytes 1769476
  19.0 3.0 %copy-start.18 = (bf16[288,512]{1,0:T(8,128)(2,1)S(1)}, bf16[288,512]{1,0:T(8,128)(2,1)}, u32[]{:S(2)}) copy-start(bf16[288,512]{1,0:T(8,128)(2,1)} %param.14) | copy-start | bytes 884740
  22.0 119.7 %copy-start.14 = (f32[128,64]{1,0:T(8,128)}, f32[128,64]{1,0:T(8,128)S(1)}, u32[]{:S(2)}) copy-start(f32[128,64]{1,0:T(8,128)S(1)} %get-tuple-element.105) | copy-start | bytes 98308
  22.0 119.7 %copy-start.16 = (f32[128,64]{1,0:T(8,128)}, f32[128,64]{1,0:T(8,128)S(1)}, u32[]{:S(2)}) copy-start(f32[128,64]{1,0:T(8,128)S(1)} %get-tuple-element.106) | copy-start | bytes 98308
  35.5 18.9 %collective-permute-start.2 = (bf16[2,288,512]{2,1,0:T(8,128)(2,1)S(1)}, bf16[2,288,512]{2,1,0:T(8,128)(2,1)S(1)}, u32[]{:S(2)}, u32[]{:S(2)}) collective-permute-start(bf16[2,288,512]{2,1,0:T(8,128)(2,1)S(1)} %pad_maximum_fusion.16), channel_id=1, source_target_pairs={{0,16},{16,0},{1,17},{17,1},{2,18},{18,2},{3,19},{19,3},{4,20},{20... | collective-permute-start | bytes 1769480 | tf_op jit(solution)/shard_map/ppermute | solution.py:110
  38.3 15.3 %collective-permute-start.3 = (bf16[2,288,512]{2,1,0:T(8,128)(2,1)}, bf16[2,288,512]{2,1,0:T(8,128)(2,1)S(1)}, u32[]{:S(2)}, u32[]{:S(2)}) collective-permute-start(bf16[2,288,512]{2,1,0:T(8,128)(2,1)} %collective-permute-done), channel_id=1, source_target_pairs={{0,4},{4,8},{8,12},{12,14},{14,10},{10,6},{6,2},{2,0},{1,5},{5,9},... | collective-permute-start | bytes 1769480 | tf_op jit(solution)/shard_map/ppermute | solution.py:105
  38.4 15.3 %collective-permute-start.4 = (bf16[2,288,512]{2,1,0:T(8,128)(2,1)}, bf16[2,288,512]{2,1,0:T(8,128)(2,1)S(1)}, u32[]{:S(2)}, u32[]{:S(2)}) collective-permute-start(bf16[2,288,512]{2,1,0:T(8,128)(2,1)} %collective-permute-done.1), channel_id=1, source_target_pairs={{0,2},{4,0},{8,4},{12,8},{14,12},{10,14},{6,10},{2,6},{1,3},{5,1},... | collective-permute-start | bytes 1769480 | tf_op jit(solution)/shard_map/ppermute | solution.py:106
  53.8 14.3 %collective-permute-start.5 = (bf16[2,288,512]{2,1,0:T(8,128)(2,1)S(1)}, bf16[2,288,512]{2,1,0:T(8,128)(2,1)S(1)}, u32[]{:S(2)}, u32[]{:S(2)}) collective-permute-start(bf16[2,288,512]{2,1,0:T(8,128)(2,1)S(1)} %pad_maximum_fusion.17), channel_id=1, source_target_pairs={{0,16},{16,0},{1,17},{17,1},{2,18},{18,2},{3,19},{19,3},{4,20},{20... | collective-permute-start | bytes 1769480 | tf_op jit(solution)/shard_map/ppermute | solution.py:110
  55.9 14.0 %collective-permute-start.6 = (bf16[2,288,512]{2,1,0:T(8,128)(2,1)S(1)}, bf16[2,288,512]{2,1,0:T(8,128)(2,1)S(1)}, u32[]{:S(2)}, u32[]{:S(2)}) collective-permute-start(bf16[2,288,512]{2,1,0:T(8,128)(2,1)S(1)} %collective-permute-done.3), channel_id=1, source_target_pairs={{0,4},{4,8},{8,12},{12,14},{14,10},{10,6},{6,2},{2,0},{1,5},{5,9},... | collective-permute-start | bytes 1769480 | tf_op jit(solution)/shard_map/ppermute | solution.py:105
  57.2 13.3 %collective-permute-start.7 = (bf16[2,288,512]{2,1,0:T(8,128)(2,1)S(1)}, bf16[2,288,512]{2,1,0:T(8,128)(2,1)S(1)}, u32[]{:S(2)}, u32[]{:S(2)}) collective-permute-start(bf16[2,288,512]{2,1,0:T(8,128)(2,1)S(1)} %collective-permute-done.4), channel_id=1, source_target_pairs={{0,2},{4,0},{8,4},{12,8},{14,12},{10,14},{6,10},{2,6},{1,3},{5,1},... | collective-permute-start | bytes 1769480 | tf_op jit(solution)/shard_map/ppermute | solution.py:106
  70.6 12.5 %collective-permute-start.8 = (bf16[2,288,512]{2,1,0:T(8,128)(2,1)S(1)}, bf16[2,288,512]{2,1,0:T(8,128)(2,1)S(1)}, u32[]{:S(2)}, u32[]{:S(2)}) collective-permute-start(bf16[2,288,512]{2,1,0:T(8,128)(2,1)S(1)} %pad_maximum_fusion.18), channel_id=1, source_target_pairs={{0,16},{16,0},{1,17},{17,1},{2,18},{18,2},{3,19},{19,3},{4,20},{20... | collective-permute-start | bytes 1769480 | tf_op jit(solution)/shard_map/ppermute | solution.py:110
  72.3 12.2 %collective-permute-start.10 = (bf16[2,288,512]{2,1,0:T(8,128)(2,1)S(1)}, bf16[2,288,512]{2,1,0:T(8,128)(2,1)S(1)}, u32[]{:S(2)}, u32[]{:S(2)}) collective-permute-start(bf16[2,288,512]{2,1,0:T(8,128)(2,1)S(1)} %collective-permute-done.7), channel_id=1, source_target_pairs={{0,2},{4,0},{8,4},{12,8},{14,12},{10,14},{6,10},{2,6},{1,3},{5,1},... | collective-permute-start | bytes 1769480 | tf_op jit(solution)/shard_map/ppermute | solution.py:106
  73.4 13.0 %collective-permute-start.9 = (bf16[2,288,512]{2,1,0:T(8,128)(2,1)S(1)}, bf16[2,288,512]{2,1,0:T(8,128)(2,1)S(1)}, u32[]{:S(2)}, u32[]{:S(2)}) collective-permute-start(bf16[2,288,512]{2,1,0:T(8,128)(2,1)S(1)} %collective-permute-done.6), channel_id=1, source_target_pairs={{0,4},{4,8},{8,12},{12,14},{14,10},{10,6},{6,2},{2,0},{1,5},{5,9},... | collective-permute-start | bytes 1769480 | tf_op jit(solution)/shard_map/ppermute | solution.py:105
  86.6 11.0 %collective-permute-start.11 = (bf16[2,288,512]{2,1,0:T(8,128)(2,1)S(1)}, bf16[2,288,512]{2,1,0:T(8,128)(2,1)S(1)}, u32[]{:S(2)}, u32[]{:S(2)}) collective-permute-start(bf16[2,288,512]{2,1,0:T(8,128)(2,1)S(1)} %pad_maximum_fusion.19), channel_id=1, source_target_pairs={{0,16},{16,0},{1,17},{17,1},{2,18},{18,2},{3,19},{19,3},{4,20},{20... | collective-permute-start | bytes 1769480 | tf_op jit(solution)/shard_map/ppermute | solution.py:110
  86.7 13.3 %collective-permute-start.12 = (bf16[2,288,512]{2,1,0:T(8,128)(2,1)S(1)}, bf16[2,288,512]{2,1,0:T(8,128)(2,1)S(1)}, u32[]{:S(2)}, u32[]{:S(2)}) collective-permute-start(bf16[2,288,512]{2,1,0:T(8,128)(2,1)S(1)} %collective-permute-done.9), channel_id=1, source_target_pairs={{0,4},{4,8},{8,12},{12,14},{14,10},{10,6},{6,2},{2,0},{1,5},{5,9},... | collective-permute-start | bytes 1769480 | tf_op jit(solution)/shard_map/ppermute | solution.py:105
  87.6 12.4 %collective-permute-start.13 = (bf16[2,288,512]{2,1,0:T(8,128)(2,1)S(1)}, bf16[2,288,512]{2,1,0:T(8,128)(2,1)S(1)}, u32[]{:S(2)}, u32[]{:S(2)}) collective-permute-start(bf16[2,288,512]{2,1,0:T(8,128)(2,1)S(1)} %collective-permute-done.10), channel_id=1, source_target_pairs={{0,2},{4,0},{8,4},{12,8},{14,12},{10,14},{6,10},{2,6},{1,3},{5,1},... | collective-permute-start | bytes 1769480 | tf_op jit(solution)/shard_map/ppermute | solution.py:106
  97.8 48.6 %copy-start.2 = (bf16[288,1536]{1,0:T(8,128)(2,1)}, bf16[288,1536]{1,0:T(8,128)(2,1)S(1)}, u32[]{:S(2)}) copy-start(bf16[288,1536]{1,0:T(8,128)(2,1)S(1)} %pad_maximum_fusion.9) | copy-start | bytes 2654212
  100.1 12.3 %collective-permute-start.14 = (bf16[2,288,512]{2,1,0:T(8,128)(2,1)S(1)}, bf16[2,288,512]{2,1,0:T(8,128)(2,1)S(1)}, u32[]{:S(2)}, u32[]{:S(2)}) collective-permute-start(bf16[2,288,512]{2,1,0:T(8,128)(2,1)S(1)} %pad_maximum_fusion.20), channel_id=1, source_target_pairs={{0,16},{16,0},{1,17},{17,1},{2,18},{18,2},{3,19},{19,3},{4,20},{20... | collective-permute-start | bytes 1769480 | tf_op jit(solution)/shard_map/ppermute | solution.py:110
  100.8 11.9 %collective-permute-start.15 = (bf16[2,288,512]{2,1,0:T(8,128)(2,1)S(1)}, bf16[2,288,512]{2,1,0:T(8,128)(2,1)S(1)}, u32[]{:S(2)}, u32[]{:S(2)}) collective-permute-start(bf16[2,288,512]{2,1,0:T(8,128)(2,1)S(1)} %collective-permute-done.12), channel_id=1, source_target_pairs={{0,4},{4,8},{8,12},{12,14},{14,10},{10,6},{6,2},{2,0},{1,5},{5,9},... | collective-permute-start | bytes 1769480 | tf_op jit(solution)/shard_map/ppermute | solution.py:105
  101.1 12.4 %collective-permute-start.16 = (bf16[2,288,512]{2,1,0:T(8,128)(2,1)S(1)}, bf16[2,288,512]{2,1,0:T(8,128)(2,1)S(1)}, u32[]{:S(2)}, u32[]{:S(2)}) collective-permute-start(bf16[2,288,512]{2,1,0:T(8,128)(2,1)S(1)} %collective-permute-done.13), channel_id=1, source_target_pairs={{0,2},{4,0},{8,4},{12,8},{14,12},{10,14},{6,10},{2,6},{1,3},{5,1},... | collective-permute-start | bytes 1769480 | tf_op jit(solution)/shard_map/ppermute | solution.py:106
  112.6 32.8 %copy-start.4 = (bf16[288,1536]{1,0:T(8,128)(2,1)}, bf16[288,1536]{1,0:T(8,128)(2,1)S(1)}, u32[]{:S(2)}) copy-start(bf16[288,1536]{1,0:T(8,128)(2,1)S(1)} %pad_maximum_fusion.11) | copy-start | bytes 2654212
  113.6 15.4 %collective-permute-start.17 = (bf16[2,288,512]{2,1,0:T(8,128)(2,1)S(1)}, bf16[2,288,512]{2,1,0:T(8,128)(2,1)S(1)}, u32[]{:S(2)}, u32[]{:S(2)}) collective-permute-start(bf16[2,288,512]{2,1,0:T(8,128)(2,1)S(1)} %pad_maximum_fusion.21), channel_id=1, source_target_pairs={{0,16},{16,0},{1,17},{17,1},{2,18},{18,2},{3,19},{19,3},{4,20},{20... | collective-permute-start | bytes 1769480 | tf_op jit(solution)/shard_map/ppermute | solution.py:110
  116.7 9.9 %collective-permute-start.19 = (bf16[2,288,512]{2,1,0:T(8,128)(2,1)S(1)}, bf16[2,288,512]{2,1,0:T(8,128)(2,1)S(1)}, u32[]{:S(2)}, u32[]{:S(2)}) collective-permute-start(bf16[2,288,512]{2,1,0:T(8,128)(2,1)S(1)} %collective-permute-done.16), channel_id=1, source_target_pairs={{0,2},{4,0},{8,4},{12,8},{14,12},{10,14},{6,10},{2,6},{1,3},{5,1},... | collective-permute-start | bytes 1769480 | tf_op jit(solution)/shard_map/ppermute | solution.py:106
  117.7 9.9 %collective-permute-start.18 = (bf16[2,288,512]{2,1,0:T(8,128)(2,1)S(1)}, bf16[2,288,512]{2,1,0:T(8,128)(2,1)S(1)}, u32[]{:S(2)}, u32[]{:S(2)}) collective-permute-start(bf16[2,288,512]{2,1,0:T(8,128)(2,1)S(1)} %collective-permute-done.15), channel_id=1, source_target_pairs={{0,4},{4,8},{8,12},{12,14},{14,10},{10,6},{6,2},{2,0},{1,5},{5,9},... | collective-permute-start | bytes 1769480 | tf_op jit(solution)/shard_map/ppermute | solution.py:105
  127.6 9.9 %collective-permute-start.20 = (bf16[2,288,512]{2,1,0:T(8,128)(2,1)S(1)}, bf16[2,288,512]{2,1,0:T(8,128)(2,1)S(1)}, u32[]{:S(2)}, u32[]{:S(2)}) collective-permute-start(bf16[2,288,512]{2,1,0:T(8,128)(2,1)S(1)} %pad_maximum_fusion.22), channel_id=1, source_target_pairs={{0,16},{16,0},{1,17},{17,1},{2,18},{18,2},{3,19},{19,3},{4,20},{20... | collective-permute-start | bytes 1769480 | tf_op jit(solution)/shard_map/ppermute | solution.py:110
  129.1 15.3 %copy-start.6 = (bf16[288,1536]{1,0:T(8,128)(2,1)}, bf16[288,1536]{1,0:T(8,128)(2,1)S(1)}, u32[]{:S(2)}) copy-start(bf16[288,1536]{1,0:T(8,128)(2,1)S(1)} %pad_maximum_fusion.13) | copy-start | bytes 2654212
  129.3 9.6 %copy-start.1 = (bf16[1024,2304]{0,1:T(8,128)(2,1)}, bf16[1024,2304]{0,1:T(8,128)(2,1)S(1)}, u32[]{:S(2)}) copy-start(bf16[1024,2304]{0,1:T(8,128)(2,1)S(1)} %bitcast_dynamic-update-slice_fusion) | copy-start | bytes 14155780
  142.4 15.5 %copy-start.31 = (bf16[4,128,64]{2,1,0:T(8,128)(2,1)}, bf16[4,128,64]{2,1,0:T(8,128)(2,1)S(1)}, u32[]{:S(2)}) copy-start(bf16[4,128,64]{2,1,0:T(8,128)(2,1)S(1)} %get-tuple-element.103) | copy-start | bytes 196612
  148.3 5.7 %copy-start.19 = (bf16[128,512]{1,0:T(8,128)(2,1)}, bf16[128,512]{1,0:T(8,128)(2,1)S(1)}, u32[]{:S(2)}) copy-start(bf16[128,512]{1,0:T(8,128)(2,1)S(1)} %fusion.15) | copy-start | bytes 393220
  149.0 4.0 %copy-start.5 = (bf16[288,1536]{1,0:T(8,128)(2,1)S(1)}, bf16[288,1536]{1,0:T(8,128)(2,1)}, u32[]{:S(2)}) copy-start(bf16[288,1536]{1,0:T(8,128)(2,1)} %copy-done.4) | copy-start | bytes 2654212
  149.0 4.9 %copy-start.3 = (bf16[288,1536]{1,0:T(8,128)(2,1)S(1)}, bf16[288,1536]{1,0:T(8,128)(2,1)}, u32[]{:S(2)}) copy-start(bf16[288,1536]{1,0:T(8,128)(2,1)} %copy-done.2) | copy-start | bytes 2654212
  154.9 2.8 %copy-start.13 = (f32[8,128,64]{2,1,0:T(8,128)S(1)}, f32[8,128,64]{2,1,0:T(8,128)}, u32[]{:S(2)}) copy-start(f32[8,128,64]{2,1,0:T(8,128)} %copy.56) | copy-start | bytes 786436
  162.0 2.8 %copy-start.30 = (f32[2304]{0:T(1024)S(1)}, f32[2304]{0:T(1024)}, u32[]{:S(2)}) copy-start(f32[2304]{0:T(1024)} %mul.542) | copy-start | bytes 27652
  162.0 2.5 %collective-permute-start.21 = (bf16[128,2304]{1,0:T(8,128)(2,1)S(1)}, bf16[128,2304]{1,0:T(8,128)(2,1)S(1)}, u32[]{:S(2)}, u32[]{:S(2)}) collective-permute-start(bf16[128,2304]{1,0:T(8,128)(2,1)S(1)} %convolution_convert_fusion), channel_id=1, source_target_pairs={{0,1},{1,0},{2,3},{3,2},{4,5},{5,4},{6,7},{7,6},{8,9},{9,8},{10,11... | collective-permute-start | bytes 1769480 | tf_op jit(solution)/shard_map/ppermute | solution.py:58
  176.5 4.2 %copy-start.9 = (bf16[512,2304]{0,1:T(8,128)(2,1)S(1)}, bf16[512,2304]{0,1:T(8,128)(2,1)}, u32[]{:S(2)}) copy-start(bf16[512,2304]{0,1:T(8,128)(2,1)} %copy-done.8) | copy-start | bytes 7077892
  176.5 4.2 %copy-start.25 = (bf16[128,4,128]{0,2,1:T(8,128)(2,1)S(1)}, bf16[128,4,128]{0,2,1:T(8,128)(2,1)}, u32[]{:S(2)}) copy-start(bf16[128,4,128]{0,2,1:T(8,128)(2,1)} %copy.74) | copy-start | bytes 393220
  184.2 2.7 %collective-permute-start.22 = (bf16[128,2304]{1,0:T(8,128)(2,1)S(1)}, bf16[128,2304]{1,0:T(8,128)(2,1)S(1)}, u32[]{:S(2)}, u32[]{:S(2)}) collective-permute-start(bf16[128,2304]{1,0:T(8,128)(2,1)S(1)} %fusion.1), channel_id=1, source_target_pairs={{0,1},{1,0},{2,3},{3,2},{4,5},{5,4},{6,7},{7,6},{8,9},{9,8},{10,11... | collective-permute-start | bytes 1769480 | tf_op jit(solution)/shard_map/ppermute | solution.py:58
  (32 other events, 52.0 us)

commit v11 on v10

--- a/solution.py
+++ b/solution.py
@@ -125,6 +125,16 @@
             )
     back_pieces = [back_pieces[(n - k) % n] for k in range(n)]
     return front_pieces, back_pieces, block_of, slot_of
+
+
+def shift_exchange(rows, seq_rank, n):
+    blocks = rows.reshape((n, rows.shape[0] // n) + rows.shape[1:])
+    received = [blocks[seq_rank]]
+    for shift in range(1, n):
+        pairs = [(i, (i + shift) % n) for i in range(n)]
+        received.append(lax.ppermute(blocks[(seq_rank + shift) % n], "seq", pairs))
+    sources = (seq_rank - jnp.arange(n, dtype=jnp.int32)) % n
+    return jnp.take(jnp.stack(received), sources, axis=0).reshape(rows.shape)
 
 
 def permute_blocks(values, block_order, n):
@@ -294,7 +304,9 @@
     own_blocks = core_rank * half_blocks + jnp.arange(half_blocks, dtype=jnp.int32)
     grad_blocks = grad_full.astype(jnp.bfloat16).reshape(tok_rows, n_seq, block_width)
     grad_rows = jnp.take(grad_blocks, slot_of[own_blocks], axis=1).reshape(tok_rows, half_width)
-    return lax.all_to_all(grad_rows, "seq", split_axis=0, concat_axis=0, tiled=True)
+    if n_seq > PIECEWISE_RING:
+        return lax.all_to_all(grad_rows, "seq", split_axis=0, concat_axis=0, tiled=True)
+    return shift_exchange(grad_rows, seq_rank, n_seq)
 
 
 def solution(mesh):

time: 208 us -> 221 us (1.062)
  blocking collectives: 17.8 us -> 2.56 us
  starting transfers between devices: 30.4 us -> 41.9 us
  other arithmetic: 23.8 us -> 30.5 us
  local copies, waits for them, and re-layouts: 32.7 us -> 38.8 us
  matrix products: 22.7 us -> 26.6 us
    all_to_all x1 -> x0, blocking collectives: 15.4 us -> none  [shards(): lax.all_to_all(grad_rows, 'seq', split_axis=0, concat_axis=0, tiled=True)]
    ppermute x0 -> x7, starting transfers between devices: none -> 11.9 us  [shift_exchange(): received.append(lax.ppermute(blocks[(seq_rank + shift) % n], 'seq', pairs))]
    all_to_all x1, waiting for transfers between devices: 5.58 us -> 2.78 us  [shards(): lax.all_to_all(generator_rows, 'seq', split_axis=0, concat_axis=0, tiled=...]
    ppermute x0 -> x7, waiting for transfers between devices: none -> 2.29 us  [shift_exchange(): received.append(lax.ppermute(blocks[(seq_rank + shift) % n], 'seq', pairs))]
    unnamed x141 -> x152, local copies, waits for them, and re-layouts: 14.6 us -> 15 us
  transfers between devices with their start and end apart: 24 -> 31, of which waited for: 16 -> 19; matrix products, arithmetic and copies ran while one was open for 13% -> 14% of each run, Pallas kernels for 0% -> 0%
where the time goes in v11:
time: 221 us; the launch traced here: 220 us
  waiting for transfers between devices  78.4 us (35%)
  starting transfers between devices  41.9 us (19%)
  local copies, waits for them, and re-layouts  38.8 us (18%)
  other arithmetic  30.5 us (14%)
  matrix products  26.6 us (12%)
  blocking collectives  2.56 us (1%)
    ppermute x7, waiting for transfers between devices, ring_gather(): lax.ppermute(jnp.stack([front_ring[step][0], back_ring[step][0]]), 'group...  44.4 us
    ppermute x7, waiting for transfers between devices, ring_gather(): front_ring.append(lax.ppermute(front_ring[-1], 'seq', forward_pairs))  18.6 us
    unnamed x152, local copies, waits for them, and re-layouts  15 us
    ppermute x7, starting transfers between devices, shift_exchange(): received.append(lax.ppermute(blocks[(seq_rank + shift) % n], 'seq', pairs))  11.9 us
    ppermute x7, waiting for transfers between devices, ring_gather(): back_ring.append(lax.ppermute(back_ring[-1], 'seq', backward_pairs))  10.4 us
    ppermute x7, starting transfers between devices, ring_gather(): back_ring.append(lax.ppermute(back_ring[-1], 'seq', backward_pairs))  7.84 us
    ppermute x7, starting transfers between devices, ring_gather(): lax.ppermute(jnp.stack([front_ring[step][0], back_ring[step][0]]), 'group...  7.69 us
    ppermute x7, starting transfers between devices, ring_gather(): front_ring.append(lax.ppermute(front_ring[-1], 'seq', forward_pairs))  7.6 us
  transfers between devices with their start and end apart: 31, of which 19 were waited for; matrix products, arithmetic and copies ran while one was open for 14% of the time, Pallas kernels for 0%

profile of v11, /device:TPU:0, one launch (start us, length us, event | category | flops | bytes accessed | tf_op | source)
XLA Modules:
  0.0 220.3 jit_solution(7994039114652513733)
XLA Ops:
  0.0 1.4 fusion.39
  2.4 3.0 %collective-permute-start = (bf16[2,288,512]{2,1,0:T(8,128)(2,1)}, bf16[2,288,512]{2,1,0:T(8,128)(2,1)}, u32[]{:S(2)}, u32[]{:S(2)}) collective-permute-start(bf16[2,288,512]{2,1,0:T(8,128)(2,1)} %pad_maximum_fusion.14), channel_id=1, source_target_pairs={{0,4},{4,8},{8,12},{12,14},{14,10},{10,6},{6,2},{2,0},{1,5},{5,9},... | collective-permute-start | bytes 1769480 | tf_op jit(solution)/shard_map/ppermute | solution.py:105
  6.3 6.3 %all-to-all-start = ((bf16[8,16,1152]{2,1,0:T(8,128)(2,1)}), bf16[8,16,1152]{2,1,0:T(8,128)(2,1)}, u32[]{:S(2)}, u32[]{:S(2)}) async-start(bf16[8,16,1152]{2,1,0:T(8,128)(2,1)} %bitcast.1), calls=%async_computation | async-start | bytes 589824 | tf_op jit(solution)/shard_map/all_to_all | solution.py:163
  17.1 1.2 compare_convert_fusion
  22.6 1.2 gather_fusion
  24.8 1.2 pad_maximum_fusion
  26.0 2.8 %all-to-all-done = bf16[8,16,1152]{2,1,0:T(8,128)(2,1)} async-done(((bf16[8,16,1152]{2,1,0:T(8,128)(2,1)}), bf16[8,16,1152]{2,1,0:T(8,128)(2,1)}, u32[]{:S(2)}, u32[]{:S(2)}) %all-to-all-start) | async-done | bytes 294944 | tf_op jit(solution)/shard_map/all_to_all | solution.py:163
  28.8 2.6 %all_gather.3 = bf16[128,2304]{1,0:T(8,128)(2,1)S(1)} all-gather(bf16[128,1152]{1,0:T(8,128)(2,1)} %bitcast.2), channel_id=1, replica_groups=mesh['groups'=2,'seq'=8,'wg'=2] {'wg'}, dimensions={1}, use_global_device_ids=true | all-gather | bytes 884736 | tf_op jit(solution)/shard_map/all_gather | solution.py:164
  35.8 1.6 collective-permute-start.2
  38.7 2.0 collective-permute-start.4
  41.8 12.1 %collective-permute-done.3 = bf16[2,288,512]{2,1,0:T(8,128)(2,1)S(1)} collective-permute-done((bf16[2,288,512]{2,1,0:T(8,128)(2,1)}, bf16[2,288,512]{2,1,0:T(8,128)(2,1)S(1)}, u32[]{:S(2)}, u32[]{:S(2)}) %collective-permute-start.3) | collective-permute-done | bytes 589856 | tf_op jit(solution)/shard_map/ppermute | solution.py:105
  54.7 1.4 select_bitcast_fusion.23
  56.2 1.3 collective-permute-start.6
  58.8 9.6 %collective-permute-done.5 = bf16[2,288,512]{2,1,0:T(8,128)(2,1)S(1)} collective-permute-done((bf16[2,288,512]{2,1,0:T(8,128)(2,1)S(1)}, bf16[2,288,512]{2,1,0:T(8,128)(2,1)S(1)}, u32[]{:S(2)}, u32[]{:S(2)}) %collective-permute-start.5) | collective-permute-done | bytes 589856 | tf_op jit(solution)/shard_map/ppermute | solution.py:110
  68.7 1.6 collective-permute-done.6
  71.0 1.6 collective-permute-start.8
  72.6 1.2 collective-permute-start.10
  75.2 8.3 %collective-permute-done.8 = bf16[2,288,512]{2,1,0:T(8,128)(2,1)S(1)} collective-permute-done((bf16[2,288,512]{2,1,0:T(8,128)(2,1)S(1)}, bf16[2,288,512]{2,1,0:T(8,128)(2,1)S(1)}, u32[]{:S(2)}, u32[]{:S(2)}) %collective-permute-start.8) | collective-permute-done | bytes 589856 | tf_op jit(solution)/shard_map/ppermute | solution.py:110
  84.8 2.0 collective-permute-done.9
  89.6 8.4 %collective-permute-done.11 = bf16[2,288,512]{2,1,0:T(8,128)(2,1)S(1)} collective-permute-done((bf16[2,288,512]{2,1,0:T(8,128)(2,1)S(1)}, bf16[2,288,512]{2,1,0:T(8,128)(2,1)S(1)}, u32[]{:S(2)}, u32[]{:S(2)}) %collective-permute-start.11) | collective-permute-done | bytes 589856 | tf_op jit(solution)/shard_map/ppermute | solution.py:110
  98.2 2.0 collective-permute-done.12
  101.4 1.8 collective-permute-start.16
  103.7 9.0 %collective-permute-done.14 = bf16[2,288,512]{2,1,0:T(8,128)(2,1)S(1)} collective-permute-done((bf16[2,288,512]{2,1,0:T(8,128)(2,1)S(1)}, bf16[2,288,512]{2,1,0:T(8,128)(2,1)S(1)}, u32[]{:S(2)}, u32[]{:S(2)}) %collective-permute-start.14) | collective-permute-done | bytes 589856 | tf_op jit(solution)/shard_map/ppermute | solution.py:110
  113.0 1.3 collective-permute-done.16
  114.4 2.6 %collective-permute-start.17 = (bf16[2,288,512]{2,1,0:T(8,128)(2,1)S(1)}, bf16[2,288,512]{2,1,0:T(8,128)(2,1)S(1)}, u32[]{:S(2)}, u32[]{:S(2)}) collective-permute-start(bf16[2,288,512]{2,1,0:T(8,128)(2,1)S(1)} %pad_maximum_fusion.21), channel_id=1, source_target_pairs={{0,16},{16,0},{1,17},{17,1},{2,18},{18,2},{3,19},{19,3},{4,20},{20... | collective-permute-start | bytes 1769480 | tf_op jit(solution)/shard_map/ppermute | solution.py:110
  119.6 7.3 %collective-permute-done.19 = bf16[2,288,512]{2,1,0:T(8,128)(2,1)S(1)} collective-permute-done((bf16[2,288,512]{2,1,0:T(8,128)(2,1)S(1)}, bf16[2,288,512]{2,1,0:T(8,128)(2,1)S(1)}, u32[]{:S(2)}, u32[]{:S(2)}) %collective-permute-start.19) | collective-permute-done | bytes 589856 | tf_op jit(solution)/shard_map/ppermute | solution.py:106
  129.7 8.2 %collective-permute-done.20 = bf16[2,288,512]{2,1,0:T(8,128)(2,1)S(1)} collective-permute-done((bf16[2,288,512]{2,1,0:T(8,128)(2,1)S(1)}, bf16[2,288,512]{2,1,0:T(8,128)(2,1)S(1)}, u32[]{:S(2)}, u32[]{:S(2)}) %collective-permute-start.20) | collective-permute-done | bytes 589856 | tf_op jit(solution)/shard_map/ppermute | solution.py:110
  149.9 2.1 fusion.28
  152.0 1.9 bitcast_dynamic-update-slice_fusion.12
  161.2 1.7 convolution_convert_fusion
  168.4 2.0 convolution_convert_fusion.2
  171.6 2.0 fusion.16
  174.5 2.8 %convolution_bitcast_fusion.1 = f32[4,128,128]{2,1,0:T(8,128)} fusion(bf16[4,2,128,128]{3,2,1,0:T(8,128)(2,1)} %copy-done.26, f32[4,2,128,128]{2,3,1,0:T(8,128)} %fusion.56, f32[4,2,128,128]{2,3,1,0:T(8,128)} %copy-done.56, f32[4,2,128]{2,1,0:T(2,128)S(1)} %copy-done.58, pred[128,128]{0,1:T(8,128)(4,1)S(1)} %copy-done.34), kind=kOutput, calls=%fused_computation.50 | convolution fusion | flops 35259520 | bytes 1593344 | tf_op jit(solution)/shard_map/kgij,kgid->kjd/dot_general | solution.py:283
  177.4 2.2 %convolution_multiply_fusion.1 = f32[4,2,128,128]{3,2,1,0:T(8,128)S(1)} fusion(f32[4,2,128,128]{2,3,1,0:T(8,128)} %fusion.56, f32[4,2,128,128]{2,3,1,0:T(8,128)} %copy-done.56, bf16[4,128,64]{2,1,0:T(8,128)(2,1)} %get-tuple-element.104, bf16[4,128,64]{2,1,0:T(8,128)(2,1)} %copy-done.29, f32[4,2,128]{2,1,0:T(2,128)} %copy-done.57, pred[128,128]{0,1:T(8,128)(4,1)} %fusion.79), kind=kOutput, calls=%fused_computation.26 | convolution fusion | flops 35652736 | bytes 1724416 | tf_op jit(solution)/shard_map/kgij,kjd->kgid/dot_general | solution.py:279
  181.6 1.7 copy.74
  185.1 4.1 %fusion.41 = f32[128,2304]{1,0:T(8,128)S(1)} fusion(bf16[1024,2304]{0,1:T(8,128)(2,1)} %fusion.29, bf16[16,8,8,128]{3,2,1,0:T(8,128)(2,1)S(1)} %bitcast.326), kind=kOutput, calls=%fused_computation.198 | convolution fusion | flops 603979776 | bytes 6160384 | tf_op jit(solution)/shard_map/dot_general | solution.py:293
  190.3 2.6 %fusion.1 = bf16[128,2304]{1,0:T(8,128)(2,1)S(1)} fusion(f32[128,2304]{1,0:T(8,128)S(1)} %convolution_add_fusion.1, bf16[128,512]{0,1:T(8,128)(2,1)S(1)} %bitcast.331, bf16[512,2304]{0,1:T(8,128)(2,1)} %bitcast_dynamic-update-slice_fusion.16), kind=kOutput, calls=%fused_computation.10 | convolution fusion | flops 302579712 | bytes 4259840 | tf_op jit(solution)/shard_map/dot_general | solution.py:295
  194.1 1.3 broadcast_in_dim.128
  197.2 1.5 fusion.14
  198.7 2.9 %fusion.13 = bf16[128,2304]{1,0:T(8,128)(2,1)} fusion(bf16[128,2304]{1,0:T(8,128)(2,1)} %collective-permute-done.22, bf16[128,2304]{1,0:T(8,128)(2,1)S(1)} %fusion.1, f32[128]{0:T(128)S(1)} %broadcast_multiply_fusion, f32[128]{0:T(128)} %get-tuple-element.115, f32[2304]{0:T(1024)S(1)} %mul.519, f32[128]{0:T(128)} %copy-done.44, ...), kind=kLoop, calls=%fused_computation.37 | loop fusion | flops 6488064 | bytes 4742912 | tf_op jit(solution)/shard_map/convert_element_type | solution.py:305
  201.6 1.4 copy.76
  204.4 2.0 collective-permute-start.23
  206.5 1.3 collective-permute-start.24
  207.9 1.7 collective-permute-start.25
  209.6 2.8 %collective-permute-start.26 = (bf16[16,1152]{1,0:T(8,128)(2,1)S(1)}, bf16[16,1152]{1,0:T(8,128)(2,1)S(1)}, u32[]{:S(2)}, u32[]{:S(2)}) collective-permute-start(bf16[16,1152]{1,0:T(8,128)(2,1)S(1)} %get-tuple-element.108), channel_id=1, source_target_pairs={{0,8},{2,10},{4,12},{6,14},{8,0},{10,2},{12,4},{14,6},{1,9},{3,11}... | collective-permute-start | bytes 110600 | tf_op jit(solution)/shard_map/ppermute | solution.py:135
  213.3 1.5 collective-permute-start.28
  214.8 1.7 collective-permute-start.29
  217.5 1.3 collective-permute-done.29
  (325 shorter events, 73.3 us)
Async XLA Ops:
  1.4 11.8 %copy-start.35 = (f32[2304]{0:T(1024)S(1)}, f32[2304]{0:T(1024)}, u32[]{:S(2)}) copy-start(f32[2304]{0:T(1024)} %param.12) | copy-start | bytes 27652
  1.4 11.9 %copy-start.36 = (f32[2304]{0:T(1024)S(1)}, f32[2304]{0:T(1024)}, u32[]{:S(2)}) copy-start(f32[2304]{0:T(1024)} %param.17) | copy-start | bytes 27652
  1.4 12.0 %copy-start.37 = (f32[2304]{0:T(1024)S(1)}, f32[2304]{0:T(1024)}, u32[]{:S(2)}) copy-start(f32[2304]{0:T(1024)} %param.18) | copy-start | bytes 27652
  1.5 12.9 %copy-start.53 = (s32[8]{0:T(128)S(1)}, s32[8]{0:T(128)}, u32[]{:S(2)}) copy-start(s32[8]{0:T(128)} %param.20) | copy-start | bytes 100
  1.5 14.9 %copy-start.54 = (s32[8]{0:T(128)S(1)}, s32[8]{0:T(128)}, u32[]{:S(2)}) copy-start(s32[8]{0:T(128)} %param.21) | copy-start | bytes 100
  1.5 17.8 %copy-start.24 = (bf16[64,2304]{1,0:T(8,128)(2,1)S(1)}, bf16[64,2304]{1,0:T(8,128)(2,1)}, u32[]{:S(2)}) copy-start(bf16[64,2304]{1,0:T(8,128)(2,1)} %param.19) | copy-start | bytes 884740
  2.4 31.4 %collective-permute-start = (bf16[2,288,512]{2,1,0:T(8,128)(2,1)}, bf16[2,288,512]{2,1,0:T(8,128)(2,1)}, u32[]{:S(2)}, u32[]{:S(2)}) collective-permute-start(bf16[2,288,512]{2,1,0:T(8,128)(2,1)} %pad_maximum_fusion.14), channel_id=1, source_target_pairs={{0,4},{4,8},{8,12},{12,14},{14,10},{10,6},{6,2},{2,0},{1,5},{5,9},... | collective-permute-start | bytes 1769480 | tf_op jit(solution)/shard_map/ppermute | solution.py:105
  6.3 28.4 %collective-permute-start.1 = (bf16[2,288,512]{2,1,0:T(8,128)(2,1)}, bf16[2,288,512]{2,1,0:T(8,128)(2,1)}, u32[]{:S(2)}, u32[]{:S(2)}) collective-permute-start(bf16[2,288,512]{2,1,0:T(8,128)(2,1)} %pad_maximum_fusion.15), channel_id=1, source_target_pairs={{0,2},{4,0},{8,4},{12,8},{14,12},{10,14},{6,10},{2,6},{1,3},{5,1},... | collective-permute-start | bytes 1769480 | tf_op jit(solution)/shard_map/ppermute | solution.py:106
  6.3 22.4 %all-to-all-start = ((bf16[8,16,1152]{2,1,0:T(8,128)(2,1)}), bf16[8,16,1152]{2,1,0:T(8,128)(2,1)}, u32[]{:S(2)}, u32[]{:S(2)}) async-start(bf16[8,16,1152]{2,1,0:T(8,128)(2,1)} %bitcast.1), calls=%async_computation | async-start | bytes 589824 | tf_op jit(solution)/shard_map/all_to_all | solution.py:163
  13.2 5.4 %copy-start.40 = (pred[8]{0:T(512)(128)(4,1)}, pred[8]{0:T(512)(128)(4,1)S(1)}, u32[]{:S(2)}) copy-start(pred[8]{0:T(512)(128)(4,1)S(1)} %get-tuple-element.127) | copy-start | bytes 28
  13.3 7.6 %copy-start.42 = (s32[1024]{0:T(1024)}, s32[1024]{0:T(1024)S(1)}, u32[]{:S(2)}) copy-start(s32[1024]{0:T(1024)S(1)} %pad_clamp_fusion.2) | copy-start | bytes 12292
  19.9 4.9 %copy-start.9 = (bf16[288,1024]{1,0:T(8,128)(2,1)S(1)}, bf16[288,1024]{1,0:T(8,128)(2,1)}, u32[]{:S(2)}) copy-start(bf16[288,1024]{1,0:T(8,128)(2,1)} %param.13) | copy-start | bytes 1769476
  19.9 4.9 %copy-start.10 = (bf16[1024,288]{0,1:T(8,128)(2,1)S(1)}, bf16[1024,288]{0,1:T(8,128)(2,1)}, u32[]{:S(2)}) copy-start(bf16[1024,288]{0,1:T(8,128)(2,1)} %param.16) | copy-start | bytes 1769476
  35.8 18.9 %collective-permute-start.2 = (bf16[2,288,512]{2,1,0:T(8,128)(2,1)S(1)}, bf16[2,288,512]{2,1,0:T(8,128)(2,1)S(1)}, u32[]{:S(2)}, u32[]{:S(2)}) collective-permute-start(bf16[2,288,512]{2,1,0:T(8,128)(2,1)S(1)} %pad_maximum_fusion.16), channel_id=1, source_target_pairs={{0,16},{16,0},{1,17},{17,1},{2,18},{18,2},{3,19},{19,3},{4,20},{20... | collective-permute-start | bytes 1769480 | tf_op jit(solution)/shard_map/ppermute | solution.py:110
  38.6 15.4 %collective-permute-start.3 = (bf16[2,288,512]{2,1,0:T(8,128)(2,1)}, bf16[2,288,512]{2,1,0:T(8,128)(2,1)S(1)}, u32[]{:S(2)}, u32[]{:S(2)}) collective-permute-start(bf16[2,288,512]{2,1,0:T(8,128)(2,1)} %collective-permute-done), channel_id=1, source_target_pairs={{0,4},{4,8},{8,12},{12,14},{14,10},{10,6},{6,2},{2,0},{1,5},{5,9},... | collective-permute-start | bytes 1769480 | tf_op jit(solution)/shard_map/ppermute | solution.py:105
  38.7 15.4 %collective-permute-start.4 = (bf16[2,288,512]{2,1,0:T(8,128)(2,1)}, bf16[2,288,512]{2,1,0:T(8,128)(2,1)S(1)}, u32[]{:S(2)}, u32[]{:S(2)}) collective-permute-start(bf16[2,288,512]{2,1,0:T(8,128)(2,1)} %collective-permute-done.1), channel_id=1, source_target_pairs={{0,2},{4,0},{8,4},{12,8},{14,12},{10,14},{6,10},{2,6},{1,3},{5,1},... | collective-permute-start | bytes 1769480 | tf_op jit(solution)/shard_map/ppermute | solution.py:106
  54.1 14.3 %collective-permute-start.5 = (bf16[2,288,512]{2,1,0:T(8,128)(2,1)S(1)}, bf16[2,288,512]{2,1,0:T(8,128)(2,1)S(1)}, u32[]{:S(2)}, u32[]{:S(2)}) collective-permute-start(bf16[2,288,512]{2,1,0:T(8,128)(2,1)S(1)} %pad_maximum_fusion.17), channel_id=1, source_target_pairs={{0,16},{16,0},{1,17},{17,1},{2,18},{18,2},{3,19},{19,3},{4,20},{20... | collective-permute-start | bytes 1769480 | tf_op jit(solution)/shard_map/ppermute | solution.py:110
  56.2 14.0 %collective-permute-start.6 = (bf16[2,288,512]{2,1,0:T(8,128)(2,1)S(1)}, bf16[2,288,512]{2,1,0:T(8,128)(2,1)S(1)}, u32[]{:S(2)}, u32[]{:S(2)}) collective-permute-start(bf16[2,288,512]{2,1,0:T(8,128)(2,1)S(1)} %collective-permute-done.3), channel_id=1, source_target_pairs={{0,4},{4,8},{8,12},{12,14},{14,10},{10,6},{6,2},{2,0},{1,5},{5,9},... | collective-permute-start | bytes 1769480 | tf_op jit(solution)/shard_map/ppermute | solution.py:105
  57.5 13.4 %collective-permute-start.7 = (bf16[2,288,512]{2,1,0:T(8,128)(2,1)S(1)}, bf16[2,288,512]{2,1,0:T(8,128)(2,1)S(1)}, u32[]{:S(2)}, u32[]{:S(2)}) collective-permute-start(bf16[2,288,512]{2,1,0:T(8,128)(2,1)S(1)} %collective-permute-done.4), channel_id=1, source_target_pairs={{0,2},{4,0},{8,4},{12,8},{14,12},{10,14},{6,10},{2,6},{1,3},{5,1},... | collective-permute-start | bytes 1769480 | tf_op jit(solution)/shard_map/ppermute | solution.py:106
  71.0 12.5 %collective-permute-start.8 = (bf16[2,288,512]{2,1,0:T(8,128)(2,1)S(1)}, bf16[2,288,512]{2,1,0:T(8,128)(2,1)S(1)}, u32[]{:S(2)}, u32[]{:S(2)}) collective-permute-start(bf16[2,288,512]{2,1,0:T(8,128)(2,1)S(1)} %pad_maximum_fusion.18), channel_id=1, source_target_pairs={{0,16},{16,0},{1,17},{17,1},{2,18},{18,2},{3,19},{19,3},{4,20},{20... | collective-permute-start | bytes 1769480 | tf_op jit(solution)/shard_map/ppermute | solution.py:110
  72.6 12.2 %collective-permute-start.10 = (bf16[2,288,512]{2,1,0:T(8,128)(2,1)S(1)}, bf16[2,288,512]{2,1,0:T(8,128)(2,1)S(1)}, u32[]{:S(2)}, u32[]{:S(2)}) collective-permute-start(bf16[2,288,512]{2,1,0:T(8,128)(2,1)S(1)} %collective-permute-done.7), channel_id=1, source_target_pairs={{0,2},{4,0},{8,4},{12,8},{14,12},{10,14},{6,10},{2,6},{1,3},{5,1},... | collective-permute-start | bytes 1769480 | tf_op jit(solution)/shard_map/ppermute | solution.py:106
  73.8 13.0 %collective-permute-start.9 = (bf16[2,288,512]{2,1,0:T(8,128)(2,1)S(1)}, bf16[2,288,512]{2,1,0:T(8,128)(2,1)S(1)}, u32[]{:S(2)}, u32[]{:S(2)}) collective-permute-start(bf16[2,288,512]{2,1,0:T(8,128)(2,1)S(1)} %collective-permute-done.6), channel_id=1, source_target_pairs={{0,4},{4,8},{8,12},{12,14},{14,10},{10,6},{6,2},{2,0},{1,5},{5,9},... | collective-permute-start | bytes 1769480 | tf_op jit(solution)/shard_map/ppermute | solution.py:105
  86.9 11.1 %collective-permute-start.11 = (bf16[2,288,512]{2,1,0:T(8,128)(2,1)S(1)}, bf16[2,288,512]{2,1,0:T(8,128)(2,1)S(1)}, u32[]{:S(2)}, u32[]{:S(2)}) collective-permute-start(bf16[2,288,512]{2,1,0:T(8,128)(2,1)S(1)} %pad_maximum_fusion.19), channel_id=1, source_target_pairs={{0,16},{16,0},{1,17},{17,1},{2,18},{18,2},{3,19},{19,3},{4,20},{20... | collective-permute-start | bytes 1769480 | tf_op jit(solution)/shard_map/ppermute | solution.py:110
  87.0 13.3 %collective-permute-start.12 = (bf16[2,288,512]{2,1,0:T(8,128)(2,1)S(1)}, bf16[2,288,512]{2,1,0:T(8,128)(2,1)S(1)}, u32[]{:S(2)}, u32[]{:S(2)}) collective-permute-start(bf16[2,288,512]{2,1,0:T(8,128)(2,1)S(1)} %collective-permute-done.9), channel_id=1, source_target_pairs={{0,4},{4,8},{8,12},{12,14},{14,10},{10,6},{6,2},{2,0},{1,5},{5,9},... | collective-permute-start | bytes 1769480 | tf_op jit(solution)/shard_map/ppermute | solution.py:105
  87.9 12.3 %collective-permute-start.13 = (bf16[2,288,512]{2,1,0:T(8,128)(2,1)S(1)}, bf16[2,288,512]{2,1,0:T(8,128)(2,1)S(1)}, u32[]{:S(2)}, u32[]{:S(2)}) collective-permute-start(bf16[2,288,512]{2,1,0:T(8,128)(2,1)S(1)} %collective-permute-done.10), channel_id=1, source_target_pairs={{0,2},{4,0},{8,4},{12,8},{14,12},{10,14},{6,10},{2,6},{1,3},{5,1},... | collective-permute-start | bytes 1769480 | tf_op jit(solution)/shard_map/ppermute | solution.py:106
  98.2 49.2 %copy-start.2 = (bf16[288,1536]{1,0:T(8,128)(2,1)}, bf16[288,1536]{1,0:T(8,128)(2,1)S(1)}, u32[]{:S(2)}) copy-start(bf16[288,1536]{1,0:T(8,128)(2,1)S(1)} %pad_maximum_fusion.9) | copy-start | bytes 2654212
  100.4 12.3 %collective-permute-start.14 = (bf16[2,288,512]{2,1,0:T(8,128)(2,1)S(1)}, bf16[2,288,512]{2,1,0:T(8,128)(2,1)S(1)}, u32[]{:S(2)}, u32[]{:S(2)}) collective-permute-start(bf16[2,288,512]{2,1,0:T(8,128)(2,1)S(1)} %pad_maximum_fusion.20), channel_id=1, source_target_pairs={{0,16},{16,0},{1,17},{17,1},{2,18},{18,2},{3,19},{19,3},{4,20},{20... | collective-permute-start | bytes 1769480 | tf_op jit(solution)/shard_map/ppermute | solution.py:110
  101.1 11.8 %collective-permute-start.15 = (bf16[2,288,512]{2,1,0:T(8,128)(2,1)S(1)}, bf16[2,288,512]{2,1,0:T(8,128)(2,1)S(1)}, u32[]{:S(2)}, u32[]{:S(2)}) collective-permute-start(bf16[2,288,512]{2,1,0:T(8,128)(2,1)S(1)} %collective-permute-done.12), channel_id=1, source_target_pairs={{0,4},{4,8},{8,12},{12,14},{14,10},{10,6},{6,2},{2,0},{1,5},{5,9},... | collective-permute-start | bytes 1769480 | tf_op jit(solution)/shard_map/ppermute | solution.py:105
  101.4 12.9 %collective-permute-start.16 = (bf16[2,288,512]{2,1,0:T(8,128)(2,1)S(1)}, bf16[2,288,512]{2,1,0:T(8,128)(2,1)S(1)}, u32[]{:S(2)}, u32[]{:S(2)}) collective-permute-start(bf16[2,288,512]{2,1,0:T(8,128)(2,1)S(1)} %collective-permute-done.13), channel_id=1, source_target_pairs={{0,2},{4,0},{8,4},{12,8},{14,12},{10,14},{6,10},{2,6},{1,3},{5,1},... | collective-permute-start | bytes 1769480 | tf_op jit(solution)/shard_map/ppermute | solution.py:106
  112.9 33.5 %copy-start.4 = (bf16[288,1536]{1,0:T(8,128)(2,1)}, bf16[288,1536]{1,0:T(8,128)(2,1)S(1)}, u32[]{:S(2)}) copy-start(bf16[288,1536]{1,0:T(8,128)(2,1)S(1)} %pad_maximum_fusion.11) | copy-start | bytes 2654212
  114.4 14.9 %collective-permute-start.17 = (bf16[2,288,512]{2,1,0:T(8,128)(2,1)S(1)}, bf16[2,288,512]{2,1,0:T(8,128)(2,1)S(1)}, u32[]{:S(2)}, u32[]{:S(2)}) collective-permute-start(bf16[2,288,512]{2,1,0:T(8,128)(2,1)S(1)} %pad_maximum_fusion.21), channel_id=1, source_target_pairs={{0,16},{16,0},{1,17},{17,1},{2,18},{18,2},{3,19},{19,3},{4,20},{20... | collective-permute-start | bytes 1769480 | tf_op jit(solution)/shard_map/ppermute | solution.py:110
  117.1 9.9 %collective-permute-start.19 = (bf16[2,288,512]{2,1,0:T(8,128)(2,1)S(1)}, bf16[2,288,512]{2,1,0:T(8,128)(2,1)S(1)}, u32[]{:S(2)}, u32[]{:S(2)}) collective-permute-start(bf16[2,288,512]{2,1,0:T(8,128)(2,1)S(1)} %collective-permute-done.16), channel_id=1, source_target_pairs={{0,2},{4,0},{8,4},{12,8},{14,12},{10,14},{6,10},{2,6},{1,3},{5,1},... | collective-permute-start | bytes 1769480 | tf_op jit(solution)/shard_map/ppermute | solution.py:106
  117.9 9.9 %collective-permute-start.18 = (bf16[2,288,512]{2,1,0:T(8,128)(2,1)S(1)}, bf16[2,288,512]{2,1,0:T(8,128)(2,1)S(1)}, u32[]{:S(2)}, u32[]{:S(2)}) collective-permute-start(bf16[2,288,512]{2,1,0:T(8,128)(2,1)S(1)} %collective-permute-done.15), channel_id=1, source_target_pairs={{0,4},{4,8},{8,12},{12,14},{14,10},{10,6},{6,2},{2,0},{1,5},{5,9},... | collective-permute-start | bytes 1769480 | tf_op jit(solution)/shard_map/ppermute | solution.py:105
  127.9 9.9 %collective-permute-start.20 = (bf16[2,288,512]{2,1,0:T(8,128)(2,1)S(1)}, bf16[2,288,512]{2,1,0:T(8,128)(2,1)S(1)}, u32[]{:S(2)}, u32[]{:S(2)}) collective-permute-start(bf16[2,288,512]{2,1,0:T(8,128)(2,1)S(1)} %pad_maximum_fusion.22), channel_id=1, source_target_pairs={{0,16},{16,0},{1,17},{17,1},{2,18},{18,2},{3,19},{19,3},{4,20},{20... | collective-permute-start | bytes 1769480 | tf_op jit(solution)/shard_map/ppermute | solution.py:110
  129.5 15.9 %copy-start.6 = (bf16[288,1536]{1,0:T(8,128)(2,1)}, bf16[288,1536]{1,0:T(8,128)(2,1)S(1)}, u32[]{:S(2)}) copy-start(bf16[288,1536]{1,0:T(8,128)(2,1)S(1)} %pad_maximum_fusion.13) | copy-start | bytes 2654212
  129.7 9.5 %copy-start.1 = (bf16[1024,2304]{0,1:T(8,128)(2,1)}, bf16[1024,2304]{0,1:T(8,128)(2,1)S(1)}, u32[]{:S(2)}) copy-start(bf16[1024,2304]{0,1:T(8,128)(2,1)S(1)} %bitcast_dynamic-update-slice_fusion) | copy-start | bytes 14155780
  143.4 15.3 %copy-start.29 = (bf16[4,128,64]{2,1,0:T(8,128)(2,1)}, bf16[4,128,64]{2,1,0:T(8,128)(2,1)S(1)}, u32[]{:S(2)}) copy-start(bf16[4,128,64]{2,1,0:T(8,128)(2,1)S(1)} %get-tuple-element.103) | copy-start | bytes 196612
  149.2 5.6 %copy-start.17 = (bf16[128,512]{1,0:T(8,128)(2,1)}, bf16[128,512]{1,0:T(8,128)(2,1)S(1)}, u32[]{:S(2)}) copy-start(bf16[128,512]{1,0:T(8,128)(2,1)S(1)} %fusion.15) | copy-start | bytes 393220
  149.9 4.9 %copy-start.3 = (bf16[288,1536]{1,0:T(8,128)(2,1)S(1)}, bf16[288,1536]{1,0:T(8,128)(2,1)}, u32[]{:S(2)}) copy-start(bf16[288,1536]{1,0:T(8,128)(2,1)} %copy-done.2) | copy-start | bytes 2654212
  162.9 2.5 %collective-permute-start.21 = (bf16[128,2304]{1,0:T(8,128)(2,1)S(1)}, bf16[128,2304]{1,0:T(8,128)(2,1)S(1)}, u32[]{:S(2)}, u32[]{:S(2)}) collective-permute-start(bf16[128,2304]{1,0:T(8,128)(2,1)S(1)} %convolution_convert_fusion), channel_id=1, source_target_pairs={{0,1},{1,0},{2,3},{3,2},{4,5},{5,4},{6,7},{7,6},{8,9},{9,8},{10,11... | collective-permute-start | bytes 1769480 | tf_op jit(solution)/shard_map/ppermute | solution.py:58
  192.9 4.4 %collective-permute-start.22 = (bf16[128,2304]{1,0:T(8,128)(2,1)S(1)}, bf16[128,2304]{1,0:T(8,128)(2,1)}, u32[]{:S(2)}, u32[]{:S(2)}) collective-permute-start(bf16[128,2304]{1,0:T(8,128)(2,1)S(1)} %fusion.1), channel_id=1, source_target_pairs={{0,1},{1,0},{2,3},{3,2},{4,5},{5,4},{6,7},{7,6},{8,9},{9,8},{10,11... | collective-permute-start | bytes 1769480 | tf_op jit(solution)/shard_map/ppermute | solution.py:58
  204.4 8.9 %collective-permute-start.23 = (bf16[16,1152]{1,0:T(8,128)(2,1)S(1)}, bf16[16,1152]{1,0:T(8,128)(2,1)S(1)}, u32[]{:S(2)}, u32[]{:S(2)}) collective-permute-start(bf16[16,1152]{1,0:T(8,128)(2,1)S(1)} %get-tuple-element.111), channel_id=1, source_target_pairs={{0,2},{2,4},{4,6},{6,8},{8,10},{10,12},{12,14},{14,0},{1,3},{3,5},... | collective-permute-start | bytes 110600 | tf_op jit(solution)/shard_map/ppermute | solution.py:135
  206.5 8.3 %collective-permute-start.24 = (bf16[16,1152]{1,0:T(8,128)(2,1)S(1)}, bf16[16,1152]{1,0:T(8,128)(2,1)S(1)}, u32[]{:S(2)}, u32[]{:S(2)}) collective-permute-start(bf16[16,1152]{1,0:T(8,128)(2,1)S(1)} %get-tuple-element.110), channel_id=1, source_target_pairs={{0,4},{2,6},{4,8},{6,10},{8,12},{10,14},{12,0},{14,2},{1,5},{3,7},... | collective-permute-start | bytes 110600 | tf_op jit(solution)/shard_map/ppermute | solution.py:135
  207.9 8.6 %collective-permute-start.25 = (bf16[16,1152]{1,0:T(8,128)(2,1)S(1)}, bf16[16,1152]{1,0:T(8,128)(2,1)S(1)}, u32[]{:S(2)}, u32[]{:S(2)}) collective-permute-start(bf16[16,1152]{1,0:T(8,128)(2,1)S(1)} %get-tuple-element.109), channel_id=1, source_target_pairs={{0,6},{2,8},{4,10},{6,12},{8,14},{10,0},{12,2},{14,4},{1,7},{3,9},... | collective-permute-start | bytes 110600 | tf_op jit(solution)/shard_map/ppermute | solution.py:135
  209.6 6.9 %collective-permute-start.26 = (bf16[16,1152]{1,0:T(8,128)(2,1)S(1)}, bf16[16,1152]{1,0:T(8,128)(2,1)S(1)}, u32[]{:S(2)}, u32[]{:S(2)}) collective-permute-start(bf16[16,1152]{1,0:T(8,128)(2,1)S(1)} %get-tuple-element.108), channel_id=1, source_target_pairs={{0,8},{2,10},{4,12},{6,14},{8,0},{10,2},{12,4},{14,6},{1,9},{3,11}... | collective-permute-start | bytes 110600 | tf_op jit(solution)/shard_map/ppermute | solution.py:135
  212.4 4.9 %collective-permute-start.27 = (bf16[16,1152]{1,0:T(8,128)(2,1)S(1)}, bf16[16,1152]{1,0:T(8,128)(2,1)S(1)}, u32[]{:S(2)}, u32[]{:S(2)}) collective-permute-start(bf16[16,1152]{1,0:T(8,128)(2,1)S(1)} %get-tuple-element.107), channel_id=1, source_target_pairs={{0,10},{2,12},{4,14},{6,0},{8,2},{10,4},{12,6},{14,8},{1,11},{3,13... | collective-permute-start | bytes 110600 | tf_op jit(solution)/shard_map/ppermute | solution.py:135
  213.3 4.2 %collective-permute-start.28 = (bf16[16,1152]{1,0:T(8,128)(2,1)S(1)}, bf16[16,1152]{1,0:T(8,128)(2,1)S(1)}, u32[]{:S(2)}, u32[]{:S(2)}) collective-permute-start(bf16[16,1152]{1,0:T(8,128)(2,1)S(1)} %get-tuple-element.106), channel_id=1, source_target_pairs={{0,12},{2,14},{4,0},{6,2},{8,4},{10,6},{12,8},{14,10},{1,13},{3,15... | collective-permute-start | bytes 110600 | tf_op jit(solution)/shard_map/ppermute | solution.py:135
  214.8 4.0 %collective-permute-start.29 = (bf16[16,1152]{1,0:T(8,128)(2,1)S(1)}, bf16[16,1152]{1,0:T(8,128)(2,1)S(1)}, u32[]{:S(2)}, u32[]{:S(2)}) collective-permute-start(bf16[16,1152]{1,0:T(8,128)(2,1)S(1)} %get-tuple-element.105), channel_id=1, source_target_pairs={{0,14},{2,0},{4,2},{6,4},{8,6},{10,8},{12,10},{14,12},{1,15},{3,1}... | collective-permute-start | bytes 110600 | tf_op jit(solution)/shard_map/ppermute | solution.py:135
  (42 other events, 90.7 us)

commit v12 on v10

--- a/solution.py
+++ b/solution.py
@@ -166,10 +166,12 @@
     label_table = permute_blocks(label_table, block_of, n_seq)
     piecewise = n_seq <= PIECEWISE_RING
     if piecewise:
-        w_query_t = jnp.concatenate([piece[:, :q_cols].T for piece in front_pieces], axis=1)
-        w_key_t = jnp.concatenate([piece[:, q_cols:].T for piece in front_pieces], axis=1)
-        w_value_t = jnp.concatenate([piece[:, :k_cols].T for piece in back_pieces], axis=1)
-        w_out = jnp.concatenate([piece[:, k_cols:].T for piece in back_pieces], axis=1)
+        front_t = jnp.concatenate([piece.T for piece in front_pieces], axis=1)
+        back_t = jnp.concatenate([piece.T for piece in back_pieces], axis=1)
+        w_query_t = front_t[:q_cols]
+        w_key_t = front_t[q_cols:]
+        w_value_t = back_t[:k_cols]
+        w_out = back_t[k_cols:]
     else:
         front_all = jnp.concatenate(front_pieces, axis=0)
         back_all = jnp.concatenate(back_pieces, axis=0)

time: 208 us -> 218 us (1.048)
  matrix products: 22.7 us -> 31.3 us
  other arithmetic: 23.8 us -> 29.4 us
  waiting for transfers between devices: 78.4 us -> 74.4 us
    ppermute x7, waiting for transfers between devices: 18.6 us -> 58.2 us  [ring_gather(): front_ring.append(lax.ppermute(front_ring[-1], 'seq', forward_pairs))]
    ppermute x7, waiting for transfers between devices: 44.4 us -> 9.6 us  [ring_gather(): lax.ppermute(jnp.stack([front_ring[step][0], back_ring[step][0]]), 'group...]
    all_to_all x1, waiting for transfers between devices: 5.58 us -> 0.01 us  [shards(): lax.all_to_all(generator_rows, 'seq', split_axis=0, concat_axis=0, tiled=...]
    ppermute x7, waiting for transfers between devices: 9.78 us -> 6.54 us  [ring_gather(): back_ring.append(lax.ppermute(back_ring[-1], 'seq', backward_pairs))]
    ppermute x7, starting transfers between devices: 7.97 us -> 4.76 us  [ring_gather(): back_ring.append(lax.ppermute(back_ring[-1], 'seq', backward_pairs))]
    dot_general x1, matrix products: 1.67 us -> 4.03 us  [shards(): out_part = jnp.dot(context_rows, w_out, preferred_element_type=jnp.float32)]
    ppermute x7, starting transfers between devices: 7.47 us -> 9.8 us  [ring_gather(): front_ring.append(lax.ppermute(front_ring[-1], 'seq', forward_pairs))]
    unnamed x141 -> x124, local copies, waits for them, and re-layouts: 14.6 us -> 12.8 us
  transfers between devices with their start and end apart: 24 -> 24, of which waited for: 16 -> 14; matrix products, arithmetic and copies ran while one was open for 13% -> 15% of each run, Pallas kernels for 0% -> 0%
where the time goes in v12:
time: 218 us; the launch traced here: 217 us
  waiting for transfers between devices  74.4 us (34%)
  local copies, waits for them, and re-layouts  33.5 us (15%)
  matrix products  31.3 us (14%)
  starting transfers between devices  31.1 us (14%)
  other arithmetic  29.4 us (13%)
  blocking collectives  15.9 us (7%)
    ppermute x7, waiting for transfers between devices, ring_gather(): front_ring.append(lax.ppermute(front_ring[-1], 'seq', forward_pairs))  58.2 us
    all_to_all x1, blocking collectives, shards(): lax.all_to_all(grad_rows, 'seq', split_axis=0, concat_axis=0, tiled=True)  13.4 us
    unnamed x124, local copies, waits for them, and re-layouts  12.8 us
    ppermute x7, starting transfers between devices, ring_gather(): front_ring.append(lax.ppermute(front_ring[-1], 'seq', forward_pairs))  9.8 us
    ppermute x7, waiting for transfers between devices, ring_gather(): lax.ppermute(jnp.stack([front_ring[step][0], back_ring[step][0]]), 'group...  9.6 us
    ppermute x7, starting transfers between devices, ring_gather(): lax.ppermute(jnp.stack([front_ring[step][0], back_ring[step][0]]), 'group...  8.92 us
    all_to_all x1, starting transfers between devices, shards(): lax.all_to_all(generator_rows, 'seq', split_axis=0, concat_axis=0, tiled=...  7.25 us
    ppermute x7, waiting for transfers between devices, ring_gather(): back_ring.append(lax.ppermute(back_ring[-1], 'seq', backward_pairs))  6.54 us
  transfers between devices with their start and end apart: 24, of which 14 were waited for; matrix products, arithmetic and copies ran while one was open for 15% of the time, Pallas kernels for 0%

profile of v12, /device:TPU:0, one launch (start us, length us, event | category | flops | bytes accessed | tf_op | source)
XLA Modules:
  0.0 216.8 jit_solution(15049169692484219374)
XLA Ops:
  0.0 7.3 %all-to-all-start = ((bf16[8,16,1152]{2,1,0:T(8,128)(2,1)}), bf16[8,16,1152]{2,1,0:T(8,128)(2,1)}, u32[]{:S(2)}, u32[]{:S(2)}) async-start(bf16[8,16,1152]{2,1,0:T(8,128)(2,1)} %bitcast.260), calls=%async_computation | async-start | bytes 589824 | tf_op jit(solution)/shard_map/all_to_all | solution.py:153
  7.3 1.4 fusion.47
  9.6 2.0 collective-permute-start
  16.9 1.2 compare_convert_fusion
  23.3 1.2 pad_maximum_fusion
  24.5 2.4 %all_gather.3 = bf16[128,2304]{1,0:T(8,128)(2,1)S(1)} all-gather(bf16[128,1152]{1,0:T(8,128)(2,1)} %bitcast.2), channel_id=1, replica_groups=mesh['groups'=2,'seq'=8,'wg'=2] {'wg'}, dimensions={1}, use_global_device_ids=true | all-gather | bytes 884736 | tf_op jit(solution)/shard_map/all_gather | solution.py:154
  28.1 1.1 multiply_reduce_fusion.4
  32.0 1.6 collective-permute-start.2
  34.0 2.1 collective-permute-start.3
  37.4 12.0 %collective-permute-done.3 = bf16[2,288,512]{2,1,0:T(8,128)(2,1)S(1)} collective-permute-done((bf16[2,288,512]{2,1,0:T(8,128)(2,1)S(1)}, bf16[2,288,512]{2,1,0:T(8,128)(2,1)S(1)}, u32[]{:S(2)}, u32[]{:S(2)}) %collective-permute-start.3) | collective-permute-done | bytes 589856 | tf_op jit(solution)/shard_map/ppermute | solution.py:105
  49.4 1.6 collective-permute-done.4
  51.7 1.2 select_bitcast_fusion.25
  53.1 1.5 collective-permute-start.6
  55.6 11.1 %collective-permute-done.6 = bf16[2,288,512]{2,1,0:T(8,128)(2,1)S(1)} collective-permute-done((bf16[2,288,512]{2,1,0:T(8,128)(2,1)S(1)}, bf16[2,288,512]{2,1,0:T(8,128)(2,1)S(1)}, u32[]{:S(2)}, u32[]{:S(2)}) %collective-permute-start.6) | collective-permute-done | bytes 589856 | tf_op jit(solution)/shard_map/ppermute | solution.py:105
  66.7 1.2 collective-permute-done.7
  68.0 1.6 collective-permute-start.8
  69.9 1.5 collective-permute-start.9
  72.4 9.6 %collective-permute-done.9 = bf16[2,288,512]{2,1,0:T(8,128)(2,1)S(1)} collective-permute-done((bf16[2,288,512]{2,1,0:T(8,128)(2,1)S(1)}, bf16[2,288,512]{2,1,0:T(8,128)(2,1)S(1)}, u32[]{:S(2)}, u32[]{:S(2)}) %collective-permute-start.9) | collective-permute-done | bytes 589856 | tf_op jit(solution)/shard_map/ppermute | solution.py:105
  82.1 1.1 collective-permute-done.10
  84.1 1.6 collective-permute-start.12
  86.7 8.8 %collective-permute-done.12 = bf16[2,288,512]{2,1,0:T(8,128)(2,1)S(1)} collective-permute-done((bf16[2,288,512]{2,1,0:T(8,128)(2,1)S(1)}, bf16[2,288,512]{2,1,0:T(8,128)(2,1)S(1)}, u32[]{:S(2)}, u32[]{:S(2)}) %collective-permute-start.12) | collective-permute-done | bytes 589856 | tf_op jit(solution)/shard_map/ppermute | solution.py:105
  95.5 1.5 collective-permute-done.13
  97.1 1.6 collective-permute-start.14
  99.4 1.6 collective-permute-start.16
  101.4 9.4 %collective-permute-done.15 = bf16[2,288,512]{2,1,0:T(8,128)(2,1)S(1)} collective-permute-done((bf16[2,288,512]{2,1,0:T(8,128)(2,1)S(1)}, bf16[2,288,512]{2,1,0:T(8,128)(2,1)S(1)}, u32[]{:S(2)}, u32[]{:S(2)}) %collective-permute-start.15) | collective-permute-done | bytes 589856 | tf_op jit(solution)/shard_map/ppermute | solution.py:105
  111.6 2.9 %collective-permute-start.17 = (bf16[2,288,512]{2,1,0:T(8,128)(2,1)S(1)}, bf16[2,288,512]{2,1,0:T(8,128)(2,1)S(1)}, u32[]{:S(2)}, u32[]{:S(2)}) collective-permute-start(bf16[2,288,512]{2,1,0:T(8,128)(2,1)S(1)} %pad_maximum_fusion.22), channel_id=1, source_target_pairs={{0,16},{16,0},{1,17},{17,1},{2,18},{18,2},{3,19},{19,3},{4,20},{20... | collective-permute-start | bytes 1769480 | tf_op jit(solution)/shard_map/ppermute | solution.py:110
  115.3 1.5 collective-permute-start.19
  117.3 7.4 %collective-permute-done.18 = bf16[2,288,512]{2,1,0:T(8,128)(2,1)S(1)} collective-permute-done((bf16[2,288,512]{2,1,0:T(8,128)(2,1)S(1)}, bf16[2,288,512]{2,1,0:T(8,128)(2,1)S(1)}, u32[]{:S(2)}, u32[]{:S(2)}) %collective-permute-start.18) | collective-permute-done | bytes 589856 | tf_op jit(solution)/shard_map/ppermute | solution.py:105
  126.4 8.8 %collective-permute-done.20 = bf16[2,288,512]{2,1,0:T(8,128)(2,1)S(1)} collective-permute-done((bf16[2,288,512]{2,1,0:T(8,128)(2,1)S(1)}, bf16[2,288,512]{2,1,0:T(8,128)(2,1)S(1)}, u32[]{:S(2)}, u32[]{:S(2)}) %collective-permute-start.20) | collective-permute-done | bytes 589856 | tf_op jit(solution)/shard_map/ppermute | solution.py:110
  141.2 1.6 copy.116
  142.9 1.2 copy.101
  144.0 1.2 subtract_convert_fusion.4
  154.9 4.0 %fusion.8 = bf16[128,2304]{1,0:T(8,128)(2,1)S(1)} fusion(bf16[128,1024]{0,1:T(8,128)(2,1)S(1)} %bitcast.264, bf16[1536,2304]{0,1:T(8,128)(2,1)} %bitcast_dynamic-update-slice_fusion.8), kind=kOutput, calls=%fused_computation.16 | convolution fusion | flops 604274688 | bytes 5570560 | tf_op jit(solution)/shard_map/dot_general | solution.py:234
  164.7 2.0 fusion.19
  166.7 1.2 copy.92
  167.8 2.0 fusion.30
  170.8 2.8 %convolution_bitcast_fusion.1 = f32[4,128,128]{2,1,0:T(8,128)} fusion(bf16[4,2,128,128]{3,2,1,0:T(8,128)(2,1)} %copy-done.27, f32[4,2,128,128]{2,3,1,0:T(8,128)} %fusion.62, f32[4,2,128,128]{2,3,1,0:T(8,128)} %copy-done.50, f32[4,2,128]{2,1,0:T(2,128)S(1)} %get-tuple-element.114, pred[128,128]{0,1:T(8,128)(4,1)S(1)} %copy-done.34), kind=kOutput, calls=%fused_computation.57 | convolution fusion | flops 35259520 | bytes 1593344 | tf_op jit(solution)/shard_map/kgij,kgid->kjd/dot_general | solution.py:275
  173.7 2.3 %convolution_multiply_fusion.1 = f32[4,2,128,128]{3,2,1,0:T(8,128)S(1)} fusion(f32[4,2,128,128]{2,3,1,0:T(8,128)} %fusion.62, f32[4,2,128,128]{2,3,1,0:T(8,128)} %copy-done.50, bf16[4,128,64]{2,1,0:T(8,128)(2,1)} %copy-done.30, bf16[4,128,64]{2,1,0:T(8,128)(2,1)} %copy-done.29, f32[4,2,128]{2,1,0:T(2,128)} %copy-done.51, pred[128,128]{0,1:T(8,128)(4,1)} %fusion.84), kind=kOutput, calls=%fused_computation.33 | convolution fusion | flops 35652736 | bytes 1724416 | tf_op jit(solution)/shard_map/kgij,kjd->kgid/dot_general | solution.py:271
  176.0 1.2 add_convert_fusion.1
  178.0 1.7 copy.74
  181.6 4.0 %fusion.1 = f32[128,2304]{1,0:T(8,128)S(1)} fusion(bf16[1536,2304]{0,1:T(8,128)(2,1)} %bitcast_dynamic-update-slice_fusion, bf16[16,8,8,128]{3,2,1,0:T(8,128)(2,1)S(1)} %bitcast.261), kind=kOutput, calls=%fused_computation.6 | convolution fusion | flops 603979776 | bytes 6160384 | tf_op jit(solution)/shard_map/dot_general | solution.py:285
  185.6 2.6 %convolution_add_fusion.1 = f32[128,2304]{1,0:T(8,128)S(1)} fusion(f32[128,2304]{1,0:T(8,128)S(1)} %fusion.1, bf16[128,512]{0,1:T(8,128)(2,1)S(1)} %bitcast.259, bf16[1536,2304]{0,1:T(8,128)(2,1)} %bitcast_dynamic-update-slice_fusion), kind=kOutput, calls=%fused_computation.13 | convolution fusion | flops 302284800 | bytes 4849664 | tf_op jit(solution)/shard_map/dot_general | solution.py:286
  188.3 2.6 %fusion.7 = bf16[128,2304]{1,0:T(8,128)(2,1)S(1)} fusion(f32[128,2304]{1,0:T(8,128)S(1)} %convolution_add_fusion.1, bf16[128,512]{0,1:T(8,128)(2,1)S(1)} %bitcast.262, bf16[1536,2304]{0,1:T(8,128)(2,1)} %bitcast_dynamic-update-slice_fusion.8), kind=kOutput, calls=%fused_computation.15 | convolution fusion | flops 302579712 | bytes 4259840 | tf_op jit(solution)/shard_map/dot_general | solution.py:287
  191.2 1.2 gather_fusion
  195.6 1.5 fusion.28
  197.1 2.9 %fusion.27 = bf16[128,2304]{1,0:T(8,128)(2,1)} fusion(bf16[128,2304]{1,0:T(8,128)(2,1)} %collective-permute-done.22, bf16[128,2304]{1,0:T(8,128)(2,1)S(1)} %fusion.7, f32[128]{0:T(128)S(1)} %broadcast_multiply_fusion, f32[128]{0:T(128)} %get-tuple-element.108, f32[2304]{0:T(1024)S(1)} %copy-done.28, f32[128]{0:T(128)} %get-tuple-element.109, ...), kind=kLoop, calls=%fused_computation.44 | loop fusion | flops 6488064 | bytes 4742912 | tf_op jit(solution)/shard_map/convert_element_type | solution.py:297
  200.0 1.4 copy.76
  202.7 13.4 %all_to_all.21 = bf16[8,16,1152]{2,1,0:T(8,128)(2,1)S(1)} all-to-all(bf16[8,16,1152]{2,1,0:T(8,128)(2,1)S(1)} %broadcast_select_fusion.2), channel_id=1, replica_groups=mesh['groups'=2,'seq'=8,'wg'=2] {'seq'}, dimensions={0} | all-to-all | bytes 589824 | tf_op jit(solution)/shard_map/all_to_all | solution.py:299
  (275 shorter events, 57.0 us)
Async XLA Ops:
  0.0 24.5 %all-to-all-start = ((bf16[8,16,1152]{2,1,0:T(8,128)(2,1)}), bf16[8,16,1152]{2,1,0:T(8,128)(2,1)}, u32[]{:S(2)}, u32[]{:S(2)}) async-start(bf16[8,16,1152]{2,1,0:T(8,128)(2,1)} %bitcast.260), calls=%async_computation | async-start | bytes 589824 | tf_op jit(solution)/shard_map/all_to_all | solution.py:153
  8.7 3.9 %copy-start.47 = (s32[8]{0:T(128)S(1)}, s32[8]{0:T(128)}, u32[]{:S(2)}) copy-start(s32[8]{0:T(128)} %param.21) | copy-start | bytes 100
  8.7 4.6 %copy-start.48 = (s32[8]{0:T(128)S(1)}, s32[8]{0:T(128)}, u32[]{:S(2)}) copy-start(s32[8]{0:T(128)} %param.20) | copy-start | bytes 100
  8.7 6.4 %copy-start.35 = (f32[2304]{0:T(1024)S(1)}, f32[2304]{0:T(1024)}, u32[]{:S(2)}) copy-start(f32[2304]{0:T(1024)} %param.12) | copy-start | bytes 27652
  8.7 6.5 %copy-start.36 = (f32[2304]{0:T(1024)S(1)}, f32[2304]{0:T(1024)}, u32[]{:S(2)}) copy-start(f32[2304]{0:T(1024)} %param.17) | copy-start | bytes 27652
  8.7 6.6 %copy-start.37 = (f32[2304]{0:T(1024)S(1)}, f32[2304]{0:T(1024)}, u32[]{:S(2)}) copy-start(f32[2304]{0:T(1024)} %param.18) | copy-start | bytes 27652
  8.7 11.0 %copy-start.25 = (bf16[64,2304]{1,0:T(8,128)(2,1)S(1)}, bf16[64,2304]{1,0:T(8,128)(2,1)}, u32[]{:S(2)}) copy-start(bf16[64,2304]{1,0:T(8,128)(2,1)} %param.19) | copy-start | bytes 884740
  9.6 21.2 %collective-permute-start = (bf16[2,288,512]{2,1,0:T(8,128)(2,1)}, bf16[2,288,512]{2,1,0:T(8,128)(2,1)S(1)}, u32[]{:S(2)}, u32[]{:S(2)}) collective-permute-start(bf16[2,288,512]{2,1,0:T(8,128)(2,1)} %pad_maximum_fusion.15), channel_id=1, source_target_pairs={{0,4},{4,8},{8,12},{12,14},{14,10},{10,6},{6,2},{2,0},{1,5},{5,9},... | collective-permute-start | bytes 1769480 | tf_op jit(solution)/shard_map/ppermute | solution.py:105
  12.5 18.4 %collective-permute-start.1 = (bf16[2,288,512]{2,1,0:T(8,128)(2,1)}, bf16[2,288,512]{2,1,0:T(8,128)(2,1)}, u32[]{:S(2)}, u32[]{:S(2)}) collective-permute-start(bf16[2,288,512]{2,1,0:T(8,128)(2,1)} %pad_maximum_fusion.16), channel_id=1, source_target_pairs={{0,2},{4,0},{8,4},{12,8},{14,12},{10,14},{6,10},{2,6},{1,3},{5,1},... | collective-permute-start | bytes 1769480 | tf_op jit(solution)/shard_map/ppermute | solution.py:106
  12.5 7.2 %copy-start.40 = (pred[8]{0:T(512)(128)(4,1)}, pred[8]{0:T(512)(128)(4,1)S(1)}, u32[]{:S(2)}) copy-start(pred[8]{0:T(512)(128)(4,1)S(1)} %compare_and_fusion) | copy-start | bytes 28
  14.5 5.2 %copy-start.45 = (pred[128]{0:T(512)(128)(4,1)}, pred[128]{0:T(512)(128)(4,1)S(1)}, u32[]{:S(2)}) copy-start(pred[128]{0:T(512)(128)(4,1)S(1)} %iota_compare_fusion.1) | copy-start | bytes 388
  14.5 6.8 %copy-start.39 = (s32[1024]{0:T(1024)}, s32[1024]{0:T(1024)S(1)}, u32[]{:S(2)}) copy-start(s32[1024]{0:T(1024)S(1)} %pad_clamp_fusion.1) | copy-start | bytes 12292
  18.3 146.0 %copy-start.33 = (pred[2304]{0:T(1024)(128)(4,1)}, pred[2304]{0:T(1024)(128)(4,1)S(1)}, u32[]{:S(2)}) copy-start(pred[2304]{0:T(1024)(128)(4,1)S(1)} %broadcast_in_dim.117) | copy-start | bytes 6916
  19.7 3.6 %copy-start.8 = (bf16[288,1024]{1,0:T(8,128)(2,1)S(1)}, bf16[288,1024]{1,0:T(8,128)(2,1)}, u32[]{:S(2)}) copy-start(bf16[288,1024]{1,0:T(8,128)(2,1)} %param.13) | copy-start | bytes 1769476
  19.7 3.6 %copy-start.9 = (bf16[1024,288]{0,1:T(8,128)(2,1)S(1)}, bf16[1024,288]{0,1:T(8,128)(2,1)}, u32[]{:S(2)}) copy-start(bf16[1024,288]{0,1:T(8,128)(2,1)} %param.16) | copy-start | bytes 1769476
  32.0 19.8 %collective-permute-start.2 = (bf16[2,288,512]{2,1,0:T(8,128)(2,1)S(1)}, bf16[2,288,512]{2,1,0:T(8,128)(2,1)S(1)}, u32[]{:S(2)}, u32[]{:S(2)}) collective-permute-start(bf16[2,288,512]{2,1,0:T(8,128)(2,1)S(1)} %pad_maximum_fusion.17), channel_id=1, source_target_pairs={{0,16},{16,0},{1,17},{17,1},{2,18},{18,2},{3,19},{19,3},{4,20},{20... | collective-permute-start | bytes 1769480 | tf_op jit(solution)/shard_map/ppermute | solution.py:110
  34.0 15.4 %collective-permute-start.3 = (bf16[2,288,512]{2,1,0:T(8,128)(2,1)S(1)}, bf16[2,288,512]{2,1,0:T(8,128)(2,1)S(1)}, u32[]{:S(2)}, u32[]{:S(2)}) collective-permute-start(bf16[2,288,512]{2,1,0:T(8,128)(2,1)S(1)} %collective-permute-done), channel_id=1, source_target_pairs={{0,4},{4,8},{8,12},{12,14},{14,10},{10,6},{6,2},{2,0},{1,5},{5,9},... | collective-permute-start | bytes 1769480 | tf_op jit(solution)/shard_map/ppermute | solution.py:105
  36.0 15.0 %collective-permute-start.4 = (bf16[2,288,512]{2,1,0:T(8,128)(2,1)}, bf16[2,288,512]{2,1,0:T(8,128)(2,1)S(1)}, u32[]{:S(2)}, u32[]{:S(2)}) collective-permute-start(bf16[2,288,512]{2,1,0:T(8,128)(2,1)} %collective-permute-done.1), channel_id=1, source_target_pairs={{0,2},{4,0},{8,4},{12,8},{14,12},{10,14},{6,10},{2,6},{1,3},{5,1},... | collective-permute-start | bytes 1769480 | tf_op jit(solution)/shard_map/ppermute | solution.py:106
  51.1 18.5 %collective-permute-start.5 = (bf16[2,288,512]{2,1,0:T(8,128)(2,1)S(1)}, bf16[2,288,512]{2,1,0:T(8,128)(2,1)S(1)}, u32[]{:S(2)}, u32[]{:S(2)}) collective-permute-start(bf16[2,288,512]{2,1,0:T(8,128)(2,1)S(1)} %pad_maximum_fusion.18), channel_id=1, source_target_pairs={{0,16},{16,0},{1,17},{17,1},{2,18},{18,2},{3,19},{19,3},{4,20},{20... | collective-permute-start | bytes 1769480 | tf_op jit(solution)/shard_map/ppermute | solution.py:110
  53.1 13.7 %collective-permute-start.6 = (bf16[2,288,512]{2,1,0:T(8,128)(2,1)S(1)}, bf16[2,288,512]{2,1,0:T(8,128)(2,1)S(1)}, u32[]{:S(2)}, u32[]{:S(2)}) collective-permute-start(bf16[2,288,512]{2,1,0:T(8,128)(2,1)S(1)} %collective-permute-done.3), channel_id=1, source_target_pairs={{0,4},{4,8},{8,12},{12,14},{14,10},{10,6},{6,2},{2,0},{1,5},{5,9},... | collective-permute-start | bytes 1769480 | tf_op jit(solution)/shard_map/ppermute | solution.py:105
  54.6 13.3 %collective-permute-start.7 = (bf16[2,288,512]{2,1,0:T(8,128)(2,1)S(1)}, bf16[2,288,512]{2,1,0:T(8,128)(2,1)S(1)}, u32[]{:S(2)}, u32[]{:S(2)}) collective-permute-start(bf16[2,288,512]{2,1,0:T(8,128)(2,1)S(1)} %collective-permute-done.4), channel_id=1, source_target_pairs={{0,2},{4,0},{8,4},{12,8},{14,12},{10,14},{6,10},{2,6},{1,3},{5,1},... | collective-permute-start | bytes 1769480 | tf_op jit(solution)/shard_map/ppermute | solution.py:106
  68.0 15.9 %collective-permute-start.8 = (bf16[2,288,512]{2,1,0:T(8,128)(2,1)S(1)}, bf16[2,288,512]{2,1,0:T(8,128)(2,1)S(1)}, u32[]{:S(2)}, u32[]{:S(2)}) collective-permute-start(bf16[2,288,512]{2,1,0:T(8,128)(2,1)S(1)} %pad_maximum_fusion.19), channel_id=1, source_target_pairs={{0,16},{16,0},{1,17},{17,1},{2,18},{18,2},{3,19},{19,3},{4,20},{20... | collective-permute-start | bytes 1769480 | tf_op jit(solution)/shard_map/ppermute | solution.py:110
  69.9 12.2 %collective-permute-start.9 = (bf16[2,288,512]{2,1,0:T(8,128)(2,1)S(1)}, bf16[2,288,512]{2,1,0:T(8,128)(2,1)S(1)}, u32[]{:S(2)}, u32[]{:S(2)}) collective-permute-start(bf16[2,288,512]{2,1,0:T(8,128)(2,1)S(1)} %collective-permute-done.6), channel_id=1, source_target_pairs={{0,4},{4,8},{8,12},{12,14},{14,10},{10,6},{6,2},{2,0},{1,5},{5,9},... | collective-permute-start | bytes 1769480 | tf_op jit(solution)/shard_map/ppermute | solution.py:105
  71.4 11.8 %collective-permute-start.10 = (bf16[2,288,512]{2,1,0:T(8,128)(2,1)S(1)}, bf16[2,288,512]{2,1,0:T(8,128)(2,1)S(1)}, u32[]{:S(2)}, u32[]{:S(2)}) collective-permute-start(bf16[2,288,512]{2,1,0:T(8,128)(2,1)S(1)} %collective-permute-done.7), channel_id=1, source_target_pairs={{0,2},{4,0},{8,4},{12,8},{14,12},{10,14},{6,10},{2,6},{1,3},{5,1},... | collective-permute-start | bytes 1769480 | tf_op jit(solution)/shard_map/ppermute | solution.py:106
  83.3 15.4 %collective-permute-start.11 = (bf16[2,288,512]{2,1,0:T(8,128)(2,1)S(1)}, bf16[2,288,512]{2,1,0:T(8,128)(2,1)S(1)}, u32[]{:S(2)}, u32[]{:S(2)}) collective-permute-start(bf16[2,288,512]{2,1,0:T(8,128)(2,1)S(1)} %pad_maximum_fusion.20), channel_id=1, source_target_pairs={{0,16},{16,0},{1,17},{17,1},{2,18},{18,2},{3,19},{19,3},{4,20},{20... | collective-permute-start | bytes 1769480 | tf_op jit(solution)/shard_map/ppermute | solution.py:110
  84.1 55.7 %copy-start = (bf16[288,1536]{1,0:T(8,128)(2,1)}, bf16[288,1536]{1,0:T(8,128)(2,1)S(1)}, u32[]{:S(2)}) copy-start(bf16[288,1536]{1,0:T(8,128)(2,1)S(1)} %pad_maximum_fusion.7) | copy-start | bytes 2654212
  84.1 11.3 %collective-permute-start.12 = (bf16[2,288,512]{2,1,0:T(8,128)(2,1)S(1)}, bf16[2,288,512]{2,1,0:T(8,128)(2,1)S(1)}, u32[]{:S(2)}, u32[]{:S(2)}) collective-permute-start(bf16[2,288,512]{2,1,0:T(8,128)(2,1)S(1)} %collective-permute-done.9), channel_id=1, source_target_pairs={{0,4},{4,8},{8,12},{12,14},{14,10},{10,6},{6,2},{2,0},{1,5},{5,9},... | collective-permute-start | bytes 1769480 | tf_op jit(solution)/shard_map/ppermute | solution.py:105
  85.8 11.2 %collective-permute-start.13 = (bf16[2,288,512]{2,1,0:T(8,128)(2,1)S(1)}, bf16[2,288,512]{2,1,0:T(8,128)(2,1)S(1)}, u32[]{:S(2)}, u32[]{:S(2)}) collective-permute-start(bf16[2,288,512]{2,1,0:T(8,128)(2,1)S(1)} %collective-permute-done.10), channel_id=1, source_target_pairs={{0,2},{4,0},{8,4},{12,8},{14,12},{10,14},{6,10},{2,6},{1,3},{5,1},... | collective-permute-start | bytes 1769480 | tf_op jit(solution)/shard_map/ppermute | solution.py:106
  97.1 17.4 %collective-permute-start.14 = (bf16[2,288,512]{2,1,0:T(8,128)(2,1)S(1)}, bf16[2,288,512]{2,1,0:T(8,128)(2,1)S(1)}, u32[]{:S(2)}, u32[]{:S(2)}) collective-permute-start(bf16[2,288,512]{2,1,0:T(8,128)(2,1)S(1)} %pad_maximum_fusion.21), channel_id=1, source_target_pairs={{0,16},{16,0},{1,17},{17,1},{2,18},{18,2},{3,19},{19,3},{4,20},{20... | collective-permute-start | bytes 1769480 | tf_op jit(solution)/shard_map/ppermute | solution.py:110
  98.9 40.6 %copy-start.2 = (bf16[288,1536]{1,0:T(8,128)(2,1)}, bf16[288,1536]{1,0:T(8,128)(2,1)S(1)}, u32[]{:S(2)}) copy-start(bf16[288,1536]{1,0:T(8,128)(2,1)S(1)} %pad_maximum_fusion.9) | copy-start | bytes 2654212
  98.9 11.9 %collective-permute-start.15 = (bf16[2,288,512]{2,1,0:T(8,128)(2,1)S(1)}, bf16[2,288,512]{2,1,0:T(8,128)(2,1)S(1)}, u32[]{:S(2)}, u32[]{:S(2)}) collective-permute-start(bf16[2,288,512]{2,1,0:T(8,128)(2,1)S(1)} %collective-permute-done.12), channel_id=1, source_target_pairs={{0,4},{4,8},{8,12},{12,14},{14,10},{10,6},{6,2},{2,0},{1,5},{5,9},... | collective-permute-start | bytes 1769480 | tf_op jit(solution)/shard_map/ppermute | solution.py:105
  99.4 12.0 %collective-permute-start.16 = (bf16[2,288,512]{2,1,0:T(8,128)(2,1)S(1)}, bf16[2,288,512]{2,1,0:T(8,128)(2,1)S(1)}, u32[]{:S(2)}, u32[]{:S(2)}) collective-permute-start(bf16[2,288,512]{2,1,0:T(8,128)(2,1)S(1)} %collective-permute-done.13), channel_id=1, source_target_pairs={{0,2},{4,0},{8,4},{12,8},{14,12},{10,14},{6,10},{2,6},{1,3},{5,1},... | collective-permute-start | bytes 1769480 | tf_op jit(solution)/shard_map/ppermute | solution.py:106
  111.6 14.5 %collective-permute-start.17 = (bf16[2,288,512]{2,1,0:T(8,128)(2,1)S(1)}, bf16[2,288,512]{2,1,0:T(8,128)(2,1)S(1)}, u32[]{:S(2)}, u32[]{:S(2)}) collective-permute-start(bf16[2,288,512]{2,1,0:T(8,128)(2,1)S(1)} %pad_maximum_fusion.22), channel_id=1, source_target_pairs={{0,16},{16,0},{1,17},{17,1},{2,18},{18,2},{3,19},{19,3},{4,20},{20... | collective-permute-start | bytes 1769480 | tf_op jit(solution)/shard_map/ppermute | solution.py:110
  114.6 24.5 %copy-start.4 = (bf16[288,1536]{1,0:T(8,128)(2,1)}, bf16[288,1536]{1,0:T(8,128)(2,1)S(1)}, u32[]{:S(2)}) copy-start(bf16[288,1536]{1,0:T(8,128)(2,1)S(1)} %pad_maximum_fusion.11) | copy-start | bytes 2654212
  114.7 9.9 %collective-permute-start.18 = (bf16[2,288,512]{2,1,0:T(8,128)(2,1)S(1)}, bf16[2,288,512]{2,1,0:T(8,128)(2,1)S(1)}, u32[]{:S(2)}, u32[]{:S(2)}) collective-permute-start(bf16[2,288,512]{2,1,0:T(8,128)(2,1)S(1)} %collective-permute-done.15), channel_id=1, source_target_pairs={{0,4},{4,8},{8,12},{12,14},{14,10},{10,6},{6,2},{2,0},{1,5},{5,9},... | collective-permute-start | bytes 1769480 | tf_op jit(solution)/shard_map/ppermute | solution.py:105
  115.3 9.9 %collective-permute-start.19 = (bf16[2,288,512]{2,1,0:T(8,128)(2,1)S(1)}, bf16[2,288,512]{2,1,0:T(8,128)(2,1)S(1)}, u32[]{:S(2)}, u32[]{:S(2)}) collective-permute-start(bf16[2,288,512]{2,1,0:T(8,128)(2,1)S(1)} %collective-permute-done.16), channel_id=1, source_target_pairs={{0,2},{4,0},{8,4},{12,8},{14,12},{10,14},{6,10},{2,6},{1,3},{5,1},... | collective-permute-start | bytes 1769480 | tf_op jit(solution)/shard_map/ppermute | solution.py:106
  117.3 18.8 %copy-start.14 = (bf16[1536,2304]{0,1:T(8,128)(2,1)}, bf16[1536,2304]{0,1:T(8,128)(2,1)S(1)}, u32[]{:S(2)}) copy-start(bf16[1536,2304]{0,1:T(8,128)(2,1)S(1)} %bitcast_dynamic-update-slice_fusion.2) | copy-start | bytes 21233668
  125.3 9.9 %collective-permute-start.20 = (bf16[2,288,512]{2,1,0:T(8,128)(2,1)S(1)}, bf16[2,288,512]{2,1,0:T(8,128)(2,1)S(1)}, u32[]{:S(2)}, u32[]{:S(2)}) collective-permute-start(bf16[2,288,512]{2,1,0:T(8,128)(2,1)S(1)} %pad_maximum_fusion.23), channel_id=1, source_target_pairs={{0,16},{16,0},{1,17},{17,1},{2,18},{18,2},{3,19},{19,3},{4,20},{20... | collective-permute-start | bytes 1769480 | tf_op jit(solution)/shard_map/ppermute | solution.py:110
  126.3 12.6 %copy-start.6 = (bf16[288,1536]{1,0:T(8,128)(2,1)}, bf16[288,1536]{1,0:T(8,128)(2,1)S(1)}, u32[]{:S(2)}) copy-start(bf16[288,1536]{1,0:T(8,128)(2,1)S(1)} %pad_maximum_fusion.13) | copy-start | bytes 2654212
  145.2 8.4 %copy-start.29 = (bf16[4,128,64]{2,1,0:T(8,128)(2,1)}, bf16[4,128,64]{2,1,0:T(8,128)(2,1)S(1)}, u32[]{:S(2)}) copy-start(bf16[4,128,64]{2,1,0:T(8,128)(2,1)S(1)} %get-tuple-element.104) | copy-start | bytes 196612
  145.2 8.4 %copy-start.30 = (bf16[4,128,64]{2,1,0:T(8,128)(2,1)}, bf16[4,128,64]{2,1,0:T(8,128)(2,1)S(1)}, u32[]{:S(2)}) copy-start(bf16[4,128,64]{2,1,0:T(8,128)(2,1)S(1)} %get-tuple-element.105) | copy-start | bytes 196612
  154.0 16.8 %copy-start.51 = (f32[4,2,128]{2,1,0:T(2,128)}, f32[4,2,128]{2,1,0:T(2,128)S(1)}, u32[]{:S(2)}) copy-start(f32[4,2,128]{2,1,0:T(2,128)S(1)} %get-tuple-element.114) | copy-start | bytes 12292
  158.9 2.3 %collective-permute-start.21 = (bf16[128,2304]{1,0:T(8,128)(2,1)S(1)}, bf16[128,2304]{1,0:T(8,128)(2,1)S(1)}, u32[]{:S(2)}, u32[]{:S(2)}) collective-permute-start(bf16[128,2304]{1,0:T(8,128)(2,1)S(1)} %fusion.8), channel_id=1, source_target_pairs={{0,1},{1,0},{2,3},{3,2},{4,5},{5,4},{6,7},{7,6},{8,9},{9,8},{10,11... | collective-permute-start | bytes 1769480 | tf_op jit(solution)/shard_map/ppermute | solution.py:58
  161.2 3.1 %slice-start = ((s8[7077888]{0:T(1024)(128)(4,1)}), s8[4194304]{0:T(1024)(128)(4,1)S(1)}, s32[]{:S(2)}) async-start(s8[7077888]{0:T(1024)(128)(4,1)} %bitcast.254), calls=%async_computation.2 | async-start | bytes 8388608
  163.6 3.1 %copy-start.44 = (f32[128]{0:T(128)}, f32[128]{0:T(128)S(1)}, u32[]{:S(2)}) copy-start(f32[128]{0:T(128)S(1)} %broadcast_multiply_fusion.2) | copy-start | bytes 1540
  166.7 3.1 %copy-start.23 = (bf16[128,512]{1,0:T(8,128)(2,1)S(1)}, bf16[128,512]{1,0:T(8,128)(2,1)}, u32[]{:S(2)}) copy-start(bf16[128,512]{1,0:T(8,128)(2,1)} %fusion.29) | copy-start | bytes 393220
  181.6 4.0 %copy-start.24 = (bf16[128,4,128]{0,2,1:T(8,128)(2,1)S(1)}, bf16[128,4,128]{0,2,1:T(8,128)(2,1)}, u32[]{:S(2)}) copy-start(bf16[128,4,128]{0,2,1:T(8,128)(2,1)} %copy.74) | copy-start | bytes 393220
  190.9 4.7 %collective-permute-start.22 = (bf16[128,2304]{1,0:T(8,128)(2,1)S(1)}, bf16[128,2304]{1,0:T(8,128)(2,1)}, u32[]{:S(2)}, u32[]{:S(2)}) collective-permute-start(bf16[128,2304]{1,0:T(8,128)(2,1)S(1)} %fusion.7), channel_id=1, source_target_pairs={{0,1},{1,0},{2,3},{3,2},{4,5},{5,4},{6,7},{7,6},{8,9},{9,8},{10,11... | collective-permute-start | bytes 1769480 | tf_op jit(solution)/shard_map/ppermute | solution.py:58
  (30 other events, 47.5 us)

commit v13 on v10

--- a/solution.py
+++ b/solution.py
@@ -124,7 +124,7 @@
                 (front_pieces[step], back_pieces[step], front_ring[step + 1], back_ring[step + 1])
             )
     back_pieces = [back_pieces[(n - k) % n] for k in range(n)]
-    return front_pieces, back_pieces, block_of, slot_of
+    return front_pieces, back_pieces, block_of, slot_of, (front_ring[1], back_ring[1])
 
 
 def permute_blocks(values, block_order, n):
@@ -151,14 +151,15 @@
     seq_rank = lax.axis_index("seq")
     core_rank = lax.axis_index("wg")
     guard_half = lax.all_to_all(generator_rows, "seq", split_axis=0, concat_axis=0, tiled=True)
-    guard_rows = lax.all_gather(guard_half, "wg", axis=1, tiled=True)
     q_cols = query_weight.shape[1]
     k_cols = key_weight.shape[1]
     front = jnp.concatenate([query_weight, key_weight], axis=1)
     back = jnp.concatenate([value_weight, out_weight.T], axis=1)
-    front_pieces, back_pieces, block_of, slot_of = ring_gather(
+    front_pieces, back_pieces, block_of, slot_of, first_arrival = ring_gather(
         front, back, seq_rank, lax.axis_index("groups"), n_seq
     )
+    guard_half, _ = lax.optimization_barrier((guard_half, first_arrival))
+    guard_rows = lax.all_gather(guard_half, "wg", axis=1, tiled=True)
     guard_rows = permute_blocks(guard_rows, block_of, n_seq)
     pre_gain, post_gain, final_gain = permute_blocks(
         jnp.stack([pre_gain, post_gain, final_gain]), block_of, n_seq

time: 208 us -> 205 us (0.986)
  waiting for transfers between devices: 78.4 us -> 71 us
  starting transfers between devices: 30.4 us -> 34.2 us
    all_to_all x1, waiting for transfers between devices: 5.58 us -> 1.28 us  [shards(): lax.all_to_all(generator_rows, 'seq', split_axis=0, concat_axis=0, tiled=...]
    ppermute x7, waiting for transfers between devices: 44.4 us -> 40.2 us  [ring_gather(): lax.ppermute(jnp.stack([front_ring[step][0], back_ring[step][0]]), 'group...]
    ppermute x7, starting transfers between devices: 8.12 us -> 11.9 us  [ring_gather(): lax.ppermute(jnp.stack([front_ring[step][0], back_ring[step][0]]), 'group...]
  transfers between devices with their start and end apart: 24 -> 24, of which waited for: 16 -> 18; matrix products, arithmetic and copies ran while one was open for 13% -> 14% of each run, Pallas kernels for 0% -> 0%
where the time goes in v13:
time: 205 us; the launch traced here: 204 us
  waiting for transfers between devices  71 us (35%)
  starting transfers between devices  34.2 us (17%)
  local copies, waits for them, and re-layouts  32.7 us (16%)
  other arithmetic  24.7 us (12%)
  matrix products  22.7 us (11%)
  blocking collectives  17.7 us (9%)
    ppermute x7, waiting for transfers between devices, ring_gather(): lax.ppermute(jnp.stack([front_ring[step][0], back_ring[step][0]]), 'group...  40.2 us
    ppermute x7, waiting for transfers between devices, ring_gather(): front_ring.append(lax.ppermute(front_ring[-1], 'seq', forward_pairs))  19.2 us
    all_to_all x1, blocking collectives, shards(): lax.all_to_all(grad_rows, 'seq', split_axis=0, concat_axis=0, tiled=True)  15.3 us
    unnamed x141, local copies, waits for them, and re-layouts  14.6 us
    ppermute x7, starting transfers between devices, ring_gather(): lax.ppermute(jnp.stack([front_ring[step][0], back_ring[step][0]]), 'group...  11.9 us
    ppermute x7, waiting for transfers between devices, ring_gather(): back_ring.append(lax.ppermute(back_ring[-1], 'seq', backward_pairs))  10.3 us
    ppermute x7, starting transfers between devices, ring_gather(): front_ring.append(lax.ppermute(front_ring[-1], 'seq', forward_pairs))  7.9 us
    ppermute x7, starting transfers between devices, ring_gather(): back_ring.append(lax.ppermute(back_ring[-1], 'seq', backward_pairs))  7.53 us
  transfers between devices with their start and end apart: 24, of which 18 were waited for; matrix products, arithmetic and copies ran while one was open for 14% of the time, Pallas kernels for 0%

profile of v13, /device:TPU:0, one launch (start us, length us, event | category | flops | bytes accessed | tf_op | source)
XLA Modules:
  0.0 204.5 jit_solution(16165219202961558408)
XLA Ops:
  0.0 1.4 fusion.39
  2.4 3.0 %collective-permute-start = (bf16[2,288,512]{2,1,0:T(8,128)(2,1)}, bf16[2,288,512]{2,1,0:T(8,128)(2,1)}, u32[]{:S(2)}, u32[]{:S(2)}) collective-permute-start(bf16[2,288,512]{2,1,0:T(8,128)(2,1)} %pad_maximum_fusion.14), channel_id=1, source_target_pairs={{0,4},{4,8},{8,12},{12,14},{14,10},{10,6},{6,2},{2,0},{1,5},{5,9},... | collective-permute-start | bytes 1769480 | tf_op jit(solution)/shard_map/ppermute | solution.py:105
  6.3 6.3 %all-to-all-start = ((bf16[8,16,1152]{2,1,0:T(8,128)(2,1)}), bf16[8,16,1152]{2,1,0:T(8,128)(2,1)}, u32[]{:S(2)}, u32[]{:S(2)}) async-start(bf16[8,16,1152]{2,1,0:T(8,128)(2,1)} %bitcast.1), calls=%async_computation | async-start | bytes 589824 | tf_op jit(solution)/shard_map/all_to_all | solution.py:153
  17.4 1.0 gather.32
  20.8 1.1 compare_convert_fusion
  21.9 1.1 pad_maximum_fusion
  23.0 1.0 slice.408
  24.0 1.0 slice.409
  25.9 1.5 collective-permute-start.2
  27.4 1.3 all-to-all-done
  28.7 2.4 %all_gather.3 = bf16[128,2304]{1,0:T(8,128)(2,1)S(1)} all-gather(bf16[128,1152]{1,0:T(8,128)(2,1)} %bitcast.2), channel_id=1, replica_groups=mesh['groups'=2,'seq'=8,'wg'=2] {'wg'}, dimensions={1}, use_global_device_ids=true | all-gather | bytes 884736 | tf_op jit(solution)/shard_map/all_gather | solution.py:162
  35.5 1.3 collective-permute-start.4
  37.9 12.4 %collective-permute-done.3 = bf16[2,288,512]{2,1,0:T(8,128)(2,1)S(1)} collective-permute-done((bf16[2,288,512]{2,1,0:T(8,128)(2,1)}, bf16[2,288,512]{2,1,0:T(8,128)(2,1)S(1)}, u32[]{:S(2)}, u32[]{:S(2)}) %collective-permute-start.3) | collective-permute-done | bytes 589856 | tf_op jit(solution)/shard_map/ppermute | solution.py:105
  50.9 1.2 collective-permute-start.5
  52.0 1.5 select_bitcast_fusion.23
  53.7 1.2 collective-permute-start.6
  56.3 8.8 %collective-permute-done.5 = bf16[2,288,512]{2,1,0:T(8,128)(2,1)S(1)} collective-permute-done((bf16[2,288,512]{2,1,0:T(8,128)(2,1)S(1)}, bf16[2,288,512]{2,1,0:T(8,128)(2,1)S(1)}, u32[]{:S(2)}, u32[]{:S(2)}) %collective-permute-start.5) | collective-permute-done | bytes 589856 | tf_op jit(solution)/shard_map/ppermute | solution.py:110
  65.5 2.6 %collective-permute-done.6 = bf16[2,288,512]{2,1,0:T(8,128)(2,1)S(1)} collective-permute-done((bf16[2,288,512]{2,1,0:T(8,128)(2,1)S(1)}, bf16[2,288,512]{2,1,0:T(8,128)(2,1)S(1)}, u32[]{:S(2)}, u32[]{:S(2)}) %collective-permute-start.6) | collective-permute-done | bytes 589856 | tf_op jit(solution)/shard_map/ppermute | solution.py:105
  68.8 1.2 collective-permute-start.8
  70.7 1.4 collective-permute-start.9
  72.6 9.0 %collective-permute-done.8 = bf16[2,288,512]{2,1,0:T(8,128)(2,1)S(1)} collective-permute-done((bf16[2,288,512]{2,1,0:T(8,128)(2,1)S(1)}, bf16[2,288,512]{2,1,0:T(8,128)(2,1)S(1)}, u32[]{:S(2)}, u32[]{:S(2)}) %collective-permute-start.8) | collective-permute-done | bytes 589856 | tf_op jit(solution)/shard_map/ppermute | solution.py:110
  83.0 2.5 %collective-permute-start.11 = (bf16[2,288,512]{2,1,0:T(8,128)(2,1)S(1)}, bf16[2,288,512]{2,1,0:T(8,128)(2,1)S(1)}, u32[]{:S(2)}, u32[]{:S(2)}) collective-permute-start(bf16[2,288,512]{2,1,0:T(8,128)(2,1)S(1)} %pad_maximum_fusion.19), channel_id=1, source_target_pairs={{0,16},{16,0},{1,17},{17,1},{2,18},{18,2},{3,19},{19,3},{4,20},{20... | collective-permute-start | bytes 1769480 | tf_op jit(solution)/shard_map/ppermute | solution.py:110
  85.6 2.0 collective-permute-start.13
  88.1 7.3 %collective-permute-done.11 = bf16[2,288,512]{2,1,0:T(8,128)(2,1)S(1)} collective-permute-done((bf16[2,288,512]{2,1,0:T(8,128)(2,1)S(1)}, bf16[2,288,512]{2,1,0:T(8,128)(2,1)S(1)}, u32[]{:S(2)}, u32[]{:S(2)}) %collective-permute-start.11) | collective-permute-done | bytes 589856 | tf_op jit(solution)/shard_map/ppermute | solution.py:110
  95.7 1.3 collective-permute-done.12
  97.1 1.9 collective-permute-start.14
  99.3 1.8 collective-permute-start.16
  101.5 7.5 %collective-permute-done.14 = bf16[2,288,512]{2,1,0:T(8,128)(2,1)S(1)} collective-permute-done((bf16[2,288,512]{2,1,0:T(8,128)(2,1)S(1)}, bf16[2,288,512]{2,1,0:T(8,128)(2,1)S(1)}, u32[]{:S(2)}, u32[]{:S(2)}) %collective-permute-start.14) | collective-permute-done | bytes 589856 | tf_op jit(solution)/shard_map/ppermute | solution.py:110
  109.3 1.6 collective-permute-done.15
  110.9 1.3 collective-permute-done.16
  112.3 1.6 collective-permute-start.17
  113.9 1.0 collective-permute-start.19
  114.9 1.0 collective-permute-start.18
  116.5 7.3 %collective-permute-done.19 = bf16[2,288,512]{2,1,0:T(8,128)(2,1)S(1)} collective-permute-done((bf16[2,288,512]{2,1,0:T(8,128)(2,1)S(1)}, bf16[2,288,512]{2,1,0:T(8,128)(2,1)S(1)}, u32[]{:S(2)}, u32[]{:S(2)}) %collective-permute-start.19) | collective-permute-done | bytes 589856 | tf_op jit(solution)/shard_map/ppermute | solution.py:106
  124.9 2.0 collective-permute-start.20
  127.3 7.6 %collective-permute-done.20 = bf16[2,288,512]{2,1,0:T(8,128)(2,1)S(1)} collective-permute-done((bf16[2,288,512]{2,1,0:T(8,128)(2,1)S(1)}, bf16[2,288,512]{2,1,0:T(8,128)(2,1)S(1)}, u32[]{:S(2)}, u32[]{:S(2)}) %collective-permute-start.20) | collective-permute-done | bytes 589856 | tf_op jit(solution)/shard_map/ppermute | solution.py:110
  146.3 2.1 %fusion.28 = bf16[1024,2304]{0,1:T(8,128)(2,1)} fusion(bf16[1024,2304]{0,1:T(8,128)(2,1)} %bitcast_dynamic-update-slice_fusion.13, bf16[288,512]{1,0:T(8,128)(2,1)} %get-tuple-element.71, bf16[288,512]{1,0:T(8,128)(2,1)} %get-tuple-element.72), kind=kLoop, calls=%fused_computation.94 | loop fusion | flops 1179648 | bytes 1179648
  148.4 1.9 bitcast_dynamic-update-slice_fusion.12
  152.2 1.0 bitcast_dynamic-update-slice_fusion.9
  156.4 1.2 copy-done
  157.6 1.7 convolution_convert_fusion
  165.0 1.3 convolution_convert_fusion.2
  167.8 1.7 convolution_bitcast_fusion.1
  169.5 1.9 convolution_multiply_fusion.1
  173.8 4.1 %fusion.41 = f32[128,2304]{1,0:T(8,128)S(1)} fusion(bf16[1024,2304]{0,1:T(8,128)(2,1)} %fusion.29, bf16[16,8,8,128]{3,2,1,0:T(8,128)(2,1)S(1)} %bitcast.296), kind=kOutput, calls=%fused_computation.196 | convolution fusion | flops 603979776 | bytes 6160384 | tf_op jit(solution)/shard_map/dot_general | solution.py:284
  178.9 2.6 %fusion.1 = bf16[128,2304]{1,0:T(8,128)(2,1)S(1)} fusion(f32[128,2304]{1,0:T(8,128)S(1)} %convolution_add_fusion.1, bf16[128,512]{0,1:T(8,128)(2,1)S(1)} %bitcast.301, bf16[512,2304]{0,1:T(8,128)(2,1)} %bitcast_dynamic-update-slice_fusion.16), kind=kOutput, calls=%fused_computation.9 | convolution fusion | flops 302579712 | bytes 4259840 | tf_op jit(solution)/shard_map/dot_general | solution.py:286
  184.5 2.2 %fusion.13 = bf16[128,2304]{1,0:T(8,128)(2,1)S(1)} fusion(bf16[128,2304]{1,0:T(8,128)(2,1)S(1)} %collective-permute-done.22, bf16[128,2304]{1,0:T(8,128)(2,1)S(1)} %fusion.1, f32[128]{0:T(128)S(1)} %broadcast_multiply_fusion, f32[128]{0:T(128)} %get-tuple-element.109, f32[2304]{0:T(1024)S(1)} %mul.519, f32[128]{0:T(128)} %copy-done.43, ...), kind=kLoop, calls=%fused_computation.36 | loop fusion | flops 6488064 | bytes 4742912 | tf_op jit(solution)/shard_map/convert_element_type | solution.py:296
  188.4 15.3 %all_to_all.21 = bf16[8,16,1152]{2,1,0:T(8,128)(2,1)S(1)} all-to-all(bf16[8,16,1152]{2,1,0:T(8,128)(2,1)S(1)} %broadcast_select_fusion.4), channel_id=1, replica_groups=mesh['groups'=2,'seq'=8,'wg'=2] {'seq'}, dimensions={0} | all-to-all | bytes 589824 | tf_op jit(solution)/shard_map/all_to_all | solution.py:298
  (293 shorter events, 56.4 us)
Async XLA Ops:
  1.4 11.2 %copy-start.37 = (f32[2304]{0:T(1024)S(1)}, f32[2304]{0:T(1024)}, u32[]{:S(2)}) copy-start(f32[2304]{0:T(1024)} %param.12) | copy-start | bytes 27652
  1.4 11.2 %copy-start.38 = (f32[2304]{0:T(1024)S(1)}, f32[2304]{0:T(1024)}, u32[]{:S(2)}) copy-start(f32[2304]{0:T(1024)} %param.17) | copy-start | bytes 27652
  1.4 11.3 %copy-start.39 = (f32[2304]{0:T(1024)S(1)}, f32[2304]{0:T(1024)}, u32[]{:S(2)}) copy-start(f32[2304]{0:T(1024)} %param.18) | copy-start | bytes 27652
  1.5 12.5 %copy-start.49 = (s32[8]{0:T(128)S(1)}, s32[8]{0:T(128)}, u32[]{:S(2)}) copy-start(s32[8]{0:T(128)} %param.20) | copy-start | bytes 100
  1.5 14.4 %copy-start.26 = (bf16[64,2304]{1,0:T(8,128)(2,1)S(1)}, bf16[64,2304]{1,0:T(8,128)(2,1)}, u32[]{:S(2)}) copy-start(bf16[64,2304]{1,0:T(8,128)(2,1)} %param.19) | copy-start | bytes 884740
  2.4 20.7 %collective-permute-start = (bf16[2,288,512]{2,1,0:T(8,128)(2,1)}, bf16[2,288,512]{2,1,0:T(8,128)(2,1)}, u32[]{:S(2)}, u32[]{:S(2)}) collective-permute-start(bf16[2,288,512]{2,1,0:T(8,128)(2,1)} %pad_maximum_fusion.14), channel_id=1, source_target_pairs={{0,4},{4,8},{8,12},{12,14},{14,10},{10,6},{6,2},{2,0},{1,5},{5,9},... | collective-permute-start | bytes 1769480 | tf_op jit(solution)/shard_map/ppermute | solution.py:105
  6.2 17.8 %collective-permute-start.1 = (bf16[2,288,512]{2,1,0:T(8,128)(2,1)}, bf16[2,288,512]{2,1,0:T(8,128)(2,1)}, u32[]{:S(2)}, u32[]{:S(2)}) collective-permute-start(bf16[2,288,512]{2,1,0:T(8,128)(2,1)} %pad_maximum_fusion.15), channel_id=1, source_target_pairs={{0,2},{4,0},{8,4},{12,8},{14,12},{10,14},{6,10},{2,6},{1,3},{5,1},... | collective-permute-start | bytes 1769480 | tf_op jit(solution)/shard_map/ppermute | solution.py:106
  6.3 22.4 %all-to-all-start = ((bf16[8,16,1152]{2,1,0:T(8,128)(2,1)}), bf16[8,16,1152]{2,1,0:T(8,128)(2,1)}, u32[]{:S(2)}, u32[]{:S(2)}) async-start(bf16[8,16,1152]{2,1,0:T(8,128)(2,1)} %bitcast.1), calls=%async_computation | async-start | bytes 589824 | tf_op jit(solution)/shard_map/all_to_all | solution.py:153
  15.2 5.5 %copy-start.47 = (pred[128]{0:T(512)(128)(4,1)}, pred[128]{0:T(512)(128)(4,1)S(1)}, u32[]{:S(2)}) copy-start(pred[128]{0:T(512)(128)(4,1)S(1)} %iota_compare_fusion.1) | copy-start | bytes 388
  15.9 3.3 %copy-start.50 = (s32[8]{0:T(128)S(1)}, s32[8]{0:T(128)}, u32[]{:S(2)}) copy-start(s32[8]{0:T(128)} %param.21) | copy-start | bytes 100
  16.5 5.4 %copy-start.10 = (bf16[288,1024]{1,0:T(8,128)(2,1)S(1)}, bf16[288,1024]{1,0:T(8,128)(2,1)}, u32[]{:S(2)}) copy-start(bf16[288,1024]{1,0:T(8,128)(2,1)} %param.13) | copy-start | bytes 1769476
  16.5 5.4 %copy-start.11 = (bf16[1024,288]{0,1:T(8,128)(2,1)S(1)}, bf16[1024,288]{0,1:T(8,128)(2,1)}, u32[]{:S(2)}) copy-start(bf16[1024,288]{0,1:T(8,128)(2,1)} %param.16) | copy-start | bytes 1769476
  16.5 5.4 %copy-start.18 = (bf16[288,512]{1,0:T(8,128)(2,1)S(1)}, bf16[288,512]{1,0:T(8,128)(2,1)}, u32[]{:S(2)}) copy-start(bf16[288,512]{1,0:T(8,128)(2,1)} %param.14) | copy-start | bytes 884740
  20.7 118.2 %copy-start.14 = (f32[128,64]{1,0:T(8,128)}, f32[128,64]{1,0:T(8,128)S(1)}, u32[]{:S(2)}) copy-start(f32[128,64]{1,0:T(8,128)S(1)} %get-tuple-element.107) | copy-start | bytes 98308
  20.7 118.2 %copy-start.16 = (f32[128,64]{1,0:T(8,128)}, f32[128,64]{1,0:T(8,128)S(1)}, u32[]{:S(2)}) copy-start(f32[128,64]{1,0:T(8,128)S(1)} %get-tuple-element.108) | copy-start | bytes 98308
  20.8 134.8 %copy-start.35 = (pred[128,128]{0,1:T(8,128)(4,1)}, pred[128,128]{0,1:T(8,128)(4,1)S(1)}, u32[]{:S(2)}) copy-start(pred[128,128]{0,1:T(8,128)(4,1)S(1)} %fusion.79) | copy-start | bytes 49156
  25.9 26.2 %collective-permute-start.2 = (bf16[2,288,512]{2,1,0:T(8,128)(2,1)}, bf16[2,288,512]{2,1,0:T(8,128)(2,1)}, u32[]{:S(2)}, u32[]{:S(2)}) collective-permute-start(bf16[2,288,512]{2,1,0:T(8,128)(2,1)} %pad_maximum_fusion.16), channel_id=1, source_target_pairs={{0,16},{16,0},{1,17},{17,1},{2,18},{18,2},{3,19},{19,3},{4,20},{20... | collective-permute-start | bytes 1769480 | tf_op jit(solution)/shard_map/ppermute | solution.py:110
  34.7 15.6 %collective-permute-start.3 = (bf16[2,288,512]{2,1,0:T(8,128)(2,1)}, bf16[2,288,512]{2,1,0:T(8,128)(2,1)S(1)}, u32[]{:S(2)}, u32[]{:S(2)}) collective-permute-start(bf16[2,288,512]{2,1,0:T(8,128)(2,1)} %collective-permute-done), channel_id=1, source_target_pairs={{0,4},{4,8},{8,12},{12,14},{14,10},{10,6},{6,2},{2,0},{1,5},{5,9},... | collective-permute-start | bytes 1769480 | tf_op jit(solution)/shard_map/ppermute | solution.py:105
  35.5 15.3 %collective-permute-start.4 = (bf16[2,288,512]{2,1,0:T(8,128)(2,1)}, bf16[2,288,512]{2,1,0:T(8,128)(2,1)S(1)}, u32[]{:S(2)}, u32[]{:S(2)}) collective-permute-start(bf16[2,288,512]{2,1,0:T(8,128)(2,1)} %collective-permute-done.1), channel_id=1, source_target_pairs={{0,2},{4,0},{8,4},{12,8},{14,12},{10,14},{6,10},{2,6},{1,3},{5,1},... | collective-permute-start | bytes 1769480 | tf_op jit(solution)/shard_map/ppermute | solution.py:106
  50.9 14.3 %collective-permute-start.5 = (bf16[2,288,512]{2,1,0:T(8,128)(2,1)S(1)}, bf16[2,288,512]{2,1,0:T(8,128)(2,1)S(1)}, u32[]{:S(2)}, u32[]{:S(2)}) collective-permute-start(bf16[2,288,512]{2,1,0:T(8,128)(2,1)S(1)} %pad_maximum_fusion.17), channel_id=1, source_target_pairs={{0,16},{16,0},{1,17},{17,1},{2,18},{18,2},{3,19},{19,3},{4,20},{20... | collective-permute-start | bytes 1769480 | tf_op jit(solution)/shard_map/ppermute | solution.py:110
  53.7 14.3 %collective-permute-start.6 = (bf16[2,288,512]{2,1,0:T(8,128)(2,1)S(1)}, bf16[2,288,512]{2,1,0:T(8,128)(2,1)S(1)}, u32[]{:S(2)}, u32[]{:S(2)}) collective-permute-start(bf16[2,288,512]{2,1,0:T(8,128)(2,1)S(1)} %collective-permute-done.3), channel_id=1, source_target_pairs={{0,4},{4,8},{8,12},{12,14},{14,10},{10,6},{6,2},{2,0},{1,5},{5,9},... | collective-permute-start | bytes 1769480 | tf_op jit(solution)/shard_map/ppermute | solution.py:105
  55.0 13.7 %collective-permute-start.7 = (bf16[2,288,512]{2,1,0:T(8,128)(2,1)S(1)}, bf16[2,288,512]{2,1,0:T(8,128)(2,1)S(1)}, u32[]{:S(2)}, u32[]{:S(2)}) collective-permute-start(bf16[2,288,512]{2,1,0:T(8,128)(2,1)S(1)} %collective-permute-done.4), channel_id=1, source_target_pairs={{0,2},{4,0},{8,4},{12,8},{14,12},{10,14},{6,10},{2,6},{1,3},{5,1},... | collective-permute-start | bytes 1769480 | tf_op jit(solution)/shard_map/ppermute | solution.py:106
  68.8 12.8 %collective-permute-start.8 = (bf16[2,288,512]{2,1,0:T(8,128)(2,1)S(1)}, bf16[2,288,512]{2,1,0:T(8,128)(2,1)S(1)}, u32[]{:S(2)}, u32[]{:S(2)}) collective-permute-start(bf16[2,288,512]{2,1,0:T(8,128)(2,1)S(1)} %pad_maximum_fusion.18), channel_id=1, source_target_pairs={{0,16},{16,0},{1,17},{17,1},{2,18},{18,2},{3,19},{19,3},{4,20},{20... | collective-permute-start | bytes 1769480 | tf_op jit(solution)/shard_map/ppermute | solution.py:110
  70.0 12.5 %collective-permute-start.10 = (bf16[2,288,512]{2,1,0:T(8,128)(2,1)S(1)}, bf16[2,288,512]{2,1,0:T(8,128)(2,1)S(1)}, u32[]{:S(2)}, u32[]{:S(2)}) collective-permute-start(bf16[2,288,512]{2,1,0:T(8,128)(2,1)S(1)} %collective-permute-done.7), channel_id=1, source_target_pairs={{0,2},{4,0},{8,4},{12,8},{14,12},{10,14},{6,10},{2,6},{1,3},{5,1},... | collective-permute-start | bytes 1769480 | tf_op jit(solution)/shard_map/ppermute | solution.py:106
  70.7 12.2 %collective-permute-start.9 = (bf16[2,288,512]{2,1,0:T(8,128)(2,1)S(1)}, bf16[2,288,512]{2,1,0:T(8,128)(2,1)S(1)}, u32[]{:S(2)}, u32[]{:S(2)}) collective-permute-start(bf16[2,288,512]{2,1,0:T(8,128)(2,1)S(1)} %collective-permute-done.6), channel_id=1, source_target_pairs={{0,4},{4,8},{8,12},{12,14},{14,10},{10,6},{6,2},{2,0},{1,5},{5,9},... | collective-permute-start | bytes 1769480 | tf_op jit(solution)/shard_map/ppermute | solution.py:105
  83.0 12.4 %collective-permute-start.11 = (bf16[2,288,512]{2,1,0:T(8,128)(2,1)S(1)}, bf16[2,288,512]{2,1,0:T(8,128)(2,1)S(1)}, u32[]{:S(2)}, u32[]{:S(2)}) collective-permute-start(bf16[2,288,512]{2,1,0:T(8,128)(2,1)S(1)} %pad_maximum_fusion.19), channel_id=1, source_target_pairs={{0,16},{16,0},{1,17},{17,1},{2,18},{18,2},{3,19},{19,3},{4,20},{20... | collective-permute-start | bytes 1769480 | tf_op jit(solution)/shard_map/ppermute | solution.py:110
  85.5 11.4 %collective-permute-start.12 = (bf16[2,288,512]{2,1,0:T(8,128)(2,1)S(1)}, bf16[2,288,512]{2,1,0:T(8,128)(2,1)S(1)}, u32[]{:S(2)}, u32[]{:S(2)}) collective-permute-start(bf16[2,288,512]{2,1,0:T(8,128)(2,1)S(1)} %collective-permute-done.9), channel_id=1, source_target_pairs={{0,4},{4,8},{8,12},{12,14},{14,10},{10,6},{6,2},{2,0},{1,5},{5,9},... | collective-permute-start | bytes 1769480 | tf_op jit(solution)/shard_map/ppermute | solution.py:105
  85.6 11.4 %collective-permute-start.13 = (bf16[2,288,512]{2,1,0:T(8,128)(2,1)S(1)}, bf16[2,288,512]{2,1,0:T(8,128)(2,1)S(1)}, u32[]{:S(2)}, u32[]{:S(2)}) collective-permute-start(bf16[2,288,512]{2,1,0:T(8,128)(2,1)S(1)} %collective-permute-done.10), channel_id=1, source_target_pairs={{0,2},{4,0},{8,4},{12,8},{14,12},{10,14},{6,10},{2,6},{1,3},{5,1},... | collective-permute-start | bytes 1769480 | tf_op jit(solution)/shard_map/ppermute | solution.py:106
  95.6 48.1 %copy-start.2 = (bf16[288,1536]{1,0:T(8,128)(2,1)}, bf16[288,1536]{1,0:T(8,128)(2,1)S(1)}, u32[]{:S(2)}) copy-start(bf16[288,1536]{1,0:T(8,128)(2,1)S(1)} %pad_maximum_fusion.9) | copy-start | bytes 2654212
  97.1 11.9 %collective-permute-start.14 = (bf16[2,288,512]{2,1,0:T(8,128)(2,1)S(1)}, bf16[2,288,512]{2,1,0:T(8,128)(2,1)S(1)}, u32[]{:S(2)}, u32[]{:S(2)}) collective-permute-start(bf16[2,288,512]{2,1,0:T(8,128)(2,1)S(1)} %pad_maximum_fusion.20), channel_id=1, source_target_pairs={{0,16},{16,0},{1,17},{17,1},{2,18},{18,2},{3,19},{19,3},{4,20},{20... | collective-permute-start | bytes 1769480 | tf_op jit(solution)/shard_map/ppermute | solution.py:110
  99.0 11.9 %collective-permute-start.15 = (bf16[2,288,512]{2,1,0:T(8,128)(2,1)S(1)}, bf16[2,288,512]{2,1,0:T(8,128)(2,1)S(1)}, u32[]{:S(2)}, u32[]{:S(2)}) collective-permute-start(bf16[2,288,512]{2,1,0:T(8,128)(2,1)S(1)} %collective-permute-done.12), channel_id=1, source_target_pairs={{0,4},{4,8},{8,12},{12,14},{14,10},{10,6},{6,2},{2,0},{1,5},{5,9},... | collective-permute-start | bytes 1769480 | tf_op jit(solution)/shard_map/ppermute | solution.py:105
  99.3 12.9 %collective-permute-start.16 = (bf16[2,288,512]{2,1,0:T(8,128)(2,1)S(1)}, bf16[2,288,512]{2,1,0:T(8,128)(2,1)S(1)}, u32[]{:S(2)}, u32[]{:S(2)}) collective-permute-start(bf16[2,288,512]{2,1,0:T(8,128)(2,1)S(1)} %collective-permute-done.13), channel_id=1, source_target_pairs={{0,2},{4,0},{8,4},{12,8},{14,12},{10,14},{6,10},{2,6},{1,3},{5,1},... | collective-permute-start | bytes 1769480 | tf_op jit(solution)/shard_map/ppermute | solution.py:106
  109.2 33.5 %copy-start.4 = (bf16[288,1536]{1,0:T(8,128)(2,1)}, bf16[288,1536]{1,0:T(8,128)(2,1)S(1)}, u32[]{:S(2)}) copy-start(bf16[288,1536]{1,0:T(8,128)(2,1)S(1)} %pad_maximum_fusion.11) | copy-start | bytes 2654212
  112.3 14.6 %collective-permute-start.17 = (bf16[2,288,512]{2,1,0:T(8,128)(2,1)S(1)}, bf16[2,288,512]{2,1,0:T(8,128)(2,1)S(1)}, u32[]{:S(2)}, u32[]{:S(2)}) collective-permute-start(bf16[2,288,512]{2,1,0:T(8,128)(2,1)S(1)} %pad_maximum_fusion.21), channel_id=1, source_target_pairs={{0,16},{16,0},{1,17},{17,1},{2,18},{18,2},{3,19},{19,3},{4,20},{20... | collective-permute-start | bytes 1769480 | tf_op jit(solution)/shard_map/ppermute | solution.py:110
  113.9 9.9 %collective-permute-start.19 = (bf16[2,288,512]{2,1,0:T(8,128)(2,1)S(1)}, bf16[2,288,512]{2,1,0:T(8,128)(2,1)S(1)}, u32[]{:S(2)}, u32[]{:S(2)}) collective-permute-start(bf16[2,288,512]{2,1,0:T(8,128)(2,1)S(1)} %collective-permute-done.16), channel_id=1, source_target_pairs={{0,2},{4,0},{8,4},{12,8},{14,12},{10,14},{6,10},{2,6},{1,3},{5,1},... | collective-permute-start | bytes 1769480 | tf_op jit(solution)/shard_map/ppermute | solution.py:106
  114.9 9.9 %collective-permute-start.18 = (bf16[2,288,512]{2,1,0:T(8,128)(2,1)S(1)}, bf16[2,288,512]{2,1,0:T(8,128)(2,1)S(1)}, u32[]{:S(2)}, u32[]{:S(2)}) collective-permute-start(bf16[2,288,512]{2,1,0:T(8,128)(2,1)S(1)} %collective-permute-done.15), channel_id=1, source_target_pairs={{0,4},{4,8},{8,12},{12,14},{14,10},{10,6},{6,2},{2,0},{1,5},{5,9},... | collective-permute-start | bytes 1769480 | tf_op jit(solution)/shard_map/ppermute | solution.py:105
  124.9 10.0 %collective-permute-start.20 = (bf16[2,288,512]{2,1,0:T(8,128)(2,1)S(1)}, bf16[2,288,512]{2,1,0:T(8,128)(2,1)S(1)}, u32[]{:S(2)}, u32[]{:S(2)}) collective-permute-start(bf16[2,288,512]{2,1,0:T(8,128)(2,1)S(1)} %pad_maximum_fusion.22), channel_id=1, source_target_pairs={{0,16},{16,0},{1,17},{17,1},{2,18},{18,2},{3,19},{19,3},{4,20},{20... | collective-permute-start | bytes 1769480 | tf_op jit(solution)/shard_map/ppermute | solution.py:110
  127.1 14.6 %copy-start.6 = (bf16[288,1536]{1,0:T(8,128)(2,1)}, bf16[288,1536]{1,0:T(8,128)(2,1)S(1)}, u32[]{:S(2)}) copy-start(bf16[288,1536]{1,0:T(8,128)(2,1)S(1)} %pad_maximum_fusion.13) | copy-start | bytes 2654212
  127.3 9.0 %copy-start.1 = (bf16[1024,2304]{0,1:T(8,128)(2,1)}, bf16[1024,2304]{0,1:T(8,128)(2,1)S(1)}, u32[]{:S(2)}) copy-start(bf16[1024,2304]{0,1:T(8,128)(2,1)S(1)} %bitcast_dynamic-update-slice_fusion) | copy-start | bytes 14155780
  139.7 15.5 %copy-start.31 = (bf16[4,128,64]{2,1,0:T(8,128)(2,1)}, bf16[4,128,64]{2,1,0:T(8,128)(2,1)S(1)}, u32[]{:S(2)}) copy-start(bf16[4,128,64]{2,1,0:T(8,128)(2,1)S(1)} %get-tuple-element.105) | copy-start | bytes 196612
  145.5 5.7 %copy-start.19 = (bf16[128,512]{1,0:T(8,128)(2,1)}, bf16[128,512]{1,0:T(8,128)(2,1)S(1)}, u32[]{:S(2)}) copy-start(bf16[128,512]{1,0:T(8,128)(2,1)S(1)} %fusion.15) | copy-start | bytes 393220
  146.3 4.0 %copy-start.5 = (bf16[288,1536]{1,0:T(8,128)(2,1)S(1)}, bf16[288,1536]{1,0:T(8,128)(2,1)}, u32[]{:S(2)}) copy-start(bf16[288,1536]{1,0:T(8,128)(2,1)} %copy-done.4) | copy-start | bytes 2654212
  146.3 4.9 %copy-start.3 = (bf16[288,1536]{1,0:T(8,128)(2,1)S(1)}, bf16[288,1536]{1,0:T(8,128)(2,1)}, u32[]{:S(2)}) copy-start(bf16[288,1536]{1,0:T(8,128)(2,1)} %copy-done.2) | copy-start | bytes 2654212
  159.2 2.8 %copy-start.30 = (f32[2304]{0:T(1024)S(1)}, f32[2304]{0:T(1024)}, u32[]{:S(2)}) copy-start(f32[2304]{0:T(1024)} %mul.542) | copy-start | bytes 27652
  159.2 2.5 %collective-permute-start.21 = (bf16[128,2304]{1,0:T(8,128)(2,1)S(1)}, bf16[128,2304]{1,0:T(8,128)(2,1)S(1)}, u32[]{:S(2)}, u32[]{:S(2)}) collective-permute-start(bf16[128,2304]{1,0:T(8,128)(2,1)S(1)} %convolution_convert_fusion), channel_id=1, source_target_pairs={{0,1},{1,0},{2,3},{3,2},{4,5},{5,4},{6,7},{7,6},{8,9},{9,8},{10,11... | collective-permute-start | bytes 1769480 | tf_op jit(solution)/shard_map/ppermute | solution.py:58
  173.7 4.2 %copy-start.9 = (bf16[512,2304]{0,1:T(8,128)(2,1)S(1)}, bf16[512,2304]{0,1:T(8,128)(2,1)}, u32[]{:S(2)}) copy-start(bf16[512,2304]{0,1:T(8,128)(2,1)} %copy-done.8) | copy-start | bytes 7077892
  173.8 4.2 %copy-start.25 = (bf16[128,4,128]{0,2,1:T(8,128)(2,1)S(1)}, bf16[128,4,128]{0,2,1:T(8,128)(2,1)}, u32[]{:S(2)}) copy-start(bf16[128,4,128]{0,2,1:T(8,128)(2,1)} %copy.74) | copy-start | bytes 393220
  181.5 2.7 %collective-permute-start.22 = (bf16[128,2304]{1,0:T(8,128)(2,1)S(1)}, bf16[128,2304]{1,0:T(8,128)(2,1)S(1)}, u32[]{:S(2)}, u32[]{:S(2)}) collective-permute-start(bf16[128,2304]{1,0:T(8,128)(2,1)S(1)} %fusion.1), channel_id=1, source_target_pairs={{0,1},{1,0},{2,3},{3,2},{4,5},{5,4},{6,7},{7,6},{8,9},{9,8},{10,11... | collective-permute-start | bytes 1769480 | tf_op jit(solution)/shard_map/ppermute | solution.py:58
  (32 other events, 51.5 us)

commit v14 on v13

--- a/solution.py
+++ b/solution.py
@@ -124,7 +124,7 @@
                 (front_pieces[step], back_pieces[step], front_ring[step + 1], back_ring[step + 1])
             )
     back_pieces = [back_pieces[(n - k) % n] for k in range(n)]
-    return front_pieces, back_pieces, block_of, slot_of, (front_ring[1], back_ring[1])
+    return front_pieces, back_pieces, block_of, slot_of, (front_ring[2], back_ring[2])
 
 
 def permute_blocks(values, block_order, n):

time: 205 us -> 207 us (level)
  local copies, waits for them, and re-layouts: 32.7 us -> 37.1 us
  starting transfers between devices: 34.2 us -> 30 us
    unnamed x141 -> x151, local copies, waits for them, and re-layouts: 14.6 us -> 22 us
    ppermute x7, waiting for transfers between devices: 40.2 us -> 34.8 us  [ring_gather(): lax.ppermute(jnp.stack([front_ring[step][0], back_ring[step][0]]), 'group...]
    ppermute x7, starting transfers between devices: 11.9 us -> 7.75 us  [ring_gather(): lax.ppermute(jnp.stack([front_ring[step][0], back_ring[step][0]]), 'group...]
    ppermute x7, starting transfers between devices: 7.53 us -> 3.86 us  [ring_gather(): back_ring.append(lax.ppermute(back_ring[-1], 'seq', backward_pairs))]
    ppermute x7, starting transfers between devices: 7.9 us -> 11.6 us  [ring_gather(): front_ring.append(lax.ppermute(front_ring[-1], 'seq', forward_pairs))]
    ppermute x7, waiting for transfers between devices: 10.3 us -> 13.4 us  [ring_gather(): back_ring.append(lax.ppermute(back_ring[-1], 'seq', backward_pairs))]
    ppermute x7, waiting for transfers between devices: 19.2 us -> 22 us  [ring_gather(): front_ring.append(lax.ppermute(front_ring[-1], 'seq', forward_pairs))]
  transfers between devices with their start and end apart: 24 -> 24, of which waited for: 18 -> 16; matrix products, arithmetic and copies ran while one was open for 14% -> 18% of each run, Pallas kernels for 0% -> 0%
where the time goes in v14:
time: 207 us; the launch traced here: 206 us
  waiting for transfers between devices  71 us (34%)
  local copies, waits for them, and re-layouts  37.1 us (18%)
  starting transfers between devices  30 us (14%)
  other arithmetic  25.8 us (12%)
  matrix products  23.8 us (11%)
  blocking collectives  17.2 us (8%)
    ppermute x7, waiting for transfers between devices, ring_gather(): lax.ppermute(jnp.stack([front_ring[step][0], back_ring[step][0]]), 'group...  34.8 us
    ppermute x7, waiting for transfers between devices, ring_gather(): front_ring.append(lax.ppermute(front_ring[-1], 'seq', forward_pairs))  22 us
    unnamed x151, local copies, waits for them, and re-layouts  22 us
    all_to_all x1, blocking collectives, shards(): lax.all_to_all(grad_rows, 'seq', split_axis=0, concat_axis=0, tiled=True)  14.8 us
    ppermute x7, waiting for transfers between devices, ring_gather(): back_ring.append(lax.ppermute(back_ring[-1], 'seq', backward_pairs))  13.4 us
    ppermute x7, starting transfers between devices, ring_gather(): front_ring.append(lax.ppermute(front_ring[-1], 'seq', forward_pairs))  11.6 us
    ppermute x7, starting transfers between devices, ring_gather(): lax.ppermute(jnp.stack([front_ring[step][0], back_ring[step][0]]), 'group...  7.75 us
    all_to_all x1, starting transfers between devices, shards(): lax.all_to_all(generator_rows, 'seq', split_axis=0, concat_axis=0, tiled=...  6.25 us
  transfers between devices with their start and end apart: 24, of which 16 were waited for; matrix products, arithmetic and copies ran while one was open for 18% of the time, Pallas kernels for 0%

profile of v14, /device:TPU:0, one launch (start us, length us, event | category | flops | bytes accessed | tf_op | source)
XLA Modules:
  0.0 206.3 jit_solution(10621105453525330964)
XLA Ops:
  0.0 1.4 fusion.39
  2.4 3.0 %collective-permute-start = (bf16[2,288,512]{2,1,0:T(8,128)(2,1)}, bf16[2,288,512]{2,1,0:T(8,128)(2,1)S(1)}, u32[]{:S(2)}, u32[]{:S(2)}) collective-permute-start(bf16[2,288,512]{2,1,0:T(8,128)(2,1)} %pad_maximum_fusion.14), channel_id=1, source_target_pairs={{0,4},{4,8},{8,12},{12,14},{14,10},{10,6},{6,2},{2,0},{1,5},{5,9},... | collective-permute-start | bytes 1769480 | tf_op jit(solution)/shard_map/ppermute | solution.py:105
  6.3 6.3 %all-to-all-start = ((bf16[8,16,1152]{2,1,0:T(8,128)(2,1)}), bf16[8,16,1152]{2,1,0:T(8,128)(2,1)}, u32[]{:S(2)}, u32[]{:S(2)}) async-start(bf16[8,16,1152]{2,1,0:T(8,128)(2,1)} %bitcast.1), calls=%async_computation | async-start | bytes 589824 | tf_op jit(solution)/shard_map/all_to_all | solution.py:153
  18.2 1.0 gather.32
  21.1 1.2 compare_convert_fusion
  24.6 2.0 collective-permute-start.1
  26.7 1.0 slice.409
  27.7 1.6 collective-permute-start.4
  31.0 8.1 %collective-permute-done.1 = bf16[2,288,512]{2,1,0:T(8,128)(2,1)S(1)} collective-permute-done((bf16[2,288,512]{2,1,0:T(8,128)(2,1)S(1)}, bf16[2,288,512]{2,1,0:T(8,128)(2,1)S(1)}, u32[]{:S(2)}, u32[]{:S(2)}) %collective-permute-start.1) | collective-permute-done | bytes 589856 | tf_op jit(solution)/shard_map/ppermute | solution.py:105
  39.0 2.0 collective-permute-done.3
  42.1 1.5 collective-permute-start.5
  43.6 1.2 select_bitcast_fusion.23
  44.8 1.0 pad_maximum_fusion.3
  45.9 2.4 %all_gather.3 = bf16[128,2304]{1,0:T(8,128)(2,1)S(1)} all-gather(bf16[128,1152]{1,0:T(8,128)(2,1)} %bitcast.2), channel_id=1, replica_groups=mesh['groups'=2,'seq'=8,'wg'=2] {'wg'}, dimensions={1}, use_global_device_ids=true | all-gather | bytes 884736 | tf_op jit(solution)/shard_map/all_gather | solution.py:162
  50.7 1.4 fusion.52
  53.1 1.0 collective-permute-start.6
  54.0 1.1 collective-permute-start.7
  56.0 1.2 select_bitcast_fusion.19
  57.3 11.2 %collective-permute-done.6 = bf16[2,288,512]{2,1,0:T(8,128)(2,1)S(1)} collective-permute-done((bf16[2,288,512]{2,1,0:T(8,128)(2,1)S(1)}, bf16[2,288,512]{2,1,0:T(8,128)(2,1)S(1)}, u32[]{:S(2)}, u32[]{:S(2)}) %collective-permute-start.6) | collective-permute-done | bytes 589856 | tf_op jit(solution)/shard_map/ppermute | solution.py:105
  69.8 1.2 collective-permute-start.10
  73.2 10.3 %collective-permute-done.8 = bf16[2,288,512]{2,1,0:T(8,128)(2,1)S(1)} collective-permute-done((bf16[2,288,512]{2,1,0:T(8,128)(2,1)S(1)}, bf16[2,288,512]{2,1,0:T(8,128)(2,1)S(1)}, u32[]{:S(2)}, u32[]{:S(2)}) %collective-permute-start.8) | collective-permute-done | bytes 589856 | tf_op jit(solution)/shard_map/ppermute | solution.py:110
  83.8 1.3 collective-permute-done.9
  85.3 1.1 collective-permute-start.11
  87.3 1.1 collective-permute-start.13
  89.8 8.7 %collective-permute-done.11 = bf16[2,288,512]{2,1,0:T(8,128)(2,1)S(1)} collective-permute-done((bf16[2,288,512]{2,1,0:T(8,128)(2,1)S(1)}, bf16[2,288,512]{2,1,0:T(8,128)(2,1)S(1)}, u32[]{:S(2)}, u32[]{:S(2)}) %collective-permute-start.11) | collective-permute-done | bytes 589856 | tf_op jit(solution)/shard_map/ppermute | solution.py:110
  99.7 1.4 collective-permute-start.14
  101.1 1.7 collective-permute-start.15
  103.1 1.0 bitcast_dynamic-update-slice_fusion.2
  104.5 6.8 %collective-permute-done.14 = bf16[2,288,512]{2,1,0:T(8,128)(2,1)S(1)} collective-permute-done((bf16[2,288,512]{2,1,0:T(8,128)(2,1)S(1)}, bf16[2,288,512]{2,1,0:T(8,128)(2,1)S(1)}, u32[]{:S(2)}, u32[]{:S(2)}) %collective-permute-start.14) | collective-permute-done | bytes 589856 | tf_op jit(solution)/shard_map/ppermute | solution.py:110
  111.5 1.2 collective-permute-done.15
  112.8 3.2 %collective-permute-done.16 = bf16[2,288,512]{2,1,0:T(8,128)(2,1)S(1)} collective-permute-done((bf16[2,288,512]{2,1,0:T(8,128)(2,1)S(1)}, bf16[2,288,512]{2,1,0:T(8,128)(2,1)S(1)}, u32[]{:S(2)}, u32[]{:S(2)}) %collective-permute-start.16) | collective-permute-done | bytes 589856 | tf_op jit(solution)/shard_map/ppermute | solution.py:106
  116.3 2.0 collective-permute-start.18
  118.3 1.0 bitcast_dynamic-update-slice_fusion.1
  119.7 6.9 %collective-permute-done.19 = bf16[2,288,512]{2,1,0:T(8,128)(2,1)S(1)} collective-permute-done((bf16[2,288,512]{2,1,0:T(8,128)(2,1)S(1)}, bf16[2,288,512]{2,1,0:T(8,128)(2,1)S(1)}, u32[]{:S(2)}, u32[]{:S(2)}) %collective-permute-start.19) | collective-permute-done | bytes 589856 | tf_op jit(solution)/shard_map/ppermute | solution.py:106
  126.8 1.5 collective-permute-start.20
  128.8 1.0 bitcast_dynamic-update-slice_fusion
  129.8 8.9 %collective-permute-done.20 = bf16[2,288,512]{2,1,0:T(8,128)(2,1)S(1)} collective-permute-done((bf16[2,288,512]{2,1,0:T(8,128)(2,1)S(1)}, bf16[2,288,512]{2,1,0:T(8,128)(2,1)S(1)}, u32[]{:S(2)}, u32[]{:S(2)}) %collective-permute-start.20) | collective-permute-done | bytes 589856 | tf_op jit(solution)/shard_map/ppermute | solution.py:110
  149.6 2.1 fusion.28
  151.6 1.9 bitcast_dynamic-update-slice_fusion.12
  159.6 1.2 copy-done
  160.8 1.7 convolution_convert_fusion
  168.2 1.3 convolution_convert_fusion.2
  170.9 1.7 convolution_bitcast_fusion.1
  172.7 1.8 convolution_multiply_fusion.1
  176.2 4.1 %fusion.41 = f32[128,2304]{1,0:T(8,128)S(1)} fusion(bf16[1024,2304]{0,1:T(8,128)(2,1)} %fusion.29, bf16[16,8,8,128]{3,2,1,0:T(8,128)(2,1)S(1)} %bitcast.296), kind=kOutput, calls=%fused_computation.196 | convolution fusion | flops 603979776 | bytes 6160384 | tf_op jit(solution)/shard_map/dot_general | solution.py:284
  181.3 2.6 %fusion.1 = bf16[128,2304]{1,0:T(8,128)(2,1)S(1)} fusion(f32[128,2304]{1,0:T(8,128)S(1)} %convolution_add_fusion.1, bf16[128,512]{0,1:T(8,128)(2,1)S(1)} %bitcast.301, bf16[512,2304]{0,1:T(8,128)(2,1)} %bitcast_dynamic-update-slice_fusion.16), kind=kOutput, calls=%fused_computation.9 | convolution fusion | flops 302579712 | bytes 4259840 | tf_op jit(solution)/shard_map/dot_general | solution.py:286
  186.9 2.4 %fusion.13 = bf16[128,2304]{1,0:T(8,128)(2,1)S(1)} fusion(bf16[128,2304]{1,0:T(8,128)(2,1)} %copy-done.14, bf16[128,2304]{1,0:T(8,128)(2,1)S(1)} %fusion.1, f32[128]{0:T(128)S(1)} %broadcast_multiply_fusion, f32[128]{0:T(128)S(1)} %copy-done.53, f32[2304]{0:T(1024)S(1)} %mul.519, f32[128]{0:T(128)S(1)} %copy-done.50, bf16[128,2304]{1,0:T(8,128)(2,1)S(1)} %copy.54, ...), kind=kLoop, calls=%fused_computation.36 | loop fusion | flops 6488064 | bytes 4742912 | tf_op jit(solution)/shard_map/convert_element_type | solution.py:296
  190.8 14.8 %all_to_all.21 = bf16[8,16,1152]{2,1,0:T(8,128)(2,1)S(1)} all-to-all(bf16[8,16,1152]{2,1,0:T(8,128)(2,1)S(1)} %broadcast_select_fusion.4), channel_id=1, replica_groups=mesh['groups'=2,'seq'=8,'wg'=2] {'seq'}, dimensions={0} | all-to-all | bytes 589824 | tf_op jit(solution)/shard_map/all_to_all | solution.py:298
  (303 shorter events, 59.2 us)
Async XLA Ops:
  1.4 11.2 %copy-start.45 = (f32[2304]{0:T(1024)S(1)}, f32[2304]{0:T(1024)}, u32[]{:S(2)}) copy-start(f32[2304]{0:T(1024)} %param.12) | copy-start | bytes 27652
  1.4 11.3 %copy-start.46 = (f32[2304]{0:T(1024)S(1)}, f32[2304]{0:T(1024)}, u32[]{:S(2)}) copy-start(f32[2304]{0:T(1024)} %param.17) | copy-start | bytes 27652
  1.4 11.4 %copy-start.47 = (f32[2304]{0:T(1024)S(1)}, f32[2304]{0:T(1024)}, u32[]{:S(2)}) copy-start(f32[2304]{0:T(1024)} %param.18) | copy-start | bytes 27652
  1.5 12.5 %copy-start.54 = (s32[8]{0:T(128)S(1)}, s32[8]{0:T(128)}, u32[]{:S(2)}) copy-start(s32[8]{0:T(128)} %param.20) | copy-start | bytes 100
  1.5 15.1 %copy-start.33 = (bf16[64,2304]{1,0:T(8,128)(2,1)S(1)}, bf16[64,2304]{1,0:T(8,128)(2,1)}, u32[]{:S(2)}) copy-start(bf16[64,2304]{1,0:T(8,128)(2,1)} %param.19) | copy-start | bytes 884740
  2.4 20.5 %collective-permute-start = (bf16[2,288,512]{2,1,0:T(8,128)(2,1)}, bf16[2,288,512]{2,1,0:T(8,128)(2,1)S(1)}, u32[]{:S(2)}, u32[]{:S(2)}) collective-permute-start(bf16[2,288,512]{2,1,0:T(8,128)(2,1)} %pad_maximum_fusion.14), channel_id=1, source_target_pairs={{0,4},{4,8},{8,12},{12,14},{14,10},{10,6},{6,2},{2,0},{1,5},{5,9},... | collective-permute-start | bytes 1769480 | tf_op jit(solution)/shard_map/ppermute | solution.py:105
  6.3 16.6 %collective-permute-start.2 = (bf16[2,288,512]{2,1,0:T(8,128)(2,1)}, bf16[2,288,512]{2,1,0:T(8,128)(2,1)}, u32[]{:S(2)}, u32[]{:S(2)}) collective-permute-start(bf16[2,288,512]{2,1,0:T(8,128)(2,1)} %pad_maximum_fusion.15), channel_id=1, source_target_pairs={{0,2},{4,0},{8,4},{12,8},{14,12},{10,14},{6,10},{2,6},{1,3},{5,1},... | collective-permute-start | bytes 1769480 | tf_op jit(solution)/shard_map/ppermute | solution.py:106
  6.3 39.6 %all-to-all-start = ((bf16[8,16,1152]{2,1,0:T(8,128)(2,1)}), bf16[8,16,1152]{2,1,0:T(8,128)(2,1)}, u32[]{:S(2)}, u32[]{:S(2)}) async-start(bf16[8,16,1152]{2,1,0:T(8,128)(2,1)} %bitcast.1), calls=%async_computation | async-start | bytes 589824 | tf_op jit(solution)/shard_map/all_to_all | solution.py:153
  15.2 4.0 %copy-start.51 = (pred[128]{0:T(512)(128)(4,1)}, pred[128]{0:T(512)(128)(4,1)S(1)}, u32[]{:S(2)}) copy-start(pred[128]{0:T(512)(128)(4,1)S(1)} %iota_compare_fusion.1) | copy-start | bytes 388
  16.6 3.3 %copy-start.55 = (s32[8]{0:T(128)S(1)}, s32[8]{0:T(128)}, u32[]{:S(2)}) copy-start(s32[8]{0:T(128)} %param.21) | copy-start | bytes 100
  17.2 5.4 %copy-start.12 = (bf16[288,1024]{1,0:T(8,128)(2,1)S(1)}, bf16[288,1024]{1,0:T(8,128)(2,1)}, u32[]{:S(2)}) copy-start(bf16[288,1024]{1,0:T(8,128)(2,1)} %param.13) | copy-start | bytes 1769476
  17.2 5.4 %copy-start.13 = (bf16[1024,288]{0,1:T(8,128)(2,1)S(1)}, bf16[1024,288]{0,1:T(8,128)(2,1)}, u32[]{:S(2)}) copy-start(bf16[1024,288]{0,1:T(8,128)(2,1)} %param.16) | copy-start | bytes 1769476
  17.2 5.4 %copy-start.25 = (bf16[288,512]{1,0:T(8,128)(2,1)S(1)}, bf16[288,512]{1,0:T(8,128)(2,1)}, u32[]{:S(2)}) copy-start(bf16[288,512]{1,0:T(8,128)(2,1)} %param.14) | copy-start | bytes 884740
  17.2 5.4 %copy-start.26 = (bf16[288,512]{1,0:T(8,128)(2,1)S(1)}, bf16[288,512]{1,0:T(8,128)(2,1)}, u32[]{:S(2)}) copy-start(bf16[288,512]{1,0:T(8,128)(2,1)} %param.15) | copy-start | bytes 884740
  22.7 120.1 %copy-start.17 = (f32[128,64]{1,0:T(8,128)}, f32[128,64]{1,0:T(8,128)S(1)}, u32[]{:S(2)}) copy-start(f32[128,64]{1,0:T(8,128)S(1)} %get-tuple-element.107) | copy-start | bytes 98308
  22.7 120.1 %copy-start.19 = (f32[128,64]{1,0:T(8,128)}, f32[128,64]{1,0:T(8,128)S(1)}, u32[]{:S(2)}) copy-start(f32[128,64]{1,0:T(8,128)S(1)} %get-tuple-element.108) | copy-start | bytes 98308
  22.8 4.9 %copy-start.1 = (bf16[288,1536]{1,0:T(8,128)(2,1)}, bf16[288,1536]{1,0:T(8,128)(2,1)S(1)}, u32[]{:S(2)}) copy-start(bf16[288,1536]{1,0:T(8,128)(2,1)S(1)} %get-tuple-element.28) | copy-start | bytes 2654212
  24.6 14.4 %collective-permute-start.1 = (bf16[2,288,512]{2,1,0:T(8,128)(2,1)S(1)}, bf16[2,288,512]{2,1,0:T(8,128)(2,1)S(1)}, u32[]{:S(2)}, u32[]{:S(2)}) collective-permute-start(bf16[2,288,512]{2,1,0:T(8,128)(2,1)S(1)} %collective-permute-done), channel_id=1, source_target_pairs={{0,4},{4,8},{8,12},{12,14},{14,10},{10,6},{6,2},{2,0},{1,5},{5,9},... | collective-permute-start | bytes 1769480 | tf_op jit(solution)/shard_map/ppermute | solution.py:105
  26.6 14.4 %collective-permute-start.3 = (bf16[2,288,512]{2,1,0:T(8,128)(2,1)}, bf16[2,288,512]{2,1,0:T(8,128)(2,1)S(1)}, u32[]{:S(2)}, u32[]{:S(2)}) collective-permute-start(bf16[2,288,512]{2,1,0:T(8,128)(2,1)} %collective-permute-done.2), channel_id=1, source_target_pairs={{0,2},{4,0},{8,4},{12,8},{14,12},{10,14},{6,10},{2,6},{1,3},{5,1},... | collective-permute-start | bytes 1769480 | tf_op jit(solution)/shard_map/ppermute | solution.py:106
  27.7 15.8 %collective-permute-start.4 = (bf16[2,288,512]{2,1,0:T(8,128)(2,1)S(1)}, bf16[2,288,512]{2,1,0:T(8,128)(2,1)S(1)}, u32[]{:S(2)}, u32[]{:S(2)}) collective-permute-start(bf16[2,288,512]{2,1,0:T(8,128)(2,1)S(1)} %pad_maximum_fusion.16), channel_id=1, source_target_pairs={{0,16},{16,0},{1,17},{17,1},{2,18},{18,2},{3,19},{19,3},{4,20},{20... | collective-permute-start | bytes 1769480 | tf_op jit(solution)/shard_map/ppermute | solution.py:110
  39.0 5.8 %copy-start.21 = (bf16[2,288,512]{2,1,0:T(8,128)(2,1)}, bf16[2,288,512]{2,1,0:T(8,128)(2,1)S(1)}, u32[]{:S(2)}) copy-start(bf16[2,288,512]{2,1,0:T(8,128)(2,1)S(1)} %collective-permute-done.1) | copy-start | bytes 1769476
  41.1 3.7 %copy-start.23 = (bf16[2,288,512]{2,1,0:T(8,128)(2,1)}, bf16[2,288,512]{2,1,0:T(8,128)(2,1)S(1)}, u32[]{:S(2)}) copy-start(bf16[2,288,512]{2,1,0:T(8,128)(2,1)S(1)} %collective-permute-done.3) | copy-start | bytes 1769476
  42.1 13.9 %collective-permute-start.5 = (bf16[2,288,512]{2,1,0:T(8,128)(2,1)}, bf16[2,288,512]{2,1,0:T(8,128)(2,1)}, u32[]{:S(2)}, u32[]{:S(2)}) collective-permute-start(bf16[2,288,512]{2,1,0:T(8,128)(2,1)} %pad_maximum_fusion.17), channel_id=1, source_target_pairs={{0,16},{16,0},{1,17},{17,1},{2,18},{18,2},{3,19},{19,3},{4,20},{20... | collective-permute-start | bytes 1769480 | tf_op jit(solution)/shard_map/ppermute | solution.py:110
  50.5 3.6 %copy-start.24 = (bf16[2,288,512]{2,1,0:T(8,128)(2,1)S(1)}, bf16[2,288,512]{2,1,0:T(8,128)(2,1)}, u32[]{:S(2)}) copy-start(bf16[2,288,512]{2,1,0:T(8,128)(2,1)} %copy-done.23) | copy-start | bytes 1769476
  53.1 15.4 %collective-permute-start.6 = (bf16[2,288,512]{2,1,0:T(8,128)(2,1)S(1)}, bf16[2,288,512]{2,1,0:T(8,128)(2,1)S(1)}, u32[]{:S(2)}, u32[]{:S(2)}) collective-permute-start(bf16[2,288,512]{2,1,0:T(8,128)(2,1)S(1)} %copy-done.22), channel_id=1, source_target_pairs={{0,4},{4,8},{8,12},{12,14},{14,10},{10,6},{6,2},{2,0},{1,5},{5,9},... | collective-permute-start | bytes 1769480 | tf_op jit(solution)/shard_map/ppermute | solution.py:105
  54.0 15.1 %collective-permute-start.7 = (bf16[2,288,512]{2,1,0:T(8,128)(2,1)S(1)}, bf16[2,288,512]{2,1,0:T(8,128)(2,1)S(1)}, u32[]{:S(2)}, u32[]{:S(2)}) collective-permute-start(bf16[2,288,512]{2,1,0:T(8,128)(2,1)S(1)} %copy-done.24), channel_id=1, source_target_pairs={{0,2},{4,0},{8,4},{12,8},{14,12},{10,14},{6,10},{2,6},{1,3},{5,1},... | collective-permute-start | bytes 1769480 | tf_op jit(solution)/shard_map/ppermute | solution.py:106
  69.2 14.3 %collective-permute-start.8 = (bf16[2,288,512]{2,1,0:T(8,128)(2,1)S(1)}, bf16[2,288,512]{2,1,0:T(8,128)(2,1)S(1)}, u32[]{:S(2)}, u32[]{:S(2)}) collective-permute-start(bf16[2,288,512]{2,1,0:T(8,128)(2,1)S(1)} %pad_maximum_fusion.18), channel_id=1, source_target_pairs={{0,16},{16,0},{1,17},{17,1},{2,18},{18,2},{3,19},{19,3},{4,20},{20... | collective-permute-start | bytes 1769480 | tf_op jit(solution)/shard_map/ppermute | solution.py:110
  69.8 14.0 %collective-permute-start.10 = (bf16[2,288,512]{2,1,0:T(8,128)(2,1)S(1)}, bf16[2,288,512]{2,1,0:T(8,128)(2,1)S(1)}, u32[]{:S(2)}, u32[]{:S(2)}) collective-permute-start(bf16[2,288,512]{2,1,0:T(8,128)(2,1)S(1)} %collective-permute-done.7), channel_id=1, source_target_pairs={{0,2},{4,0},{8,4},{12,8},{14,12},{10,14},{6,10},{2,6},{1,3},{5,1},... | collective-permute-start | bytes 1769480 | tf_op jit(solution)/shard_map/ppermute | solution.py:106
  71.0 14.1 %collective-permute-start.9 = (bf16[2,288,512]{2,1,0:T(8,128)(2,1)S(1)}, bf16[2,288,512]{2,1,0:T(8,128)(2,1)S(1)}, u32[]{:S(2)}, u32[]{:S(2)}) collective-permute-start(bf16[2,288,512]{2,1,0:T(8,128)(2,1)S(1)} %collective-permute-done.6), channel_id=1, source_target_pairs={{0,4},{4,8},{8,12},{12,14},{14,10},{10,6},{6,2},{2,0},{1,5},{5,9},... | collective-permute-start | bytes 1769480 | tf_op jit(solution)/shard_map/ppermute | solution.py:105
  85.3 13.3 %collective-permute-start.11 = (bf16[2,288,512]{2,1,0:T(8,128)(2,1)S(1)}, bf16[2,288,512]{2,1,0:T(8,128)(2,1)S(1)}, u32[]{:S(2)}, u32[]{:S(2)}) collective-permute-start(bf16[2,288,512]{2,1,0:T(8,128)(2,1)S(1)} %pad_maximum_fusion.19), channel_id=1, source_target_pairs={{0,16},{16,0},{1,17},{17,1},{2,18},{18,2},{3,19},{19,3},{4,20},{20... | collective-permute-start | bytes 1769480 | tf_op jit(solution)/shard_map/ppermute | solution.py:110
  86.4 12.6 %collective-permute-start.12 = (bf16[2,288,512]{2,1,0:T(8,128)(2,1)S(1)}, bf16[2,288,512]{2,1,0:T(8,128)(2,1)S(1)}, u32[]{:S(2)}, u32[]{:S(2)}) collective-permute-start(bf16[2,288,512]{2,1,0:T(8,128)(2,1)S(1)} %collective-permute-done.9), channel_id=1, source_target_pairs={{0,4},{4,8},{8,12},{12,14},{14,10},{10,6},{6,2},{2,0},{1,5},{5,9},... | collective-permute-start | bytes 1769480 | tf_op jit(solution)/shard_map/ppermute | solution.py:105
  87.3 12.2 %collective-permute-start.13 = (bf16[2,288,512]{2,1,0:T(8,128)(2,1)S(1)}, bf16[2,288,512]{2,1,0:T(8,128)(2,1)S(1)}, u32[]{:S(2)}, u32[]{:S(2)}) collective-permute-start(bf16[2,288,512]{2,1,0:T(8,128)(2,1)S(1)} %collective-permute-done.10), channel_id=1, source_target_pairs={{0,2},{4,0},{8,4},{12,8},{14,12},{10,14},{6,10},{2,6},{1,3},{5,1},... | collective-permute-start | bytes 1769480 | tf_op jit(solution)/shard_map/ppermute | solution.py:106
  98.7 48.9 %copy-start.3 = (bf16[288,1536]{1,0:T(8,128)(2,1)}, bf16[288,1536]{1,0:T(8,128)(2,1)S(1)}, u32[]{:S(2)}) copy-start(bf16[288,1536]{1,0:T(8,128)(2,1)S(1)} %pad_maximum_fusion.9) | copy-start | bytes 2654212
  99.7 11.6 %collective-permute-start.14 = (bf16[2,288,512]{2,1,0:T(8,128)(2,1)S(1)}, bf16[2,288,512]{2,1,0:T(8,128)(2,1)S(1)}, u32[]{:S(2)}, u32[]{:S(2)}) collective-permute-start(bf16[2,288,512]{2,1,0:T(8,128)(2,1)S(1)} %pad_maximum_fusion.20), channel_id=1, source_target_pairs={{0,16},{16,0},{1,17},{17,1},{2,18},{18,2},{3,19},{19,3},{4,20},{20... | collective-permute-start | bytes 1769480 | tf_op jit(solution)/shard_map/ppermute | solution.py:110
  101.1 11.7 %collective-permute-start.15 = (bf16[2,288,512]{2,1,0:T(8,128)(2,1)S(1)}, bf16[2,288,512]{2,1,0:T(8,128)(2,1)S(1)}, u32[]{:S(2)}, u32[]{:S(2)}) collective-permute-start(bf16[2,288,512]{2,1,0:T(8,128)(2,1)S(1)} %collective-permute-done.12), channel_id=1, source_target_pairs={{0,4},{4,8},{8,12},{12,14},{14,10},{10,6},{6,2},{2,0},{1,5},{5,9},... | collective-permute-start | bytes 1769480 | tf_op jit(solution)/shard_map/ppermute | solution.py:105
  102.8 13.2 %collective-permute-start.16 = (bf16[2,288,512]{2,1,0:T(8,128)(2,1)S(1)}, bf16[2,288,512]{2,1,0:T(8,128)(2,1)S(1)}, u32[]{:S(2)}, u32[]{:S(2)}) collective-permute-start(bf16[2,288,512]{2,1,0:T(8,128)(2,1)S(1)} %collective-permute-done.13), channel_id=1, source_target_pairs={{0,2},{4,0},{8,4},{12,8},{14,12},{10,14},{6,10},{2,6},{1,3},{5,1},... | collective-permute-start | bytes 1769480 | tf_op jit(solution)/shard_map/ppermute | solution.py:106
  111.5 35.1 %copy-start.5 = (bf16[288,1536]{1,0:T(8,128)(2,1)}, bf16[288,1536]{1,0:T(8,128)(2,1)S(1)}, u32[]{:S(2)}) copy-start(bf16[288,1536]{1,0:T(8,128)(2,1)S(1)} %pad_maximum_fusion.11) | copy-start | bytes 2654212
  116.1 12.3 %collective-permute-start.17 = (bf16[2,288,512]{2,1,0:T(8,128)(2,1)S(1)}, bf16[2,288,512]{2,1,0:T(8,128)(2,1)S(1)}, u32[]{:S(2)}, u32[]{:S(2)}) collective-permute-start(bf16[2,288,512]{2,1,0:T(8,128)(2,1)S(1)} %pad_maximum_fusion.21), channel_id=1, source_target_pairs={{0,16},{16,0},{1,17},{17,1},{2,18},{18,2},{3,19},{19,3},{4,20},{20... | collective-permute-start | bytes 1769480 | tf_op jit(solution)/shard_map/ppermute | solution.py:110
  116.2 10.4 %collective-permute-start.19 = (bf16[2,288,512]{2,1,0:T(8,128)(2,1)S(1)}, bf16[2,288,512]{2,1,0:T(8,128)(2,1)S(1)}, u32[]{:S(2)}, u32[]{:S(2)}) collective-permute-start(bf16[2,288,512]{2,1,0:T(8,128)(2,1)S(1)} %collective-permute-done.16), channel_id=1, source_target_pairs={{0,2},{4,0},{8,4},{12,8},{14,12},{10,14},{6,10},{2,6},{1,3},{5,1},... | collective-permute-start | bytes 1769480 | tf_op jit(solution)/shard_map/ppermute | solution.py:106
  116.3 10.4 %collective-permute-start.18 = (bf16[2,288,512]{2,1,0:T(8,128)(2,1)S(1)}, bf16[2,288,512]{2,1,0:T(8,128)(2,1)S(1)}, u32[]{:S(2)}, u32[]{:S(2)}) collective-permute-start(bf16[2,288,512]{2,1,0:T(8,128)(2,1)S(1)} %collective-permute-done.15), channel_id=1, source_target_pairs={{0,4},{4,8},{8,12},{12,14},{14,10},{10,6},{6,2},{2,0},{1,5},{5,9},... | collective-permute-start | bytes 1769480 | tf_op jit(solution)/shard_map/ppermute | solution.py:105
  126.8 12.0 %collective-permute-start.20 = (bf16[2,288,512]{2,1,0:T(8,128)(2,1)S(1)}, bf16[2,288,512]{2,1,0:T(8,128)(2,1)S(1)}, u32[]{:S(2)}, u32[]{:S(2)}) collective-permute-start(bf16[2,288,512]{2,1,0:T(8,128)(2,1)S(1)} %pad_maximum_fusion.22), channel_id=1, source_target_pairs={{0,16},{16,0},{1,17},{17,1},{2,18},{18,2},{3,19},{19,3},{4,20},{20... | collective-permute-start | bytes 1769480 | tf_op jit(solution)/shard_map/ppermute | solution.py:110
  128.7 16.9 %copy-start.7 = (bf16[288,1536]{1,0:T(8,128)(2,1)}, bf16[288,1536]{1,0:T(8,128)(2,1)S(1)}, u32[]{:S(2)}) copy-start(bf16[288,1536]{1,0:T(8,128)(2,1)S(1)} %pad_maximum_fusion.13) | copy-start | bytes 2654212
  149.4 5.1 %copy-start.27 = (bf16[128,512]{1,0:T(8,128)(2,1)}, bf16[128,512]{1,0:T(8,128)(2,1)S(1)}, u32[]{:S(2)}) copy-start(bf16[128,512]{1,0:T(8,128)(2,1)S(1)} %fusion.15) | copy-start | bytes 393220
  149.5 4.0 %copy-start.6 = (bf16[288,1536]{1,0:T(8,128)(2,1)S(1)}, bf16[288,1536]{1,0:T(8,128)(2,1)}, u32[]{:S(2)}) copy-start(bf16[288,1536]{1,0:T(8,128)(2,1)} %copy-done.5) | copy-start | bytes 2654212
  149.6 4.9 %copy-start.4 = (bf16[288,1536]{1,0:T(8,128)(2,1)S(1)}, bf16[288,1536]{1,0:T(8,128)(2,1)}, u32[]{:S(2)}) copy-start(bf16[288,1536]{1,0:T(8,128)(2,1)} %copy-done.3) | copy-start | bytes 2654212
  162.4 2.5 %collective-permute-start.21 = (bf16[128,2304]{1,0:T(8,128)(2,1)S(1)}, bf16[128,2304]{1,0:T(8,128)(2,1)S(1)}, u32[]{:S(2)}, u32[]{:S(2)}) collective-permute-start(bf16[128,2304]{1,0:T(8,128)(2,1)S(1)} %convolution_convert_fusion), channel_id=1, source_target_pairs={{0,1},{1,0},{2,3},{3,2},{4,5},{5,4},{6,7},{7,6},{8,9},{9,8},{10,11... | collective-permute-start | bytes 1769480 | tf_op jit(solution)/shard_map/ppermute | solution.py:58
  176.2 4.2 %copy-start.11 = (bf16[512,2304]{0,1:T(8,128)(2,1)S(1)}, bf16[512,2304]{0,1:T(8,128)(2,1)}, u32[]{:S(2)}) copy-start(bf16[512,2304]{0,1:T(8,128)(2,1)} %copy-done.10) | copy-start | bytes 7077892
  183.9 2.2 %collective-permute-start.22 = (bf16[128,2304]{1,0:T(8,128)(2,1)S(1)}, bf16[128,2304]{1,0:T(8,128)(2,1)S(1)}, u32[]{:S(2)}, u32[]{:S(2)}) collective-permute-start(bf16[128,2304]{1,0:T(8,128)(2,1)S(1)} %fusion.1), channel_id=1, source_target_pairs={{0,1},{1,0},{2,3},{3,2},{4,5},{5,4},{6,7},{7,6},{8,9},{9,8},{10,11... | collective-permute-start | bytes 1769480 | tf_op jit(solution)/shard_map/ppermute | solution.py:58
  (37 other events, 65.6 us)

commit v15 on v13

--- a/solution.py
+++ b/solution.py
@@ -159,7 +159,12 @@
         front, back, seq_rank, lax.axis_index("groups"), n_seq
     )
     guard_half, _ = lax.optimization_barrier((guard_half, first_arrival))
-    guard_rows = lax.all_gather(guard_half, "wg", axis=1, tiled=True)
+    partner_half = lax.ppermute(guard_half, "wg", perm=[(0, 1), (1, 0)])
+    guard_rows = jnp.where(
+        core_rank == 0,
+        jnp.concatenate([guard_half, partner_half], axis=1),
+        jnp.concatenate([partner_half, guard_half], axis=1),
+    )
     guard_rows = permute_blocks(guard_rows, block_of, n_seq)
     pre_gain, post_gain, final_gain = permute_blocks(
         jnp.stack([pre_gain, post_gain, final_gain]), block_of, n_seq

time: 205 us -> 221 us (1.078)
  local copies, waits for them, and re-layouts: 32.7 us -> 48.3 us
  starting transfers between devices: 34.2 us -> 28.8 us
  matrix products: 22.7 us -> 26.8 us
  other arithmetic: 24.7 us -> 28.7 us
  blocking collectives: 17.7 us -> 14.6 us
    unnamed x141, local copies, waits for them, and re-layouts: 14.6 us -> 23.2 us
    ppermute x7, starting transfers between devices: 11.9 us -> 6.5 us  [ring_gather(): lax.ppermute(jnp.stack([front_ring[step][0], back_ring[step][0]]), 'group...]
    ppermute x7, waiting for transfers between devices: 19.2 us -> 14.6 us  [ring_gather(): front_ring.append(lax.ppermute(front_ring[-1], 'seq', forward_pairs))]
    all_to_all x1, waiting for transfers between devices: 1.28 us -> 4.89 us  [shards(): lax.all_to_all(generator_rows, 'seq', split_axis=0, concat_axis=0, tiled=...]
    all_gather x1 -> x0, blocking collectives: 2.43 us -> none  [shards(): guard_rows = lax.all_gather(guard_half, 'wg', axis=1, tiled=True)]
  transfers between devices with their start and end apart: 24 -> 25, of which waited for: 18 -> 15; matrix products, arithmetic and copies ran while one was open for 14% -> 18% of each run, Pallas kernels for 0% -> 0%
where the time goes in v15:
time: 221 us; the launch traced here: 220 us
  waiting for transfers between devices  71.2 us (32%)
  local copies, waits for them, and re-layouts  48.3 us (22%)
  starting transfers between devices  28.8 us (13%)
  other arithmetic  28.7 us (13%)
  matrix products  26.8 us (12%)
  blocking collectives  14.6 us (7%)
    ppermute x7, waiting for transfers between devices, ring_gather(): lax.ppermute(jnp.stack([front_ring[step][0], back_ring[step][0]]), 'group...  42.1 us
    unnamed x141, local copies, waits for them, and re-layouts  23.2 us
    all_to_all x1, blocking collectives, shards(): lax.all_to_all(grad_rows, 'seq', split_axis=0, concat_axis=0, tiled=True)  14.6 us
    ppermute x7, waiting for transfers between devices, ring_gather(): front_ring.append(lax.ppermute(front_ring[-1], 'seq', forward_pairs))  14.6 us
    ppermute x7, waiting for transfers between devices, ring_gather(): back_ring.append(lax.ppermute(back_ring[-1], 'seq', backward_pairs))  9.54 us
    ppermute x7, starting transfers between devices, ring_gather(): back_ring.append(lax.ppermute(back_ring[-1], 'seq', backward_pairs))  8.09 us
    ppermute x7, starting transfers between devices, ring_gather(): front_ring.append(lax.ppermute(front_ring[-1], 'seq', forward_pairs))  7.37 us
    ppermute x7, starting transfers between devices, ring_gather(): lax.ppermute(jnp.stack([front_ring[step][0], back_ring[step][0]]), 'group...  6.5 us
  transfers between devices with their start and end apart: 25, of which 15 were waited for; matrix products, arithmetic and copies ran while one was open for 18% of the time, Pallas kernels for 0%

profile of v15, /device:TPU:0, one launch (start us, length us, event | category | flops | bytes accessed | tf_op | source)
XLA Modules:
  0.0 219.8 jit_solution(5190891468151002530)
XLA Ops:
  0.0 1.4 fusion.39
  2.4 3.0 %collective-permute-start = (bf16[2,288,512]{2,1,0:T(8,128)(2,1)}, bf16[2,288,512]{2,1,0:T(8,128)(2,1)}, u32[]{:S(2)}, u32[]{:S(2)}) collective-permute-start(bf16[2,288,512]{2,1,0:T(8,128)(2,1)} %pad_maximum_fusion.14), channel_id=1, source_target_pairs={{0,4},{4,8},{8,12},{12,14},{14,10},{10,6},{6,2},{2,0},{1,5},{5,9},... | collective-permute-start | bytes 1769480 | tf_op jit(solution)/shard_map/ppermute | solution.py:105
  6.3 6.3 %all-to-all-start = ((bf16[8,16,1152]{2,1,0:T(8,128)(2,1)}), bf16[8,16,1152]{2,1,0:T(8,128)(2,1)}, u32[]{:S(2)}, u32[]{:S(2)}) async-start(bf16[8,16,1152]{2,1,0:T(8,128)(2,1)} %bitcast.1), calls=%async_computation | async-start | bytes 589824 | tf_op jit(solution)/shard_map/all_to_all | solution.py:153
  16.9 1.2 compare_convert_fusion
  22.7 1.1 pad_maximum_fusion
  23.8 4.9 %all-to-all-done = bf16[8,16,1152]{2,1,0:T(8,128)(2,1)} async-done(((bf16[8,16,1152]{2,1,0:T(8,128)(2,1)}), bf16[8,16,1152]{2,1,0:T(8,128)(2,1)}, u32[]{:S(2)}, u32[]{:S(2)}) %all-to-all-start) | async-done | bytes 294944 | tf_op jit(solution)/shard_map/all_to_all | solution.py:153
  28.7 1.2 copy.53
  34.4 1.5 collective-permute-start.3
  36.7 2.0 collective-permute-start.5
  42.6 9.9 %collective-permute-done.4 = bf16[2,288,512]{2,1,0:T(8,128)(2,1)} collective-permute-done((bf16[2,288,512]{2,1,0:T(8,128)(2,1)}, bf16[2,288,512]{2,1,0:T(8,128)(2,1)}, u32[]{:S(2)}, u32[]{:S(2)}) %collective-permute-start.4) | collective-permute-done | bytes 589856 | tf_op jit(solution)/shard_map/ppermute | solution.py:105
  55.1 1.5 select_bitcast_fusion.23
  56.8 1.5 copy-done.6
  58.6 1.7 collective-permute-start.8
  61.7 7.5 %collective-permute-done.6 = bf16[2,288,512]{2,1,0:T(8,128)(2,1)S(1)} collective-permute-done((bf16[2,288,512]{2,1,0:T(8,128)(2,1)S(1)}, bf16[2,288,512]{2,1,0:T(8,128)(2,1)S(1)}, u32[]{:S(2)}, u32[]{:S(2)}) %collective-permute-start.6) | collective-permute-done | bytes 589856 | tf_op jit(solution)/shard_map/ppermute | solution.py:110
  69.2 1.4 select_bitcast_fusion.19
  70.7 2.2 collective-permute-done.7
  73.4 1.6 collective-permute-start.9
  76.0 1.1 collective-permute-start.11
  78.4 8.6 %collective-permute-done.9 = bf16[2,288,512]{2,1,0:T(8,128)(2,1)S(1)} collective-permute-done((bf16[2,288,512]{2,1,0:T(8,128)(2,1)S(1)}, bf16[2,288,512]{2,1,0:T(8,128)(2,1)S(1)}, u32[]{:S(2)}, u32[]{:S(2)}) %collective-permute-start.9) | collective-permute-done | bytes 589856 | tf_op jit(solution)/shard_map/ppermute | solution.py:110
  90.0 1.3 collective-permute-start.14
  92.7 8.9 %collective-permute-done.12 = bf16[2,288,512]{2,1,0:T(8,128)(2,1)S(1)} collective-permute-done((bf16[2,288,512]{2,1,0:T(8,128)(2,1)S(1)}, bf16[2,288,512]{2,1,0:T(8,128)(2,1)S(1)}, u32[]{:S(2)}, u32[]{:S(2)}) %collective-permute-start.12) | collective-permute-done | bytes 589856 | tf_op jit(solution)/shard_map/ppermute | solution.py:110
  102.0 1.6 collective-permute-start.15
  103.6 1.7 collective-permute-start.16
  107.0 8.1 %collective-permute-done.15 = bf16[2,288,512]{2,1,0:T(8,128)(2,1)S(1)} collective-permute-done((bf16[2,288,512]{2,1,0:T(8,128)(2,1)S(1)}, bf16[2,288,512]{2,1,0:T(8,128)(2,1)S(1)}, u32[]{:S(2)}, u32[]{:S(2)}) %collective-permute-start.15) | collective-permute-done | bytes 589856 | tf_op jit(solution)/shard_map/ppermute | solution.py:110
  115.3 2.4 %collective-permute-done.17 = bf16[2,288,512]{2,1,0:T(8,128)(2,1)S(1)} collective-permute-done((bf16[2,288,512]{2,1,0:T(8,128)(2,1)S(1)}, bf16[2,288,512]{2,1,0:T(8,128)(2,1)S(1)}, u32[]{:S(2)}, u32[]{:S(2)}) %collective-permute-start.17) | collective-permute-done | bytes 589856 | tf_op jit(solution)/shard_map/ppermute | solution.py:106
  117.9 1.5 collective-permute-start.20
  121.4 6.5 %collective-permute-done.20 = bf16[2,288,512]{2,1,0:T(8,128)(2,1)S(1)} collective-permute-done((bf16[2,288,512]{2,1,0:T(8,128)(2,1)S(1)}, bf16[2,288,512]{2,1,0:T(8,128)(2,1)S(1)}, u32[]{:S(2)}, u32[]{:S(2)}) %collective-permute-start.20) | collective-permute-done | bytes 589856 | tf_op jit(solution)/shard_map/ppermute | solution.py:106
  127.9 1.4 collective-permute-done.19
  130.0 1.4 collective-permute-done.18
  132.7 7.7 %collective-permute-done.21 = bf16[2,288,512]{2,1,0:T(8,128)(2,1)S(1)} collective-permute-done((bf16[2,288,512]{2,1,0:T(8,128)(2,1)S(1)}, bf16[2,288,512]{2,1,0:T(8,128)(2,1)S(1)}, u32[]{:S(2)}, u32[]{:S(2)}) %collective-permute-start.21) | collective-permute-done | bytes 589856 | tf_op jit(solution)/shard_map/ppermute | solution.py:110
  151.9 2.1 fusion.28
  153.9 1.9 bitcast_dynamic-update-slice_fusion.12
  161.8 1.2 copy-done
  163.0 1.7 convolution_convert_fusion
  170.2 2.0 convolution_convert_fusion.2
  172.2 1.2 copy.93
  173.4 2.0 fusion.16
  176.4 2.8 %convolution_bitcast_fusion.1 = f32[4,128,128]{2,1,0:T(8,128)} fusion(bf16[4,2,128,128]{3,2,1,0:T(8,128)(2,1)} %copy-done.27, f32[4,2,128,128]{2,3,1,0:T(8,128)} %fusion.56, f32[4,2,128,128]{2,3,1,0:T(8,128)} %copy-done.53, f32[4,2,128]{2,1,0:T(2,128)S(1)} %copy-done.55, pred[128,128]{0,1:T(8,128)(4,1)S(1)} %copy-done.35), kind=kOutput, calls=%fused_computation.49 | convolution fusion | flops 35259520 | bytes 1593344 | tf_op jit(solution)/shard_map/kgij,kgid->kjd/dot_general | solution.py:279
  179.2 2.4 %convolution_multiply_fusion.1 = f32[4,2,128,128]{3,2,1,0:T(8,128)S(1)} fusion(f32[4,2,128,128]{2,3,1,0:T(8,128)} %fusion.56, f32[4,2,128,128]{2,3,1,0:T(8,128)} %copy-done.53, bf16[4,128,64]{2,1,0:T(8,128)(2,1)} %get-tuple-element.106, bf16[4,128,64]{2,1,0:T(8,128)(2,1)} %copy-done.30, f32[4,2,128]{2,1,0:T(2,128)} %copy-done.54, ...), kind=kOutput, calls=%fused_computation.25 | convolution fusion | flops 35652736 | bytes 1724416 | tf_op jit(solution)/shard_map/kgij,kjd->kgid/dot_general | solution.py:275
  181.6 1.2 add_convert_fusion.1
  183.6 1.7 copy.75
  187.1 4.1 %fusion.41 = f32[128,2304]{1,0:T(8,128)S(1)} fusion(bf16[1024,2304]{0,1:T(8,128)(2,1)} %fusion.29, bf16[16,8,8,128]{3,2,1,0:T(8,128)(2,1)S(1)} %bitcast.298), kind=kOutput, calls=%fused_computation.197 | convolution fusion | flops 603979776 | bytes 6160384 | tf_op jit(solution)/shard_map/dot_general | solution.py:289
  192.3 2.6 %fusion.1 = bf16[128,2304]{1,0:T(8,128)(2,1)S(1)} fusion(f32[128,2304]{1,0:T(8,128)S(1)} %convolution_add_fusion.1, bf16[128,512]{0,1:T(8,128)(2,1)S(1)} %bitcast.303, bf16[512,2304]{0,1:T(8,128)(2,1)} %bitcast_dynamic-update-slice_fusion.16), kind=kOutput, calls=%fused_computation.9 | convolution fusion | flops 302579712 | bytes 4259840 | tf_op jit(solution)/shard_map/dot_general | solution.py:291
  196.0 1.3 broadcast_in_dim.111
  197.4 1.5 fusion.14
  198.9 2.9 %fusion.13 = bf16[128,2304]{1,0:T(8,128)(2,1)} fusion(bf16[128,2304]{1,0:T(8,128)(2,1)} %collective-permute-done.23, bf16[128,2304]{1,0:T(8,128)(2,1)S(1)} %fusion.1, f32[128]{0:T(128)S(1)} %broadcast_multiply_fusion, f32[128]{0:T(128)} %get-tuple-element.109, f32[2304]{0:T(1024)S(1)} %mul.519, f32[128]{0:T(128)} %copy-done.42, ...), kind=kLoop, calls=%fused_computation.36 | loop fusion | flops 6488064 | bytes 4742912 | tf_op jit(solution)/shard_map/convert_element_type | solution.py:301
  201.7 1.4 copy.77
  204.5 14.6 %all_to_all.21 = bf16[8,16,1152]{2,1,0:T(8,128)(2,1)S(1)} all-to-all(bf16[8,16,1152]{2,1,0:T(8,128)(2,1)S(1)} %broadcast_select_fusion.4), channel_id=1, replica_groups=mesh['groups'=2,'seq'=8,'wg'=2] {'seq'}, dimensions={0} | all-to-all | bytes 589824 | tf_op jit(solution)/shard_map/all_to_all | solution.py:303
  (295 shorter events, 68.0 us)
Async XLA Ops:
  1.4 11.9 %copy-start.36 = (f32[2304]{0:T(1024)S(1)}, f32[2304]{0:T(1024)}, u32[]{:S(2)}) copy-start(f32[2304]{0:T(1024)} %param.12) | copy-start | bytes 27652
  1.4 11.9 %copy-start.37 = (f32[2304]{0:T(1024)S(1)}, f32[2304]{0:T(1024)}, u32[]{:S(2)}) copy-start(f32[2304]{0:T(1024)} %param.17) | copy-start | bytes 27652
  1.4 12.0 %copy-start.38 = (f32[2304]{0:T(1024)S(1)}, f32[2304]{0:T(1024)}, u32[]{:S(2)}) copy-start(f32[2304]{0:T(1024)} %param.18) | copy-start | bytes 27652
  1.5 13.5 %copy-start.50 = (s32[8]{0:T(128)S(1)}, s32[8]{0:T(128)}, u32[]{:S(2)}) copy-start(s32[8]{0:T(128)} %param.20) | copy-start | bytes 100
  1.5 14.9 %copy-start.51 = (s32[8]{0:T(128)S(1)}, s32[8]{0:T(128)}, u32[]{:S(2)}) copy-start(s32[8]{0:T(128)} %param.21) | copy-start | bytes 100
  1.5 17.5 %copy-start.25 = (bf16[64,2304]{1,0:T(8,128)(2,1)S(1)}, bf16[64,2304]{1,0:T(8,128)(2,1)}, u32[]{:S(2)}) copy-start(bf16[64,2304]{1,0:T(8,128)(2,1)} %param.19) | copy-start | bytes 884740
  2.4 26.3 %collective-permute-start = (bf16[2,288,512]{2,1,0:T(8,128)(2,1)}, bf16[2,288,512]{2,1,0:T(8,128)(2,1)}, u32[]{:S(2)}, u32[]{:S(2)}) collective-permute-start(bf16[2,288,512]{2,1,0:T(8,128)(2,1)} %pad_maximum_fusion.14), channel_id=1, source_target_pairs={{0,4},{4,8},{8,12},{12,14},{14,10},{10,6},{6,2},{2,0},{1,5},{5,9},... | collective-permute-start | bytes 1769480 | tf_op jit(solution)/shard_map/ppermute | solution.py:105
  6.3 22.4 %collective-permute-start.1 = (bf16[2,288,512]{2,1,0:T(8,128)(2,1)}, bf16[2,288,512]{2,1,0:T(8,128)(2,1)}, u32[]{:S(2)}, u32[]{:S(2)}) collective-permute-start(bf16[2,288,512]{2,1,0:T(8,128)(2,1)} %pad_maximum_fusion.15), channel_id=1, source_target_pairs={{0,2},{4,0},{8,4},{12,8},{14,12},{10,14},{6,10},{2,6},{1,3},{5,1},... | collective-permute-start | bytes 1769480 | tf_op jit(solution)/shard_map/ppermute | solution.py:106
  6.3 22.4 %all-to-all-start = ((bf16[8,16,1152]{2,1,0:T(8,128)(2,1)}), bf16[8,16,1152]{2,1,0:T(8,128)(2,1)}, u32[]{:S(2)}, u32[]{:S(2)}) async-start(bf16[8,16,1152]{2,1,0:T(8,128)(2,1)} %bitcast.1), calls=%async_computation | async-start | bytes 589824 | tf_op jit(solution)/shard_map/all_to_all | solution.py:153
  13.3 7.3 %copy-start.48 = (s32[4]{0:T(128)}, s32[4]{0:T(128)S(1)}, u32[]{:S(2)}) copy-start(s32[4]{0:T(128)S(1)} %gather_fusion) | copy-start | bytes 52
  16.3 144.7 %copy-start.34 = (pred[128,128]{0,1:T(8,128)(4,1)}, pred[128,128]{0,1:T(8,128)(4,1)S(1)}, u32[]{:S(2)}) copy-start(pred[128,128]{0,1:T(8,128)(4,1)S(1)} %fusion.79) | copy-start | bytes 49156
  22.7 121.8 %copy-start.13 = (f32[128,64]{1,0:T(8,128)}, f32[128,64]{1,0:T(8,128)S(1)}, u32[]{:S(2)}) copy-start(f32[128,64]{1,0:T(8,128)S(1)} %get-tuple-element.107) | copy-start | bytes 98308
  22.7 121.8 %copy-start.15 = (f32[128,64]{1,0:T(8,128)}, f32[128,64]{1,0:T(8,128)S(1)}, u32[]{:S(2)}) copy-start(f32[128,64]{1,0:T(8,128)S(1)} %get-tuple-element.108) | copy-start | bytes 98308
  28.7 10.9 %collective-permute-start.2 = (bf16[128,1152]{1,0:T(8,128)(2,1)}, bf16[128,1152]{1,0:T(8,128)(2,1)S(1)}, u32[]{:S(2)}, u32[]{:S(2)}) collective-permute-start(bf16[128,1152]{1,0:T(8,128)(2,1)} %bitcast.2), channel_id=1, source_target_pairs={{0,1},{1,0},{2,3},{3,2},{4,5},{5,4},{6,7},{7,6},{8,9},{9,8},{10,11... | collective-permute-start | bytes 884744 | tf_op jit(solution)/shard_map/ppermute | solution.py:162
  34.4 20.7 %collective-permute-start.3 = (bf16[2,288,512]{2,1,0:T(8,128)(2,1)}, bf16[2,288,512]{2,1,0:T(8,128)(2,1)}, u32[]{:S(2)}, u32[]{:S(2)}) collective-permute-start(bf16[2,288,512]{2,1,0:T(8,128)(2,1)} %pad_maximum_fusion.16), channel_id=1, source_target_pairs={{0,16},{16,0},{1,17},{17,1},{2,18},{18,2},{3,19},{19,3},{4,20},{20... | collective-permute-start | bytes 1769480 | tf_op jit(solution)/shard_map/ppermute | solution.py:110
  36.7 15.8 %collective-permute-start.4 = (bf16[2,288,512]{2,1,0:T(8,128)(2,1)}, bf16[2,288,512]{2,1,0:T(8,128)(2,1)}, u32[]{:S(2)}, u32[]{:S(2)}) collective-permute-start(bf16[2,288,512]{2,1,0:T(8,128)(2,1)} %collective-permute-done), channel_id=1, source_target_pairs={{0,4},{4,8},{8,12},{12,14},{14,10},{10,6},{6,2},{2,0},{1,5},{5,9},... | collective-permute-start | bytes 1769480 | tf_op jit(solution)/shard_map/ppermute | solution.py:105
  36.7 16.8 %collective-permute-start.5 = (bf16[2,288,512]{2,1,0:T(8,128)(2,1)}, bf16[2,288,512]{2,1,0:T(8,128)(2,1)}, u32[]{:S(2)}, u32[]{:S(2)}) collective-permute-start(bf16[2,288,512]{2,1,0:T(8,128)(2,1)} %collective-permute-done.1), channel_id=1, source_target_pairs={{0,2},{4,0},{8,4},{12,8},{14,12},{10,14},{6,10},{2,6},{1,3},{5,1},... | collective-permute-start | bytes 1769480 | tf_op jit(solution)/shard_map/ppermute | solution.py:106
  54.5 14.7 %collective-permute-start.6 = (bf16[2,288,512]{2,1,0:T(8,128)(2,1)S(1)}, bf16[2,288,512]{2,1,0:T(8,128)(2,1)S(1)}, u32[]{:S(2)}, u32[]{:S(2)}) collective-permute-start(bf16[2,288,512]{2,1,0:T(8,128)(2,1)S(1)} %pad_maximum_fusion.17), channel_id=1, source_target_pairs={{0,16},{16,0},{1,17},{17,1},{2,18},{18,2},{3,19},{19,3},{4,20},{20... | collective-permute-start | bytes 1769480 | tf_op jit(solution)/shard_map/ppermute | solution.py:110
  58.3 14.6 %collective-permute-start.7 = (bf16[2,288,512]{2,1,0:T(8,128)(2,1)}, bf16[2,288,512]{2,1,0:T(8,128)(2,1)S(1)}, u32[]{:S(2)}, u32[]{:S(2)}) collective-permute-start(bf16[2,288,512]{2,1,0:T(8,128)(2,1)} %collective-permute-done.4), channel_id=1, source_target_pairs={{0,4},{4,8},{8,12},{12,14},{14,10},{10,6},{6,2},{2,0},{1,5},{5,9},... | collective-permute-start | bytes 1769480 | tf_op jit(solution)/shard_map/ppermute | solution.py:105
  58.6 14.6 %collective-permute-start.8 = (bf16[2,288,512]{2,1,0:T(8,128)(2,1)}, bf16[2,288,512]{2,1,0:T(8,128)(2,1)S(1)}, u32[]{:S(2)}, u32[]{:S(2)}) collective-permute-start(bf16[2,288,512]{2,1,0:T(8,128)(2,1)} %collective-permute-done.5), channel_id=1, source_target_pairs={{0,2},{4,0},{8,4},{12,8},{14,12},{10,14},{6,10},{2,6},{1,3},{5,1},... | collective-permute-start | bytes 1769480 | tf_op jit(solution)/shard_map/ppermute | solution.py:106
  73.4 13.5 %collective-permute-start.9 = (bf16[2,288,512]{2,1,0:T(8,128)(2,1)S(1)}, bf16[2,288,512]{2,1,0:T(8,128)(2,1)S(1)}, u32[]{:S(2)}, u32[]{:S(2)}) collective-permute-start(bf16[2,288,512]{2,1,0:T(8,128)(2,1)S(1)} %pad_maximum_fusion.18), channel_id=1, source_target_pairs={{0,16},{16,0},{1,17},{17,1},{2,18},{18,2},{3,19},{19,3},{4,20},{20... | collective-permute-start | bytes 1769480 | tf_op jit(solution)/shard_map/ppermute | solution.py:110
  75.0 13.2 %collective-permute-start.10 = (bf16[2,288,512]{2,1,0:T(8,128)(2,1)S(1)}, bf16[2,288,512]{2,1,0:T(8,128)(2,1)S(1)}, u32[]{:S(2)}, u32[]{:S(2)}) collective-permute-start(bf16[2,288,512]{2,1,0:T(8,128)(2,1)S(1)} %collective-permute-done.7), channel_id=1, source_target_pairs={{0,4},{4,8},{8,12},{12,14},{14,10},{10,6},{6,2},{2,0},{1,5},{5,9},... | collective-permute-start | bytes 1769480 | tf_op jit(solution)/shard_map/ppermute | solution.py:105
  76.0 12.6 %collective-permute-start.11 = (bf16[2,288,512]{2,1,0:T(8,128)(2,1)S(1)}, bf16[2,288,512]{2,1,0:T(8,128)(2,1)S(1)}, u32[]{:S(2)}, u32[]{:S(2)}) collective-permute-start(bf16[2,288,512]{2,1,0:T(8,128)(2,1)S(1)} %collective-permute-done.8), channel_id=1, source_target_pairs={{0,2},{4,0},{8,4},{12,8},{14,12},{10,14},{6,10},{2,6},{1,3},{5,1},... | collective-permute-start | bytes 1769480 | tf_op jit(solution)/shard_map/ppermute | solution.py:106
  88.7 12.8 %collective-permute-start.12 = (bf16[2,288,512]{2,1,0:T(8,128)(2,1)S(1)}, bf16[2,288,512]{2,1,0:T(8,128)(2,1)S(1)}, u32[]{:S(2)}, u32[]{:S(2)}) collective-permute-start(bf16[2,288,512]{2,1,0:T(8,128)(2,1)S(1)} %pad_maximum_fusion.19), channel_id=1, source_target_pairs={{0,16},{16,0},{1,17},{17,1},{2,18},{18,2},{3,19},{19,3},{4,20},{20... | collective-permute-start | bytes 1769480 | tf_op jit(solution)/shard_map/ppermute | solution.py:110
  89.3 12.6 %collective-permute-start.13 = (bf16[2,288,512]{2,1,0:T(8,128)(2,1)S(1)}, bf16[2,288,512]{2,1,0:T(8,128)(2,1)S(1)}, u32[]{:S(2)}, u32[]{:S(2)}) collective-permute-start(bf16[2,288,512]{2,1,0:T(8,128)(2,1)S(1)} %collective-permute-done.10), channel_id=1, source_target_pairs={{0,4},{4,8},{8,12},{12,14},{14,10},{10,6},{6,2},{2,0},{1,5},{5,9},... | collective-permute-start | bytes 1769480 | tf_op jit(solution)/shard_map/ppermute | solution.py:105
  90.0 11.8 %collective-permute-start.14 = (bf16[2,288,512]{2,1,0:T(8,128)(2,1)S(1)}, bf16[2,288,512]{2,1,0:T(8,128)(2,1)S(1)}, u32[]{:S(2)}, u32[]{:S(2)}) collective-permute-start(bf16[2,288,512]{2,1,0:T(8,128)(2,1)S(1)} %collective-permute-done.11), channel_id=1, source_target_pairs={{0,2},{4,0},{8,4},{12,8},{14,12},{10,14},{6,10},{2,6},{1,3},{5,1},... | collective-permute-start | bytes 1769480 | tf_op jit(solution)/shard_map/ppermute | solution.py:106
  101.7 47.6 %copy-start.1 = (bf16[288,1536]{1,0:T(8,128)(2,1)}, bf16[288,1536]{1,0:T(8,128)(2,1)S(1)}, u32[]{:S(2)}) copy-start(bf16[288,1536]{1,0:T(8,128)(2,1)S(1)} %pad_maximum_fusion.9) | copy-start | bytes 2654212
  102.0 13.1 %collective-permute-start.15 = (bf16[2,288,512]{2,1,0:T(8,128)(2,1)S(1)}, bf16[2,288,512]{2,1,0:T(8,128)(2,1)S(1)}, u32[]{:S(2)}, u32[]{:S(2)}) collective-permute-start(bf16[2,288,512]{2,1,0:T(8,128)(2,1)S(1)} %pad_maximum_fusion.20), channel_id=1, source_target_pairs={{0,16},{16,0},{1,17},{17,1},{2,18},{18,2},{3,19},{19,3},{4,20},{20... | collective-permute-start | bytes 1769480 | tf_op jit(solution)/shard_map/ppermute | solution.py:110
  103.6 11.7 %collective-permute-start.16 = (bf16[2,288,512]{2,1,0:T(8,128)(2,1)S(1)}, bf16[2,288,512]{2,1,0:T(8,128)(2,1)S(1)}, u32[]{:S(2)}, u32[]{:S(2)}) collective-permute-start(bf16[2,288,512]{2,1,0:T(8,128)(2,1)S(1)} %collective-permute-done.13), channel_id=1, source_target_pairs={{0,4},{4,8},{8,12},{12,14},{14,10},{10,6},{6,2},{2,0},{1,5},{5,9},... | collective-permute-start | bytes 1769480 | tf_op jit(solution)/shard_map/ppermute | solution.py:105
  105.3 12.5 %collective-permute-start.17 = (bf16[2,288,512]{2,1,0:T(8,128)(2,1)S(1)}, bf16[2,288,512]{2,1,0:T(8,128)(2,1)S(1)}, u32[]{:S(2)}, u32[]{:S(2)}) collective-permute-start(bf16[2,288,512]{2,1,0:T(8,128)(2,1)S(1)} %collective-permute-done.14), channel_id=1, source_target_pairs={{0,2},{4,0},{8,4},{12,8},{14,12},{10,14},{6,10},{2,6},{1,3},{5,1},... | collective-permute-start | bytes 1769480 | tf_op jit(solution)/shard_map/ppermute | solution.py:106
  115.2 33.0 %copy-start.3 = (bf16[288,1536]{1,0:T(8,128)(2,1)}, bf16[288,1536]{1,0:T(8,128)(2,1)S(1)}, u32[]{:S(2)}) copy-start(bf16[288,1536]{1,0:T(8,128)(2,1)S(1)} %pad_maximum_fusion.11) | copy-start | bytes 2654212
  117.8 13.6 %collective-permute-start.18 = (bf16[2,288,512]{2,1,0:T(8,128)(2,1)S(1)}, bf16[2,288,512]{2,1,0:T(8,128)(2,1)S(1)}, u32[]{:S(2)}, u32[]{:S(2)}) collective-permute-start(bf16[2,288,512]{2,1,0:T(8,128)(2,1)S(1)} %pad_maximum_fusion.21), channel_id=1, source_target_pairs={{0,16},{16,0},{1,17},{17,1},{2,18},{18,2},{3,19},{19,3},{4,20},{20... | collective-permute-start | bytes 1769480 | tf_op jit(solution)/shard_map/ppermute | solution.py:110
  117.9 10.0 %collective-permute-start.20 = (bf16[2,288,512]{2,1,0:T(8,128)(2,1)S(1)}, bf16[2,288,512]{2,1,0:T(8,128)(2,1)S(1)}, u32[]{:S(2)}, u32[]{:S(2)}) collective-permute-start(bf16[2,288,512]{2,1,0:T(8,128)(2,1)S(1)} %collective-permute-done.17), channel_id=1, source_target_pairs={{0,2},{4,0},{8,4},{12,8},{14,12},{10,14},{6,10},{2,6},{1,3},{5,1},... | collective-permute-start | bytes 1769480 | tf_op jit(solution)/shard_map/ppermute | solution.py:106
  119.4 9.9 %collective-permute-start.19 = (bf16[2,288,512]{2,1,0:T(8,128)(2,1)S(1)}, bf16[2,288,512]{2,1,0:T(8,128)(2,1)S(1)}, u32[]{:S(2)}, u32[]{:S(2)}) collective-permute-start(bf16[2,288,512]{2,1,0:T(8,128)(2,1)S(1)} %collective-permute-done.16), channel_id=1, source_target_pairs={{0,4},{4,8},{8,12},{12,14},{14,10},{10,6},{6,2},{2,0},{1,5},{5,9},... | collective-permute-start | bytes 1769480 | tf_op jit(solution)/shard_map/ppermute | solution.py:105
  129.4 11.0 %collective-permute-start.21 = (bf16[2,288,512]{2,1,0:T(8,128)(2,1)S(1)}, bf16[2,288,512]{2,1,0:T(8,128)(2,1)S(1)}, u32[]{:S(2)}, u32[]{:S(2)}) collective-permute-start(bf16[2,288,512]{2,1,0:T(8,128)(2,1)S(1)} %pad_maximum_fusion.22), channel_id=1, source_target_pairs={{0,16},{16,0},{1,17},{17,1},{2,18},{18,2},{3,19},{19,3},{4,20},{20... | collective-permute-start | bytes 1769480 | tf_op jit(solution)/shard_map/ppermute | solution.py:110
  131.6 15.6 %copy-start.5 = (bf16[288,1536]{1,0:T(8,128)(2,1)}, bf16[288,1536]{1,0:T(8,128)(2,1)S(1)}, u32[]{:S(2)}) copy-start(bf16[288,1536]{1,0:T(8,128)(2,1)S(1)} %pad_maximum_fusion.13) | copy-start | bytes 2654212
  145.3 15.4 %copy-start.30 = (bf16[4,128,64]{2,1,0:T(8,128)(2,1)}, bf16[4,128,64]{2,1,0:T(8,128)(2,1)S(1)}, u32[]{:S(2)}) copy-start(bf16[4,128,64]{2,1,0:T(8,128)(2,1)S(1)} %get-tuple-element.105) | copy-start | bytes 196612
  151.1 5.7 %copy-start.18 = (bf16[128,512]{1,0:T(8,128)(2,1)}, bf16[128,512]{1,0:T(8,128)(2,1)S(1)}, u32[]{:S(2)}) copy-start(bf16[128,512]{1,0:T(8,128)(2,1)S(1)} %fusion.15) | copy-start | bytes 393220
  151.9 4.0 %copy-start.4 = (bf16[288,1536]{1,0:T(8,128)(2,1)S(1)}, bf16[288,1536]{1,0:T(8,128)(2,1)}, u32[]{:S(2)}) copy-start(bf16[288,1536]{1,0:T(8,128)(2,1)} %copy-done.3) | copy-start | bytes 2654212
  151.9 4.9 %copy-start.2 = (bf16[288,1536]{1,0:T(8,128)(2,1)S(1)}, bf16[288,1536]{1,0:T(8,128)(2,1)}, u32[]{:S(2)}) copy-start(bf16[288,1536]{1,0:T(8,128)(2,1)} %copy-done.1) | copy-start | bytes 2654212
  164.7 2.5 %collective-permute-start.22 = (bf16[128,2304]{1,0:T(8,128)(2,1)S(1)}, bf16[128,2304]{1,0:T(8,128)(2,1)S(1)}, u32[]{:S(2)}, u32[]{:S(2)}) collective-permute-start(bf16[128,2304]{1,0:T(8,128)(2,1)S(1)} %convolution_convert_fusion), channel_id=1, source_target_pairs={{0,1},{1,0},{2,3},{3,2},{4,5},{5,4},{6,7},{7,6},{8,9},{9,8},{10,11... | collective-permute-start | bytes 1769480 | tf_op jit(solution)/shard_map/ppermute | solution.py:58
  170.2 3.2 %copy-start.35 = (pred[128,128]{0,1:T(8,128)(4,1)S(1)}, pred[128,128]{0,1:T(8,128)(4,1)}, u32[]{:S(2)}) copy-start(pred[128,128]{0,1:T(8,128)(4,1)} %copy-done.34) | copy-start | bytes 49156
  170.2 3.2 %copy-start.55 = (f32[4,2,128]{2,1,0:T(2,128)S(1)}, f32[4,2,128]{2,1,0:T(2,128)}, u32[]{:S(2)}) copy-start(f32[4,2,128]{2,1,0:T(2,128)} %copy-done.54) | copy-start | bytes 12292
  172.2 3.2 %copy-start.19 = (bf16[128,512]{1,0:T(8,128)(2,1)S(1)}, bf16[128,512]{1,0:T(8,128)(2,1)}, u32[]{:S(2)}) copy-start(bf16[128,512]{1,0:T(8,128)(2,1)} %copy-done.18) | copy-start | bytes 393220
  187.1 4.2 %copy-start.8 = (bf16[512,2304]{0,1:T(8,128)(2,1)S(1)}, bf16[512,2304]{0,1:T(8,128)(2,1)}, u32[]{:S(2)}) copy-start(bf16[512,2304]{0,1:T(8,128)(2,1)} %copy-done.7) | copy-start | bytes 7077892
  187.1 4.2 %copy-start.24 = (bf16[128,4,128]{0,2,1:T(8,128)(2,1)S(1)}, bf16[128,4,128]{0,2,1:T(8,128)(2,1)}, u32[]{:S(2)}) copy-start(bf16[128,4,128]{0,2,1:T(8,128)(2,1)} %copy.75) | copy-start | bytes 393220
  192.3 3.1 %copy-start.49 = (s32[4]{0:T(128)S(1)}, s32[4]{0:T(128)}, u32[]{:S(2)}) copy-start(s32[4]{0:T(128)} %copy-done.48) | copy-start | bytes 52
  194.8 2.5 %collective-permute-start.23 = (bf16[128,2304]{1,0:T(8,128)(2,1)S(1)}, bf16[128,2304]{1,0:T(8,128)(2,1)}, u32[]{:S(2)}, u32[]{:S(2)}) collective-permute-start(bf16[128,2304]{1,0:T(8,128)(2,1)S(1)} %fusion.1), channel_id=1, source_target_pairs={{0,1},{1,0},{2,3},{3,2},{4,5},{5,4},{6,7},{7,6},{8,9},{9,8},{10,11... | collective-permute-start | bytes 1769480 | tf_op jit(solution)/shard_map/ppermute | solution.py:58
  (33 other events, 58.4 us)

commit v16 on v13

--- a/solution.py
+++ b/solution.py
@@ -119,7 +119,7 @@
                 )
             )
     if n <= PIECEWISE_RING:
-        for step in range(n - 1):
+        for step in range(n - 2):
             front_pieces[step], back_pieces[step], _, _ = lax.optimization_barrier(
                 (front_pieces[step], back_pieces[step], front_ring[step + 1], back_ring[step + 1])
             )

time: 205 us -> 222 us (1.083)
  local copies, waits for them, and re-layouts: 32.7 us -> 47 us
  other arithmetic: 24.7 us -> 33.8 us
  waiting for transfers between devices: 71 us -> 65 us
  starting transfers between devices: 34.2 us -> 30.3 us
  matrix products: 22.7 us -> 26.4 us
    ppermute x7, waiting for transfers between devices: 40.2 us -> 7.13 us  [ring_gather(): lax.ppermute(jnp.stack([front_ring[step][0], back_ring[step][0]]), 'group...]
    ppermute x7, waiting for transfers between devices: 19.2 us -> 49.3 us  [ring_gather(): front_ring.append(lax.ppermute(front_ring[-1], 'seq', forward_pairs))]
    unnamed x141 -> x157, local copies, waits for them, and re-layouts: 14.6 us -> 23.9 us
    ppermute x7, starting transfers between devices: 11.9 us -> 8.08 us  [ring_gather(): lax.ppermute(jnp.stack([front_ring[step][0], back_ring[step][0]]), 'group...]
  transfers between devices with their start and end apart: 24 -> 24, of which waited for: 18 -> 16; matrix products, arithmetic and copies ran while one was open for 14% -> 20% of each run, Pallas kernels for 0% -> 0%
where the time goes in v16:
time: 222 us; the launch traced here: 220 us
  waiting for transfers between devices  65 us (29%)
  local copies, waits for them, and re-layouts  47 us (21%)
  other arithmetic  33.8 us (15%)
  starting transfers between devices  30.3 us (14%)
  matrix products  26.4 us (12%)
  blocking collectives  16.6 us (7%)
    ppermute x7, waiting for transfers between devices, ring_gather(): front_ring.append(lax.ppermute(front_ring[-1], 'seq', forward_pairs))  49.3 us
    unnamed x157, local copies, waits for them, and re-layouts  23.9 us
    all_to_all x1, blocking collectives, shards(): lax.all_to_all(grad_rows, 'seq', split_axis=0, concat_axis=0, tiled=True)  14.1 us
    ppermute x7, starting transfers between devices, ring_gather(): front_ring.append(lax.ppermute(front_ring[-1], 'seq', forward_pairs))  9.05 us
    ppermute x7, waiting for transfers between devices, ring_gather(): back_ring.append(lax.ppermute(back_ring[-1], 'seq', backward_pairs))  8.36 us
    ppermute x7, starting transfers between devices, ring_gather(): lax.ppermute(jnp.stack([front_ring[step][0], back_ring[step][0]]), 'group...  8.08 us
    all_to_all x1, starting transfers between devices, shards(): lax.all_to_all(generator_rows, 'seq', split_axis=0, concat_axis=0, tiled=...  7.25 us
    ppermute x7, waiting for transfers between devices, ring_gather(): lax.ppermute(jnp.stack([front_ring[step][0], back_ring[step][0]]), 'group...  7.13 us
  transfers between devices with their start and end apart: 24, of which 16 were waited for; matrix products, arithmetic and copies ran while one was open for 20% of the time, Pallas kernels for 0%

profile of v16, /device:TPU:0, one launch (start us, length us, event | category | flops | bytes accessed | tf_op | source)
XLA Modules:
  0.0 220.3 jit_solution(12361332216597826023)
XLA Ops:
  0.0 7.3 %all-to-all-start = ((bf16[8,16,1152]{2,1,0:T(8,128)(2,1)}), bf16[8,16,1152]{2,1,0:T(8,128)(2,1)}, u32[]{:S(2)}, u32[]{:S(2)}) async-start(bf16[8,16,1152]{2,1,0:T(8,128)(2,1)} %bitcast.306), calls=%async_computation | async-start | bytes 589824 | tf_op jit(solution)/shard_map/all_to_all | solution.py:153
  7.3 1.4 fusion.47
  9.7 2.0 collective-permute-start
  18.5 1.2 pad_maximum_fusion
  19.7 1.2 compare_convert_fusion
  22.5 1.4 mul.519
  23.8 1.6 reshape.410
  30.0 2.4 %all_gather.3 = bf16[128,2304]{1,0:T(8,128)(2,1)S(1)} all-gather(bf16[128,1152]{1,0:T(8,128)(2,1)} %bitcast.2), channel_id=1, replica_groups=mesh['groups'=2,'seq'=8,'wg'=2] {'wg'}, dimensions={1}, use_global_device_ids=true | all-gather | bytes 884736 | tf_op jit(solution)/shard_map/all_gather | solution.py:162
  37.6 1.9 collective-permute-start.3
  40.7 1.6 collective-permute-start.2
  43.5 9.5 %collective-permute-done.3 = bf16[2,288,512]{2,1,0:T(8,128)(2,1)S(1)} collective-permute-done((bf16[2,288,512]{2,1,0:T(8,128)(2,1)S(1)}, bf16[2,288,512]{2,1,0:T(8,128)(2,1)S(1)}, u32[]{:S(2)}, u32[]{:S(2)}) %collective-permute-start.3) | collective-permute-done | bytes 589856 | tf_op jit(solution)/shard_map/ppermute | solution.py:105
  53.0 2.7 %collective-permute-done.4 = bf16[2,288,512]{2,1,0:T(8,128)(2,1)S(1)} collective-permute-done((bf16[2,288,512]{2,1,0:T(8,128)(2,1)}, bf16[2,288,512]{2,1,0:T(8,128)(2,1)S(1)}, u32[]{:S(2)}, u32[]{:S(2)}) %collective-permute-start.4) | collective-permute-done | bytes 589856 | tf_op jit(solution)/shard_map/ppermute | solution.py:106
  55.9 1.6 collective-permute-start.5
  57.4 1.2 select_bitcast_fusion.21
  59.6 1.2 collective-permute-start.7
  62.9 9.9 %collective-permute-done.6 = bf16[2,288,512]{2,1,0:T(8,128)(2,1)S(1)} collective-permute-done((bf16[2,288,512]{2,1,0:T(8,128)(2,1)S(1)}, bf16[2,288,512]{2,1,0:T(8,128)(2,1)S(1)}, u32[]{:S(2)}, u32[]{:S(2)}) %collective-permute-start.6) | collective-permute-done | bytes 589856 | tf_op jit(solution)/shard_map/ppermute | solution.py:105
  74.4 1.4 collective-permute-start.9
  78.5 8.4 %collective-permute-done.9 = bf16[2,288,512]{2,1,0:T(8,128)(2,1)S(1)} collective-permute-done((bf16[2,288,512]{2,1,0:T(8,128)(2,1)S(1)}, bf16[2,288,512]{2,1,0:T(8,128)(2,1)S(1)}, u32[]{:S(2)}, u32[]{:S(2)}) %collective-permute-start.9) | collective-permute-done | bytes 589856 | tf_op jit(solution)/shard_map/ppermute | solution.py:105
  86.9 1.1 collective-permute-done.10
  88.0 1.6 collective-permute-start.11
  89.9 1.5 collective-permute-start.12
  94.0 7.8 %collective-permute-done.12 = bf16[2,288,512]{2,1,0:T(8,128)(2,1)S(1)} collective-permute-done((bf16[2,288,512]{2,1,0:T(8,128)(2,1)S(1)}, bf16[2,288,512]{2,1,0:T(8,128)(2,1)S(1)}, u32[]{:S(2)}, u32[]{:S(2)}) %collective-permute-start.12) | collective-permute-done | bytes 589856 | tf_op jit(solution)/shard_map/ppermute | solution.py:105
  101.8 1.6 collective-permute-done.13
  104.8 1.2 collective-permute-start.16
  108.0 7.8 %collective-permute-done.15 = bf16[2,288,512]{2,1,0:T(8,128)(2,1)S(1)} collective-permute-done((bf16[2,288,512]{2,1,0:T(8,128)(2,1)S(1)}, bf16[2,288,512]{2,1,0:T(8,128)(2,1)S(1)}, u32[]{:S(2)}, u32[]{:S(2)}) %collective-permute-start.15) | collective-permute-done | bytes 589856 | tf_op jit(solution)/shard_map/ppermute | solution.py:105
  117.0 2.4 %collective-permute-start.17 = (bf16[2,288,512]{2,1,0:T(8,128)(2,1)S(1)}, bf16[2,288,512]{2,1,0:T(8,128)(2,1)S(1)}, u32[]{:S(2)}, u32[]{:S(2)}) collective-permute-start(bf16[2,288,512]{2,1,0:T(8,128)(2,1)S(1)} %pad_maximum_fusion.19), channel_id=1, source_target_pairs={{0,16},{16,0},{1,17},{17,1},{2,18},{18,2},{3,19},{19,3},{4,20},{20... | collective-permute-start | bytes 1769480 | tf_op jit(solution)/shard_map/ppermute | solution.py:110
  120.2 1.5 collective-permute-start.19
  123.7 5.9 %collective-permute-done.18 = bf16[2,288,512]{2,1,0:T(8,128)(2,1)S(1)} collective-permute-done((bf16[2,288,512]{2,1,0:T(8,128)(2,1)S(1)}, bf16[2,288,512]{2,1,0:T(8,128)(2,1)S(1)}, u32[]{:S(2)}, u32[]{:S(2)}) %collective-permute-start.18) | collective-permute-done | bytes 589856 | tf_op jit(solution)/shard_map/ppermute | solution.py:105
  133.3 6.8 %collective-permute-done.20 = bf16[2,288,512]{2,1,0:T(8,128)(2,1)S(1)} collective-permute-done((bf16[2,288,512]{2,1,0:T(8,128)(2,1)S(1)}, bf16[2,288,512]{2,1,0:T(8,128)(2,1)S(1)}, u32[]{:S(2)}, u32[]{:S(2)}) %collective-permute-start.20) | collective-permute-done | bytes 589856 | tf_op jit(solution)/shard_map/ppermute | solution.py:110
  145.5 1.7 copy.116
  147.2 1.2 copy.101
  148.4 1.1 subtract_convert_fusion.4
  160.7 1.4 copy-done
  162.1 1.7 convolution_convert_fusion
  167.4 1.5 multiply_reduce_fusion.1
  169.7 2.1 convolution_convert_fusion.2
  171.8 1.2 copy.92
  173.0 2.0 fusion.17
  176.0 2.7 %convolution_bitcast_fusion.1 = f32[4,128,128]{2,1,0:T(8,128)} fusion(bf16[4,2,128,128]{3,2,1,0:T(8,128)(2,1)} %copy-done.38, f32[4,2,128,128]{2,3,1,0:T(8,128)} %fusion.65, f32[4,2,128,128]{2,3,1,0:T(8,128)} %copy-done.63, f32[4,2,128]{2,1,0:T(2,128)S(1)} %copy-done.65, pred[128,128]{0,1:T(8,128)(4,1)S(1)} %copy-done.47), kind=kOutput, calls=%fused_computation.49 | convolution fusion | flops 35259520 | bytes 1593344 | tf_op jit(solution)/shard_map/kgij,kgid->kjd/dot_general | solution.py:274
  178.7 2.2 %convolution_multiply_fusion.1 = f32[4,2,128,128]{3,2,1,0:T(8,128)S(1)} fusion(f32[4,2,128,128]{2,3,1,0:T(8,128)} %fusion.65, f32[4,2,128,128]{2,3,1,0:T(8,128)} %copy-done.63, bf16[4,128,64]{2,1,0:T(8,128)(2,1)} %copy-done.41, bf16[4,128,64]{2,1,0:T(8,128)(2,1)} %copy-done.40, f32[4,2,128]{2,1,0:T(2,128)S(1)} %copy-done.65, pred[128,128]{0,1:T(8,128)(4,1)} %fusion.89), kind=kOutput, calls=%fused_computation.25 | convolution fusion | flops 35652736 | bytes 1724416 | tf_op jit(solution)/shard_map/kgij,kjd->kgid/dot_general | solution.py:270
  180.9 1.2 add_convert_fusion.1
  182.9 1.7 copy.74
  186.5 4.1 %fusion.50 = f32[128,2304]{1,0:T(8,128)S(1)} fusion(bf16[1024,2304]{0,1:T(8,128)(2,1)} %fusion.37, bf16[16,8,8,128]{3,2,1,0:T(8,128)(2,1)S(1)} %bitcast.302), kind=kOutput, calls=%fused_computation.202 | convolution fusion | flops 603979776 | bytes 6160384 | tf_op jit(solution)/shard_map/dot_general | solution.py:284
  193.6 1.3 gather_fusion
  198.2 1.5 fusion.14
  199.8 3.0 %fusion.13 = bf16[128,2304]{1,0:T(8,128)(2,1)} fusion(bf16[128,2304]{1,0:T(8,128)(2,1)} %collective-permute-done.22, bf16[128,2304]{1,0:T(8,128)(2,1)S(1)} %fusion.1, f32[128]{0:T(128)S(1)} %broadcast_multiply_fusion, f32[128]{0:T(128)} %get-tuple-element.102, f32[2304]{0:T(1024)S(1)} %copy-done.39, f32[128]{0:T(128)} %get-tuple-element.103, ...), kind=kLoop, calls=%fused_computation.36 | loop fusion | flops 6488064 | bytes 4742912 | tf_op jit(solution)/shard_map/convert_element_type | solution.py:296
  202.7 1.4 copy.76
  205.4 14.1 %all_to_all.21 = bf16[8,16,1152]{2,1,0:T(8,128)(2,1)S(1)} all-to-all(bf16[8,16,1152]{2,1,0:T(8,128)(2,1)S(1)} %broadcast_select_fusion.6), channel_id=1, replica_groups=mesh['groups'=2,'seq'=8,'wg'=2] {'seq'}, dimensions={0} | all-to-all | bytes 589824 | tf_op jit(solution)/shard_map/all_to_all | solution.py:298
  (311 shorter events, 74.9 us)
Async XLA Ops:
  0.0 30.0 %all-to-all-start = ((bf16[8,16,1152]{2,1,0:T(8,128)(2,1)}), bf16[8,16,1152]{2,1,0:T(8,128)(2,1)}, u32[]{:S(2)}, u32[]{:S(2)}) async-start(bf16[8,16,1152]{2,1,0:T(8,128)(2,1)} %bitcast.306), calls=%async_computation | async-start | bytes 589824 | tf_op jit(solution)/shard_map/all_to_all | solution.py:153
  8.7 4.0 %copy-start.60 = (s32[8]{0:T(128)S(1)}, s32[8]{0:T(128)}, u32[]{:S(2)}) copy-start(s32[8]{0:T(128)} %param.21) | copy-start | bytes 100
  8.7 4.6 %copy-start.61 = (s32[8]{0:T(128)S(1)}, s32[8]{0:T(128)}, u32[]{:S(2)}) copy-start(s32[8]{0:T(128)} %param.20) | copy-start | bytes 100
  8.7 6.5 %copy-start.48 = (f32[2304]{0:T(1024)S(1)}, f32[2304]{0:T(1024)}, u32[]{:S(2)}) copy-start(f32[2304]{0:T(1024)} %param.12) | copy-start | bytes 27652
  8.7 6.5 %copy-start.49 = (f32[2304]{0:T(1024)S(1)}, f32[2304]{0:T(1024)}, u32[]{:S(2)}) copy-start(f32[2304]{0:T(1024)} %param.17) | copy-start | bytes 27652
  8.7 6.6 %copy-start.50 = (f32[2304]{0:T(1024)S(1)}, f32[2304]{0:T(1024)}, u32[]{:S(2)}) copy-start(f32[2304]{0:T(1024)} %param.18) | copy-start | bytes 27652
  8.7 9.7 %copy-start.17 = (bf16[288,1024]{1,0:T(8,128)(2,1)S(1)}, bf16[288,1024]{1,0:T(8,128)(2,1)}, u32[]{:S(2)}) copy-start(bf16[288,1024]{1,0:T(8,128)(2,1)} %param.13) | copy-start | bytes 1769476
  8.7 9.7 %copy-start.18 = (bf16[1024,288]{0,1:T(8,128)(2,1)S(1)}, bf16[1024,288]{0,1:T(8,128)(2,1)}, u32[]{:S(2)}) copy-start(bf16[1024,288]{0,1:T(8,128)(2,1)} %param.16) | copy-start | bytes 1769476
  9.7 17.8 %collective-permute-start = (bf16[2,288,512]{2,1,0:T(8,128)(2,1)}, bf16[2,288,512]{2,1,0:T(8,128)(2,1)S(1)}, u32[]{:S(2)}, u32[]{:S(2)}) collective-permute-start(bf16[2,288,512]{2,1,0:T(8,128)(2,1)} %pad_maximum_fusion.12), channel_id=1, source_target_pairs={{0,4},{4,8},{8,12},{12,14},{14,10},{10,6},{6,2},{2,0},{1,5},{5,9},... | collective-permute-start | bytes 1769480 | tf_op jit(solution)/shard_map/ppermute | solution.py:105
  12.6 15.8 %collective-permute-start.1 = (bf16[2,288,512]{2,1,0:T(8,128)(2,1)}, bf16[2,288,512]{2,1,0:T(8,128)(2,1)}, u32[]{:S(2)}, u32[]{:S(2)}) collective-permute-start(bf16[2,288,512]{2,1,0:T(8,128)(2,1)} %pad_maximum_fusion.13), channel_id=1, source_target_pairs={{0,2},{4,0},{8,4},{12,8},{14,12},{10,14},{6,10},{2,6},{1,3},{5,1},... | collective-permute-start | bytes 1769480 | tf_op jit(solution)/shard_map/ppermute | solution.py:106
  12.6 8.2 %copy-start.53 = (pred[8]{0:T(512)(128)(4,1)}, pred[8]{0:T(512)(128)(4,1)S(1)}, u32[]{:S(2)}) copy-start(pred[8]{0:T(512)(128)(4,1)S(1)} %compare_and_fusion) | copy-start | bytes 28
  14.5 3.3 %copy-start.58 = (pred[128]{0:T(512)(128)(4,1)}, pred[128]{0:T(512)(128)(4,1)S(1)}, u32[]{:S(2)}) copy-start(pred[128]{0:T(512)(128)(4,1)S(1)} %iota_compare_fusion.1) | copy-start | bytes 388
  21.0 145.7 %copy-start.44 = (pred[2304]{0:T(1024)(128)(4,1)}, pred[2304]{0:T(1024)(128)(4,1)S(1)}, u32[]{:S(2)}) copy-start(pred[2304]{0:T(1024)(128)(4,1)S(1)} %broadcast_in_dim.117) | copy-start | bytes 6916
  37.6 15.4 %collective-permute-start.3 = (bf16[2,288,512]{2,1,0:T(8,128)(2,1)S(1)}, bf16[2,288,512]{2,1,0:T(8,128)(2,1)S(1)}, u32[]{:S(2)}, u32[]{:S(2)}) collective-permute-start(bf16[2,288,512]{2,1,0:T(8,128)(2,1)S(1)} %collective-permute-done), channel_id=1, source_target_pairs={{0,4},{4,8},{8,12},{12,14},{14,10},{10,6},{6,2},{2,0},{1,5},{5,9},... | collective-permute-start | bytes 1769480 | tf_op jit(solution)/shard_map/ppermute | solution.py:105
  40.4 15.3 %collective-permute-start.4 = (bf16[2,288,512]{2,1,0:T(8,128)(2,1)}, bf16[2,288,512]{2,1,0:T(8,128)(2,1)S(1)}, u32[]{:S(2)}, u32[]{:S(2)}) collective-permute-start(bf16[2,288,512]{2,1,0:T(8,128)(2,1)} %collective-permute-done.1), channel_id=1, source_target_pairs={{0,2},{4,0},{8,4},{12,8},{14,12},{10,14},{6,10},{2,6},{1,3},{5,1},... | collective-permute-start | bytes 1769480 | tf_op jit(solution)/shard_map/ppermute | solution.py:106
  40.7 16.7 %collective-permute-start.2 = (bf16[2,288,512]{2,1,0:T(8,128)(2,1)S(1)}, bf16[2,288,512]{2,1,0:T(8,128)(2,1)S(1)}, u32[]{:S(2)}, u32[]{:S(2)}) collective-permute-start(bf16[2,288,512]{2,1,0:T(8,128)(2,1)S(1)} %pad_maximum_fusion.14), channel_id=1, source_target_pairs={{0,16},{16,0},{1,17},{17,1},{2,18},{18,2},{3,19},{19,3},{4,20},{20... | collective-permute-start | bytes 1769480 | tf_op jit(solution)/shard_map/ppermute | solution.py:110
  55.9 18.3 %collective-permute-start.5 = (bf16[2,288,512]{2,1,0:T(8,128)(2,1)S(1)}, bf16[2,288,512]{2,1,0:T(8,128)(2,1)S(1)}, u32[]{:S(2)}, u32[]{:S(2)}) collective-permute-start(bf16[2,288,512]{2,1,0:T(8,128)(2,1)S(1)} %pad_maximum_fusion.15), channel_id=1, source_target_pairs={{0,16},{16,0},{1,17},{17,1},{2,18},{18,2},{3,19},{19,3},{4,20},{20... | collective-permute-start | bytes 1769480 | tf_op jit(solution)/shard_map/ppermute | solution.py:110
  58.8 14.0 %collective-permute-start.6 = (bf16[2,288,512]{2,1,0:T(8,128)(2,1)S(1)}, bf16[2,288,512]{2,1,0:T(8,128)(2,1)S(1)}, u32[]{:S(2)}, u32[]{:S(2)}) collective-permute-start(bf16[2,288,512]{2,1,0:T(8,128)(2,1)S(1)} %collective-permute-done.3), channel_id=1, source_target_pairs={{0,4},{4,8},{8,12},{12,14},{14,10},{10,6},{6,2},{2,0},{1,5},{5,9},... | collective-permute-start | bytes 1769480 | tf_op jit(solution)/shard_map/ppermute | solution.py:105
  59.6 13.6 %collective-permute-start.7 = (bf16[2,288,512]{2,1,0:T(8,128)(2,1)S(1)}, bf16[2,288,512]{2,1,0:T(8,128)(2,1)S(1)}, u32[]{:S(2)}, u32[]{:S(2)}) collective-permute-start(bf16[2,288,512]{2,1,0:T(8,128)(2,1)S(1)} %collective-permute-done.4), channel_id=1, source_target_pairs={{0,2},{4,0},{8,4},{12,8},{14,12},{10,14},{6,10},{2,6},{1,3},{5,1},... | collective-permute-start | bytes 1769480 | tf_op jit(solution)/shard_map/ppermute | solution.py:106
  73.4 16.2 %collective-permute-start.8 = (bf16[2,288,512]{2,1,0:T(8,128)(2,1)S(1)}, bf16[2,288,512]{2,1,0:T(8,128)(2,1)S(1)}, u32[]{:S(2)}, u32[]{:S(2)}) collective-permute-start(bf16[2,288,512]{2,1,0:T(8,128)(2,1)S(1)} %pad_maximum_fusion.16), channel_id=1, source_target_pairs={{0,16},{16,0},{1,17},{17,1},{2,18},{18,2},{3,19},{19,3},{4,20},{20... | collective-permute-start | bytes 1769480 | tf_op jit(solution)/shard_map/ppermute | solution.py:110
  74.4 12.5 %collective-permute-start.9 = (bf16[2,288,512]{2,1,0:T(8,128)(2,1)S(1)}, bf16[2,288,512]{2,1,0:T(8,128)(2,1)S(1)}, u32[]{:S(2)}, u32[]{:S(2)}) collective-permute-start(bf16[2,288,512]{2,1,0:T(8,128)(2,1)S(1)} %collective-permute-done.6), channel_id=1, source_target_pairs={{0,4},{4,8},{8,12},{12,14},{14,10},{10,6},{6,2},{2,0},{1,5},{5,9},... | collective-permute-start | bytes 1769480 | tf_op jit(solution)/shard_map/ppermute | solution.py:105
  75.8 12.2 %collective-permute-start.10 = (bf16[2,288,512]{2,1,0:T(8,128)(2,1)S(1)}, bf16[2,288,512]{2,1,0:T(8,128)(2,1)S(1)}, u32[]{:S(2)}, u32[]{:S(2)}) collective-permute-start(bf16[2,288,512]{2,1,0:T(8,128)(2,1)S(1)} %collective-permute-done.7), channel_id=1, source_target_pairs={{0,2},{4,0},{8,4},{12,8},{14,12},{10,14},{6,10},{2,6},{1,3},{5,1},... | collective-permute-start | bytes 1769480 | tf_op jit(solution)/shard_map/ppermute | solution.py:106
  88.0 15.6 %collective-permute-start.11 = (bf16[2,288,512]{2,1,0:T(8,128)(2,1)S(1)}, bf16[2,288,512]{2,1,0:T(8,128)(2,1)S(1)}, u32[]{:S(2)}, u32[]{:S(2)}) collective-permute-start(bf16[2,288,512]{2,1,0:T(8,128)(2,1)S(1)} %pad_maximum_fusion.17), channel_id=1, source_target_pairs={{0,16},{16,0},{1,17},{17,1},{2,18},{18,2},{3,19},{19,3},{4,20},{20... | collective-permute-start | bytes 1769480 | tf_op jit(solution)/shard_map/ppermute | solution.py:110
  89.9 11.9 %collective-permute-start.12 = (bf16[2,288,512]{2,1,0:T(8,128)(2,1)S(1)}, bf16[2,288,512]{2,1,0:T(8,128)(2,1)S(1)}, u32[]{:S(2)}, u32[]{:S(2)}) collective-permute-start(bf16[2,288,512]{2,1,0:T(8,128)(2,1)S(1)} %collective-permute-done.9), channel_id=1, source_target_pairs={{0,4},{4,8},{8,12},{12,14},{14,10},{10,6},{6,2},{2,0},{1,5},{5,9},... | collective-permute-start | bytes 1769480 | tf_op jit(solution)/shard_map/ppermute | solution.py:105
  91.4 12.1 %collective-permute-start.13 = (bf16[2,288,512]{2,1,0:T(8,128)(2,1)S(1)}, bf16[2,288,512]{2,1,0:T(8,128)(2,1)S(1)}, u32[]{:S(2)}, u32[]{:S(2)}) collective-permute-start(bf16[2,288,512]{2,1,0:T(8,128)(2,1)S(1)} %collective-permute-done.10), channel_id=1, source_target_pairs={{0,2},{4,0},{8,4},{12,8},{14,12},{10,14},{6,10},{2,6},{1,3},{5,1},... | collective-permute-start | bytes 1769480 | tf_op jit(solution)/shard_map/ppermute | solution.py:106
  103.6 15.9 %collective-permute-start.14 = (bf16[2,288,512]{2,1,0:T(8,128)(2,1)S(1)}, bf16[2,288,512]{2,1,0:T(8,128)(2,1)S(1)}, u32[]{:S(2)}, u32[]{:S(2)}) collective-permute-start(bf16[2,288,512]{2,1,0:T(8,128)(2,1)S(1)} %pad_maximum_fusion.18), channel_id=1, source_target_pairs={{0,16},{16,0},{1,17},{17,1},{2,18},{18,2},{3,19},{19,3},{4,20},{20... | collective-permute-start | bytes 1769480 | tf_op jit(solution)/shard_map/ppermute | solution.py:110
  103.8 40.0 %copy-start.1 = (bf16[288,1536]{1,0:T(8,128)(2,1)}, bf16[288,1536]{1,0:T(8,128)(2,1)S(1)}, u32[]{:S(2)}) copy-start(bf16[288,1536]{1,0:T(8,128)(2,1)S(1)} %pad_maximum_fusion.9) | copy-start | bytes 2654212
  103.9 11.9 %collective-permute-start.15 = (bf16[2,288,512]{2,1,0:T(8,128)(2,1)S(1)}, bf16[2,288,512]{2,1,0:T(8,128)(2,1)S(1)}, u32[]{:S(2)}, u32[]{:S(2)}) collective-permute-start(bf16[2,288,512]{2,1,0:T(8,128)(2,1)S(1)} %collective-permute-done.12), channel_id=1, source_target_pairs={{0,4},{4,8},{8,12},{12,14},{14,10},{10,6},{6,2},{2,0},{1,5},{5,9},... | collective-permute-start | bytes 1769480 | tf_op jit(solution)/shard_map/ppermute | solution.py:105
  104.8 12.1 %collective-permute-start.16 = (bf16[2,288,512]{2,1,0:T(8,128)(2,1)S(1)}, bf16[2,288,512]{2,1,0:T(8,128)(2,1)S(1)}, u32[]{:S(2)}, u32[]{:S(2)}) collective-permute-start(bf16[2,288,512]{2,1,0:T(8,128)(2,1)S(1)} %collective-permute-done.13), channel_id=1, source_target_pairs={{0,2},{4,0},{8,4},{12,8},{14,12},{10,14},{6,10},{2,6},{1,3},{5,1},... | collective-permute-start | bytes 1769480 | tf_op jit(solution)/shard_map/ppermute | solution.py:106
  115.8 14.8 %copy-start.21 = (bf16[2,288,512]{2,1,0:T(8,128)(2,1)}, bf16[2,288,512]{2,1,0:T(8,128)(2,1)S(1)}, u32[]{:S(2)}) copy-start(bf16[2,288,512]{2,1,0:T(8,128)(2,1)S(1)} %collective-permute-done.15) | copy-start | bytes 1769476
  116.9 26.6 %copy-start.9 = (bf16[2,288,512]{2,1,0:T(8,128)(2,1)}, bf16[2,288,512]{2,1,0:T(8,128)(2,1)S(1)}, u32[]{:S(2)}) copy-start(bf16[2,288,512]{2,1,0:T(8,128)(2,1)S(1)} %collective-permute-done.16) | copy-start | bytes 1769476
  117.0 13.6 %collective-permute-start.17 = (bf16[2,288,512]{2,1,0:T(8,128)(2,1)S(1)}, bf16[2,288,512]{2,1,0:T(8,128)(2,1)S(1)}, u32[]{:S(2)}, u32[]{:S(2)}) collective-permute-start(bf16[2,288,512]{2,1,0:T(8,128)(2,1)S(1)} %pad_maximum_fusion.19), channel_id=1, source_target_pairs={{0,16},{16,0},{1,17},{17,1},{2,18},{18,2},{3,19},{19,3},{4,20},{20... | collective-permute-start | bytes 1769480 | tf_op jit(solution)/shard_map/ppermute | solution.py:110
  119.6 4.1 %copy-start.3 = (bf16[288,1536]{1,0:T(8,128)(2,1)}, bf16[288,1536]{1,0:T(8,128)(2,1)S(1)}, u32[]{:S(2)}) copy-start(bf16[288,1536]{1,0:T(8,128)(2,1)S(1)} %pad_maximum_fusion.11) | copy-start | bytes 2654212
  119.7 9.9 %collective-permute-start.18 = (bf16[2,288,512]{2,1,0:T(8,128)(2,1)S(1)}, bf16[2,288,512]{2,1,0:T(8,128)(2,1)S(1)}, u32[]{:S(2)}, u32[]{:S(2)}) collective-permute-start(bf16[2,288,512]{2,1,0:T(8,128)(2,1)S(1)} %collective-permute-done.15), channel_id=1, source_target_pairs={{0,4},{4,8},{8,12},{12,14},{14,10},{10,6},{6,2},{2,0},{1,5},{5,9},... | collective-permute-start | bytes 1769480 | tf_op jit(solution)/shard_map/ppermute | solution.py:105
  120.2 9.9 %collective-permute-start.19 = (bf16[2,288,512]{2,1,0:T(8,128)(2,1)S(1)}, bf16[2,288,512]{2,1,0:T(8,128)(2,1)S(1)}, u32[]{:S(2)}, u32[]{:S(2)}) collective-permute-start(bf16[2,288,512]{2,1,0:T(8,128)(2,1)S(1)} %collective-permute-done.16), channel_id=1, source_target_pairs={{0,2},{4,0},{8,4},{12,8},{14,12},{10,14},{6,10},{2,6},{1,3},{5,1},... | collective-permute-start | bytes 1769480 | tf_op jit(solution)/shard_map/ppermute | solution.py:106
  129.6 10.5 %copy-start.19 = (bf16[2,288,512]{2,1,0:T(8,128)(2,1)}, bf16[2,288,512]{2,1,0:T(8,128)(2,1)S(1)}, u32[]{:S(2)}) copy-start(bf16[2,288,512]{2,1,0:T(8,128)(2,1)S(1)} %collective-permute-done.18) | copy-start | bytes 1769476
  130.1 13.1 %copy-start.7 = (bf16[2,288,512]{2,1,0:T(8,128)(2,1)}, bf16[2,288,512]{2,1,0:T(8,128)(2,1)S(1)}, u32[]{:S(2)}) copy-start(bf16[2,288,512]{2,1,0:T(8,128)(2,1)S(1)} %collective-permute-done.19) | copy-start | bytes 1769476
  130.2 9.9 %collective-permute-start.20 = (bf16[2,288,512]{2,1,0:T(8,128)(2,1)S(1)}, bf16[2,288,512]{2,1,0:T(8,128)(2,1)S(1)}, u32[]{:S(2)}, u32[]{:S(2)}) collective-permute-start(bf16[2,288,512]{2,1,0:T(8,128)(2,1)S(1)} %pad_maximum_fusion.20), channel_id=1, source_target_pairs={{0,16},{16,0},{1,17},{17,1},{2,18},{18,2},{3,19},{19,3},{4,20},{20... | collective-permute-start | bytes 1769480 | tf_op jit(solution)/shard_map/ppermute | solution.py:110
  130.6 12.9 %copy-start.11 = (bf16[2,288,512]{2,1,0:T(8,128)(2,1)}, bf16[2,288,512]{2,1,0:T(8,128)(2,1)S(1)}, u32[]{:S(2)}) copy-start(bf16[2,288,512]{2,1,0:T(8,128)(2,1)S(1)} %collective-permute-done.17) | copy-start | bytes 1769476
  148.3 3.3 %copy-start.22 = (bf16[2,288,512]{2,1,0:T(8,128)(2,1)S(1)}, bf16[2,288,512]{2,1,0:T(8,128)(2,1)}, u32[]{:S(2)}) copy-start(bf16[2,288,512]{2,1,0:T(8,128)(2,1)} %copy-done.21) | copy-start | bytes 1769476
  149.4 10.2 %copy-start.40 = (bf16[4,128,64]{2,1,0:T(8,128)(2,1)}, bf16[4,128,64]{2,1,0:T(8,128)(2,1)S(1)}, u32[]{:S(2)}) copy-start(bf16[4,128,64]{2,1,0:T(8,128)(2,1)S(1)} %get-tuple-element.98) | copy-start | bytes 196612
  149.5 10.2 %copy-start.41 = (bf16[4,128,64]{2,1,0:T(8,128)(2,1)}, bf16[4,128,64]{2,1,0:T(8,128)(2,1)S(1)}, u32[]{:S(2)}) copy-start(bf16[4,128,64]{2,1,0:T(8,128)(2,1)S(1)} %get-tuple-element.99) | copy-start | bytes 196612
  160.1 3.7 %copy-start.63 = (f32[4,2,128,128]{2,3,1,0:T(8,128)}, f32[4,2,128,128]{2,3,1,0:T(8,128)S(1)}, u32[]{:S(2)}) copy-start(f32[4,2,128,128]{2,3,1,0:T(8,128)S(1)} %get-tuple-element.109) | copy-start | bytes 1572868
  163.8 2.1 collective-permute-start.21
  166.2 3.5 %copy-start.54 = (f32[128]{0:T(128)}, f32[128]{0:T(128)S(1)}, u32[]{:S(2)}) copy-start(f32[128]{0:T(128)S(1)} %get-tuple-element.105) | copy-start | bytes 1540
  186.4 4.2 %copy-start.16 = (bf16[512,2304]{0,1:T(8,128)(2,1)S(1)}, bf16[512,2304]{0,1:T(8,128)(2,1)}, u32[]{:S(2)}) copy-start(bf16[512,2304]{0,1:T(8,128)(2,1)} %bitcast_dynamic-update-slice_fusion.14) | copy-start | bytes 7077892
  186.4 4.2 %copy-start.36 = (bf16[128,4,128]{0,2,1:T(8,128)(2,1)S(1)}, bf16[128,4,128]{0,2,1:T(8,128)(2,1)}, u32[]{:S(2)}) copy-start(bf16[128,4,128]{0,2,1:T(8,128)(2,1)} %copy.74) | copy-start | bytes 393220
  193.2 5.0 %collective-permute-start.22 = (bf16[128,2304]{1,0:T(8,128)(2,1)S(1)}, bf16[128,2304]{1,0:T(8,128)(2,1)}, u32[]{:S(2)}, u32[]{:S(2)}) collective-permute-start(bf16[128,2304]{1,0:T(8,128)(2,1)S(1)} %fusion.1), channel_id=1, source_target_pairs={{0,1},{1,0},{2,3},{3,2},{4,5},{5,4},{6,7},{7,6},{8,9},{9,8},{10,11... | collective-permute-start | bytes 1769480 | tf_op jit(solution)/shard_map/ppermute | solution.py:58
  (42 other events, 77.5 us)

commit v17 on v13

--- a/solution.py
+++ b/solution.py
@@ -120,9 +120,8 @@
             )
     if n <= PIECEWISE_RING:
         for step in range(n - 1):
-            front_pieces[step], back_pieces[step], _, _ = lax.optimization_barrier(
-                (front_pieces[step], back_pieces[step], front_ring[step + 1], back_ring[step + 1])
-            )
+            front_pieces[step], _ = lax.optimization_barrier((front_pieces[step], front_ring[step + 1]))
+            back_pieces[step], _ = lax.optimization_barrier((back_pieces[step], back_ring[step + 1]))
     back_pieces = [back_pieces[(n - k) % n] for k in range(n)]
     return front_pieces, back_pieces, block_of, slot_of, (front_ring[1], back_ring[1])
 

time: 205 us -> 212 us (1.034)
  local copies, waits for them, and re-layouts: 32.7 us -> 40.9 us
    ppermute x7, waiting for transfers between devices: 10.3 us -> 20.5 us  [ring_gather(): back_ring.append(lax.ppermute(back_ring[-1], 'seq', backward_pairs))]
    ppermute x7, waiting for transfers between devices: 19.2 us -> 10.3 us  [ring_gather(): front_ring.append(lax.ppermute(front_ring[-1], 'seq', forward_pairs))]
    unnamed x141 -> x147, local copies, waits for them, and re-layouts: 14.6 us -> 21.8 us
    ppermute x7, waiting for transfers between devices: 40.2 us -> 35.7 us  [ring_gather(): lax.ppermute(jnp.stack([front_ring[step][0], back_ring[step][0]]), 'group...]
    all_to_all x1, waiting for transfers between devices: 1.28 us -> 4.82 us  [shards(): lax.all_to_all(generator_rows, 'seq', split_axis=0, concat_axis=0, tiled=...]
    ppermute x7, starting transfers between devices: 7.53 us -> 9.98 us  [ring_gather(): back_ring.append(lax.ppermute(back_ring[-1], 'seq', backward_pairs))]
    ppermute x7, starting transfers between devices: 11.9 us -> 9.63 us  [ring_gather(): lax.ppermute(jnp.stack([front_ring[step][0], back_ring[step][0]]), 'group...]
where the time goes in v17:
time: 212 us; the launch traced here: 211 us
  waiting for transfers between devices  71.3 us (34%)
  local copies, waits for them, and re-layouts  40.9 us (19%)
  starting transfers between devices  32.3 us (15%)
  matrix products  24.7 us (12%)
  other arithmetic  22.7 us (11%)
  blocking collectives  17.6 us (8%)
    ppermute x7, waiting for transfers between devices, ring_gather(): lax.ppermute(jnp.stack([front_ring[step][0], back_ring[step][0]]), 'group...  35.7 us
    unnamed x147, local copies, waits for them, and re-layouts  21.8 us
    ppermute x7, waiting for transfers between devices, ring_gather(): back_ring.append(lax.ppermute(back_ring[-1], 'seq', backward_pairs))  20.5 us
    all_to_all x1, blocking collectives, shards(): lax.all_to_all(grad_rows, 'seq', split_axis=0, concat_axis=0, tiled=True)  15.2 us
    ppermute x7, waiting for transfers between devices, ring_gather(): front_ring.append(lax.ppermute(front_ring[-1], 'seq', forward_pairs))  10.3 us
    ppermute x7, starting transfers between devices, ring_gather(): back_ring.append(lax.ppermute(back_ring[-1], 'seq', backward_pairs))  9.98 us
    ppermute x7, starting transfers between devices, ring_gather(): lax.ppermute(jnp.stack([front_ring[step][0], back_ring[step][0]]), 'group...  9.63 us
    all_to_all x1, starting transfers between devices, shards(): lax.all_to_all(generator_rows, 'seq', split_axis=0, concat_axis=0, tiled=...  6.24 us
  transfers between devices with their start and end apart: 24, of which 18 were waited for; matrix products, arithmetic and copies ran while one was open for 14% of the time, Pallas kernels for 0%

profile of v17, /device:TPU:0, one launch (start us, length us, event | category | flops | bytes accessed | tf_op | source)
XLA Modules:
  0.0 210.9 jit_solution(5175058861649997425)
XLA Ops:
  0.0 1.4 fusion.39
  2.3 2.9 %collective-permute-start.1 = (bf16[2,288,512]{2,1,0:T(8,128)(2,1)}, bf16[2,288,512]{2,1,0:T(8,128)(2,1)}, u32[]{:S(2)}, u32[]{:S(2)}) collective-permute-start(bf16[2,288,512]{2,1,0:T(8,128)(2,1)} %pad_maximum_fusion.15), channel_id=1, source_target_pairs={{0,2},{4,0},{8,4},{12,8},{14,12},{10,14},{6,10},{2,6},{1,3},{5,1},... | collective-permute-start | bytes 1769480 | tf_op jit(solution)/shard_map/ppermute | solution.py:106
  6.3 6.2 %all-to-all-start = ((bf16[8,16,1152]{2,1,0:T(8,128)(2,1)}), bf16[8,16,1152]{2,1,0:T(8,128)(2,1)}, u32[]{:S(2)}, u32[]{:S(2)}) async-start(bf16[8,16,1152]{2,1,0:T(8,128)(2,1)} %bitcast.1), calls=%async_computation | async-start | bytes 589824 | tf_op jit(solution)/shard_map/all_to_all | solution.py:152
  16.8 1.2 compare_convert_fusion
  20.5 1.0 gather.32
  23.8 4.8 %all-to-all-done = bf16[8,16,1152]{2,1,0:T(8,128)(2,1)} async-done(((bf16[8,16,1152]{2,1,0:T(8,128)(2,1)}), bf16[8,16,1152]{2,1,0:T(8,128)(2,1)}, u32[]{:S(2)}, u32[]{:S(2)}) %all-to-all-start) | async-done | bytes 294944 | tf_op jit(solution)/shard_map/all_to_all | solution.py:152
  28.7 2.4 %all_gather.3 = bf16[128,2304]{1,0:T(8,128)(2,1)S(1)} all-gather(bf16[128,1152]{1,0:T(8,128)(2,1)} %bitcast.2), channel_id=1, replica_groups=mesh['groups'=2,'seq'=8,'wg'=2] {'wg'}, dimensions={1}, use_global_device_ids=true | all-gather | bytes 884736 | tf_op jit(solution)/shard_map/all_gather | solution.py:161
  34.6 1.6 collective-permute-start.4
  36.7 1.0 slice.409
  37.7 1.0 slice.408
  38.7 1.6 collective-permute-start.2
  41.5 8.8 %collective-permute-done.4 = bf16[2,288,512]{2,1,0:T(8,128)(2,1)S(1)} collective-permute-done((bf16[2,288,512]{2,1,0:T(8,128)(2,1)}, bf16[2,288,512]{2,1,0:T(8,128)(2,1)S(1)}, u32[]{:S(2)}, u32[]{:S(2)}) %collective-permute-start.4) | collective-permute-done | bytes 589856 | tf_op jit(solution)/shard_map/ppermute | solution.py:106
  50.3 1.2 collective-permute-done.3
  51.6 1.6 collective-permute-start.5
  54.0 1.4 select_bitcast_fusion.2
  56.4 1.8 collective-permute-start.6
  59.3 6.9 %collective-permute-done.5 = bf16[2,288,512]{2,1,0:T(8,128)(2,1)S(1)} collective-permute-done((bf16[2,288,512]{2,1,0:T(8,128)(2,1)S(1)}, bf16[2,288,512]{2,1,0:T(8,128)(2,1)S(1)}, u32[]{:S(2)}, u32[]{:S(2)}) %collective-permute-start.5) | collective-permute-done | bytes 589856 | tf_op jit(solution)/shard_map/ppermute | solution.py:110
  66.5 3.6 %collective-permute-done.6 = bf16[2,288,512]{2,1,0:T(8,128)(2,1)S(1)} collective-permute-done((bf16[2,288,512]{2,1,0:T(8,128)(2,1)S(1)}, bf16[2,288,512]{2,1,0:T(8,128)(2,1)S(1)}, u32[]{:S(2)}, u32[]{:S(2)}) %collective-permute-start.6) | collective-permute-done | bytes 589856 | tf_op jit(solution)/shard_map/ppermute | solution.py:105
  70.9 1.6 collective-permute-start.8
  74.1 1.4 collective-permute-start.10
  76.0 6.8 %collective-permute-done.8 = bf16[2,288,512]{2,1,0:T(8,128)(2,1)S(1)} collective-permute-done((bf16[2,288,512]{2,1,0:T(8,128)(2,1)S(1)}, bf16[2,288,512]{2,1,0:T(8,128)(2,1)S(1)}, u32[]{:S(2)}, u32[]{:S(2)}) %collective-permute-start.8) | collective-permute-done | bytes 589856 | tf_op jit(solution)/shard_map/ppermute | solution.py:110
  83.0 2.0 collective-permute-done.9
  88.3 1.4 collective-permute-start.13
  90.1 8.2 %collective-permute-done.11 = bf16[2,288,512]{2,1,0:T(8,128)(2,1)S(1)} collective-permute-done((bf16[2,288,512]{2,1,0:T(8,128)(2,1)S(1)}, bf16[2,288,512]{2,1,0:T(8,128)(2,1)S(1)}, u32[]{:S(2)}, u32[]{:S(2)}) %collective-permute-start.11) | collective-permute-done | bytes 589856 | tf_op jit(solution)/shard_map/ppermute | solution.py:110
  99.3 2.1 %collective-permute-start.14 = (bf16[2,288,512]{2,1,0:T(8,128)(2,1)S(1)}, bf16[2,288,512]{2,1,0:T(8,128)(2,1)S(1)}, u32[]{:S(2)}, u32[]{:S(2)}) collective-permute-start(bf16[2,288,512]{2,1,0:T(8,128)(2,1)S(1)} %pad_maximum_fusion.20), channel_id=1, source_target_pairs={{0,16},{16,0},{1,17},{17,1},{2,18},{18,2},{3,19},{19,3},{4,20},{20... | collective-permute-start | bytes 1769480 | tf_op jit(solution)/shard_map/ppermute | solution.py:110
  102.8 1.7 collective-permute-start.16
  104.9 6.4 %collective-permute-done.14 = bf16[2,288,512]{2,1,0:T(8,128)(2,1)S(1)} collective-permute-done((bf16[2,288,512]{2,1,0:T(8,128)(2,1)S(1)}, bf16[2,288,512]{2,1,0:T(8,128)(2,1)S(1)}, u32[]{:S(2)}, u32[]{:S(2)}) %collective-permute-start.14) | collective-permute-done | bytes 589856 | tf_op jit(solution)/shard_map/ppermute | solution.py:110
  111.5 3.4 %collective-permute-done.15 = bf16[2,288,512]{2,1,0:T(8,128)(2,1)S(1)} collective-permute-done((bf16[2,288,512]{2,1,0:T(8,128)(2,1)S(1)}, bf16[2,288,512]{2,1,0:T(8,128)(2,1)S(1)}, u32[]{:S(2)}, u32[]{:S(2)}) %collective-permute-start.15) | collective-permute-done | bytes 589856 | tf_op jit(solution)/shard_map/ppermute | solution.py:105
  115.4 1.0 bitcast_dynamic-update-slice_fusion.1
  116.3 1.7 collective-permute-start.18
  118.9 9.1 %collective-permute-done.19 = bf16[2,288,512]{2,1,0:T(8,128)(2,1)S(1)} collective-permute-done((bf16[2,288,512]{2,1,0:T(8,128)(2,1)S(1)}, bf16[2,288,512]{2,1,0:T(8,128)(2,1)S(1)}, u32[]{:S(2)}, u32[]{:S(2)}) %collective-permute-start.19) | collective-permute-done | bytes 589856 | tf_op jit(solution)/shard_map/ppermute | solution.py:106
  128.1 2.1 collective-permute-start.20
  130.5 1.0 bitcast_dynamic-update-slice_fusion
  131.4 6.6 %collective-permute-done.20 = bf16[2,288,512]{2,1,0:T(8,128)(2,1)S(1)} collective-permute-done((bf16[2,288,512]{2,1,0:T(8,128)(2,1)S(1)}, bf16[2,288,512]{2,1,0:T(8,128)(2,1)S(1)}, u32[]{:S(2)}, u32[]{:S(2)}) %collective-permute-start.20) | collective-permute-done | bytes 589856 | tf_op jit(solution)/shard_map/ppermute | solution.py:110
  138.0 0.9 fusion.78
  149.5 2.1 fusion.28
  151.5 1.9 bitcast_dynamic-update-slice_fusion.12
  159.4 1.2 copy-done
  160.6 1.7 convolution_convert_fusion
  167.8 2.0 convolution_convert_fusion.2
  169.8 1.2 copy.92
  171.0 2.0 fusion.16
  174.0 1.7 convolution_bitcast_fusion.1
  175.8 2.2 %convolution_multiply_fusion.1 = f32[4,2,128,128]{3,2,1,0:T(8,128)S(1)} fusion(f32[4,2,128,128]{2,3,1,0:T(8,128)} %copy-done.26, f32[4,2,128,128]{2,3,1,0:T(8,128)} %copy-done.56, bf16[4,128,64]{2,1,0:T(8,128)(2,1)S(1)} %copy-done.36, bf16[4,128,64]{2,1,0:T(8,128)(2,1)S(1)} %copy-done.34, f32[4,2,128]{2,1,0:T(2,128)S(1)} %copy-done.58, ...), kind=kOutput, calls=%fused_computation.25 | convolution fusion | flops 35652736 | bytes 1724416 | tf_op jit(solution)/shard_map/kgij,kjd->kgid/dot_general | solution.py:269
  180.3 4.1 %fusion.41 = f32[128,2304]{1,0:T(8,128)S(1)} fusion(bf16[1024,2304]{0,1:T(8,128)(2,1)} %fusion.29, bf16[16,8,8,128]{3,2,1,0:T(8,128)(2,1)S(1)} %bitcast.296), kind=kOutput, calls=%fused_computation.196 | convolution fusion | flops 603979776 | bytes 6160384 | tf_op jit(solution)/shard_map/dot_general | solution.py:283
  185.4 2.6 %fusion.1 = bf16[128,2304]{1,0:T(8,128)(2,1)S(1)} fusion(f32[128,2304]{1,0:T(8,128)S(1)} %convolution_add_fusion.1, bf16[128,512]{0,1:T(8,128)(2,1)S(1)} %bitcast.301, bf16[512,2304]{0,1:T(8,128)(2,1)} %bitcast_dynamic-update-slice_fusion.16), kind=kOutput, calls=%fused_computation.9 | convolution fusion | flops 302579712 | bytes 4259840 | tf_op jit(solution)/shard_map/dot_general | solution.py:285
  191.1 2.2 %fusion.13 = bf16[128,2304]{1,0:T(8,128)(2,1)S(1)} fusion(bf16[128,2304]{1,0:T(8,128)(2,1)S(1)} %collective-permute-done.22, bf16[128,2304]{1,0:T(8,128)(2,1)S(1)} %fusion.1, f32[128]{0:T(128)S(1)} %broadcast_multiply_fusion, f32[128]{0:T(128)} %get-tuple-element.109, f32[2304]{0:T(1024)S(1)} %mul.519, f32[128]{0:T(128)} %copy-done.47, ...), kind=kLoop, calls=%fused_computation.36 | loop fusion | flops 6488064 | bytes 4742912 | tf_op jit(solution)/shard_map/convert_element_type | solution.py:295
  195.0 15.2 %all_to_all.21 = bf16[8,16,1152]{2,1,0:T(8,128)(2,1)S(1)} all-to-all(bf16[8,16,1152]{2,1,0:T(8,128)(2,1)S(1)} %broadcast_select_fusion.4), channel_id=1, replica_groups=mesh['groups'=2,'seq'=8,'wg'=2] {'seq'}, dimensions={0} | all-to-all | bytes 589824 | tf_op jit(solution)/shard_map/all_to_all | solution.py:297
  (300 shorter events, 61.7 us)
Async XLA Ops:
  1.4 11.1 %copy-start.10 = (bf16[288,1024]{1,0:T(8,128)(2,1)S(1)}, bf16[288,1024]{1,0:T(8,128)(2,1)}, u32[]{:S(2)}) copy-start(bf16[288,1024]{1,0:T(8,128)(2,1)} %param.13) | copy-start | bytes 1769476
  1.4 11.1 %copy-start.18 = (bf16[288,512]{1,0:T(8,128)(2,1)S(1)}, bf16[288,512]{1,0:T(8,128)(2,1)}, u32[]{:S(2)}) copy-start(bf16[288,512]{1,0:T(8,128)(2,1)} %param.14) | copy-start | bytes 884740
  2.3 19.9 %collective-permute-start.1 = (bf16[2,288,512]{2,1,0:T(8,128)(2,1)}, bf16[2,288,512]{2,1,0:T(8,128)(2,1)}, u32[]{:S(2)}, u32[]{:S(2)}) collective-permute-start(bf16[2,288,512]{2,1,0:T(8,128)(2,1)} %pad_maximum_fusion.15), channel_id=1, source_target_pairs={{0,2},{4,0},{8,4},{12,8},{14,12},{10,14},{6,10},{2,6},{1,3},{5,1},... | collective-permute-start | bytes 1769480 | tf_op jit(solution)/shard_map/ppermute | solution.py:106
  5.3 7.4 %copy-start.41 = (f32[2304]{0:T(1024)S(1)}, f32[2304]{0:T(1024)}, u32[]{:S(2)}) copy-start(f32[2304]{0:T(1024)} %param.12) | copy-start | bytes 27652
  5.3 7.5 %copy-start.42 = (f32[2304]{0:T(1024)S(1)}, f32[2304]{0:T(1024)}, u32[]{:S(2)}) copy-start(f32[2304]{0:T(1024)} %param.17) | copy-start | bytes 27652
  5.3 7.6 %copy-start.43 = (f32[2304]{0:T(1024)S(1)}, f32[2304]{0:T(1024)}, u32[]{:S(2)}) copy-start(f32[2304]{0:T(1024)} %param.18) | copy-start | bytes 27652
  5.3 8.5 %copy-start.53 = (s32[8]{0:T(128)S(1)}, s32[8]{0:T(128)}, u32[]{:S(2)}) copy-start(s32[8]{0:T(128)} %param.20) | copy-start | bytes 100
  5.3 9.8 %copy-start.54 = (s32[8]{0:T(128)S(1)}, s32[8]{0:T(128)}, u32[]{:S(2)}) copy-start(s32[8]{0:T(128)} %param.21) | copy-start | bytes 100
  6.2 10.5 %copy-start.11 = (bf16[1024,288]{0,1:T(8,128)(2,1)S(1)}, bf16[1024,288]{0,1:T(8,128)(2,1)}, u32[]{:S(2)}) copy-start(bf16[1024,288]{0,1:T(8,128)(2,1)} %param.16) | copy-start | bytes 1769476
  6.2 10.6 %copy-start.19 = (bf16[288,512]{1,0:T(8,128)(2,1)S(1)}, bf16[288,512]{1,0:T(8,128)(2,1)}, u32[]{:S(2)}) copy-start(bf16[288,512]{1,0:T(8,128)(2,1)} %param.15) | copy-start | bytes 884740
  6.2 16.0 %collective-permute-start = (bf16[2,288,512]{2,1,0:T(8,128)(2,1)}, bf16[2,288,512]{2,1,0:T(8,128)(2,1)}, u32[]{:S(2)}, u32[]{:S(2)}) collective-permute-start(bf16[2,288,512]{2,1,0:T(8,128)(2,1)} %pad_maximum_fusion.14), channel_id=1, source_target_pairs={{0,4},{4,8},{8,12},{12,14},{14,10},{10,6},{6,2},{2,0},{1,5},{5,9},... | collective-permute-start | bytes 1769480 | tf_op jit(solution)/shard_map/ppermute | solution.py:105
  6.3 22.4 %all-to-all-start = ((bf16[8,16,1152]{2,1,0:T(8,128)(2,1)}), bf16[8,16,1152]{2,1,0:T(8,128)(2,1)}, u32[]{:S(2)}, u32[]{:S(2)}) async-start(bf16[8,16,1152]{2,1,0:T(8,128)(2,1)} %bitcast.1), calls=%async_computation | async-start | bytes 589824 | tf_op jit(solution)/shard_map/all_to_all | solution.py:152
  12.6 6.4 %copy-start.28 = (bf16[64,2304]{1,0:T(8,128)(2,1)S(1)}, bf16[64,2304]{1,0:T(8,128)(2,1)}, u32[]{:S(2)}) copy-start(bf16[64,2304]{1,0:T(8,128)(2,1)} %param.19) | copy-start | bytes 884740
  16.6 125.5 %copy-start.14 = (f32[128,64]{1,0:T(8,128)}, f32[128,64]{1,0:T(8,128)S(1)}, u32[]{:S(2)}) copy-start(f32[128,64]{1,0:T(8,128)S(1)} %get-tuple-element.107) | copy-start | bytes 98308
  16.6 125.5 %copy-start.16 = (f32[128,64]{1,0:T(8,128)}, f32[128,64]{1,0:T(8,128)S(1)}, u32[]{:S(2)}) copy-start(f32[128,64]{1,0:T(8,128)S(1)} %get-tuple-element.108) | copy-start | bytes 98308
  16.7 141.9 %copy-start.39 = (pred[128,128]{0,1:T(8,128)(4,1)}, pred[128,128]{0,1:T(8,128)(4,1)S(1)}, u32[]{:S(2)}) copy-start(pred[128,128]{0,1:T(8,128)(4,1)S(1)} %fusion.79) | copy-start | bytes 49156
  33.3 4.4 %copy-start.47 = (f32[128]{0:T(128)}, f32[128]{0:T(128)S(1)}, u32[]{:S(2)}) copy-start(f32[128]{0:T(128)S(1)} %get-tuple-element.110) | copy-start | bytes 1540
  34.6 15.6 %collective-permute-start.4 = (bf16[2,288,512]{2,1,0:T(8,128)(2,1)}, bf16[2,288,512]{2,1,0:T(8,128)(2,1)S(1)}, u32[]{:S(2)}, u32[]{:S(2)}) collective-permute-start(bf16[2,288,512]{2,1,0:T(8,128)(2,1)} %collective-permute-done.1), channel_id=1, source_target_pairs={{0,2},{4,0},{8,4},{12,8},{14,12},{10,14},{6,10},{2,6},{1,3},{5,1},... | collective-permute-start | bytes 1769480 | tf_op jit(solution)/shard_map/ppermute | solution.py:106
  36.2 15.3 %collective-permute-start.3 = (bf16[2,288,512]{2,1,0:T(8,128)(2,1)}, bf16[2,288,512]{2,1,0:T(8,128)(2,1)S(1)}, u32[]{:S(2)}, u32[]{:S(2)}) collective-permute-start(bf16[2,288,512]{2,1,0:T(8,128)(2,1)} %collective-permute-done), channel_id=1, source_target_pairs={{0,4},{4,8},{8,12},{12,14},{14,10},{10,6},{6,2},{2,0},{1,5},{5,9},... | collective-permute-start | bytes 1769480 | tf_op jit(solution)/shard_map/ppermute | solution.py:105
  38.7 15.2 %collective-permute-start.2 = (bf16[2,288,512]{2,1,0:T(8,128)(2,1)S(1)}, bf16[2,288,512]{2,1,0:T(8,128)(2,1)S(1)}, u32[]{:S(2)}, u32[]{:S(2)}) collective-permute-start(bf16[2,288,512]{2,1,0:T(8,128)(2,1)S(1)} %pad_maximum_fusion.16), channel_id=1, source_target_pairs={{0,16},{16,0},{1,17},{17,1},{2,18},{18,2},{3,19},{19,3},{4,20},{20... | collective-permute-start | bytes 1769480 | tf_op jit(solution)/shard_map/ppermute | solution.py:110
  51.6 14.7 %collective-permute-start.5 = (bf16[2,288,512]{2,1,0:T(8,128)(2,1)S(1)}, bf16[2,288,512]{2,1,0:T(8,128)(2,1)S(1)}, u32[]{:S(2)}, u32[]{:S(2)}) collective-permute-start(bf16[2,288,512]{2,1,0:T(8,128)(2,1)S(1)} %pad_maximum_fusion.17), channel_id=1, source_target_pairs={{0,16},{16,0},{1,17},{17,1},{2,18},{18,2},{3,19},{19,3},{4,20},{20... | collective-permute-start | bytes 1769480 | tf_op jit(solution)/shard_map/ppermute | solution.py:110
  56.4 13.6 %collective-permute-start.6 = (bf16[2,288,512]{2,1,0:T(8,128)(2,1)S(1)}, bf16[2,288,512]{2,1,0:T(8,128)(2,1)S(1)}, u32[]{:S(2)}, u32[]{:S(2)}) collective-permute-start(bf16[2,288,512]{2,1,0:T(8,128)(2,1)S(1)} %collective-permute-done.3), channel_id=1, source_target_pairs={{0,4},{4,8},{8,12},{12,14},{14,10},{10,6},{6,2},{2,0},{1,5},{5,9},... | collective-permute-start | bytes 1769480 | tf_op jit(solution)/shard_map/ppermute | solution.py:105
  58.2 12.7 %collective-permute-start.7 = (bf16[2,288,512]{2,1,0:T(8,128)(2,1)S(1)}, bf16[2,288,512]{2,1,0:T(8,128)(2,1)S(1)}, u32[]{:S(2)}, u32[]{:S(2)}) collective-permute-start(bf16[2,288,512]{2,1,0:T(8,128)(2,1)S(1)} %collective-permute-done.4), channel_id=1, source_target_pairs={{0,2},{4,0},{8,4},{12,8},{14,12},{10,14},{6,10},{2,6},{1,3},{5,1},... | collective-permute-start | bytes 1769480 | tf_op jit(solution)/shard_map/ppermute | solution.py:106
  70.9 11.8 %collective-permute-start.8 = (bf16[2,288,512]{2,1,0:T(8,128)(2,1)S(1)}, bf16[2,288,512]{2,1,0:T(8,128)(2,1)S(1)}, u32[]{:S(2)}, u32[]{:S(2)}) collective-permute-start(bf16[2,288,512]{2,1,0:T(8,128)(2,1)S(1)} %pad_maximum_fusion.18), channel_id=1, source_target_pairs={{0,16},{16,0},{1,17},{17,1},{2,18},{18,2},{3,19},{19,3},{4,20},{20... | collective-permute-start | bytes 1769480 | tf_op jit(solution)/shard_map/ppermute | solution.py:110
  73.5 11.5 %collective-permute-start.9 = (bf16[2,288,512]{2,1,0:T(8,128)(2,1)S(1)}, bf16[2,288,512]{2,1,0:T(8,128)(2,1)S(1)}, u32[]{:S(2)}, u32[]{:S(2)}) collective-permute-start(bf16[2,288,512]{2,1,0:T(8,128)(2,1)S(1)} %collective-permute-done.6), channel_id=1, source_target_pairs={{0,4},{4,8},{8,12},{12,14},{14,10},{10,6},{6,2},{2,0},{1,5},{5,9},... | collective-permute-start | bytes 1769480 | tf_op jit(solution)/shard_map/ppermute | solution.py:105
  74.1 11.8 %collective-permute-start.10 = (bf16[2,288,512]{2,1,0:T(8,128)(2,1)S(1)}, bf16[2,288,512]{2,1,0:T(8,128)(2,1)S(1)}, u32[]{:S(2)}, u32[]{:S(2)}) collective-permute-start(bf16[2,288,512]{2,1,0:T(8,128)(2,1)S(1)} %collective-permute-done.7), channel_id=1, source_target_pairs={{0,2},{4,0},{8,4},{12,8},{14,12},{10,14},{6,10},{2,6},{1,3},{5,1},... | collective-permute-start | bytes 1769480 | tf_op jit(solution)/shard_map/ppermute | solution.py:106
  86.0 12.3 %collective-permute-start.11 = (bf16[2,288,512]{2,1,0:T(8,128)(2,1)S(1)}, bf16[2,288,512]{2,1,0:T(8,128)(2,1)S(1)}, u32[]{:S(2)}, u32[]{:S(2)}) collective-permute-start(bf16[2,288,512]{2,1,0:T(8,128)(2,1)S(1)} %pad_maximum_fusion.19), channel_id=1, source_target_pairs={{0,16},{16,0},{1,17},{17,1},{2,18},{18,2},{3,19},{19,3},{4,20},{20... | collective-permute-start | bytes 1769480 | tf_op jit(solution)/shard_map/ppermute | solution.py:110
  87.6 11.1 %collective-permute-start.12 = (bf16[2,288,512]{2,1,0:T(8,128)(2,1)S(1)}, bf16[2,288,512]{2,1,0:T(8,128)(2,1)S(1)}, u32[]{:S(2)}, u32[]{:S(2)}) collective-permute-start(bf16[2,288,512]{2,1,0:T(8,128)(2,1)S(1)} %collective-permute-done.9), channel_id=1, source_target_pairs={{0,4},{4,8},{8,12},{12,14},{14,10},{10,6},{6,2},{2,0},{1,5},{5,9},... | collective-permute-start | bytes 1769480 | tf_op jit(solution)/shard_map/ppermute | solution.py:105
  88.3 10.9 %collective-permute-start.13 = (bf16[2,288,512]{2,1,0:T(8,128)(2,1)S(1)}, bf16[2,288,512]{2,1,0:T(8,128)(2,1)S(1)}, u32[]{:S(2)}, u32[]{:S(2)}) collective-permute-start(bf16[2,288,512]{2,1,0:T(8,128)(2,1)S(1)} %collective-permute-done.10), channel_id=1, source_target_pairs={{0,2},{4,0},{8,4},{12,8},{14,12},{10,14},{6,10},{2,6},{1,3},{5,1},... | collective-permute-start | bytes 1769480 | tf_op jit(solution)/shard_map/ppermute | solution.py:106
  99.3 12.0 %collective-permute-start.14 = (bf16[2,288,512]{2,1,0:T(8,128)(2,1)S(1)}, bf16[2,288,512]{2,1,0:T(8,128)(2,1)S(1)}, u32[]{:S(2)}, u32[]{:S(2)}) collective-permute-start(bf16[2,288,512]{2,1,0:T(8,128)(2,1)S(1)} %pad_maximum_fusion.20), channel_id=1, source_target_pairs={{0,16},{16,0},{1,17},{17,1},{2,18},{18,2},{3,19},{19,3},{4,20},{20... | collective-permute-start | bytes 1769480 | tf_op jit(solution)/shard_map/ppermute | solution.py:110
  102.4 44.5 %copy-start.1 = (bf16[288,1536]{1,0:T(8,128)(2,1)}, bf16[288,1536]{1,0:T(8,128)(2,1)S(1)}, u32[]{:S(2)}) copy-start(bf16[288,1536]{1,0:T(8,128)(2,1)S(1)} %pad_maximum_fusion.10) | copy-start | bytes 2654212
  102.4 12.4 %collective-permute-start.15 = (bf16[2,288,512]{2,1,0:T(8,128)(2,1)S(1)}, bf16[2,288,512]{2,1,0:T(8,128)(2,1)S(1)}, u32[]{:S(2)}, u32[]{:S(2)}) collective-permute-start(bf16[2,288,512]{2,1,0:T(8,128)(2,1)S(1)} %collective-permute-done.12), channel_id=1, source_target_pairs={{0,4},{4,8},{8,12},{12,14},{14,10},{10,6},{6,2},{2,0},{1,5},{5,9},... | collective-permute-start | bytes 1769480 | tf_op jit(solution)/shard_map/ppermute | solution.py:105
  102.8 12.4 %collective-permute-start.16 = (bf16[2,288,512]{2,1,0:T(8,128)(2,1)S(1)}, bf16[2,288,512]{2,1,0:T(8,128)(2,1)S(1)}, u32[]{:S(2)}, u32[]{:S(2)}) collective-permute-start(bf16[2,288,512]{2,1,0:T(8,128)(2,1)S(1)} %collective-permute-done.13), channel_id=1, source_target_pairs={{0,2},{4,0},{8,4},{12,8},{14,12},{10,14},{6,10},{2,6},{1,3},{5,1},... | collective-permute-start | bytes 1769480 | tf_op jit(solution)/shard_map/ppermute | solution.py:106
  115.3 14.9 %collective-permute-start.17 = (bf16[2,288,512]{2,1,0:T(8,128)(2,1)S(1)}, bf16[2,288,512]{2,1,0:T(8,128)(2,1)S(1)}, u32[]{:S(2)}, u32[]{:S(2)}) collective-permute-start(bf16[2,288,512]{2,1,0:T(8,128)(2,1)S(1)} %pad_maximum_fusion.21), channel_id=1, source_target_pairs={{0,16},{16,0},{1,17},{17,1},{2,18},{18,2},{3,19},{19,3},{4,20},{20... | collective-permute-start | bytes 1769480 | tf_op jit(solution)/shard_map/ppermute | solution.py:110
  116.3 11.6 %collective-permute-start.18 = (bf16[2,288,512]{2,1,0:T(8,128)(2,1)S(1)}, bf16[2,288,512]{2,1,0:T(8,128)(2,1)S(1)}, u32[]{:S(2)}, u32[]{:S(2)}) collective-permute-start(bf16[2,288,512]{2,1,0:T(8,128)(2,1)S(1)} %collective-permute-done.15), channel_id=1, source_target_pairs={{0,4},{4,8},{8,12},{12,14},{14,10},{10,6},{6,2},{2,0},{1,5},{5,9},... | collective-permute-start | bytes 1769480 | tf_op jit(solution)/shard_map/ppermute | solution.py:105
  118.1 9.9 %collective-permute-start.19 = (bf16[2,288,512]{2,1,0:T(8,128)(2,1)S(1)}, bf16[2,288,512]{2,1,0:T(8,128)(2,1)S(1)}, u32[]{:S(2)}, u32[]{:S(2)}) collective-permute-start(bf16[2,288,512]{2,1,0:T(8,128)(2,1)S(1)} %collective-permute-done.16), channel_id=1, source_target_pairs={{0,2},{4,0},{8,4},{12,8},{14,12},{10,14},{6,10},{2,6},{1,3},{5,1},... | collective-permute-start | bytes 1769480 | tf_op jit(solution)/shard_map/ppermute | solution.py:106
  118.4 27.4 %copy-start.3 = (bf16[288,1536]{1,0:T(8,128)(2,1)}, bf16[288,1536]{1,0:T(8,128)(2,1)S(1)}, u32[]{:S(2)}) copy-start(bf16[288,1536]{1,0:T(8,128)(2,1)S(1)} %pad_maximum_fusion.9) | copy-start | bytes 2654212
  128.1 9.9 %collective-permute-start.20 = (bf16[2,288,512]{2,1,0:T(8,128)(2,1)S(1)}, bf16[2,288,512]{2,1,0:T(8,128)(2,1)S(1)}, u32[]{:S(2)}, u32[]{:S(2)}) collective-permute-start(bf16[2,288,512]{2,1,0:T(8,128)(2,1)S(1)} %pad_maximum_fusion.22), channel_id=1, source_target_pairs={{0,16},{16,0},{1,17},{17,1},{2,18},{18,2},{3,19},{19,3},{4,20},{20... | collective-permute-start | bytes 1769480 | tf_op jit(solution)/shard_map/ppermute | solution.py:110
  130.4 14.4 %copy-start.5 = (bf16[288,1536]{1,0:T(8,128)(2,1)}, bf16[288,1536]{1,0:T(8,128)(2,1)S(1)}, u32[]{:S(2)}) copy-start(bf16[288,1536]{1,0:T(8,128)(2,1)S(1)} %pad_maximum_fusion.8) | copy-start | bytes 2654212
  142.9 15.3 %copy-start.33 = (bf16[4,128,64]{2,1,0:T(8,128)(2,1)}, bf16[4,128,64]{2,1,0:T(8,128)(2,1)S(1)}, u32[]{:S(2)}) copy-start(bf16[4,128,64]{2,1,0:T(8,128)(2,1)S(1)} %get-tuple-element.105) | copy-start | bytes 196612
  148.7 5.7 %copy-start.20 = (bf16[128,512]{1,0:T(8,128)(2,1)}, bf16[128,512]{1,0:T(8,128)(2,1)S(1)}, u32[]{:S(2)}) copy-start(bf16[128,512]{1,0:T(8,128)(2,1)S(1)} %fusion.15) | copy-start | bytes 393220
  149.5 4.0 %copy-start.4 = (bf16[288,1536]{1,0:T(8,128)(2,1)S(1)}, bf16[288,1536]{1,0:T(8,128)(2,1)}, u32[]{:S(2)}) copy-start(bf16[288,1536]{1,0:T(8,128)(2,1)} %copy-done.3) | copy-start | bytes 2654212
  149.5 4.9 %copy-start.2 = (bf16[288,1536]{1,0:T(8,128)(2,1)S(1)}, bf16[288,1536]{1,0:T(8,128)(2,1)}, u32[]{:S(2)}) copy-start(bf16[288,1536]{1,0:T(8,128)(2,1)} %copy-done.1) | copy-start | bytes 2654212
  162.3 2.5 %collective-permute-start.21 = (bf16[128,2304]{1,0:T(8,128)(2,1)S(1)}, bf16[128,2304]{1,0:T(8,128)(2,1)S(1)}, u32[]{:S(2)}, u32[]{:S(2)}) collective-permute-start(bf16[128,2304]{1,0:T(8,128)(2,1)S(1)} %convolution_convert_fusion), channel_id=1, source_target_pairs={{0,1},{1,0},{2,3},{3,2},{4,5},{5,4},{6,7},{7,6},{8,9},{9,8},{10,11... | collective-permute-start | bytes 1769480 | tf_op jit(solution)/shard_map/ppermute | solution.py:58
  169.8 3.2 %copy-start.21 = (bf16[128,512]{1,0:T(8,128)(2,1)S(1)}, bf16[128,512]{1,0:T(8,128)(2,1)}, u32[]{:S(2)}) copy-start(bf16[128,512]{1,0:T(8,128)(2,1)} %copy-done.20) | copy-start | bytes 393220
  180.3 4.2 %copy-start.9 = (bf16[512,2304]{0,1:T(8,128)(2,1)S(1)}, bf16[512,2304]{0,1:T(8,128)(2,1)}, u32[]{:S(2)}) copy-start(bf16[512,2304]{0,1:T(8,128)(2,1)} %copy-done.8) | copy-start | bytes 7077892
  180.3 4.2 %copy-start.27 = (bf16[128,4,128]{0,2,1:T(8,128)(2,1)S(1)}, bf16[128,4,128]{0,2,1:T(8,128)(2,1)}, u32[]{:S(2)}) copy-start(bf16[128,4,128]{0,2,1:T(8,128)(2,1)} %copy.74) | copy-start | bytes 393220
  188.0 2.7 %collective-permute-start.22 = (bf16[128,2304]{1,0:T(8,128)(2,1)S(1)}, bf16[128,2304]{1,0:T(8,128)(2,1)S(1)}, u32[]{:S(2)}, u32[]{:S(2)}) collective-permute-start(bf16[128,2304]{1,0:T(8,128)(2,1)S(1)} %fusion.1), channel_id=1, source_target_pairs={{0,1},{1,0},{2,3},{3,2},{4,5},{5,4},{6,7},{7,6},{8,9},{9,8},{10,11... | collective-permute-start | bytes 1769480 | tf_op jit(solution)/shard_map/ppermute | solution.py:58
  (35 other events, 68.1 us)

commit v18 on v13

--- a/solution.py
+++ b/solution.py
@@ -121,7 +121,8 @@
     if n <= PIECEWISE_RING:
         for step in range(n - 1):
             front_pieces[step], back_pieces[step], _, _ = lax.optimization_barrier(
-                (front_pieces[step], back_pieces[step], front_ring[step + 1], back_ring[step + 1])
+                (front_pieces[step], back_pieces[step], front_ring[min(step + 2, n - 1) if step == 0 else step + 1],
+                 back_ring[min(step + 2, n - 1) if step == 0 else step + 1])
             )
     back_pieces = [back_pieces[(n - k) % n] for k in range(n)]
     return front_pieces, back_pieces, block_of, slot_of, (front_ring[1], back_ring[1])

time: 205 us -> 206 us (level)
  waiting for transfers between devices: 71 us -> 74.6 us
    ppermute x7, waiting for transfers between devices: 40.2 us -> 43.2 us  [ring_gather(): lax.ppermute(jnp.stack([front_ring[step][0], back_ring[step][0]]), 'group...]
    unnamed x141 -> x123, local copies, waits for them, and re-layouts: 14.6 us -> 15.9 us
  transfers between devices with their start and end apart: 24 -> 24, of which waited for: 18 -> 17; matrix products, arithmetic and copies ran while one was open for 14% -> 12% of each run, Pallas kernels for 0% -> 0%
where the time goes in v18:
time: 206 us
  waiting for transfers between devices  74.6 us (36%)
  starting transfers between devices  32.9 us (16%)
  local copies, waits for them, and re-layouts  31.9 us (15%)
  other arithmetic  23.8 us (12%)
  matrix products  22.9 us (11%)
  blocking collectives  18.4 us (9%)
    ppermute x7, waiting for transfers between devices, ring_gather(): lax.ppermute(jnp.stack([front_ring[step][0], back_ring[step][0]]), 'group...  43.2 us
    ppermute x7, waiting for transfers between devices, ring_gather(): front_ring.append(lax.ppermute(front_ring[-1], 'seq', forward_pairs))  18.5 us
    all_to_all x1, blocking collectives, shards(): lax.all_to_all(grad_rows, 'seq', split_axis=0, concat_axis=0, tiled=True)  16 us
    unnamed x123, local copies, waits for them, and re-layouts  15.9 us
    ppermute x7, starting transfers between devices, ring_gather(): lax.ppermute(jnp.stack([front_ring[step][0], back_ring[step][0]]), 'group...  10.5 us
    ppermute x7, waiting for transfers between devices, ring_gather(): back_ring.append(lax.ppermute(back_ring[-1], 'seq', backward_pairs))  9.66 us
    ppermute x7, starting transfers between devices, ring_gather(): front_ring.append(lax.ppermute(front_ring[-1], 'seq', forward_pairs))  7.92 us
    ppermute x7, starting transfers between devices, ring_gather(): back_ring.append(lax.ppermute(back_ring[-1], 'seq', backward_pairs))  7.65 us
  transfers between devices with their start and end apart: 24, of which 17 were waited for; matrix products, arithmetic and copies ran while one was open for 12% of the time, Pallas kernels for 0%

profile of v18, /device:TPU:0, one launch (start us, length us, event | category | flops | bytes accessed | tf_op | source)
XLA Modules:
  0.0 205.8 jit_solution(17852611275232352325)
XLA Ops:
  0.0 1.4 fusion.39
  2.4 3.0 %collective-permute-start = (bf16[2,288,512]{2,1,0:T(8,128)(2,1)}, bf16[2,288,512]{2,1,0:T(8,128)(2,1)}, u32[]{:S(2)}, u32[]{:S(2)}) collective-permute-start(bf16[2,288,512]{2,1,0:T(8,128)(2,1)} %pad_maximum_fusion.14), channel_id=1, source_target_pairs={{0,4},{4,8},{8,12},{12,14},{14,10},{10,6},{6,2},{2,0},{1,5},{5,9},... | collective-permute-start | bytes 1769480 | tf_op jit(solution)/shard_map/ppermute | solution.py:105
  6.3 6.3 %all-to-all-start = ((bf16[8,16,1152]{2,1,0:T(8,128)(2,1)}), bf16[8,16,1152]{2,1,0:T(8,128)(2,1)}, u32[]{:S(2)}, u32[]{:S(2)}) async-start(bf16[8,16,1152]{2,1,0:T(8,128)(2,1)} %bitcast.1), calls=%async_computation | async-start | bytes 589824 | tf_op jit(solution)/shard_map/all_to_all | solution.py:154
  16.9 1.0 gather.32
  19.6 1.2 compare_convert_fusion
  20.8 1.1 pad_maximum_fusion
  21.9 1.0 slice.408
  22.9 1.0 slice.409
  24.8 1.5 collective-permute-start.4
  26.3 2.4 %all-to-all-done = bf16[8,16,1152]{2,1,0:T(8,128)(2,1)} async-done(((bf16[8,16,1152]{2,1,0:T(8,128)(2,1)}), bf16[8,16,1152]{2,1,0:T(8,128)(2,1)}, u32[]{:S(2)}, u32[]{:S(2)}) %all-to-all-start) | async-done | bytes 294944 | tf_op jit(solution)/shard_map/all_to_all | solution.py:154
  28.7 2.4 %all_gather.3 = bf16[128,2304]{1,0:T(8,128)(2,1)S(1)} all-gather(bf16[128,1152]{1,0:T(8,128)(2,1)} %bitcast.2), channel_id=1, replica_groups=mesh['groups'=2,'seq'=8,'wg'=2] {'wg'}, dimensions={1}, use_global_device_ids=true | all-gather | bytes 884736 | tf_op jit(solution)/shard_map/all_gather | solution.py:163
  33.4 2.0 collective-permute-start.3
  35.6 13.4 %collective-permute-done.2 = bf16[2,288,512]{2,1,0:T(8,128)(2,1)S(1)} collective-permute-done((bf16[2,288,512]{2,1,0:T(8,128)(2,1)}, bf16[2,288,512]{2,1,0:T(8,128)(2,1)S(1)}, u32[]{:S(2)}, u32[]{:S(2)}) %collective-permute-start.2) | collective-permute-done | bytes 589856 | tf_op jit(solution)/shard_map/ppermute | solution.py:105
  50.7 1.5 select_bitcast_fusion.23
  52.5 1.6 collective-permute-start.5
  54.4 1.3 collective-permute-start.6
  57.3 9.8 %collective-permute-done.5 = bf16[2,288,512]{2,1,0:T(8,128)(2,1)S(1)} collective-permute-done((bf16[2,288,512]{2,1,0:T(8,128)(2,1)S(1)}, bf16[2,288,512]{2,1,0:T(8,128)(2,1)S(1)}, u32[]{:S(2)}, u32[]{:S(2)}) %collective-permute-start.5) | collective-permute-done | bytes 589856 | tf_op jit(solution)/shard_map/ppermute | solution.py:110
  67.4 1.3 collective-permute-done.6
  70.1 1.1 collective-permute-start.10
  71.2 0.9 collective-permute-start.9
  72.7 9.6 %collective-permute-done.8 = bf16[2,288,512]{2,1,0:T(8,128)(2,1)S(1)} collective-permute-done((bf16[2,288,512]{2,1,0:T(8,128)(2,1)S(1)}, bf16[2,288,512]{2,1,0:T(8,128)(2,1)S(1)}, u32[]{:S(2)}, u32[]{:S(2)}) %collective-permute-start.8) | collective-permute-done | bytes 589856 | tf_op jit(solution)/shard_map/ppermute | solution.py:110
  82.6 1.1 collective-permute-done.9
  83.9 2.1 %collective-permute-start.11 = (bf16[2,288,512]{2,1,0:T(8,128)(2,1)S(1)}, bf16[2,288,512]{2,1,0:T(8,128)(2,1)S(1)}, u32[]{:S(2)}, u32[]{:S(2)}) collective-permute-start(bf16[2,288,512]{2,1,0:T(8,128)(2,1)S(1)} %pad_maximum_fusion.19), channel_id=1, source_target_pairs={{0,16},{16,0},{1,17},{17,1},{2,18},{18,2},{3,19},{19,3},{4,20},{20... | collective-permute-start | bytes 1769480 | tf_op jit(solution)/shard_map/ppermute | solution.py:110
  86.0 1.0 collective-permute-start.12
  87.0 1.1 collective-permute-start.13
  88.5 7.7 %collective-permute-done.11 = bf16[2,288,512]{2,1,0:T(8,128)(2,1)S(1)} collective-permute-done((bf16[2,288,512]{2,1,0:T(8,128)(2,1)S(1)}, bf16[2,288,512]{2,1,0:T(8,128)(2,1)S(1)}, u32[]{:S(2)}, u32[]{:S(2)}) %collective-permute-start.11) | collective-permute-done | bytes 589856 | tf_op jit(solution)/shard_map/ppermute | solution.py:110
  97.6 1.9 collective-permute-start.14
  100.3 1.3 collective-permute-start.16
  102.0 8.0 %collective-permute-done.14 = bf16[2,288,512]{2,1,0:T(8,128)(2,1)S(1)} collective-permute-done((bf16[2,288,512]{2,1,0:T(8,128)(2,1)S(1)}, bf16[2,288,512]{2,1,0:T(8,128)(2,1)S(1)}, u32[]{:S(2)}, u32[]{:S(2)}) %collective-permute-start.14) | collective-permute-done | bytes 589856 | tf_op jit(solution)/shard_map/ppermute | solution.py:110
  111.0 1.6 collective-permute-done.16
  113.5 1.4 collective-permute-start.19
  116.2 7.3 %collective-permute-done.19 = bf16[2,288,512]{2,1,0:T(8,128)(2,1)S(1)} collective-permute-done((bf16[2,288,512]{2,1,0:T(8,128)(2,1)S(1)}, bf16[2,288,512]{2,1,0:T(8,128)(2,1)S(1)}, u32[]{:S(2)}, u32[]{:S(2)}) %collective-permute-start.19) | collective-permute-done | bytes 589856 | tf_op jit(solution)/shard_map/ppermute | solution.py:106
  123.6 1.2 collective-permute-done.18
  124.8 2.0 collective-permute-start.20
  127.2 8.0 %collective-permute-done.20 = bf16[2,288,512]{2,1,0:T(8,128)(2,1)S(1)} collective-permute-done((bf16[2,288,512]{2,1,0:T(8,128)(2,1)S(1)}, bf16[2,288,512]{2,1,0:T(8,128)(2,1)S(1)}, u32[]{:S(2)}, u32[]{:S(2)}) %collective-permute-start.20) | collective-permute-done | bytes 589856 | tf_op jit(solution)/shard_map/ppermute | solution.py:110
  146.7 2.0 fusion.28
  148.7 1.9 bitcast_dynamic-update-slice_fusion.12
  151.6 0.9 bitcast_dynamic-update-slice_fusion.10
  156.7 1.2 copy-done
  157.9 1.7 convolution_convert_fusion
  165.4 1.3 convolution_convert_fusion.2
  166.9 0.9 fusion.16
  168.9 1.7 convolution_bitcast_fusion.1
  170.6 2.1 %convolution_multiply_fusion.1 = f32[4,2,128,128]{3,2,1,0:T(8,128)S(1)} fusion(f32[4,2,128,128]{2,3,1,0:T(8,128)} %copy-done.20, f32[4,2,128,128]{2,3,1,0:T(8,128)} %copy-done.43, bf16[4,128,64]{2,1,0:T(8,128)(2,1)S(1)} %copy-done.28, bf16[4,128,64]{2,1,0:T(8,128)(2,1)S(1)} %copy-done.26, f32[4,2,128]{2,1,0:T(2,128)S(1)} %copy-done.46, ...), kind=kOutput, calls=%fused_computation.25 | convolution fusion | flops 35652736 | bytes 1724416 | tf_op jit(solution)/shard_map/kgij,kjd->kgid/dot_general | solution.py:271
  174.5 4.1 %fusion.41 = f32[128,2304]{1,0:T(8,128)S(1)} fusion(bf16[1024,2304]{0,1:T(8,128)(2,1)} %fusion.29, bf16[16,8,8,128]{3,2,1,0:T(8,128)(2,1)S(1)} %bitcast.296), kind=kOutput, calls=%fused_computation.196 | convolution fusion | flops 603979776 | bytes 6160384 | tf_op jit(solution)/shard_map/dot_general | solution.py:285
  179.6 2.6 %fusion.1 = bf16[128,2304]{1,0:T(8,128)(2,1)S(1)} fusion(f32[128,2304]{1,0:T(8,128)S(1)} %convolution_add_fusion.1, bf16[128,512]{0,1:T(8,128)(2,1)S(1)} %bitcast.301, bf16[512,2304]{0,1:T(8,128)(2,1)} %bitcast_dynamic-update-slice_fusion.16), kind=kOutput, calls=%fused_computation.9 | convolution fusion | flops 302579712 | bytes 4259840 | tf_op jit(solution)/shard_map/dot_general | solution.py:287
  185.2 2.4 %fusion.13 = bf16[128,2304]{1,0:T(8,128)(2,1)S(1)} fusion(bf16[128,2304]{1,0:T(8,128)(2,1)} %copy-done.12, bf16[128,2304]{1,0:T(8,128)(2,1)S(1)} %fusion.1, f32[128]{0:T(128)S(1)} %broadcast_multiply_fusion, f32[128]{0:T(128)S(1)} %copy-done.39, f32[2304]{0:T(1024)S(1)} %mul.519, f32[128]{0:T(128)S(1)} %copy-done.36, bf16[128,2304]{1,0:T(8,128)(2,1)S(1)} %copy.54, ...), kind=kLoop, calls=%fused_computation.36 | loop fusion | flops 6488064 | bytes 4742912 | tf_op jit(solution)/shard_map/convert_element_type | solution.py:297
  189.1 16.0 %all_to_all.21 = bf16[8,16,1152]{2,1,0:T(8,128)(2,1)S(1)} all-to-all(bf16[8,16,1152]{2,1,0:T(8,128)(2,1)S(1)} %broadcast_select_fusion.4), channel_id=1, replica_groups=mesh['groups'=2,'seq'=8,'wg'=2] {'seq'}, dimensions={0} | all-to-all | bytes 589824 | tf_op jit(solution)/shard_map/all_to_all | solution.py:299
  (275 shorter events, 54.9 us)
Async XLA Ops:
  1.4 11.2 %copy-start.31 = (f32[2304]{0:T(1024)S(1)}, f32[2304]{0:T(1024)}, u32[]{:S(2)}) copy-start(f32[2304]{0:T(1024)} %param.12) | copy-start | bytes 27652
  1.4 11.3 %copy-start.32 = (f32[2304]{0:T(1024)S(1)}, f32[2304]{0:T(1024)}, u32[]{:S(2)}) copy-start(f32[2304]{0:T(1024)} %param.17) | copy-start | bytes 27652
  1.4 11.4 %copy-start.33 = (f32[2304]{0:T(1024)S(1)}, f32[2304]{0:T(1024)}, u32[]{:S(2)}) copy-start(f32[2304]{0:T(1024)} %param.18) | copy-start | bytes 27652
  1.5 12.5 %copy-start.40 = (s32[8]{0:T(128)S(1)}, s32[8]{0:T(128)}, u32[]{:S(2)}) copy-start(s32[8]{0:T(128)} %param.20) | copy-start | bytes 100
  1.5 13.8 %copy-start.21 = (bf16[64,2304]{1,0:T(8,128)(2,1)S(1)}, bf16[64,2304]{1,0:T(8,128)(2,1)}, u32[]{:S(2)}) copy-start(bf16[64,2304]{1,0:T(8,128)(2,1)} %param.19) | copy-start | bytes 884740
  2.4 19.5 %collective-permute-start = (bf16[2,288,512]{2,1,0:T(8,128)(2,1)}, bf16[2,288,512]{2,1,0:T(8,128)(2,1)}, u32[]{:S(2)}, u32[]{:S(2)}) collective-permute-start(bf16[2,288,512]{2,1,0:T(8,128)(2,1)} %pad_maximum_fusion.14), channel_id=1, source_target_pairs={{0,4},{4,8},{8,12},{12,14},{14,10},{10,6},{6,2},{2,0},{1,5},{5,9},... | collective-permute-start | bytes 1769480 | tf_op jit(solution)/shard_map/ppermute | solution.py:105
  6.3 16.6 %collective-permute-start.1 = (bf16[2,288,512]{2,1,0:T(8,128)(2,1)}, bf16[2,288,512]{2,1,0:T(8,128)(2,1)}, u32[]{:S(2)}, u32[]{:S(2)}) collective-permute-start(bf16[2,288,512]{2,1,0:T(8,128)(2,1)} %pad_maximum_fusion.15), channel_id=1, source_target_pairs={{0,2},{4,0},{8,4},{12,8},{14,12},{10,14},{6,10},{2,6},{1,3},{5,1},... | collective-permute-start | bytes 1769480 | tf_op jit(solution)/shard_map/ppermute | solution.py:106
  6.3 22.4 %all-to-all-start = ((bf16[8,16,1152]{2,1,0:T(8,128)(2,1)}), bf16[8,16,1152]{2,1,0:T(8,128)(2,1)}, u32[]{:S(2)}, u32[]{:S(2)}) async-start(bf16[8,16,1152]{2,1,0:T(8,128)(2,1)} %bitcast.1), calls=%async_computation | async-start | bytes 589824 | tf_op jit(solution)/shard_map/all_to_all | solution.py:154
  15.2 4.3 %copy-start.37 = (pred[128]{0:T(512)(128)(4,1)}, pred[128]{0:T(512)(128)(4,1)S(1)}, u32[]{:S(2)}) copy-start(pred[128]{0:T(512)(128)(4,1)S(1)} %iota_compare_fusion.1) | copy-start | bytes 388
  15.3 3.3 %copy-start.41 = (s32[8]{0:T(128)S(1)}, s32[8]{0:T(128)}, u32[]{:S(2)}) copy-start(s32[8]{0:T(128)} %param.21) | copy-start | bytes 100
  15.9 4.9 %copy-start.10 = (bf16[288,1024]{1,0:T(8,128)(2,1)S(1)}, bf16[288,1024]{1,0:T(8,128)(2,1)}, u32[]{:S(2)}) copy-start(bf16[288,1024]{1,0:T(8,128)(2,1)} %param.13) | copy-start | bytes 1769476
  15.9 4.9 %copy-start.11 = (bf16[1024,288]{0,1:T(8,128)(2,1)S(1)}, bf16[1024,288]{0,1:T(8,128)(2,1)}, u32[]{:S(2)}) copy-start(bf16[1024,288]{0,1:T(8,128)(2,1)} %param.16) | copy-start | bytes 1769476
  15.9 4.8 %copy-start.15 = (bf16[288,512]{1,0:T(8,128)(2,1)S(1)}, bf16[288,512]{1,0:T(8,128)(2,1)}, u32[]{:S(2)}) copy-start(bf16[288,512]{1,0:T(8,128)(2,1)} %param.14) | copy-start | bytes 884740
  24.8 25.9 %collective-permute-start.4 = (bf16[2,288,512]{2,1,0:T(8,128)(2,1)}, bf16[2,288,512]{2,1,0:T(8,128)(2,1)}, u32[]{:S(2)}, u32[]{:S(2)}) collective-permute-start(bf16[2,288,512]{2,1,0:T(8,128)(2,1)} %pad_maximum_fusion.16), channel_id=1, source_target_pairs={{0,16},{16,0},{1,17},{17,1},{2,18},{18,2},{3,19},{19,3},{4,20},{20... | collective-permute-start | bytes 1769480 | tf_op jit(solution)/shard_map/ppermute | solution.py:110
  33.3 17.3 %copy-start.35 = (f32[128]{0:T(128)}, f32[128]{0:T(128)S(1)}, u32[]{:S(2)}) copy-start(f32[128]{0:T(128)S(1)} %get-tuple-element.110) | copy-start | bytes 1540
  33.3 15.6 %collective-permute-start.2 = (bf16[2,288,512]{2,1,0:T(8,128)(2,1)}, bf16[2,288,512]{2,1,0:T(8,128)(2,1)S(1)}, u32[]{:S(2)}, u32[]{:S(2)}) collective-permute-start(bf16[2,288,512]{2,1,0:T(8,128)(2,1)} %collective-permute-done), channel_id=1, source_target_pairs={{0,4},{4,8},{8,12},{12,14},{14,10},{10,6},{6,2},{2,0},{1,5},{5,9},... | collective-permute-start | bytes 1769480 | tf_op jit(solution)/shard_map/ppermute | solution.py:105
  33.4 15.6 %collective-permute-start.3 = (bf16[2,288,512]{2,1,0:T(8,128)(2,1)}, bf16[2,288,512]{2,1,0:T(8,128)(2,1)S(1)}, u32[]{:S(2)}, u32[]{:S(2)}) collective-permute-start(bf16[2,288,512]{2,1,0:T(8,128)(2,1)} %collective-permute-done.1), channel_id=1, source_target_pairs={{0,2},{4,0},{8,4},{12,8},{14,12},{10,14},{6,10},{2,6},{1,3},{5,1},... | collective-permute-start | bytes 1769480 | tf_op jit(solution)/shard_map/ppermute | solution.py:106
  52.3 93.4 %copy-start.2 = (bf16[288,1536]{1,0:T(8,128)(2,1)}, bf16[288,1536]{1,0:T(8,128)(2,1)S(1)}, u32[]{:S(2)}) copy-start(bf16[288,1536]{1,0:T(8,128)(2,1)S(1)} %pad_maximum_fusion.3) | copy-start | bytes 2654212
  52.5 14.6 %collective-permute-start.5 = (bf16[2,288,512]{2,1,0:T(8,128)(2,1)S(1)}, bf16[2,288,512]{2,1,0:T(8,128)(2,1)S(1)}, u32[]{:S(2)}, u32[]{:S(2)}) collective-permute-start(bf16[2,288,512]{2,1,0:T(8,128)(2,1)S(1)} %pad_maximum_fusion.17), channel_id=1, source_target_pairs={{0,16},{16,0},{1,17},{17,1},{2,18},{18,2},{3,19},{19,3},{4,20},{20... | collective-permute-start | bytes 1769480 | tf_op jit(solution)/shard_map/ppermute | solution.py:110
  54.4 14.3 %collective-permute-start.6 = (bf16[2,288,512]{2,1,0:T(8,128)(2,1)S(1)}, bf16[2,288,512]{2,1,0:T(8,128)(2,1)S(1)}, u32[]{:S(2)}, u32[]{:S(2)}) collective-permute-start(bf16[2,288,512]{2,1,0:T(8,128)(2,1)S(1)} %collective-permute-done.2), channel_id=1, source_target_pairs={{0,4},{4,8},{8,12},{12,14},{14,10},{10,6},{6,2},{2,0},{1,5},{5,9},... | collective-permute-start | bytes 1769480 | tf_op jit(solution)/shard_map/ppermute | solution.py:105
  55.7 13.7 %collective-permute-start.7 = (bf16[2,288,512]{2,1,0:T(8,128)(2,1)S(1)}, bf16[2,288,512]{2,1,0:T(8,128)(2,1)S(1)}, u32[]{:S(2)}, u32[]{:S(2)}) collective-permute-start(bf16[2,288,512]{2,1,0:T(8,128)(2,1)S(1)} %collective-permute-done.3), channel_id=1, source_target_pairs={{0,2},{4,0},{8,4},{12,8},{14,12},{10,14},{6,10},{2,6},{1,3},{5,1},... | collective-permute-start | bytes 1769480 | tf_op jit(solution)/shard_map/ppermute | solution.py:106
  69.5 12.8 %collective-permute-start.8 = (bf16[2,288,512]{2,1,0:T(8,128)(2,1)S(1)}, bf16[2,288,512]{2,1,0:T(8,128)(2,1)S(1)}, u32[]{:S(2)}, u32[]{:S(2)}) collective-permute-start(bf16[2,288,512]{2,1,0:T(8,128)(2,1)S(1)} %pad_maximum_fusion.18), channel_id=1, source_target_pairs={{0,16},{16,0},{1,17},{17,1},{2,18},{18,2},{3,19},{19,3},{4,20},{20... | collective-permute-start | bytes 1769480 | tf_op jit(solution)/shard_map/ppermute | solution.py:110
  70.1 12.5 %collective-permute-start.10 = (bf16[2,288,512]{2,1,0:T(8,128)(2,1)S(1)}, bf16[2,288,512]{2,1,0:T(8,128)(2,1)S(1)}, u32[]{:S(2)}, u32[]{:S(2)}) collective-permute-start(bf16[2,288,512]{2,1,0:T(8,128)(2,1)S(1)} %collective-permute-done.7), channel_id=1, source_target_pairs={{0,2},{4,0},{8,4},{12,8},{14,12},{10,14},{6,10},{2,6},{1,3},{5,1},... | collective-permute-start | bytes 1769480 | tf_op jit(solution)/shard_map/ppermute | solution.py:106
  71.2 12.5 %collective-permute-start.9 = (bf16[2,288,512]{2,1,0:T(8,128)(2,1)S(1)}, bf16[2,288,512]{2,1,0:T(8,128)(2,1)S(1)}, u32[]{:S(2)}, u32[]{:S(2)}) collective-permute-start(bf16[2,288,512]{2,1,0:T(8,128)(2,1)S(1)} %collective-permute-done.6), channel_id=1, source_target_pairs={{0,4},{4,8},{8,12},{12,14},{14,10},{10,6},{6,2},{2,0},{1,5},{5,9},... | collective-permute-start | bytes 1769480 | tf_op jit(solution)/shard_map/ppermute | solution.py:105
  83.9 12.4 %collective-permute-start.11 = (bf16[2,288,512]{2,1,0:T(8,128)(2,1)S(1)}, bf16[2,288,512]{2,1,0:T(8,128)(2,1)S(1)}, u32[]{:S(2)}, u32[]{:S(2)}) collective-permute-start(bf16[2,288,512]{2,1,0:T(8,128)(2,1)S(1)} %pad_maximum_fusion.19), channel_id=1, source_target_pairs={{0,16},{16,0},{1,17},{17,1},{2,18},{18,2},{3,19},{19,3},{4,20},{20... | collective-permute-start | bytes 1769480 | tf_op jit(solution)/shard_map/ppermute | solution.py:110
  86.0 11.4 %collective-permute-start.12 = (bf16[2,288,512]{2,1,0:T(8,128)(2,1)S(1)}, bf16[2,288,512]{2,1,0:T(8,128)(2,1)S(1)}, u32[]{:S(2)}, u32[]{:S(2)}) collective-permute-start(bf16[2,288,512]{2,1,0:T(8,128)(2,1)S(1)} %collective-permute-done.9), channel_id=1, source_target_pairs={{0,4},{4,8},{8,12},{12,14},{14,10},{10,6},{6,2},{2,0},{1,5},{5,9},... | collective-permute-start | bytes 1769480 | tf_op jit(solution)/shard_map/ppermute | solution.py:105
  87.0 10.5 %collective-permute-start.13 = (bf16[2,288,512]{2,1,0:T(8,128)(2,1)S(1)}, bf16[2,288,512]{2,1,0:T(8,128)(2,1)S(1)}, u32[]{:S(2)}, u32[]{:S(2)}) collective-permute-start(bf16[2,288,512]{2,1,0:T(8,128)(2,1)S(1)} %collective-permute-done.10), channel_id=1, source_target_pairs={{0,2},{4,0},{8,4},{12,8},{14,12},{10,14},{6,10},{2,6},{1,3},{5,1},... | collective-permute-start | bytes 1769480 | tf_op jit(solution)/shard_map/ppermute | solution.py:106
  97.6 12.4 %collective-permute-start.14 = (bf16[2,288,512]{2,1,0:T(8,128)(2,1)S(1)}, bf16[2,288,512]{2,1,0:T(8,128)(2,1)S(1)}, u32[]{:S(2)}, u32[]{:S(2)}) collective-permute-start(bf16[2,288,512]{2,1,0:T(8,128)(2,1)S(1)} %pad_maximum_fusion.20), channel_id=1, source_target_pairs={{0,16},{16,0},{1,17},{17,1},{2,18},{18,2},{3,19},{19,3},{4,20},{20... | collective-permute-start | bytes 1769480 | tf_op jit(solution)/shard_map/ppermute | solution.py:110
  99.5 11.5 %collective-permute-start.15 = (bf16[2,288,512]{2,1,0:T(8,128)(2,1)S(1)}, bf16[2,288,512]{2,1,0:T(8,128)(2,1)S(1)}, u32[]{:S(2)}, u32[]{:S(2)}) collective-permute-start(bf16[2,288,512]{2,1,0:T(8,128)(2,1)S(1)} %collective-permute-done.12), channel_id=1, source_target_pairs={{0,4},{4,8},{8,12},{12,14},{14,10},{10,6},{6,2},{2,0},{1,5},{5,9},... | collective-permute-start | bytes 1769480 | tf_op jit(solution)/shard_map/ppermute | solution.py:105
  100.3 12.3 %collective-permute-start.16 = (bf16[2,288,512]{2,1,0:T(8,128)(2,1)S(1)}, bf16[2,288,512]{2,1,0:T(8,128)(2,1)S(1)}, u32[]{:S(2)}, u32[]{:S(2)}) collective-permute-start(bf16[2,288,512]{2,1,0:T(8,128)(2,1)S(1)} %collective-permute-done.13), channel_id=1, source_target_pairs={{0,2},{4,0},{8,4},{12,8},{14,12},{10,14},{6,10},{2,6},{1,3},{5,1},... | collective-permute-start | bytes 1769480 | tf_op jit(solution)/shard_map/ppermute | solution.py:106
  110.2 33.0 %copy-start.4 = (bf16[288,1536]{1,0:T(8,128)(2,1)}, bf16[288,1536]{1,0:T(8,128)(2,1)S(1)}, u32[]{:S(2)}) copy-start(bf16[288,1536]{1,0:T(8,128)(2,1)S(1)} %pad_maximum_fusion.11) | copy-start | bytes 2654212
  112.7 14.2 %collective-permute-start.17 = (bf16[2,288,512]{2,1,0:T(8,128)(2,1)S(1)}, bf16[2,288,512]{2,1,0:T(8,128)(2,1)S(1)}, u32[]{:S(2)}, u32[]{:S(2)}) collective-permute-start(bf16[2,288,512]{2,1,0:T(8,128)(2,1)S(1)} %pad_maximum_fusion.21), channel_id=1, source_target_pairs={{0,16},{16,0},{1,17},{17,1},{2,18},{18,2},{3,19},{19,3},{4,20},{20... | collective-permute-start | bytes 1769480 | tf_op jit(solution)/shard_map/ppermute | solution.py:110
  113.5 10.1 %collective-permute-start.19 = (bf16[2,288,512]{2,1,0:T(8,128)(2,1)S(1)}, bf16[2,288,512]{2,1,0:T(8,128)(2,1)S(1)}, u32[]{:S(2)}, u32[]{:S(2)}) collective-permute-start(bf16[2,288,512]{2,1,0:T(8,128)(2,1)S(1)} %collective-permute-done.16), channel_id=1, source_target_pairs={{0,2},{4,0},{8,4},{12,8},{14,12},{10,14},{6,10},{2,6},{1,3},{5,1},... | collective-permute-start | bytes 1769480 | tf_op jit(solution)/shard_map/ppermute | solution.py:106
  114.9 9.9 %collective-permute-start.18 = (bf16[2,288,512]{2,1,0:T(8,128)(2,1)S(1)}, bf16[2,288,512]{2,1,0:T(8,128)(2,1)S(1)}, u32[]{:S(2)}, u32[]{:S(2)}) collective-permute-start(bf16[2,288,512]{2,1,0:T(8,128)(2,1)S(1)} %collective-permute-done.15), channel_id=1, source_target_pairs={{0,4},{4,8},{8,12},{12,14},{14,10},{10,6},{6,2},{2,0},{1,5},{5,9},... | collective-permute-start | bytes 1769480 | tf_op jit(solution)/shard_map/ppermute | solution.py:105
  124.8 10.4 %collective-permute-start.20 = (bf16[2,288,512]{2,1,0:T(8,128)(2,1)S(1)}, bf16[2,288,512]{2,1,0:T(8,128)(2,1)S(1)}, u32[]{:S(2)}, u32[]{:S(2)}) collective-permute-start(bf16[2,288,512]{2,1,0:T(8,128)(2,1)S(1)} %pad_maximum_fusion.22), channel_id=1, source_target_pairs={{0,16},{16,0},{1,17},{17,1},{2,18},{18,2},{3,19},{19,3},{4,20},{20... | collective-permute-start | bytes 1769480 | tf_op jit(solution)/shard_map/ppermute | solution.py:110
  127.1 15.1 %copy-start.6 = (bf16[288,1536]{1,0:T(8,128)(2,1)}, bf16[288,1536]{1,0:T(8,128)(2,1)S(1)}, u32[]{:S(2)}) copy-start(bf16[288,1536]{1,0:T(8,128)(2,1)S(1)} %pad_maximum_fusion.13) | copy-start | bytes 2654212
  127.2 9.4 %copy-start.1 = (bf16[1024,2304]{0,1:T(8,128)(2,1)}, bf16[1024,2304]{0,1:T(8,128)(2,1)S(1)}, u32[]{:S(2)}) copy-start(bf16[1024,2304]{0,1:T(8,128)(2,1)S(1)} %bitcast_dynamic-update-slice_fusion) | copy-start | bytes 14155780
  141.1 2.4 %copy-start.8 = (bf16[512,2304]{0,1:T(8,128)(2,1)}, bf16[512,2304]{0,1:T(8,128)(2,1)S(1)}, u32[]{:S(2)}) copy-start(bf16[512,2304]{0,1:T(8,128)(2,1)S(1)} %get-tuple-element.69) | copy-start | bytes 7077892
  146.7 4.0 %copy-start.5 = (bf16[288,1536]{1,0:T(8,128)(2,1)S(1)}, bf16[288,1536]{1,0:T(8,128)(2,1)}, u32[]{:S(2)}) copy-start(bf16[288,1536]{1,0:T(8,128)(2,1)} %copy-done.4) | copy-start | bytes 2654212
  151.6 2.8 %copy-start.3 = (bf16[288,1536]{1,0:T(8,128)(2,1)S(1)}, bf16[288,1536]{1,0:T(8,128)(2,1)}, u32[]{:S(2)}) copy-start(bf16[288,1536]{1,0:T(8,128)(2,1)} %copy-done.2) | copy-start | bytes 2654212
  152.5 2.8 %copy-start.13 = (f32[8,128,64]{2,1,0:T(8,128)S(1)}, f32[8,128,64]{2,1,0:T(8,128)}, u32[]{:S(2)}) copy-start(f32[8,128,64]{2,1,0:T(8,128)} %copy.55) | copy-start | bytes 786436
  152.5 2.8 %copy-start.14 = (f32[8,128,64]{2,1,0:T(8,128)S(1)}, f32[8,128,64]{2,1,0:T(8,128)}, u32[]{:S(2)}) copy-start(f32[8,128,64]{2,1,0:T(8,128)} %copy.56) | copy-start | bytes 786436
  155.3 2.6 %copy-start = (bf16[1024,2304]{0,1:T(8,128)(2,1)S(1)}, bf16[1024,2304]{0,1:T(8,128)(2,1)}, u32[]{:S(2)}) copy-start(bf16[1024,2304]{0,1:T(8,128)(2,1)} %bitcast_dynamic-update-slice_fusion.7) | copy-start | bytes 14155780
  159.6 2.5 %collective-permute-start.21 = (bf16[128,2304]{1,0:T(8,128)(2,1)S(1)}, bf16[128,2304]{1,0:T(8,128)(2,1)S(1)}, u32[]{:S(2)}, u32[]{:S(2)}) collective-permute-start(bf16[128,2304]{1,0:T(8,128)(2,1)S(1)} %convolution_convert_fusion), channel_id=1, source_target_pairs={{0,1},{1,0},{2,3},{3,2},{4,5},{5,4},{6,7},{7,6},{8,9},{9,8},{10,11... | collective-permute-start | bytes 1769480 | tf_op jit(solution)/shard_map/ppermute | solution.py:58
  174.5 4.2 %copy-start.9 = (bf16[512,2304]{0,1:T(8,128)(2,1)S(1)}, bf16[512,2304]{0,1:T(8,128)(2,1)}, u32[]{:S(2)}) copy-start(bf16[512,2304]{0,1:T(8,128)(2,1)} %copy-done.8) | copy-start | bytes 7077892
  182.2 3.1 %copy-start.36 = (f32[128]{0:T(128)S(1)}, f32[128]{0:T(128)}, u32[]{:S(2)}) copy-start(f32[128]{0:T(128)} %copy-done.35) | copy-start | bytes 1540
  182.2 3.0 %copy-start.39 = (f32[128]{0:T(128)S(1)}, f32[128]{0:T(128)}, u32[]{:S(2)}) copy-start(f32[128]{0:T(128)} %get-tuple-element.109) | copy-start | bytes 1540
  182.2 2.2 %collective-permute-start.22 = (bf16[128,2304]{1,0:T(8,128)(2,1)S(1)}, bf16[128,2304]{1,0:T(8,128)(2,1)S(1)}, u32[]{:S(2)}, u32[]{:S(2)}) collective-permute-start(bf16[128,2304]{1,0:T(8,128)(2,1)S(1)} %fusion.1), channel_id=1, source_target_pairs={{0,1},{1,0},{2,3},{3,2},{4,5},{5,4},{6,7},{7,6},{8,9},{9,8},{10,11... | collective-permute-start | bytes 1769480 | tf_op jit(solution)/shard_map/ppermute | solution.py:58
  (23 other events, 29.9 us)

commit v19 on v13

--- a/solution.py
+++ b/solution.py
@@ -107,9 +107,7 @@
     front_pieces = [front]
     back_pieces = [back]
     for step in range(1, n):
-        handed = lax.ppermute(
-            jnp.stack([front_ring[step][0], back_ring[step][0]]), "groups", group_pairs
-        )
+        handed = [lax.ppermute(ring[step][0], "groups", group_pairs) for ring in (front_ring, back_ring)]
         for ring, pieces, other in ((front_ring, front_pieces, handed[0]), (back_ring, back_pieces, handed[1])):
             own, middle = ring[step][0], ring[step][1]
             pieces.append(

time: 205 us -> 223 us (1.088)
  local copies, waits for them, and re-layouts: 32.7 us -> 42.1 us
  other arithmetic: 24.7 us -> 29.1 us
  starting transfers between devices: 34.2 us -> 37.8 us
  matrix products: 22.7 us -> 25.5 us
  waiting for transfers between devices: 71 us -> 68.2 us
    ppermute x7, waiting for transfers between devices: 19.2 us -> 7.9 us  [ring_gather(): front_ring.append(lax.ppermute(front_ring[-1], 'seq', forward_pairs))]
    ppermute x7, waiting for transfers between devices: 10.3 us -> 18.2 us  [ring_gather(): back_ring.append(lax.ppermute(back_ring[-1], 'seq', backward_pairs))]
    ppermute x7, starting transfers between devices: 7.9 us -> 12.9 us  [ring_gather(): front_ring.append(lax.ppermute(front_ring[-1], 'seq', forward_pairs))]
    squeeze x0 -> x14, local copies, waits for them, and re-layouts: none -> 4.92 us  [ring_gather(): own, middle = (ring[step][0], ring[step][1])]
    ppermute x7, starting transfers between devices: 7.53 us -> 2.69 us  [ring_gather(): back_ring.append(lax.ppermute(back_ring[-1], 'seq', backward_pairs))]
    ppermute x7 -> x14, starting transfers between devices: 11.9 us -> 15.3 us  [ring_gather(): lax.ppermute(ring[step][0], 'groups', group_pairs)]
    ppermute x7 -> x14, waiting for transfers between devices: 40.2 us -> 42.1 us  [ring_gather(): lax.ppermute(ring[step][0], 'groups', group_pairs)]
    unnamed x141 -> x149, local copies, waits for them, and re-layouts: 14.6 us -> 15.2 us
  transfers between devices with their start and end apart: 24 -> 31, of which waited for: 18 -> 20; matrix products, arithmetic and copies ran while one was open for 14% -> 17% of each run, Pallas kernels for 0% -> 0%
where the time goes in v19:
time: 223 us; the launch traced here: 222 us
  waiting for transfers between devices  68.2 us (31%)
  local copies, waits for them, and re-layouts  42.1 us (19%)
  starting transfers between devices  37.8 us (17%)
  other arithmetic  29.1 us (13%)
  matrix products  25.5 us (11%)
  blocking collectives  17.8 us (8%)
    ppermute x14, waiting for transfers between devices, ring_gather(): lax.ppermute(ring[step][0], 'groups', group_pairs)  42.1 us
    ppermute x7, waiting for transfers between devices, ring_gather(): back_ring.append(lax.ppermute(back_ring[-1], 'seq', backward_pairs))  18.2 us
    all_to_all x1, blocking collectives, shards(): lax.all_to_all(grad_rows, 'seq', split_axis=0, concat_axis=0, tiled=True)  15.4 us
    ppermute x14, starting transfers between devices, ring_gather(): lax.ppermute(ring[step][0], 'groups', group_pairs)  15.3 us
    unnamed x149, local copies, waits for them, and re-layouts  15.2 us
    ppermute x7, starting transfers between devices, ring_gather(): front_ring.append(lax.ppermute(front_ring[-1], 'seq', forward_pairs))  12.9 us
    ppermute x7, waiting for transfers between devices, ring_gather(): front_ring.append(lax.ppermute(front_ring[-1], 'seq', forward_pairs))  7.9 us
    all_to_all x1, starting transfers between devices, shards(): lax.all_to_all(generator_rows, 'seq', split_axis=0, concat_axis=0, tiled=...  6.25 us
  transfers between devices with their start and end apart: 31, of which 20 were waited for; matrix products, arithmetic and copies ran while one was open for 17% of the time, Pallas kernels for 0%

profile of v19, /device:TPU:0, one launch (start us, length us, event | category | flops | bytes accessed | tf_op | source)
XLA Modules:
  0.0 221.8 jit_solution(17410148814577543128)
XLA Ops:
  0.0 1.4 fusion.39
  2.3 3.0 %collective-permute-start = (bf16[2,288,512]{2,1,0:T(8,128)(2,1)}, bf16[2,288,512]{2,1,0:T(8,128)(2,1)}, u32[]{:S(2)}, u32[]{:S(2)}) collective-permute-start(bf16[2,288,512]{2,1,0:T(8,128)(2,1)} %pad_maximum_fusion.14), channel_id=1, source_target_pairs={{0,4},{4,8},{8,12},{12,14},{14,10},{10,6},{6,2},{2,0},{1,5},{5,9},... | collective-permute-start | bytes 1769480 | tf_op jit(solution)/shard_map/ppermute | solution.py:105
  6.2 6.3 %all-to-all-start = ((bf16[8,16,1152]{2,1,0:T(8,128)(2,1)}), bf16[8,16,1152]{2,1,0:T(8,128)(2,1)}, u32[]{:S(2)}, u32[]{:S(2)}) async-start(bf16[8,16,1152]{2,1,0:T(8,128)(2,1)} %bitcast.1), calls=%async_computation | async-start | bytes 589824 | tf_op jit(solution)/shard_map/all_to_all | solution.py:151
  23.7 1.9 slice_bitcast_fusion.25
  25.6 1.5 collective-permute-start.3
  27.1 1.8 slice_bitcast_fusion.27
  31.1 2.4 %all_gather.3 = bf16[128,2304]{1,0:T(8,128)(2,1)S(1)} all-gather(bf16[128,1152]{1,0:T(8,128)(2,1)} %bitcast.2), channel_id=1, replica_groups=mesh['groups'=2,'seq'=8,'wg'=2] {'wg'}, dimensions={1}, use_global_device_ids=true | all-gather | bytes 884736 | tf_op jit(solution)/shard_map/all_gather | solution.py:160
  36.0 2.1 collective-permute-start.4
  41.3 12.1 %collective-permute-done.5 = bf16[2,288,512]{2,1,0:T(8,128)(2,1)S(1)} collective-permute-done((bf16[2,288,512]{2,1,0:T(8,128)(2,1)}, bf16[2,288,512]{2,1,0:T(8,128)(2,1)S(1)}, u32[]{:S(2)}, u32[]{:S(2)}) %collective-permute-start.5) | collective-permute-done | bytes 589856 | tf_op jit(solution)/shard_map/ppermute | solution.py:106
  53.5 1.6 collective-permute-start.7
  55.8 1.5 collective-permute-start.8
  58.3 5.2 %collective-permute-done.7 = bf16[288,512]{1,0:T(8,128)(2,1)S(1)} collective-permute-done((bf16[288,512]{1,0:T(8,128)(2,1)S(1)}, bf16[288,512]{1,0:T(8,128)(2,1)S(1)}, u32[]{:S(2)}, u32[]{:S(2)}) %collective-permute-start.7) | collective-permute-done | bytes 294944 | tf_op jit(solution)/shard_map/ppermute | solution.py:110
  63.6 4.1 %collective-permute-done.6 = bf16[288,512]{1,0:T(8,128)(2,1)S(1)} collective-permute-done((bf16[288,512]{1,0:T(8,128)(2,1)S(1)}, bf16[288,512]{1,0:T(8,128)(2,1)S(1)}, u32[]{:S(2)}, u32[]{:S(2)}) %collective-permute-start.6) | collective-permute-done | bytes 294944 | tf_op jit(solution)/shard_map/ppermute | solution.py:110
  67.9 1.6 collective-permute-done.8
  69.5 1.6 collective-permute-start.10
  72.4 1.5 collective-permute-start.12
  74.9 4.3 %collective-permute-done.10 = bf16[288,512]{1,0:T(8,128)(2,1)S(1)} collective-permute-done((bf16[288,512]{1,0:T(8,128)(2,1)S(1)}, bf16[288,512]{1,0:T(8,128)(2,1)S(1)}, u32[]{:S(2)}, u32[]{:S(2)}) %collective-permute-start.10) | collective-permute-done | bytes 294944 | tf_op jit(solution)/shard_map/ppermute | solution.py:110
  79.3 3.0 %collective-permute-done.11 = bf16[288,512]{1,0:T(8,128)(2,1)S(1)} collective-permute-done((bf16[288,512]{1,0:T(8,128)(2,1)S(1)}, bf16[288,512]{1,0:T(8,128)(2,1)S(1)}, u32[]{:S(2)}, u32[]{:S(2)}) %collective-permute-start.11) | collective-permute-done | bytes 294944 | tf_op jit(solution)/shard_map/ppermute | solution.py:110
  82.4 2.2 collective-permute-done.12
  87.0 1.5 collective-permute-start.16
  89.5 3.4 %collective-permute-done.14 = bf16[288,512]{1,0:T(8,128)(2,1)S(1)} collective-permute-done((bf16[288,512]{1,0:T(8,128)(2,1)S(1)}, bf16[288,512]{1,0:T(8,128)(2,1)S(1)}, u32[]{:S(2)}, u32[]{:S(2)}) %collective-permute-start.14) | collective-permute-done | bytes 294944 | tf_op jit(solution)/shard_map/ppermute | solution.py:110
  92.9 4.0 %collective-permute-done.15 = bf16[288,512]{1,0:T(8,128)(2,1)S(1)} collective-permute-done((bf16[288,512]{1,0:T(8,128)(2,1)S(1)}, bf16[288,512]{1,0:T(8,128)(2,1)S(1)}, u32[]{:S(2)}, u32[]{:S(2)}) %collective-permute-start.15) | collective-permute-done | bytes 294944 | tf_op jit(solution)/shard_map/ppermute | solution.py:110
  97.1 1.5 collective-permute-done.16
  98.6 1.3 collective-permute-start.18
  101.1 1.4 collective-permute-start.20
  103.6 1.9 collective-permute-done.18
  105.6 4.7 %collective-permute-done.19 = bf16[288,512]{1,0:T(8,128)(2,1)S(1)} collective-permute-done((bf16[288,512]{1,0:T(8,128)(2,1)S(1)}, bf16[288,512]{1,0:T(8,128)(2,1)S(1)}, u32[]{:S(2)}, u32[]{:S(2)}) %collective-permute-start.19) | collective-permute-done | bytes 294944 | tf_op jit(solution)/shard_map/ppermute | solution.py:110
  110.5 2.4 %collective-permute-done.20 = bf16[2,288,512]{2,1,0:T(8,128)(2,1)S(1)} collective-permute-done((bf16[2,288,512]{2,1,0:T(8,128)(2,1)S(1)}, bf16[2,288,512]{2,1,0:T(8,128)(2,1)S(1)}, u32[]{:S(2)}, u32[]{:S(2)}) %collective-permute-start.20) | collective-permute-done | bytes 589856 | tf_op jit(solution)/shard_map/ppermute | solution.py:105
  113.5 2.3 %collective-permute-done.21 = bf16[2,288,512]{2,1,0:T(8,128)(2,1)S(1)} collective-permute-done((bf16[2,288,512]{2,1,0:T(8,128)(2,1)S(1)}, bf16[2,288,512]{2,1,0:T(8,128)(2,1)S(1)}, u32[]{:S(2)}, u32[]{:S(2)}) %collective-permute-start.21) | collective-permute-done | bytes 589856 | tf_op jit(solution)/shard_map/ppermute | solution.py:106
  117.5 1.8 collective-permute-start.24
  119.8 3.4 %collective-permute-done.23 = bf16[288,512]{1,0:T(8,128)(2,1)S(1)} collective-permute-done((bf16[288,512]{1,0:T(8,128)(2,1)S(1)}, bf16[288,512]{1,0:T(8,128)(2,1)S(1)}, u32[]{:S(2)}, u32[]{:S(2)}) %collective-permute-start.23) | collective-permute-done | bytes 294944 | tf_op jit(solution)/shard_map/ppermute | solution.py:110
  123.4 3.7 %collective-permute-done.25 = bf16[2,288,512]{2,1,0:T(8,128)(2,1)S(1)} collective-permute-done((bf16[2,288,512]{2,1,0:T(8,128)(2,1)S(1)}, bf16[2,288,512]{2,1,0:T(8,128)(2,1)S(1)}, u32[]{:S(2)}, u32[]{:S(2)}) %collective-permute-start.25) | collective-permute-done | bytes 589856 | tf_op jit(solution)/shard_map/ppermute | solution.py:106
  128.1 1.4 collective-permute-start.27
  130.4 7.6 %collective-permute-done.26 = bf16[288,512]{1,0:T(8,128)(2,1)S(1)} collective-permute-done((bf16[288,512]{1,0:T(8,128)(2,1)S(1)}, bf16[288,512]{1,0:T(8,128)(2,1)S(1)}, u32[]{:S(2)}, u32[]{:S(2)}) %collective-permute-start.26) | collective-permute-done | bytes 294944 | tf_op jit(solution)/shard_map/ppermute | solution.py:110
  149.2 1.7 copy.116
  152.0 1.9 fusion.28
  162.1 1.7 convolution_convert_fusion
  165.6 1.7 bitcast_dynamic-update-slice_fusion.14
  170.3 2.0 convolution_convert_fusion.2
  173.4 2.0 fusion.16
  176.4 2.7 %convolution_bitcast_fusion.1 = f32[4,128,128]{2,1,0:T(8,128)} fusion(bf16[4,2,128,128]{3,2,1,0:T(8,128)(2,1)} %copy-done.35, f32[4,2,128,128]{2,3,1,0:T(8,128)} %fusion.54, f32[4,2,128,128]{2,3,1,0:T(8,128)} %copy-done.58, f32[4,2,128]{2,1,0:T(2,128)S(1)} %get-tuple-element.114, pred[128,128]{0,1:T(8,128)(4,1)S(1)} %copy-done.43), kind=kOutput, calls=%fused_computation.49 | convolution fusion | flops 35259520 | bytes 1593344 | tf_op jit(solution)/shard_map/kgij,kgid->kjd/dot_general | solution.py:272
  179.2 2.2 %convolution_multiply_fusion.1 = f32[4,2,128,128]{3,2,1,0:T(8,128)S(1)} fusion(f32[4,2,128,128]{2,3,1,0:T(8,128)} %fusion.54, f32[4,2,128,128]{2,3,1,0:T(8,128)} %copy-done.58, bf16[4,128,64]{2,1,0:T(8,128)(2,1)} %get-tuple-element.105, bf16[4,128,64]{2,1,0:T(8,128)(2,1)} %get-tuple-element.104, f32[4,2,128]{2,1,0:T(2,128)} %copy-done.59, ...), kind=kOutput, calls=%fused_computation.25 | convolution fusion | flops 35652736 | bytes 1724416 | tf_op jit(solution)/shard_map/kgij,kjd->kgid/dot_general | solution.py:268
  183.4 1.7 copy.74
  186.9 4.1 %fusion.40 = f32[128,2304]{1,0:T(8,128)S(1)} fusion(bf16[1024,2304]{0,1:T(8,128)(2,1)} %fusion.29, bf16[16,8,8,128]{3,2,1,0:T(8,128)(2,1)S(1)} %bitcast.325), kind=kOutput, calls=%fused_computation.202 | convolution fusion | flops 603979776 | bytes 6160384 | tf_op jit(solution)/shard_map/dot_general | solution.py:282
  198.7 1.5 fusion.14
  200.2 2.9 %fusion.13 = bf16[128,2304]{1,0:T(8,128)(2,1)} fusion(bf16[128,2304]{1,0:T(8,128)(2,1)} %collective-permute-done.29, bf16[128,2304]{1,0:T(8,128)(2,1)S(1)} %fusion.1, f32[128]{0:T(128)S(1)} %broadcast_multiply_fusion, f32[128]{0:T(128)} %get-tuple-element.108, f32[2304]{0:T(1024)S(1)} %mul.519, f32[128]{0:T(128)} %copy-done.49, ...), kind=kLoop, calls=%fused_computation.36 | loop fusion | flops 6488064 | bytes 4742912 | tf_op jit(solution)/shard_map/convert_element_type | solution.py:294
  203.1 1.4 copy.76
  205.7 15.4 %all_to_all.21 = bf16[8,16,1152]{2,1,0:T(8,128)(2,1)S(1)} all-to-all(bf16[8,16,1152]{2,1,0:T(8,128)(2,1)S(1)} %broadcast_select_fusion.30), channel_id=1, replica_groups=mesh['groups'=2,'seq'=8,'wg'=2] {'seq'}, dimensions={0} | all-to-all | bytes 589824 | tf_op jit(solution)/shard_map/all_to_all | solution.py:296
  (316 shorter events, 76.1 us)
Async XLA Ops:
  1.4 11.2 %copy-start.44 = (f32[2304]{0:T(1024)S(1)}, f32[2304]{0:T(1024)}, u32[]{:S(2)}) copy-start(f32[2304]{0:T(1024)} %param.12) | copy-start | bytes 27652
  1.4 11.2 %copy-start.45 = (f32[2304]{0:T(1024)S(1)}, f32[2304]{0:T(1024)}, u32[]{:S(2)}) copy-start(f32[2304]{0:T(1024)} %param.17) | copy-start | bytes 27652
  1.4 11.3 %copy-start.46 = (f32[2304]{0:T(1024)S(1)}, f32[2304]{0:T(1024)}, u32[]{:S(2)}) copy-start(f32[2304]{0:T(1024)} %param.18) | copy-start | bytes 27652
  1.5 12.5 %copy-start.55 = (s32[8]{0:T(128)S(1)}, s32[8]{0:T(128)}, u32[]{:S(2)}) copy-start(s32[8]{0:T(128)} %param.20) | copy-start | bytes 100
  1.5 15.1 %copy-start.33 = (bf16[64,2304]{1,0:T(8,128)(2,1)S(1)}, bf16[64,2304]{1,0:T(8,128)(2,1)}, u32[]{:S(2)}) copy-start(bf16[64,2304]{1,0:T(8,128)(2,1)} %param.19) | copy-start | bytes 884740
  2.3 21.3 %collective-permute-start = (bf16[2,288,512]{2,1,0:T(8,128)(2,1)}, bf16[2,288,512]{2,1,0:T(8,128)(2,1)}, u32[]{:S(2)}, u32[]{:S(2)}) collective-permute-start(bf16[2,288,512]{2,1,0:T(8,128)(2,1)} %pad_maximum_fusion.14), channel_id=1, source_target_pairs={{0,4},{4,8},{8,12},{12,14},{14,10},{10,6},{6,2},{2,0},{1,5},{5,9},... | collective-permute-start | bytes 1769480 | tf_op jit(solution)/shard_map/ppermute | solution.py:105
  6.2 17.4 %collective-permute-start.1 = (bf16[2,288,512]{2,1,0:T(8,128)(2,1)}, bf16[2,288,512]{2,1,0:T(8,128)(2,1)}, u32[]{:S(2)}, u32[]{:S(2)}) collective-permute-start(bf16[2,288,512]{2,1,0:T(8,128)(2,1)} %pad_maximum_fusion.15), channel_id=1, source_target_pairs={{0,2},{4,0},{8,4},{12,8},{14,12},{10,14},{6,10},{2,6},{1,3},{5,1},... | collective-permute-start | bytes 1769480 | tf_op jit(solution)/shard_map/ppermute | solution.py:106
  6.2 24.8 %all-to-all-start = ((bf16[8,16,1152]{2,1,0:T(8,128)(2,1)}), bf16[8,16,1152]{2,1,0:T(8,128)(2,1)}, u32[]{:S(2)}, u32[]{:S(2)}) async-start(bf16[8,16,1152]{2,1,0:T(8,128)(2,1)} %bitcast.1), calls=%async_computation | async-start | bytes 589824 | tf_op jit(solution)/shard_map/all_to_all | solution.py:151
  13.9 156.3 %copy-start.42 = (pred[2304]{0:T(1024)(128)(4,1)}, pred[2304]{0:T(1024)(128)(4,1)S(1)}, u32[]{:S(2)}) copy-start(pred[2304]{0:T(1024)(128)(4,1)S(1)} %broadcast_in_dim.117) | copy-start | bytes 6916
  22.5 119.4 %copy-start.21 = (f32[128,64]{1,0:T(8,128)}, f32[128,64]{1,0:T(8,128)S(1)}, u32[]{:S(2)}) copy-start(f32[128,64]{1,0:T(8,128)S(1)} %get-tuple-element.106) | copy-start | bytes 98308
  22.5 119.4 %copy-start.23 = (f32[128,64]{1,0:T(8,128)}, f32[128,64]{1,0:T(8,128)S(1)}, u32[]{:S(2)}) copy-start(f32[128,64]{1,0:T(8,128)S(1)} %get-tuple-element.107) | copy-start | bytes 98308
  25.6 12.9 %collective-permute-start.3 = (bf16[288,512]{1,0:T(8,128)(2,1)}, bf16[288,512]{1,0:T(8,128)(2,1)}, u32[]{:S(2)}, u32[]{:S(2)}) collective-permute-start(bf16[288,512]{1,0:T(8,128)(2,1)} %get-tuple-element.93), channel_id=1, source_target_pairs={{0,16},{16,0},{1,17},{17,1},{2,18},{18,2},{3,19},{19,3},{4,20},{20... | collective-permute-start | bytes 884744 | tf_op jit(solution)/shard_map/ppermute | solution.py:110
  28.9 11.2 %collective-permute-start.2 = (bf16[288,512]{1,0:T(8,128)(2,1)}, bf16[288,512]{1,0:T(8,128)(2,1)}, u32[]{:S(2)}, u32[]{:S(2)}) collective-permute-start(bf16[288,512]{1,0:T(8,128)(2,1)} %get-tuple-element.95), channel_id=1, source_target_pairs={{0,16},{16,0},{1,17},{17,1},{2,18},{18,2},{3,19},{19,3},{4,20},{20... | collective-permute-start | bytes 884744 | tf_op jit(solution)/shard_map/ppermute | solution.py:110
  36.0 19.0 %collective-permute-start.4 = (bf16[2,288,512]{2,1,0:T(8,128)(2,1)}, bf16[2,288,512]{2,1,0:T(8,128)(2,1)S(1)}, u32[]{:S(2)}, u32[]{:S(2)}) collective-permute-start(bf16[2,288,512]{2,1,0:T(8,128)(2,1)} %collective-permute-done), channel_id=1, source_target_pairs={{0,4},{4,8},{8,12},{12,14},{14,10},{10,6},{6,2},{2,0},{1,5},{5,9},... | collective-permute-start | bytes 1769480 | tf_op jit(solution)/shard_map/ppermute | solution.py:105
  38.1 15.3 %collective-permute-start.5 = (bf16[2,288,512]{2,1,0:T(8,128)(2,1)}, bf16[2,288,512]{2,1,0:T(8,128)(2,1)S(1)}, u32[]{:S(2)}, u32[]{:S(2)}) collective-permute-start(bf16[2,288,512]{2,1,0:T(8,128)(2,1)} %collective-permute-done.1), channel_id=1, source_target_pairs={{0,2},{4,0},{8,4},{12,8},{14,12},{10,14},{6,10},{2,6},{1,3},{5,1},... | collective-permute-start | bytes 1769480 | tf_op jit(solution)/shard_map/ppermute | solution.py:106
  39.7 118.8 %copy-start.2 = (bf16[288,1536]{1,0:T(8,128)(2,1)}, bf16[288,1536]{1,0:T(8,128)(2,1)S(1)}, u32[]{:S(2)}) copy-start(bf16[288,1536]{1,0:T(8,128)(2,1)S(1)} %pad_maximum_fusion.3) | copy-start | bytes 2654212
  53.5 10.0 %collective-permute-start.7 = (bf16[288,512]{1,0:T(8,128)(2,1)S(1)}, bf16[288,512]{1,0:T(8,128)(2,1)S(1)}, u32[]{:S(2)}, u32[]{:S(2)}) collective-permute-start(bf16[288,512]{1,0:T(8,128)(2,1)S(1)} %get-tuple-element.89), channel_id=1, source_target_pairs={{0,16},{16,0},{1,17},{17,1},{2,18},{18,2},{3,19},{19,3},{4,20},{20... | collective-permute-start | bytes 884744 | tf_op jit(solution)/shard_map/ppermute | solution.py:110
  55.1 12.7 %collective-permute-start.6 = (bf16[288,512]{1,0:T(8,128)(2,1)S(1)}, bf16[288,512]{1,0:T(8,128)(2,1)S(1)}, u32[]{:S(2)}, u32[]{:S(2)}) collective-permute-start(bf16[288,512]{1,0:T(8,128)(2,1)S(1)} %get-tuple-element.91), channel_id=1, source_target_pairs={{0,16},{16,0},{1,17},{17,1},{2,18},{18,2},{3,19},{19,3},{4,20},{20... | collective-permute-start | bytes 884744 | tf_op jit(solution)/shard_map/ppermute | solution.py:110
  55.8 13.7 %collective-permute-start.8 = (bf16[2,288,512]{2,1,0:T(8,128)(2,1)S(1)}, bf16[2,288,512]{2,1,0:T(8,128)(2,1)S(1)}, u32[]{:S(2)}, u32[]{:S(2)}) collective-permute-start(bf16[2,288,512]{2,1,0:T(8,128)(2,1)S(1)} %collective-permute-done.4), channel_id=1, source_target_pairs={{0,4},{4,8},{8,12},{12,14},{14,10},{10,6},{6,2},{2,0},{1,5},{5,9},... | collective-permute-start | bytes 1769480 | tf_op jit(solution)/shard_map/ppermute | solution.py:105
  57.3 13.8 %collective-permute-start.9 = (bf16[2,288,512]{2,1,0:T(8,128)(2,1)S(1)}, bf16[2,288,512]{2,1,0:T(8,128)(2,1)S(1)}, u32[]{:S(2)}, u32[]{:S(2)}) collective-permute-start(bf16[2,288,512]{2,1,0:T(8,128)(2,1)S(1)} %collective-permute-done.5), channel_id=1, source_target_pairs={{0,2},{4,0},{8,4},{12,8},{14,12},{10,14},{6,10},{2,6},{1,3},{5,1},... | collective-permute-start | bytes 1769480 | tf_op jit(solution)/shard_map/ppermute | solution.py:106
  63.6 84.4 %copy-start.3 = (bf16[288,1536]{1,0:T(8,128)(2,1)}, bf16[288,1536]{1,0:T(8,128)(2,1)S(1)}, u32[]{:S(2)}) copy-start(bf16[288,1536]{1,0:T(8,128)(2,1)S(1)} %pad_maximum_fusion.5) | copy-start | bytes 2654212
  69.5 9.6 %collective-permute-start.10 = (bf16[288,512]{1,0:T(8,128)(2,1)S(1)}, bf16[288,512]{1,0:T(8,128)(2,1)S(1)}, u32[]{:S(2)}, u32[]{:S(2)}) collective-permute-start(bf16[288,512]{1,0:T(8,128)(2,1)S(1)} %get-tuple-element.87), channel_id=1, source_target_pairs={{0,16},{16,0},{1,17},{17,1},{2,18},{18,2},{3,19},{19,3},{4,20},{20... | collective-permute-start | bytes 884744 | tf_op jit(solution)/shard_map/ppermute | solution.py:110
  71.2 11.2 %collective-permute-start.11 = (bf16[288,512]{1,0:T(8,128)(2,1)S(1)}, bf16[288,512]{1,0:T(8,128)(2,1)S(1)}, u32[]{:S(2)}, u32[]{:S(2)}) collective-permute-start(bf16[288,512]{1,0:T(8,128)(2,1)S(1)} %get-tuple-element.85), channel_id=1, source_target_pairs={{0,16},{16,0},{1,17},{17,1},{2,18},{18,2},{3,19},{19,3},{4,20},{20... | collective-permute-start | bytes 884744 | tf_op jit(solution)/shard_map/ppermute | solution.py:110
  72.4 12.2 %collective-permute-start.12 = (bf16[2,288,512]{2,1,0:T(8,128)(2,1)S(1)}, bf16[2,288,512]{2,1,0:T(8,128)(2,1)S(1)}, u32[]{:S(2)}, u32[]{:S(2)}) collective-permute-start(bf16[2,288,512]{2,1,0:T(8,128)(2,1)S(1)} %collective-permute-done.8), channel_id=1, source_target_pairs={{0,4},{4,8},{8,12},{12,14},{14,10},{10,6},{6,2},{2,0},{1,5},{5,9},... | collective-permute-start | bytes 1769480 | tf_op jit(solution)/shard_map/ppermute | solution.py:105
  73.9 11.9 %collective-permute-start.13 = (bf16[2,288,512]{2,1,0:T(8,128)(2,1)S(1)}, bf16[2,288,512]{2,1,0:T(8,128)(2,1)S(1)}, u32[]{:S(2)}, u32[]{:S(2)}) collective-permute-start(bf16[2,288,512]{2,1,0:T(8,128)(2,1)S(1)} %collective-permute-done.9), channel_id=1, source_target_pairs={{0,2},{4,0},{8,4},{12,8},{14,12},{10,14},{6,10},{2,6},{1,3},{5,1},... | collective-permute-start | bytes 1769480 | tf_op jit(solution)/shard_map/ppermute | solution.py:106
  82.4 65.3 %copy-start.5 = (bf16[288,1536]{1,0:T(8,128)(2,1)}, bf16[288,1536]{1,0:T(8,128)(2,1)S(1)}, u32[]{:S(2)}) copy-start(bf16[288,1536]{1,0:T(8,128)(2,1)S(1)} %pad_maximum_fusion.7) | copy-start | bytes 2654212
  84.7 8.2 %collective-permute-start.14 = (bf16[288,512]{1,0:T(8,128)(2,1)S(1)}, bf16[288,512]{1,0:T(8,128)(2,1)S(1)}, u32[]{:S(2)}, u32[]{:S(2)}) collective-permute-start(bf16[288,512]{1,0:T(8,128)(2,1)S(1)} %get-tuple-element.83), channel_id=1, source_target_pairs={{0,16},{16,0},{1,17},{17,1},{2,18},{18,2},{3,19},{19,3},{4,20},{20... | collective-permute-start | bytes 884744 | tf_op jit(solution)/shard_map/ppermute | solution.py:110
  85.8 11.1 %collective-permute-start.15 = (bf16[288,512]{1,0:T(8,128)(2,1)S(1)}, bf16[288,512]{1,0:T(8,128)(2,1)S(1)}, u32[]{:S(2)}, u32[]{:S(2)}) collective-permute-start(bf16[288,512]{1,0:T(8,128)(2,1)S(1)} %get-tuple-element.81), channel_id=1, source_target_pairs={{0,16},{16,0},{1,17},{17,1},{2,18},{18,2},{3,19},{19,3},{4,20},{20... | collective-permute-start | bytes 884744 | tf_op jit(solution)/shard_map/ppermute | solution.py:110
  87.0 11.6 %collective-permute-start.16 = (bf16[2,288,512]{2,1,0:T(8,128)(2,1)S(1)}, bf16[2,288,512]{2,1,0:T(8,128)(2,1)S(1)}, u32[]{:S(2)}, u32[]{:S(2)}) collective-permute-start(bf16[2,288,512]{2,1,0:T(8,128)(2,1)S(1)} %collective-permute-done.12), channel_id=1, source_target_pairs={{0,4},{4,8},{8,12},{12,14},{14,10},{10,6},{6,2},{2,0},{1,5},{5,9},... | collective-permute-start | bytes 1769480 | tf_op jit(solution)/shard_map/ppermute | solution.py:105
  88.5 11.4 %collective-permute-start.17 = (bf16[2,288,512]{2,1,0:T(8,128)(2,1)S(1)}, bf16[2,288,512]{2,1,0:T(8,128)(2,1)S(1)}, u32[]{:S(2)}, u32[]{:S(2)}) collective-permute-start(bf16[2,288,512]{2,1,0:T(8,128)(2,1)S(1)} %collective-permute-done.13), channel_id=1, source_target_pairs={{0,2},{4,0},{8,4},{12,8},{14,12},{10,14},{6,10},{2,6},{1,3},{5,1},... | collective-permute-start | bytes 1769480 | tf_op jit(solution)/shard_map/ppermute | solution.py:106
  97.1 49.7 %copy-start.7 = (bf16[288,1536]{1,0:T(8,128)(2,1)}, bf16[288,1536]{1,0:T(8,128)(2,1)S(1)}, u32[]{:S(2)}) copy-start(bf16[288,1536]{1,0:T(8,128)(2,1)S(1)} %pad_maximum_fusion.9) | copy-start | bytes 2654212
  98.6 6.9 %collective-permute-start.18 = (bf16[288,512]{1,0:T(8,128)(2,1)S(1)}, bf16[288,512]{1,0:T(8,128)(2,1)S(1)}, u32[]{:S(2)}, u32[]{:S(2)}) collective-permute-start(bf16[288,512]{1,0:T(8,128)(2,1)S(1)} %get-tuple-element.79), channel_id=1, source_target_pairs={{0,16},{16,0},{1,17},{17,1},{2,18},{18,2},{3,19},{19,3},{4,20},{20... | collective-permute-start | bytes 884744 | tf_op jit(solution)/shard_map/ppermute | solution.py:110
  99.9 10.4 %collective-permute-start.19 = (bf16[288,512]{1,0:T(8,128)(2,1)S(1)}, bf16[288,512]{1,0:T(8,128)(2,1)S(1)}, u32[]{:S(2)}, u32[]{:S(2)}) collective-permute-start(bf16[288,512]{1,0:T(8,128)(2,1)S(1)} %get-tuple-element.77), channel_id=1, source_target_pairs={{0,16},{16,0},{1,17},{17,1},{2,18},{18,2},{3,19},{19,3},{4,20},{20... | collective-permute-start | bytes 884744 | tf_op jit(solution)/shard_map/ppermute | solution.py:110
  101.1 11.7 %collective-permute-start.20 = (bf16[2,288,512]{2,1,0:T(8,128)(2,1)S(1)}, bf16[2,288,512]{2,1,0:T(8,128)(2,1)S(1)}, u32[]{:S(2)}, u32[]{:S(2)}) collective-permute-start(bf16[2,288,512]{2,1,0:T(8,128)(2,1)S(1)} %collective-permute-done.16), channel_id=1, source_target_pairs={{0,4},{4,8},{8,12},{12,14},{14,10},{10,6},{6,2},{2,0},{1,5},{5,9},... | collective-permute-start | bytes 1769480 | tf_op jit(solution)/shard_map/ppermute | solution.py:105
  102.5 13.3 %collective-permute-start.21 = (bf16[2,288,512]{2,1,0:T(8,128)(2,1)S(1)}, bf16[2,288,512]{2,1,0:T(8,128)(2,1)S(1)}, u32[]{:S(2)}, u32[]{:S(2)}) collective-permute-start(bf16[2,288,512]{2,1,0:T(8,128)(2,1)S(1)} %collective-permute-done.17), channel_id=1, source_target_pairs={{0,2},{4,0},{8,4},{12,8},{14,12},{10,14},{6,10},{2,6},{1,3},{5,1},... | collective-permute-start | bytes 1769480 | tf_op jit(solution)/shard_map/ppermute | solution.py:106
  110.4 35.3 %copy-start.9 = (bf16[288,1536]{1,0:T(8,128)(2,1)}, bf16[288,1536]{1,0:T(8,128)(2,1)S(1)}, u32[]{:S(2)}) copy-start(bf16[288,1536]{1,0:T(8,128)(2,1)S(1)} %pad_maximum_fusion.11) | copy-start | bytes 2654212
  112.9 6.8 %collective-permute-start.22 = (bf16[288,512]{1,0:T(8,128)(2,1)S(1)}, bf16[288,512]{1,0:T(8,128)(2,1)S(1)}, u32[]{:S(2)}, u32[]{:S(2)}) collective-permute-start(bf16[288,512]{1,0:T(8,128)(2,1)S(1)} %get-tuple-element.75), channel_id=1, source_target_pairs={{0,16},{16,0},{1,17},{17,1},{2,18},{18,2},{3,19},{19,3},{4,20},{20... | collective-permute-start | bytes 884744 | tf_op jit(solution)/shard_map/ppermute | solution.py:110
  115.8 7.4 %collective-permute-start.23 = (bf16[288,512]{1,0:T(8,128)(2,1)S(1)}, bf16[288,512]{1,0:T(8,128)(2,1)S(1)}, u32[]{:S(2)}, u32[]{:S(2)}) collective-permute-start(bf16[288,512]{1,0:T(8,128)(2,1)S(1)} %get-tuple-element.73), channel_id=1, source_target_pairs={{0,16},{16,0},{1,17},{17,1},{2,18},{18,2},{3,19},{19,3},{4,20},{20... | collective-permute-start | bytes 884744 | tf_op jit(solution)/shard_map/ppermute | solution.py:110
  117.2 9.9 %collective-permute-start.25 = (bf16[2,288,512]{2,1,0:T(8,128)(2,1)S(1)}, bf16[2,288,512]{2,1,0:T(8,128)(2,1)S(1)}, u32[]{:S(2)}, u32[]{:S(2)}) collective-permute-start(bf16[2,288,512]{2,1,0:T(8,128)(2,1)S(1)} %collective-permute-done.21), channel_id=1, source_target_pairs={{0,2},{4,0},{8,4},{12,8},{14,12},{10,14},{6,10},{2,6},{1,3},{5,1},... | collective-permute-start | bytes 1769480 | tf_op jit(solution)/shard_map/ppermute | solution.py:106
  117.5 9.9 %collective-permute-start.24 = (bf16[2,288,512]{2,1,0:T(8,128)(2,1)S(1)}, bf16[2,288,512]{2,1,0:T(8,128)(2,1)S(1)}, u32[]{:S(2)}, u32[]{:S(2)}) collective-permute-start(bf16[2,288,512]{2,1,0:T(8,128)(2,1)S(1)} %collective-permute-done.20), channel_id=1, source_target_pairs={{0,4},{4,8},{8,12},{12,14},{14,10},{10,6},{6,2},{2,0},{1,5},{5,9},... | collective-permute-start | bytes 1769480 | tf_op jit(solution)/shard_map/ppermute | solution.py:105
  123.4 21.4 %copy-start.11 = (bf16[288,1536]{1,0:T(8,128)(2,1)}, bf16[288,1536]{1,0:T(8,128)(2,1)S(1)}, u32[]{:S(2)}) copy-start(bf16[288,1536]{1,0:T(8,128)(2,1)S(1)} %pad_maximum_fusion.13) | copy-start | bytes 2654212
  127.1 16.1 %copy-start.13 = (bf16[2,288,512]{2,1,0:T(8,128)(2,1)}, bf16[2,288,512]{2,1,0:T(8,128)(2,1)S(1)}, u32[]{:S(2)}) copy-start(bf16[2,288,512]{2,1,0:T(8,128)(2,1)S(1)} %collective-permute-done.25) | copy-start | bytes 1769476
  128.1 14.6 %collective-permute-start.27 = (bf16[288,512]{1,0:T(8,128)(2,1)S(1)}, bf16[288,512]{1,0:T(8,128)(2,1)S(1)}, u32[]{:S(2)}, u32[]{:S(2)}) collective-permute-start(bf16[288,512]{1,0:T(8,128)(2,1)S(1)} %get-tuple-element.69), channel_id=1, source_target_pairs={{0,16},{16,0},{1,17},{17,1},{2,18},{18,2},{3,19},{19,3},{4,20},{20... | collective-permute-start | bytes 884744 | tf_op jit(solution)/shard_map/ppermute | solution.py:110
  129.6 8.4 %collective-permute-start.26 = (bf16[288,512]{1,0:T(8,128)(2,1)S(1)}, bf16[288,512]{1,0:T(8,128)(2,1)S(1)}, u32[]{:S(2)}, u32[]{:S(2)}) collective-permute-start(bf16[288,512]{1,0:T(8,128)(2,1)S(1)} %get-tuple-element.70), channel_id=1, source_target_pairs={{0,16},{16,0},{1,17},{17,1},{2,18},{18,2},{3,19},{19,3},{4,20},{20... | collective-permute-start | bytes 884744 | tf_op jit(solution)/shard_map/ppermute | solution.py:110
  130.4 9.7 %copy-start.1 = (bf16[1024,2304]{0,1:T(8,128)(2,1)}, bf16[1024,2304]{0,1:T(8,128)(2,1)S(1)}, u32[]{:S(2)}) copy-start(bf16[1024,2304]{0,1:T(8,128)(2,1)S(1)} %bitcast_dynamic-update-slice_fusion) | copy-start | bytes 14155780
  160.2 16.3 %copy-start.59 = (f32[4,2,128]{2,1,0:T(2,128)}, f32[4,2,128]{2,1,0:T(2,128)S(1)}, u32[]{:S(2)}) copy-start(f32[4,2,128]{2,1,0:T(2,128)S(1)} %get-tuple-element.114) | copy-start | bytes 12292
  163.8 3.5 %collective-permute-start.28 = (bf16[128,2304]{1,0:T(8,128)(2,1)S(1)}, bf16[128,2304]{1,0:T(8,128)(2,1)S(1)}, u32[]{:S(2)}, u32[]{:S(2)}) collective-permute-start(bf16[128,2304]{1,0:T(8,128)(2,1)S(1)} %convolution_convert_fusion), channel_id=1, source_target_pairs={{0,1},{1,0},{2,3},{3,2},{4,5},{5,4},{6,7},{7,6},{8,9},{9,8},{10,11... | collective-permute-start | bytes 1769480 | tf_op jit(solution)/shard_map/ppermute | solution.py:58
  193.7 5.0 %collective-permute-start.29 = (bf16[128,2304]{1,0:T(8,128)(2,1)S(1)}, bf16[128,2304]{1,0:T(8,128)(2,1)}, u32[]{:S(2)}, u32[]{:S(2)}) collective-permute-start(bf16[128,2304]{1,0:T(8,128)(2,1)S(1)} %fusion.1), channel_id=1, source_target_pairs={{0,1},{1,0},{2,3},{3,2},{4,5},{5,4},{6,7},{7,6},{8,9},{9,8},{10,11... | collective-permute-start | bytes 1769480 | tf_op jit(solution)/shard_map/ppermute | solution.py:58
  (43 other events, 121.3 us)
